TPU v7x, 256 devices: a whole 4x4x8 slice. The times are simulated.
256 devices in a mesh: gx: 8 (over x, core), yz: 32 (over z, y).
Axes of the slice: x: 4, y: 4, z: 8, core: 2. Of those that a mesh axis runs over, the one named last changes fastest.
Arguments:
- velocity: float32 [3, 256, 512, 128], P(None, 'gx', 'yz'), may hold values from -6 to 6
- old_pressure: float32 [256, 512, 128], P('gx', 'yz'), may hold values from -3 to 3
- delta_weight: bfloat16 [8, 1024, 128, 128], P('gx', 'yz'), may hold values from -0.5 to 0.5
- marker_target: float32 [8, 1024, 3, 128], P('gx', 'yz'), may hold values from -6 to 6
- pair_owner: int32 [8, 1024, 1], P('gx', 'yz'), may hold values from 0 to 31; in each aligned block of 32 rows (0 to 31, 32 to 63, ..., all dimensions but the last counted through in order) at most 4 rows name the same one
- pair_grain: int32 [8, 1024], P('gx', 'yz'), may hold values from 0 to 31
- box_anchor: int32 [8, 1024, 3], P('gx', 'yz'), may hold values from 0 to 120, as said below
Outputs:
- new_velocity: float32 [3, 256, 512, 128], P(None, 'gx', 'yz')
- pressure: float32 [256, 512, 128], P('gx', 'yz')
Inputs may be any that keep to these rules, and one draw needn't show every extreme that they name: Block r of slab i lies on tile r // 32 of that slab; its grain is owned by tile pair_owner of the same slab. Among the 32 blocks of one tile at most 4 name the same owner, and some tile reaches 4. `pair_grain`: blocks of one slab with equal owner and grain slot belong to one grain. `box_anchor`: column 0 is at most 28, column 1 at most 12, column 2 at most 120, and each of these is reached, so every box lies inside its tile.
All inputs are finite; a program needn't handle non-finite values.
Results may differ from a plain program's by a relative error of at most 0.002.
Values may be sent and summed in bfloat16 or wider, within the bound.
No kernel may reach another device: no remote copies, remote signals or barrier semaphores. Data moves between devices by JAX's collectives and lax.ppermute only.
A program may use at most 128 MiB of HBM per device.

v0:
```python
import jax
import jax.numpy as jnp
from jax import lax
from jax.sharding import PartitionSpec as P

BX = 4
BZ = 4
BY = 8


step_size = 0.1
viscosity = 1.5


def extended(block, sides, width):
    for axis, dim in sides:
        count = lax.axis_size(axis)
        forward = [(i, i + 1) for i in range(count - 1)]
        forward.append((count - 1, 0))
        backward = [(target, source) for source, target in forward]
        low = lax.ppermute(
            lax.slice_in_dim(block, block.shape[dim] - width, None, axis=dim), axis, forward
        )
        high = lax.ppermute(lax.slice_in_dim(block, 0, width, axis=dim), axis, backward)
        block = jnp.concatenate([low, block, high], axis=dim)
    return block


def inner(padded):
    return padded[..., 1:-1, 1:-1, :]


def along_x(padded):
    return 0.5 * (padded[..., 2:, 1:-1, :] - padded[..., :-2, 1:-1, :])


def along_z(padded):
    return 0.5 * (padded[..., 1:-1, 2:, :] - padded[..., 1:-1, :-2, :])


def along_y(field):
    return 0.5 * (jnp.roll(field, -1, -1) - jnp.roll(field, 1, -1))


def neighbours(padded):
    middle = inner(padded)
    total = padded[..., 2:, 1:-1, :] + padded[..., :-2, 1:-1, :]
    total = total + padded[..., 1:-1, 2:, :] + padded[..., 1:-1, :-2, :]
    return total + jnp.roll(middle, 1, -1) + jnp.roll(middle, -1, -1)


def gradient_of(padded):
    middle = inner(padded)
    return jnp.stack([along_x(padded), along_y(middle), along_z(padded)])


def predict(flow_padded):
    velocity_padded = flow_padded[:3]
    pressure_padded = flow_padded[3]
    current = inner(velocity_padded)
    laplace = neighbours(velocity_padded) - 6.0 * current
    advect = current[0] * along_x(velocity_padded)
    return current + step_size * (viscosity * laplace - advect) - gradient_of(pressure_padded)


def kernel_box_cells(anchors, box_x, box_z, box_y):
    steps_x = jnp.arange(box_x, dtype=jnp.int32)
    steps_z = jnp.arange(box_z, dtype=jnp.int32)
    steps_y = jnp.arange(box_y, dtype=jnp.int32)
    cell_x = anchors[:, 0, None, None, None] + steps_x[None, :, None, None]
    cell_z = anchors[:, 1, None, None, None] + steps_z[None, None, :, None]
    cell_y = anchors[:, 2, None, None, None] + steps_y[None, None, None, :]
    return (cell_x, cell_z, cell_y)


def walls(padded, vertical_dim):
    tile_index = lax.axis_index("yz")
    tile_total = lax.axis_size("yz")
    extent = padded.shape[vertical_dim]
    position = lax.broadcasted_iota(jnp.int32, padded.shape, vertical_dim)
    bottom_rim = jnp.logical_and(position == 0, tile_index == 0)
    top_rim = jnp.logical_and(position == extent - 1, tile_index == tile_total - 1)
    return jnp.where(jnp.logical_or(bottom_rim, top_rim), jnp.zeros((), padded.dtype), padded)


def pressure_cycle(pressure):
    padded = extended(pressure, (("gx", 0), ("yz", 1)), 1)
    return walls(padded, 1)


def body(velocity, old_pressure, delta_weight, marker_target, pair_owner, pair_grain, box_anchor):
    flow_fields = jnp.concatenate([velocity, old_pressure[None]], 0)
    flow_padded = walls(extended(flow_fields, (("gx", 1), ("yz", 2)), 1), 2)
    predicted = predict(flow_padded)
    anchors = box_anchor[0]
    owners = pair_owner[0, :, 0]
    grains = pair_grain[0]
    delta_weights = delta_weight[0]
    grain_slots = marker_target.shape[1]
    pair_total = anchors.shape[0]
    cell_x, cell_z, cell_y = kernel_box_cells(anchors, BX, BZ, BY)
    kernel_box_values = (
        predicted[:, cell_x, cell_z, cell_y].astype(jnp.bfloat16).reshape(3, pair_total, -1)
    )
    partial_force_value = jnp.einsum(
        "eky,iey->eik", delta_weights, kernel_box_values, preferred_element_type=jnp.float32
    )
    row_width = partial_force_value.shape[1] * partial_force_value.shape[2]
    flat_partial = partial_force_value.reshape(pair_total, row_width)
    targets = marker_target[0].reshape(grain_slots, row_width)
    slot_numbers = jnp.arange(grain_slots, dtype=jnp.int32)
    all_partial, all_owner, all_grain = (
        lax.all_gather(flat_partial, "yz", axis=0, tiled=True),
        lax.all_gather(owners, "yz", axis=0, tiled=True),
        lax.all_gather(grains, "yz", axis=0, tiled=True),
    )
    own_tile = lax.axis_index("yz")
    grain_keys = jnp.where(all_owner == own_tile, all_grain, grain_slots)
    select = (grain_keys[None, :] == slot_numbers[:, None]).astype(jnp.float32)
    summed = jnp.dot(
        select, all_partial, precision=lax.Precision.HIGHEST, preferred_element_type=jnp.float32
    )
    grain_force = (targets - summed).astype(jnp.bfloat16)
    all_force = lax.all_gather(grain_force, "yz", axis=0, tiled=True)
    marker_pair_force = jnp.take(all_force, owners * grain_slots + grains, axis=0)
    spread_force = jnp.einsum(
        "zwx,znw->nzx",
        delta_weights,
        marker_pair_force.reshape(pair_total, 3, -1),
        preferred_element_type=jnp.float32,
    )
    spread_force = spread_force.reshape(3, pair_total, BX, BZ, BY)
    forced_velocity = predicted + jnp.zeros_like(predicted).at[:, cell_x, cell_z, cell_y].add(
        spread_force
    )
    forced_padded = walls(extended(forced_velocity, (("gx", 1), ("yz", 2)), 1), 2)
    divergence = along_x(forced_padded[0]) + along_y(forced_velocity[1]) + along_z(forced_padded[2])
    first_padded = pressure_cycle(old_pressure)
    pressure = (neighbours(first_padded) - divergence) / 6.0
    pressure = (neighbours(pressure_cycle(pressure)) - divergence) / 6.0
    new_velocity = forced_velocity - gradient_of(pressure_cycle(pressure))
    return (new_velocity, pressure)


def solution(mesh):
    placed = (
        P(None, "gx", "yz", None),
        P("gx", "yz", None),
        P("gx", "yz", None, None),
        P("gx", "yz", None, None),
        P("gx", "yz", None),
        P("gx", "yz"),
        P("gx", "yz", None),
    )
    return jax.shard_map(
        body,
        mesh=mesh,
        in_specs=placed,
        out_specs=(P(None, "gx", "yz", None), P("gx", "yz", None)),
        check_vma=False,
    )
```

profile of v0, /device:TPU:1, one launch (start us, length us, event | category | flops | bytes accessed | tf_op | source)
XLA Modules:
  0.0 357.0 jit_solution(16332044363483749540)
XLA Ops:
  7.2 0.9 pad_maximum_fusion.6
  8.2 2.6 collective-permute-start
  10.8 0.6 collective-permute-start.1
  11.4 0.7 copy.560
  12.1 0.6 clamp_shift-left_fusion.1
  12.9 0.6 clamp_shift-left_fusion
  14.2 1.4 collective-permute-start.2
  15.6 6.8 %collective-permute-start.3 = (f32[4,34,1,128]{3,0,2,1:T(4,128)S(1)}, f32[4,34,1,128]{3,0,2,1:T(4,128)S(1)}, u32[]{:S(2)}, u32[]{:S(2)}) collective-permute-start(f32[4,34,1,128]{3,0,2,1:T(4,128)S(1)} %copy.535), channel_id=1, source_target_pairs={{1,0},{2,1},{3,2},{4,3},{5,4},{6,5},{7,6},{8,7},{9,8},{10,9},{11,1... | collective-permute-start | bytes 208904 | tf_op jit(solution)/shard_map/ppermute | solution.py:24
  22.5 1.6 collective-permute-done.2
  24.2 1.3 maximum_select_fusion
  25.6 0.9 fusion.52
  26.5 0.3 slice_reduce_fusion.3
  26.8 0.9 fusion.26
  27.7 1.2 fusion.43
  28.9 1.5 fusion.44
  30.3 0.7 fusion.27
  31.1 0.9 copy.491
  31.9 0.9 copy.493
  32.8 1.5 copy_bitcast_fusion.6
  34.3 1.3 copy_bitcast_fusion.5
  35.9 1.6 fusion.11
  37.6 17.1 %copy.528 = f32[3,32,16,128]{0,3,2,1:T(8,128)} copy(f32[3,32,16,128]{3,2,1,0:T(8,128)} %fusion.11) | data formatting | bytes 1572864
  54.6 43.8 %gather_fusion = bf16[4096,3]{1,0:T(8,128)(2,1)S(1)} fusion(f32[3,32,16,128]{0,3,2,1:T(8,128)} %copy.528, s32[4096]{0:T(1024)S(1)} %reshape.255), kind=kCustom, calls=%fused_computation | custom fusion | bytes 98304 | tf_op jit(solution)/shard_map/gather | solution.py:103
  98.6 0.7 fusion.2
  99.3 0.6 copy.559
  100.0 2.6 collective-permute-start.4
  102.5 0.6 dynamic-slice
  104.0 15.5 %all-reduce.2 = (s32[1024]{0:T(1024)S(1)}, s32[1024]{0:T(1024)S(1)}) all-reduce(s32[1024]{0:T(1024)S(1)} %bitcast_dynamic-update-slice_fusion.1, s32[1024]{0:T(1024)S(1)} %bitcast_dynamic-update-slice_fusion), channel_id=3, replica_groups=mesh['gx'=8,'yz'=32] {'yz'}, use_global_device_ids=true, to_apply=%add.1 | all-reduce | flops 2048 | bytes 16384 | tf_op jit(solution)/shard_map/all_gather | solution.py:115
  120.0 0.9 collective-permute-start.6
  121.0 3.9 %collective-permute-start.7 = (f32[34,1,128]{2,0,1:T(8,128)S(1)}, f32[34,1,128]{2,0,1:T(8,128)S(1)}, u32[]{:S(2)}, u32[]{:S(2)}) collective-permute-start(f32[34,1,128]{2,0,1:T(8,128)S(1)} %get-tuple-element.71), channel_id=1, source_target_pairs={{1,0},{2,1},{3,2},{4,3},{5,4},{6,5},{7,6},{8,7},{9,8},{10,9},{11,1... | collective-permute-start | bytes 52232 | tf_op jit(solution)/shard_map/ppermute | solution.py:24
  125.2 0.2 reshape.269
  125.4 0.8 collective-permute-done.6
  126.4 0.9 fusion.51
  127.3 45.5 %all-gather.4.cloned.1.call-done = f32[1024,384]{1,0:T(8,128)} async-done(((f32[32,384]{1,0:T(8,128)}), f32[1024,384]{1,0:T(8,128)}) %all-gather.4.cloned.1.call-update) | async-done | bytes 1572880 | tf_op jit(solution)/shard_map/all_gather | solution.py:113
  172.8 2.1 fusion
  174.9 36.8 %all_gather.15 = bf16[1024,384]{1,0:T(8,128)(2,1)S(1)} all-gather(bf16[32,384]{1,0:T(8,128)(2,1)S(1)} %fusion), channel_id=1, replica_groups=mesh['gx'=8,'yz'=32] {'yz'}, dimensions={0}, use_global_device_ids=true | all-gather | bytes 811008 | tf_op jit(solution)/shard_map/all_gather | solution.py:124
  211.7 0.6 gather_fusion.1
  212.3 0.4 convolution_bitcast_fusion
  212.7 2.0 copy.532
  214.7 42.0 %scatter_fusion = f32[3,65536]{0,1:T(8,128)} fusion(f32[3,65536]{0,1:T(8,128)} %bitcast.96, s32[4096]{0:T(1024)S(1)} %reshape.269, f32[4096,3]{1,0:T(8,128)} %bitcast.106), kind=kCustom, calls=%fused_computation.2 | custom fusion | flops 12288 | bytes 163840
  256.7 20.3 %slice_reduce_fusion = f32[65536]{0:T(1024)S(1)} fusion(f32[3,65536]{0,1:T(8,128)} %scatter_fusion), kind=kLoop, calls=%fused_computation.3 | loop fusion | bytes 524288 | tf_op jit(solution)/shard_map/slice | solution.py:137
  277.0 18.8 %copy.526 = f32[3,32,16,128]{3,2,1,0:T(8,128)S(1)} copy(f32[3,32,16,128]{0,3,2,1:T(8,128)} %bitcast.97) | data formatting | bytes 1572864 | tf_op jit(solution)/shard_map/scatter-add | solution.py:133
  295.8 18.2 %collective-permute-start.8 = (f32[3,1,16,128]{3,2,1,0:T(8,128)S(1)}, f32[3,1,16,128]{3,2,1,0:T(8,128)S(1)}, u32[]{:S(2)}, u32[]{:S(2)}) collective-permute-start(f32[3,1,16,128]{3,2,1,0:T(8,128)S(1)} %get-tuple-element.48), channel_id=1, source_target_pairs={{0,32},{32,64},{64,96},{96,128},{128,160},{160,192},{192,224},{224... | collective-permute-start | bytes 73736 | tf_op jit(solution)/shard_map/ppermute | solution.py:21
  314.2 0.8 collective-permute-done.8
  315.0 2.3 collective-permute-done.9
  317.6 4.8 %collective-permute-start.11 = (f32[3,34,1,128]{3,2,1,0:T(1,128)S(1)}, f32[3,34,1,128]{3,2,1,0:T(1,128)S(1)}, u32[]{:S(2)}, u32[]{:S(2)}) collective-permute-start(f32[3,34,1,128]{3,2,1,0:T(1,128)S(1)} %get-tuple-element.47), channel_id=1, source_target_pairs={{1,0},{2,1},{3,2},{4,3},{5,4},{6,5},{7,6},{8,7},{9,8},{10,9},{11,1... | collective-permute-start | bytes 156680 | tf_op jit(solution)/shard_map/ppermute | solution.py:24
  322.8 0.3 copy.514
  323.1 0.7 collective-permute-done.10
  324.1 0.7 copy-done.11
  324.9 0.5 fusion.24
  325.4 1.2 collective-permute-start.12
  326.7 0.6 collective-permute-done.12
  327.4 2.3 collective-permute-done.13
  329.7 5.6 %collective-permute-start.15 = (f32[34,1,128]{2,0,1:T(8,128)S(1)}, f32[34,1,128]{2,0,1:T(8,128)S(1)}, u32[]{:S(2)}, u32[]{:S(2)}) collective-permute-start(f32[34,1,128]{2,0,1:T(8,128)S(1)} %get-tuple-element.69), channel_id=1, source_target_pairs={{1,0},{2,1},{3,2},{4,3},{5,4},{6,5},{7,6},{8,7},{9,8},{10,9},{11,1... | collective-permute-start | bytes 52232 | tf_op jit(solution)/shard_map/ppermute | solution.py:24
  335.4 1.1 collective-permute-done.14
  336.8 0.2 fusion.17
  337.1 0.6 collective-permute-start.16
  337.7 1.2 collective-permute-start.17
  338.9 0.6 collective-permute-done.16
  339.5 1.3 collective-permute-done.17
  340.9 5.2 %collective-permute-start.19 = (f32[34,1,128]{2,0,1:T(8,128)S(1)}, f32[34,1,128]{2,0,1:T(8,128)S(1)}, u32[]{:S(2)}, u32[]{:S(2)}) collective-permute-start(f32[34,1,128]{2,0,1:T(8,128)S(1)} %get-tuple-element.67), channel_id=1, source_target_pairs={{1,0},{2,1},{3,2},{4,3},{5,4},{6,5},{7,6},{8,7},{9,8},{10,9},{11,1... | collective-permute-start | bytes 52232 | tf_op jit(solution)/shard_map/ppermute | solution.py:24
  346.1 0.9 copy.527
  347.5 0.3 slice_reduce_fusion.1
  349.2 1.0 maximum_subtract_fusion
  (134 shorter events, 6.4 us)
Async XLA Ops:
  7.2 91.4 %copy-start = (bf16[1,32,128,128]{3,2,1,0:T(8,128)(2,1)S(1)}, bf16[1,32,128,128]{3,2,1,0:T(8,128)(2,1)}, u32[]{:S(2)}) copy-start(bf16[1,32,128,128]{3,2,1,0:T(8,128)(2,1)} %param.9) | copy-start | bytes 3145732
  7.2 6.9 %copy-start.3 = (f32[32,16,128]{2,1,0:T(8,128)S(1)}, f32[32,16,128]{2,1,0:T(8,128)}, u32[]{:S(2)}) copy-start(f32[32,16,128]{2,1,0:T(8,128)} %param.8) | copy-start | bytes 786436
  7.2 6.9 %copy-start.2 = (f32[3,32,16,128]{3,2,1,0:T(8,128)S(1)}, f32[3,32,16,128]{3,2,1,0:T(8,128)}, u32[]{:S(2)}) copy-start(f32[3,32,16,128]{3,2,1,0:T(8,128)} %param.7) | copy-start | bytes 2359300
  7.2 165.6 %all-gather.4.cloned.1.call-start = ((), (), s32[]{:S(2)}) async-start(), calls=%async_computation | async-start | bytes 1622016 | tf_op jit(solution)/shard_map/all_gather | solution.py:113
  8.2 5.8 %collective-permute-start = (f32[4,1,16,128]{3,2,1,0:T(8,128)S(1)}, f32[4,1,16,128]{3,2,1,0:T(8,128)S(1)}, u32[]{:S(2)}, u32[]{:S(2)}) collective-permute-start(f32[4,1,16,128]{3,2,1,0:T(8,128)S(1)} %get-tuple-element.44), channel_id=1, source_target_pairs={{0,32},{32,64},{64,96},{96,128},{128,160},{160,192},{192,224},{224... | collective-permute-start | bytes 98312 | tf_op jit(solution)/shard_map/ppermute | solution.py:21
  10.8 3.3 collective-permute-start.1
  14.1 10.0 %copy-start.13 = (f32[4,1,16,128]{3,2,1,0:T(8,128)}, f32[4,1,16,128]{3,2,1,0:T(8,128)S(1)}, u32[]{:S(2)}) copy-start(f32[4,1,16,128]{3,2,1,0:T(8,128)S(1)} %collective-permute-done.1) | copy-start | bytes 98308
  14.2 9.8 %collective-permute-start.2 = (f32[4,34,1,128]{3,0,2,1:T(4,128)S(1)}, f32[4,34,1,128]{3,0,2,1:T(4,128)S(1)}, u32[]{:S(2)}, u32[]{:S(2)}) collective-permute-start(f32[4,34,1,128]{3,0,2,1:T(4,128)S(1)} %copy.534), channel_id=1, source_target_pairs={{0,1},{1,2},{2,3},{3,4},{4,5},{5,6},{6,7},{7,8},{8,9},{9,10},{10,1... | collective-permute-start | bytes 208904 | tf_op jit(solution)/shard_map/ppermute | solution.py:21
  15.6 8.5 %collective-permute-start.3 = (f32[4,34,1,128]{3,0,2,1:T(4,128)S(1)}, f32[4,34,1,128]{3,0,2,1:T(4,128)S(1)}, u32[]{:S(2)}, u32[]{:S(2)}) collective-permute-start(f32[4,34,1,128]{3,0,2,1:T(4,128)S(1)} %copy.535), channel_id=1, source_target_pairs={{1,0},{2,1},{3,2},{4,3},{5,4},{6,5},{7,6},{8,7},{9,8},{10,9},{11,1... | collective-permute-start | bytes 208904 | tf_op jit(solution)/shard_map/ppermute | solution.py:24
  22.5 3.1 copy-start.16
  32.8 2.9 copy-start.9
  32.8 2.9 copy-start.10
  32.8 3.1 copy-start.5
  32.8 3.1 copy-start.6
  32.8 3.1 copy-start.7
  32.8 3.1 copy-start.8
  98.5 1.5 copy-start.4
  98.5 4.1 %copy-start.24 = (u32[256]{0:T(256)S(1)}, u32[256]{0:T(256)}, u32[]{:S(2)}) copy-start(u32[256]{0:T(256)} %constant.93) | copy-start | bytes 3076
  98.5 5.3 %copy-start.23 = (s32[1,32,1]{1,2,0:T(1,128)S(1)}, s32[1,32,1]{1,2,0:T(1,128)}, u32[]{:S(2)}) copy-start(s32[1,32,1]{1,2,0:T(1,128)} %param.11) | copy-start | bytes 388
  98.5 5.4 %copy-start.22 = (s32[1,32]{1,0:T(1,128)S(1)}, s32[1,32]{1,0:T(1,128)}, u32[]{:S(2)}) copy-start(s32[1,32]{1,0:T(1,128)} %param.12) | copy-start | bytes 388
  98.5 21.0 %copy-start.19 = (s32[32,4]{0,1:T(4,128)S(1)}, s32[32,4]{0,1:T(4,128)}, u32[]{:S(2)}) copy-start(s32[32,4]{0,1:T(4,128)} %get-tuple-element.95) | copy-start | bytes 1540
  98.5 21.0 %copy-start.18 = (s32[32,4]{0,1:T(4,128)S(1)}, s32[32,4]{0,1:T(4,128)}, u32[]{:S(2)}) copy-start(s32[32,4]{0,1:T(4,128)} %get-tuple-element.88) | copy-start | bytes 1540
  98.5 21.1 %copy-start.15 = (s32[32,8]{0,1:T(8,128)S(1)}, s32[32,8]{0,1:T(8,128)}, u32[]{:S(2)}) copy-start(s32[32,8]{0,1:T(8,128)} %get-tuple-element.90) | copy-start | bytes 3076
  98.6 21.1 %copy-start.21 = (s32[3]{0:T(128)S(1)}, s32[3]{0:T(128)}, u32[]{:S(2)}) copy-start(s32[3]{0:T(128)} %constant.64) | copy-start | bytes 40
  98.6 21.2 %copy-start.20 = (s32[3]{0:T(128)S(1)}, s32[3]{0:T(128)}, u32[]{:S(2)}) copy-start(s32[3]{0:T(128)} %constant.67) | copy-start | bytes 40
  98.6 26.3 %copy-start.14 = (f32[1,32,3,128]{3,1,2,0:T(8,128)S(1)}, f32[1,32,3,128]{3,1,2,0:T(8,128)}, u32[]{:S(2)}) copy-start(f32[1,32,3,128]{3,1,2,0:T(8,128)} %param.10) | copy-start | bytes 147460
  99.3 26.9 %copy-start.17 = (pred[18]{0:T(512)(128)(4,1)S(1)}, pred[18]{0:T(512)(128)(4,1)}, u32[]{:S(2)}) copy-start(pred[18]{0:T(512)(128)(4,1)} %copy-done.16) | copy-start | bytes 58
  100.0 20.0 %collective-permute-start.4 = (f32[1,16,128]{2,0,1:T(1,128)S(1)}, f32[1,16,128]{2,0,1:T(1,128)S(1)}, u32[]{:S(2)}, u32[]{:S(2)}) collective-permute-start(f32[1,16,128]{2,0,1:T(1,128)S(1)} %bitcast.120), channel_id=1, source_target_pairs={{0,32},{32,64},{64,96},{96,128},{128,160},{160,192},{192,224},{224... | collective-permute-start | bytes 24584 | tf_op jit(solution)/shard_map/ppermute | solution.py:21
  102.5 17.5 %collective-permute-start.5 = (f32[1,16,128]{2,0,1:T(1,128)S(1)}, f32[1,16,128]{2,0,1:T(1,128)S(1)}, u32[]{:S(2)}, u32[]{:S(2)}) collective-permute-start(f32[1,16,128]{2,0,1:T(1,128)S(1)} %bitcast.119), channel_id=1, source_target_pairs={{32,0},{64,32},{96,64},{128,96},{160,128},{192,160},{224,192},{0,2... | collective-permute-start | bytes 24584 | tf_op jit(solution)/shard_map/ppermute | solution.py:24
  120.0 6.1 %collective-permute-start.6 = (f32[34,1,128]{2,0,1:T(8,128)S(1)}, f32[34,1,128]{2,0,1:T(8,128)S(1)}, u32[]{:S(2)}, u32[]{:S(2)}) collective-permute-start(f32[34,1,128]{2,0,1:T(8,128)S(1)} %get-tuple-element.70), channel_id=1, source_target_pairs={{0,1},{1,2},{2,3},{3,4},{4,5},{5,6},{6,7},{7,8},{8,9},{9,10},{10,1... | collective-permute-start | bytes 52232 | tf_op jit(solution)/shard_map/ppermute | solution.py:21
  121.0 5.2 %collective-permute-start.7 = (f32[34,1,128]{2,0,1:T(8,128)S(1)}, f32[34,1,128]{2,0,1:T(8,128)S(1)}, u32[]{:S(2)}, u32[]{:S(2)}) collective-permute-start(f32[34,1,128]{2,0,1:T(8,128)S(1)} %get-tuple-element.71), channel_id=1, source_target_pairs={{1,0},{2,1},{3,2},{4,3},{5,4},{6,5},{7,6},{8,7},{9,8},{10,9},{11,1... | collective-permute-start | bytes 52232 | tf_op jit(solution)/shard_map/ppermute | solution.py:24
  295.8 19.2 %collective-permute-start.8 = (f32[3,1,16,128]{3,2,1,0:T(8,128)S(1)}, f32[3,1,16,128]{3,2,1,0:T(8,128)S(1)}, u32[]{:S(2)}, u32[]{:S(2)}) collective-permute-start(f32[3,1,16,128]{3,2,1,0:T(8,128)S(1)} %get-tuple-element.48), channel_id=1, source_target_pairs={{0,32},{32,64},{64,96},{96,128},{128,160},{160,192},{192,224},{224... | collective-permute-start | bytes 73736 | tf_op jit(solution)/shard_map/ppermute | solution.py:21
  314.1 3.3 collective-permute-start.9
  317.5 6.4 %collective-permute-start.10 = (f32[3,34,1,128]{3,2,1,0:T(1,128)S(1)}, f32[3,34,1,128]{3,2,1,0:T(1,128)S(1)}, u32[]{:S(2)}, u32[]{:S(2)}) collective-permute-start(f32[3,34,1,128]{3,2,1,0:T(1,128)S(1)} %get-tuple-element.46), channel_id=1, source_target_pairs={{0,1},{1,2},{2,3},{3,4},{4,5},{5,6},{6,7},{7,8},{8,9},{9,10},{10,1... | collective-permute-start | bytes 156680 | tf_op jit(solution)/shard_map/ppermute | solution.py:21
  317.6 6.3 %collective-permute-start.11 = (f32[3,34,1,128]{3,2,1,0:T(1,128)S(1)}, f32[3,34,1,128]{3,2,1,0:T(1,128)S(1)}, u32[]{:S(2)}, u32[]{:S(2)}) collective-permute-start(f32[3,34,1,128]{3,2,1,0:T(1,128)S(1)} %get-tuple-element.47), channel_id=1, source_target_pairs={{1,0},{2,1},{3,2},{4,3},{5,4},{6,5},{7,6},{8,7},{9,8},{10,9},{11,1... | collective-permute-start | bytes 156680 | tf_op jit(solution)/shard_map/ppermute | solution.py:24
  323.9 1.0 copy-start.11
  323.9 1.0 copy-start.12
  325.4 2.0 collective-permute-start.12
  326.6 3.1 collective-permute-start.13
  329.6 6.8 %collective-permute-start.14 = (f32[34,1,128]{2,0,1:T(8,128)S(1)}, f32[34,1,128]{2,0,1:T(8,128)S(1)}, u32[]{:S(2)}, u32[]{:S(2)}) collective-permute-start(f32[34,1,128]{2,0,1:T(8,128)S(1)} %get-tuple-element.68), channel_id=1, source_target_pairs={{0,1},{1,2},{2,3},{3,4},{4,5},{5,6},{6,7},{7,8},{8,9},{9,10},{10,1... | collective-permute-start | bytes 52232 | tf_op jit(solution)/shard_map/ppermute | solution.py:21
  329.7 6.7 %collective-permute-start.15 = (f32[34,1,128]{2,0,1:T(8,128)S(1)}, f32[34,1,128]{2,0,1:T(8,128)S(1)}, u32[]{:S(2)}, u32[]{:S(2)}) collective-permute-start(f32[34,1,128]{2,0,1:T(8,128)S(1)} %get-tuple-element.69), channel_id=1, source_target_pairs={{1,0},{2,1},{3,2},{4,3},{5,4},{6,5},{7,6},{8,7},{9,8},{10,9},{11,1... | collective-permute-start | bytes 52232 | tf_op jit(solution)/shard_map/ppermute | solution.py:24
  337.1 2.4 collective-permute-start.16
  337.7 3.1 collective-permute-start.17
  340.8 6.4 %collective-permute-start.18 = (f32[34,1,128]{2,0,1:T(8,128)S(1)}, f32[34,1,128]{2,0,1:T(8,128)S(1)}, u32[]{:S(2)}, u32[]{:S(2)}) collective-permute-start(f32[34,1,128]{2,0,1:T(8,128)S(1)} %get-tuple-element.66), channel_id=1, source_target_pairs={{0,1},{1,2},{2,3},{3,4},{4,5},{5,6},{6,7},{7,8},{8,9},{9,10},{10,1... | collective-permute-start | bytes 52232 | tf_op jit(solution)/shard_map/ppermute | solution.py:21
  340.9 6.3 %collective-permute-start.19 = (f32[34,1,128]{2,0,1:T(8,128)S(1)}, f32[34,1,128]{2,0,1:T(8,128)S(1)}, u32[]{:S(2)}, u32[]{:S(2)}) collective-permute-start(f32[34,1,128]{2,0,1:T(8,128)S(1)} %get-tuple-element.67), channel_id=1, source_target_pairs={{1,0},{2,1},{3,2},{4,3},{5,4},{6,5},{7,6},{8,7},{9,8},{10,9},{11,1... | collective-permute-start | bytes 52232 | tf_op jit(solution)/shard_map/ppermute | solution.py:24
  348.9 1.2 copy-start.1
Sparse Core Ops, SparseCore 0:
  100.1 72.7 all-gather.3
where the time goes:
time: 360 us; the launch traced here: 357 us
  local copies, waits for them, and re-layouts  120 us (33%)
  waiting for transfers between devices  58 us (16%)
  starting transfers between devices  56.1 us (16%)
  blocking collectives  52.3 us (15%)
  other arithmetic  51.9 us (14%)
  between operations  15.4 us (4%)
    all_gather x1, waiting for transfers between devices, body(): lax.all_gather(flat_partial, 'yz', axis=0, tiled=True)  45.5 us
    gather x1, local copies, waits for them, and re-layouts, body(): predicted[:, cell_x, cell_z, cell_y].astype(jnp.bfloat16)  43.8 us
    unnamed x4, other arithmetic  42.2 us
    all_gather x1, blocking collectives, body(): all_force = lax.all_gather(grain_force, 'yz', axis=0, tiled=True)  36.8 us
    ppermute x10, starting transfers between devices, extended(): lax.ppermute(lax.slice_in_dim(block, 0, width, axis=dim), axis, backward)  28.4 us
    ppermute x10, starting transfers between devices, extended(): lax.ppermute(lax.slice_in_dim(block, block.shape[dim] - width, None, axis...  27.7 us
    unnamed x69, local copies, waits for them, and re-layouts  22 us
    slice x1, local copies, waits for them, and re-layouts, body(): forced_velocity[1]  20.3 us
  transfers between devices with their start and end apart: 21, of which 13 were waited for; matrix products, arithmetic and copies ran while one was open for 2% of the time, Pallas kernels for 0%

commit v1 on v0

v1 whole, which is shorter than its diff:
```python
import jax
import jax.numpy as jnp
from jax import lax
from jax.sharding import PartitionSpec as P

BX = 4
BZ = 4
BY = 8
S = 4


step_size = 0.1
viscosity = 1.5


def faces(block, axis, dim):
    count = lax.axis_size(axis)
    forward = [(i, (i + 1) % count) for i in range(count)]
    backward = [(target, source) for source, target in forward]
    low = lax.ppermute(
        lax.slice_in_dim(block, block.shape[dim] - 1, None, axis=dim), axis, forward
    )
    high = lax.ppermute(lax.slice_in_dim(block, 0, 1, axis=dim), axis, backward)
    return low, high


def padded_of(block, x_dim, z_dim, x_faces=None, z_faces=None):
    if x_faces is None:
        x_faces = faces(block, "gx", x_dim)
    if z_faces is None:
        z_faces = faces(block, "yz", z_dim)
    tile_index = lax.axis_index("yz")
    tile_total = lax.axis_size("yz")
    low_z, high_z = z_faces
    low_z = jnp.where(tile_index == 0, jnp.zeros_like(low_z), low_z)
    high_z = jnp.where(tile_index == tile_total - 1, jnp.zeros_like(high_z), high_z)
    middle = jnp.concatenate([low_z, block, high_z], axis=z_dim)
    pad_widths = [(0, 0)] * block.ndim
    pad_widths[z_dim] = (1, 1)
    low_x = jnp.pad(x_faces[0], pad_widths)
    high_x = jnp.pad(x_faces[1], pad_widths)
    return jnp.concatenate([low_x, middle, high_x], axis=x_dim)


def inner(padded):
    return padded[..., 1:-1, 1:-1, :]


def along_x(padded):
    return 0.5 * (padded[..., 2:, 1:-1, :] - padded[..., :-2, 1:-1, :])


def along_z(padded):
    return 0.5 * (padded[..., 1:-1, 2:, :] - padded[..., 1:-1, :-2, :])


def along_y(field):
    return 0.5 * (jnp.roll(field, -1, -1) - jnp.roll(field, 1, -1))


def neighbours(padded):
    middle = inner(padded)
    total = padded[..., 2:, 1:-1, :] + padded[..., :-2, 1:-1, :]
    total = total + padded[..., 1:-1, 2:, :] + padded[..., 1:-1, :-2, :]
    return total + jnp.roll(middle, 1, -1) + jnp.roll(middle, -1, -1)


def gradient_of(padded):
    middle = inner(padded)
    return jnp.stack([along_x(padded), along_y(middle), along_z(padded)])


def predict(flow_padded):
    velocity_padded = flow_padded[:3]
    pressure_padded = flow_padded[3]
    current = inner(velocity_padded)
    laplace = neighbours(velocity_padded) - 6.0 * current
    advect = current[0] * along_x(velocity_padded)
    return current + step_size * (viscosity * laplace - advect) - gradient_of(pressure_padded)


def body(velocity, old_pressure, delta_weight, marker_target, pair_owner, pair_grain, box_anchor):
    fields, cx, cz, ny = velocity.shape
    flow_fields = jnp.concatenate([velocity, old_pressure[None]], 0)
    flow_padded = padded_of(flow_fields, 1, 2)
    predicted = predict(flow_padded)

    anchors = box_anchor[0]
    owners = pair_owner[0, :, 0]
    grains = pair_grain[0]
    delta_weights = delta_weight[0]
    pair_total = anchors.shape[0]
    grain_slots = marker_target.shape[1]
    tiles = lax.axis_size("yz")
    box_rows = BX * BZ
    row_total = cx * cz

    steps = jnp.arange(box_rows, dtype=jnp.int32)
    rows_of = (anchors[:, 0, None] + steps[None, :] // BZ) * cz + anchors[:, 1, None] + steps[None, :] % BZ
    row_select = (
        rows_of.reshape(-1)[:, None] == jnp.arange(row_total, dtype=jnp.int32)[None, :]
    )
    lanes = jnp.arange(ny, dtype=jnp.int32)
    y_select = (
        lanes[None, :, None] == anchors[:, 2, None, None] + jnp.arange(BY, dtype=jnp.int32)[None, None, :]
    )

    predicted_rows = predicted.astype(jnp.bfloat16).reshape(fields, row_total, ny)
    box_lines = jnp.einsum(
        "qr,cry->qcy",
        row_select.astype(jnp.bfloat16),
        predicted_rows,
        preferred_element_type=jnp.float32,
    ).astype(jnp.bfloat16)
    box_lines = box_lines.reshape(pair_total, box_rows, fields, ny)
    kernel_box_values = jnp.einsum(
        "pkcy,pyj->pckj", box_lines, y_select.astype(jnp.bfloat16), preferred_element_type=jnp.float32
    ).astype(jnp.bfloat16).reshape(pair_total, fields, -1)
    partial_force_value = jnp.einsum(
        "pmb,pcb->pcm", delta_weights, kernel_box_values, preferred_element_type=jnp.float32
    )
    row_width = fields * partial_force_value.shape[2]
    flat_partial = partial_force_value.reshape(pair_total, row_width)

    same_owner = owners[:, None] == owners[None, :]
    earlier = jnp.arange(pair_total)[None, :] < jnp.arange(pair_total)[:, None]
    slots = jnp.sum(jnp.logical_and(same_owner, earlier), axis=1).astype(jnp.int32)
    places = owners * S + slots
    dispatch = (jnp.arange(tiles * S, dtype=jnp.int32)[:, None] == places[None, :]).astype(jnp.float32)
    packed = jnp.concatenate(
        [flat_partial, (grains + 1).astype(jnp.float32)[:, None]], axis=1
    )
    send = jnp.dot(
        dispatch, packed, precision=lax.Precision.HIGHEST, preferred_element_type=jnp.float32
    )
    received = lax.all_to_all(send, "yz", 0, 0, tiled=True)
    received_grain = received[:, row_width]
    received_values = received[:, :row_width]
    slot_numbers = jnp.arange(grain_slots, dtype=jnp.float32) + 1.0
    select = (slot_numbers[:, None] == received_grain[None, :]).astype(jnp.float32)
    summed = jnp.dot(
        select, received_values, precision=lax.Precision.HIGHEST, preferred_element_type=jnp.float32
    )
    targets = marker_target[0].reshape(grain_slots, row_width)
    grain_force = (targets - summed).astype(jnp.bfloat16)
    returned = jnp.einsum(
        "gq,gw->qw", select.astype(jnp.bfloat16), grain_force, preferred_element_type=jnp.float32
    ).astype(jnp.bfloat16)
    back = lax.all_to_all(returned, "yz", 0, 0, tiled=True)
    marker_pair_force = jnp.einsum(
        "qr,qw->rw", dispatch.astype(jnp.bfloat16), back, preferred_element_type=jnp.float32
    ).astype(jnp.bfloat16)

    spread_force = jnp.einsum(
        "pmb,pcm->pcb",
        delta_weights,
        marker_pair_force.reshape(pair_total, fields, -1),
        preferred_element_type=jnp.float32,
    )
    spread_lines = jnp.einsum(
        "pckj,pyj->pkcy",
        spread_force.reshape(pair_total, fields, box_rows, BY),
        y_select.astype(jnp.float32),
        precision=lax.Precision.HIGHEST,
        preferred_element_type=jnp.float32,
    ).reshape(pair_total * box_rows, fields, ny)
    added = jnp.einsum(
        "qr,qcy->cry",
        row_select.astype(jnp.float32),
        spread_lines,
        precision=lax.Precision.HIGHEST,
        preferred_element_type=jnp.float32,
    )
    forced_velocity = predicted + added.reshape(fields, cx, cz, ny)

    forced_x = padded_of(forced_velocity[0], 0, 1, z_faces=(jnp.zeros((cx, 1, ny), jnp.float32),) * 2)
    forced_z = padded_of(forced_velocity[2], 0, 1, x_faces=(jnp.zeros((1, cz, ny), jnp.float32),) * 2)
    divergence = along_x(forced_x) + along_y(forced_velocity[1]) + along_z(forced_z)
    pressure = (neighbours(flow_padded[3]) - divergence) / 6.0
    pressure = (neighbours(padded_of(pressure, 0, 1)) - divergence) / 6.0
    new_velocity = forced_velocity - gradient_of(padded_of(pressure, 0, 1))
    return (new_velocity, pressure)


def solution(mesh):
    placed = (
        P(None, "gx", "yz", None),
        P("gx", "yz", None),
        P("gx", "yz", None, None),
        P("gx", "yz", None, None),
        P("gx", "yz", None),
        P("gx", "yz"),
        P("gx", "yz", None),
    )
    return jax.shard_map(
        body,
        mesh=mesh,
        in_specs=placed,
        out_specs=(P(None, "gx", "yz", None), P("gx", "yz", None)),
        check_vma=False,
    )
```

time: 360 us -> 197 us (0.55)
  the two profiles are of different devices: /device:TPU:1 before, /device:TPU:7 now
where the time goes in v1:
time: 197 us; the launch traced here: 194 us
  local copies, waits for them, and re-layouts  67.6 us (34%)
  other arithmetic  51.4 us (26%)
  starting transfers between devices  32.2 us (16%)
  waiting for transfers between devices  23 us (12%)
  blocking collectives  12.7 us (6%)
  matrix products  5.18 us (3%)
    convert_element_type x1, other arithmetic, body(): predicted.astype(jnp.bfloat16).reshape(fields, row_total, ny)  13.9 us
    ppermute x8, starting transfers between devices, faces(): high = lax.ppermute(lax.slice_in_dim(block, 0, 1, axis=dim), axis, backward)  13.1 us
    all_to_all x1, blocking collectives, body(): back = lax.all_to_all(returned, 'yz', 0, 0, tiled=True)  12.7 us
    all_to_all x1, waiting for transfers between devices, body(): received = lax.all_to_all(send, 'yz', 0, 0, tiled=True)  12.6 us
    ppermute x8, starting transfers between devices, faces(): lax.ppermute(lax.slice_in_dim(block, block.shape[dim] - 1, None, axis=dim...  11.9 us
    ppermute x8, waiting for transfers between devices, faces(): lax.ppermute(lax.slice_in_dim(block, block.shape[dim] - 1, None, axis=dim...  10.3 us
    unnamed x42, local copies, waits for them, and re-layouts  8.26 us
    slice x9, local copies, waits for them, and re-layouts, faces(): high = lax.ppermute(lax.slice_in_dim(block, 0, 1, axis=dim), axis, backward)  7.41 us
  transfers between devices with their start and end apart: 17, of which 4 were waited for; matrix products, arithmetic and copies ran while one was open for 23% of the time, Pallas kernels for 0%

profile of v1, /device:TPU:7, one launch (start us, length us, event | category | flops | bytes accessed | tf_op | source)
XLA Modules:
  0.0 193.5 jit_solution(4095175829593723239)
XLA Ops:
  0.6 1.4 pad_maximum_fusion.8
  2.1 3.0 %copy.253 = f32[4,32,16,128]{1,2,3,0:T(8,128)} copy(f32[4,32,16,128]{3,2,1,0:T(8,128)S(1)} %pad_maximum_fusion.8) | data formatting | bytes 2097152 | tf_op jit(solution)/shard_map/concatenate | solution.py:84
  5.0 3.4 %fusion.79 = (f32[4,32,1,128]{1,2,3,0:T(1,128)}, f32[4,32,1,128]{1,2,3,0:T(1,128)}) fusion(f32[4,32,16,128]{1,2,3,0:T(8,128)} %copy.253), kind=kLoop, calls=%fused_computation.174 | loop fusion | bytes 262144 | tf_op jit(solution)/shard_map/slice | solution.py:21
  8.4 8.0 %collective-permute-start.1 = (f32[4,32,1,128]{1,2,3,0:T(1,128)}, f32[4,32,1,128]{1,2,3,0:T(1,128)}, u32[]{:S(2)}, u32[]{:S(2)}) collective-permute-start(f32[4,32,1,128]{1,2,3,0:T(1,128)} %get-tuple-element.17), channel_id=1, source_target_pairs={{1,0},{2,1},{3,2},{4,3},{5,4},{6,5},{7,6},{8,7},{9,8},{10,9},{11,1... | collective-permute-start | bytes 196616 | tf_op jit(solution)/shard_map/ppermute | solution.py:23
  17.6 1.0 collective-permute-start.2
  18.5 2.0 %collective-permute-start.3 = (f32[4,1,16,128]{3,2,1,0:T(8,128)S(1)}, f32[4,1,16,128]{3,2,1,0:T(8,128)S(1)}, u32[]{:S(2)}, u32[]{:S(2)}) collective-permute-start(f32[4,1,16,128]{3,2,1,0:T(8,128)S(1)} %get-tuple-element.57), channel_id=1, source_target_pairs={{0,32},{32,64},{64,96},{96,128},{128,160},{160,192},{192,224},{224... | collective-permute-start | bytes 98312 | tf_op jit(solution)/shard_map/ppermute | solution.py:20
  20.8 1.4 fusion.93
  22.3 2.2 %copy.264 = f32[3,32,16,128]{1,2,3,0:T(8,128)} copy(f32[3,32,16,128]{3,2,1,0:T(8,128)S(1)} %copy-done.7) | data formatting | bytes 1572864 | tf_op args[0]
  24.5 2.3 %fusion.37 = f32[32,16,128]{0,1,2:T(8,128)} fusion(f32[3,32,16,128]{1,2,3,0:T(8,128)} %copy.264), kind=kLoop, calls=%fused_computation.92 | loop fusion | flops 65536 | bytes 524288 | tf_op jit(solution)/shard_map/mul | solution.py:78
  27.1 2.7 %pad_maximum_fusion.31 = (f32[3,32,16,128]{3,2,1,0:T(8,128)}, f32[3,32,16,128]{3,2,1,0:T(8,128)S(1)}) fusion(f32[3,32,16,127]{3,2,1,0:T(8,128)} %get-tuple-element.61, f32[3,32,16,1]{3,2,1,0:T(8,128)S(1)} %get-tuple-element.59, f32[3,32,16,1]{3,2,1,0:T(8,128)S(1)} %get-tuple-element.60, f32[3,32,16,127]{3,2,1,0:T(8,128)} %get-tuple-element.62), kind=kLoop, calls=%fused_computation.112 | loop fusion | flops 393216 | bytes 3145728 | tf_op jit(solution)/shard_map/jit(_roll_static)/concatenate | solution.py:65
  29.9 3.2 %copy.260 = f32[3,32,16,128]{1,2,3,0:T(8,128)} copy(f32[3,32,16,128]{3,2,1,0:T(8,128)} %get-tuple-element.66) | data formatting | bytes 1572864 | tf_op jit(solution)/shard_map/jit(_roll_static)/concatenate | solution.py:65
  33.0 2.3 %copy.261 = f32[3,32,16,128]{1,2,3,0:T(8,128)} copy(f32[3,32,16,128]{3,2,1,0:T(8,128)S(1)} %get-tuple-element.67) | data formatting | bytes 1572864 | tf_op jit(solution)/shard_map/jit(_roll_static)/concatenate | solution.py:65
  35.5 2.9 %copy.256 = f32[4,1,16,128]{1,2,3,0:T(8,128)} copy(f32[4,1,16,128]{3,2,1,0:T(8,128)S(1)} %collective-permute-done.2) | data formatting | bytes 65536 | tf_op jit(solution)/shard_map/ppermute | solution.py:23
  38.4 5.6 %pad.26 = f32[4,1,18,128]{1,2,3,0:T(8,128)} pad(f32[4,1,16,128]{1,2,3,0:T(8,128)} %copy.256, f32[]{:T(128)} %constant.48.clone.1), padding=0_0x0_0x1_1x0_0 | pad | bytes 69636 | tf_op jit(solution)/shard_map/jit(_pad)/pad | solution.py:41
  44.0 2.9 %copy.257 = f32[4,1,16,128]{1,2,3,0:T(8,128)} copy(f32[4,1,16,128]{3,2,1,0:T(8,128)S(1)} %collective-permute-done.3) | data formatting | bytes 65536 | tf_op jit(solution)/shard_map/ppermute | solution.py:20
  46.9 3.1 %pad.27 = f32[4,1,18,128]{1,2,3,0:T(8,128)S(1)} pad(f32[4,1,16,128]{1,2,3,0:T(8,128)} %copy.257, f32[]{:T(128)} %constant.48.clone.1), padding=0_0x0_0x1_1x0_0 | pad | bytes 69636 | tf_op jit(solution)/shard_map/jit(_pad)/pad | solution.py:40
  50.0 1.4 broadcast_select_fusion
  51.6 3.1 %fusion.10 = f32[34,18,128]{0,1,2:T(8,128)S(1)} fusion(f32[4,1,18,128]{1,2,3,0:T(8,128)} %pad.26, f32[4,1,18,128]{1,2,3,0:T(8,128)S(1)} %pad.27, f32[4,32,1,128]{1,2,3,0:T(1,128)S(1)} %broadcast_select_fusion, f32[4,32,16,128]{1,2,3,0:T(8,128)S(1)} %copy-done.5, f32[4,32,1,128]{1,2,3,0:T(1,128)S(1)} %broadcast_select_fusion.1), kind=kLoop, calls=%fused_computation.23 | loop fusion | flops 313344 | bytes 1566720 | tf_op jit(solution)/shard_map/squeeze | solution.py:75
  54.8 1.9 fusion.81
  56.8 2.3 %multiply_bitcast_fusion.1 = (f32[1,32,16,128]{1,2,3,0:T(8,128)}, f32[1,32,16,128]{1,2,3,0:T(8,128)}) fusion(f32[34,18,128]{0,1,2:T(8,128)S(1)} %fusion.10), kind=kLoop, calls=%fused_computation.108 | loop fusion | flops 262144 | bytes 1572864 | tf_op jit(solution)/shard_map/stack | solution.py:70
  59.1 1.1 fusion.38
  60.2 1.1 copy-done.8
  61.3 13.9 %fusion.77 = (bf16[3,32,16,128]{1,2,3,0:T(8,128)(2,1)}, f32[3,32,16,128]{1,2,3,0:T(8,128)}) fusion(f32[1,32,16,128]{1,2,3,0:T(8,128)} %get-tuple-element.32, f32[1,32,16,128]{1,2,3,0:T(8,128)} %fusion.38, f32[1,32,16,128]{1,2,3,0:T(8,128)} %get-tuple-element.31, f32[3,32,16,128]{1,2,3,0:T(8,128)S(1)} %copy-done.8, f32[32,16,128]{0,1,2:T(8,128)} %fusion.37, ...), kind=kLoop, calls=%fused_computation.173 | loop fusion | flops 4915200 | bytes 5840896 | tf_op jit(solution)/shard_map/convert_element_type | solution.py:108
  75.2 2.4 %copy.265 = bf16[3,32,16,128]{3,2,1,0:T(8,128)(2,1)S(1)} copy(bf16[3,32,16,128]{1,2,3,0:T(8,128)(2,1)} %get-tuple-element.14) | data formatting | bytes 786432 | tf_op jit(solution)/shard_map/convert_element_type | solution.py:108
  78.1 0.8 fusion.11
  80.2 0.8 all_to_all.16
  81.0 7.2 %all-to-all-start = ((f32[32,4,385]{2,1,0:T(4,128)}), f32[32,4,385]{2,1,0:T(4,128)S(1)}, u32[]{:S(2)}, u32[]{:S(2)}) async-start(f32[32,4,385]{2,1,0:T(4,128)} %all_to_all.16), calls=%async_computation | async-start | bytes 524288 | tf_op jit(solution)/shard_map/all_to_all | solution.py:136
  88.2 12.6 %all-to-all-done = f32[32,4,385]{2,1,0:T(4,128)S(1)} async-done(((f32[32,4,385]{2,1,0:T(4,128)}), f32[32,4,385]{2,1,0:T(4,128)S(1)}, u32[]{:S(2)}, u32[]{:S(2)}) %all-to-all-start) | async-done | bytes 197152 | tf_op jit(solution)/shard_map/all_to_all | solution.py:136
  101.6 12.7 %all_to_all.24 = bf16[32,4,384]{2,1,0:T(4,128)(2,1)S(1)} all-to-all(bf16[32,4,384]{2,1,0:T(4,128)(2,1)S(1)} %all_to_all.19), channel_id=1, replica_groups=mesh['gx'=8,'yz'=32] {'yz'}, dimensions={0} | all-to-all | bytes 196608 | tf_op jit(solution)/shard_map/all_to_all | solution.py:149
  115.2 0.9 convolution_bitcast_fusion.1
  116.2 1.0 convolution_bitcast_fusion
  117.5 2.2 %copy.277 = f32[3,32,16,128]{1,2,3,0:T(8,128)} copy(f32[3,32,16,128]{3,2,1,0:T(8,128)S(1)} %bitcast.95) | data formatting | bytes 1572864 | tf_op jit(solution)/shard_map/reshape | solution.py:174
  119.7 3.2 %add.219 = f32[3,32,16,128]{1,2,3,0:T(8,128)S(1)} add(f32[3,32,16,128]{1,2,3,0:T(8,128)} %get-tuple-element.15, f32[3,32,16,128]{1,2,3,0:T(8,128)} %copy.277) | non-fusion elementwise | flops 196608 | bytes 2359296 | tf_op jit(solution)/shard_map/add | solution.py:174
  123.0 1.4 slice_bitcast_fusion.2
  124.9 1.7 fusion.80
  126.6 1.4 fusion.89
  128.2 0.8 collective-permute-start.6
  128.9 1.6 copy.278
  130.6 1.6 collective-permute-start.4
  132.2 1.6 copy.280
  133.8 1.3 collective-permute-start.5
  135.2 0.8 collective-permute-start.7
  135.9 1.5 copy.279
  137.4 1.4 copy.281
  138.9 3.0 %collective-permute-done.7 = f32[32,1,128]{0,1,2:T(1,128)S(1)} collective-permute-done((f32[32,1,128]{0,1,2:T(1,128)S(1)}, f32[32,1,128]{0,1,2:T(1,128)S(1)}, u32[]{:S(2)}, u32[]{:S(2)}) %collective-permute-start.7) | collective-permute-done | bytes 16416 | tf_op jit(solution)/shard_map/ppermute | solution.py:20
  142.1 7.2 %fusion.41 = (f32[32,16,128]{0,1,2:T(8,128)S(1)}, f32[32,16,128]{0,1,2:T(8,128)}) fusion(f32[32,16,127]{0,1,2:T(8,128)} %get-tuple-element.26, f32[32,16,1]{0,1,2:T(8,128)S(1)} %get-tuple-element.30, f32[32,16,1]{0,1,2:T(8,128)S(1)} %get-tuple-element.27, f32[32,16,127]{0,1,2:T(8,128)} %get-tuple-element.23, f32[34,18,128]{0,1,2:T(8,128)S(1)} %fusion.10, ...), kind=kLoop, calls=%fused_computation.98 | loop fusion | flops 2031616 | bytes 3211264 | tf_op jit(solution)/shard_map/div | solution.py:179
  149.2 1.3 fusion.87
  150.6 1.5 fusion.85
  152.2 1.7 copy.282
  154.7 2.6 %collective-permute-start.11 = (f32[1,16,128]{2,1,0:T(8,128)S(1)}, f32[1,16,128]{2,1,0:T(8,128)S(1)}, u32[]{:S(2)}, u32[]{:S(2)}) collective-permute-start(f32[1,16,128]{2,1,0:T(8,128)S(1)} %copy.284), channel_id=1, source_target_pairs={{0,32},{32,64},{64,96},{96,128},{128,160},{160,192},{192,224},{224... | collective-permute-start | bytes 24584 | tf_op jit(solution)/shard_map/ppermute | solution.py:20
  157.3 1.0 collective-permute-start.9
  159.3 1.4 copy.285
  160.8 3.9 %collective-permute-done.8 = f32[32,1,128]{0,1,2:T(1,128)S(1)} collective-permute-done((f32[32,1,128]{0,1,2:T(1,128)S(1)}, f32[32,1,128]{0,1,2:T(1,128)S(1)}, u32[]{:S(2)}, u32[]{:S(2)}) %collective-permute-start.8) | collective-permute-done | bytes 16416 | tf_op jit(solution)/shard_map/ppermute | solution.py:20
  164.8 4.9 %fusion.25 = f32[32,16,128]{0,1,2:T(8,128)S(1)} fusion(f32[32,16,128]{0,1,2:T(8,128)S(1)} %copy-done.10, f32[32,16,128]{0,1,2:T(8,128)} %copy-done.6, f32[32,1,128]{0,1,2:T(1,128)S(1)} %broadcast_select_fusion.6, f32[32,1,128]{0,1,2:T(1,128)S(1)} %broadcast_select_fusion.3, f32[1,16,128]{0,1,2:T(8,128)} %copy.285, f32[1,16,128]{0,1,2:T(8,128)S(1)} %copy.283, ...), kind=kLoop, calls=%fused_computation.59 | loop fusion | flops 1507328 | bytes 1359872 | tf_op jit(solution)/shard_map/div | solution.py:180
  169.6 1.5 slice_bitcast_fusion.3
  172.5 3.0 %collective-permute-start.15 = (f32[1,16,128]{2,1,0:T(8,128)S(1)}, f32[1,16,128]{2,1,0:T(8,128)S(1)}, u32[]{:S(2)}, u32[]{:S(2)}) collective-permute-start(f32[1,16,128]{2,1,0:T(8,128)S(1)} %copy.288), channel_id=1, source_target_pairs={{0,32},{32,64},{64,96},{96,128},{128,160},{160,192},{192,224},{224... | collective-permute-start | bytes 24584 | tf_op jit(solution)/shard_map/ppermute | solution.py:20
  175.8 1.7 fusion.42
  177.5 1.2 copy.291
  178.7 1.3 collective-permute-start.12
  180.5 1.4 copy.289
  182.0 3.3 %collective-permute-done.12 = f32[32,1,128]{0,1,2:T(1,128)S(1)} collective-permute-done((f32[32,1,128]{0,1,2:T(1,128)S(1)}, f32[32,1,128]{0,1,2:T(1,128)S(1)}, u32[]{:S(2)}, u32[]{:S(2)}) %collective-permute-start.12) | collective-permute-done | bytes 16416 | tf_op jit(solution)/shard_map/ppermute | solution.py:20
  185.4 2.7 %fusion.19 = (f32[1,32,16,128]{1,2,3,0:T(8,128)S(1)}, f32[1,32,16,128]{1,2,3,0:T(8,128)S(1)}) fusion(f32[1,16,128]{0,1,2:T(8,128)} %copy.289, f32[32,1,128]{0,1,2:T(1,128)S(1)} %broadcast_select_fusion.2, f32[32,16,128]{0,1,2:T(8,128)S(1)} %fusion.25, f32[32,1,128]{0,1,2:T(1,128)S(1)} %broadcast_select_fusion.5, f32[1,16,128]{0,1,2:T(8,128)S(1)} %copy.287), kind=kLoop, calls=%fused_computation.47 | loop fusion | flops 1179648 | bytes 835584 | tf_op jit(solution)/shard_map/stack | solution.py:70
  188.1 2.0 %maximum_subtract_fusion = f32[3,32,16,128]{1,2,3,0:T(8,128)} fusion(f32[3,32,16,128]{1,2,3,0:T(8,128)S(1)} %copy-done.4, f32[1,32,16,128]{1,2,3,0:T(8,128)S(1)} %get-tuple-element.34, f32[1,32,16,128]{1,2,3,0:T(8,128)S(1)} %fusion.42, f32[1,32,16,128]{1,2,3,0:T(8,128)S(1)} %get-tuple-element.33), kind=kLoop, calls=%fused_computation.18 | loop fusion | flops 589824 | bytes 2359296 | tf_op jit(solution)/shard_map/sub | solution.py:181
  190.2 3.1 %copy.290 = f32[3,32,16,128]{3,2,1,0:T(8,128)} copy(f32[3,32,16,128]{1,2,3,0:T(8,128)} %maximum_subtract_fusion) | data formatting | bytes 1572864
  (108 shorter events, 11.2 us)
Async XLA Ops:
  0.6 78.6 %copy-start = (bf16[1,32,128,128]{3,2,1,0:T(8,128)(2,1)S(1)}, bf16[1,32,128,128]{3,2,1,0:T(8,128)(2,1)}, u32[]{:S(2)}) copy-start(bf16[1,32,128,128]{3,2,1,0:T(8,128)(2,1)} %param.9) | copy-start | bytes 3145732
  2.0 14.9 %copy-start.7 = (f32[3,32,16,128]{3,2,1,0:T(8,128)S(1)}, f32[3,32,16,128]{3,2,1,0:T(8,128)}, u32[]{:S(2)}) copy-start(f32[3,32,16,128]{3,2,1,0:T(8,128)} %param.7) | copy-start | bytes 2359300
  2.0 14.9 %copy-start.11 = (f32[32,16,128]{2,1,0:T(8,128)S(1)}, f32[32,16,128]{2,1,0:T(8,128)}, u32[]{:S(2)}) copy-start(f32[32,16,128]{2,1,0:T(8,128)} %param.8) | copy-start | bytes 786436
  8.4 41.5 %collective-permute-start.1 = (f32[4,32,1,128]{1,2,3,0:T(1,128)}, f32[4,32,1,128]{1,2,3,0:T(1,128)}, u32[]{:S(2)}, u32[]{:S(2)}) collective-permute-start(f32[4,32,1,128]{1,2,3,0:T(1,128)} %get-tuple-element.17), channel_id=1, source_target_pairs={{1,0},{2,1},{3,2},{4,3},{5,4},{6,5},{7,6},{8,7},{9,8},{10,9},{11,1... | collective-permute-start | bytes 196616 | tf_op jit(solution)/shard_map/ppermute | solution.py:23
  16.4 34.9 %collective-permute-start = (f32[4,32,1,128]{1,2,3,0:T(1,128)}, f32[4,32,1,128]{1,2,3,0:T(1,128)}, u32[]{:S(2)}, u32[]{:S(2)}) collective-permute-start(f32[4,32,1,128]{1,2,3,0:T(1,128)} %get-tuple-element.16), channel_id=1, source_target_pairs={{0,1},{1,2},{2,3},{3,4},{4,5},{5,6},{6,7},{7,8},{8,9},{9,10},{10,1... | collective-permute-start | bytes 196616 | tf_op jit(solution)/shard_map/ppermute | solution.py:20
  17.6 17.9 %collective-permute-start.2 = (f32[4,1,16,128]{3,2,1,0:T(8,128)}, f32[4,1,16,128]{3,2,1,0:T(8,128)S(1)}, u32[]{:S(2)}, u32[]{:S(2)}) collective-permute-start(f32[4,1,16,128]{3,2,1,0:T(8,128)} %get-tuple-element.58), channel_id=1, source_target_pairs={{32,0},{64,32},{96,64},{128,96},{160,128},{192,160},{224,192},{0,2... | collective-permute-start | bytes 98312 | tf_op jit(solution)/shard_map/ppermute | solution.py:23
  18.5 25.4 %collective-permute-start.3 = (f32[4,1,16,128]{3,2,1,0:T(8,128)S(1)}, f32[4,1,16,128]{3,2,1,0:T(8,128)S(1)}, u32[]{:S(2)}, u32[]{:S(2)}) collective-permute-start(f32[4,1,16,128]{3,2,1,0:T(8,128)S(1)} %get-tuple-element.57), channel_id=1, source_target_pairs={{0,32},{32,64},{64,96},{96,128},{128,160},{160,192},{192,224},{224... | collective-permute-start | bytes 98312 | tf_op jit(solution)/shard_map/ppermute | solution.py:20
  22.2 4.5 %copy-start.13 = (s32[1,32,3]{1,0,2:T(1,128)S(1)}, s32[1,32,3]{1,0,2:T(1,128)}, u32[]{:S(2)}) copy-start(s32[1,32,3]{1,0,2:T(1,128)} %param.13) | copy-start | bytes 1156
  22.3 4.6 %copy-start.14 = (s32[1,32,1]{1,2,0:T(1,128)S(1)}, s32[1,32,1]{1,2,0:T(1,128)}, u32[]{:S(2)}) copy-start(s32[1,32,1]{1,2,0:T(1,128)} %param.11) | copy-start | bytes 388
  22.3 4.8 %copy-start.15 = (s32[1,32]{1,0:T(1,128)S(1)}, s32[1,32]{1,0:T(1,128)}, u32[]{:S(2)}) copy-start(s32[1,32]{1,0:T(1,128)} %param.12) | copy-start | bytes 388
  46.9 4.8 %copy-start.5 = (f32[4,32,16,128]{1,2,3,0:T(8,128)S(1)}, f32[4,32,16,128]{1,2,3,0:T(8,128)}, u32[]{:S(2)}) copy-start(f32[4,32,16,128]{1,2,3,0:T(8,128)} %copy.253) | copy-start | bytes 3145732
  49.9 4.8 %copy-start.2 = (f32[4,1,18,128]{1,2,3,0:T(8,128)}, f32[4,1,18,128]{1,2,3,0:T(8,128)S(1)}, u32[]{:S(2)}) copy-start(f32[4,1,18,128]{1,2,3,0:T(8,128)S(1)} %pad.27) | copy-start | bytes 110596
  54.8 5.4 %slice-start = ((s8[6291456]{0:T(1024)(128)(4,1)}), s8[4194304]{0:T(1024)(128)(4,1)S(1)}, s32[]{:S(2)}) async-start(s8[6291456]{0:T(1024)(128)(4,1)} %bitcast.92), calls=%async_computation.2 | async-start | bytes 8388608
  56.8 3.4 %slice-start.1 = ((s8[6291456]{0:T(1024)(128)(4,1)}), s8[2097152]{0:T(1024)(128)(4,1)S(1)}, s32[]{:S(2)}) async-start(s8[6291456]{0:T(1024)(128)(4,1)} %bitcast.92), calls=%async_computation.3 | async-start | bytes 4194304
  59.1 2.3 %copy-start.8 = (f32[3,32,16,128]{1,2,3,0:T(8,128)S(1)}, f32[3,32,16,128]{1,2,3,0:T(8,128)}, u32[]{:S(2)}) copy-start(f32[3,32,16,128]{1,2,3,0:T(8,128)} %copy.264) | copy-start | bytes 2359300
  75.2 12.9 %copy-start.12 = (f32[1,32,3,128]{3,1,2,0:T(8,128)S(1)}, f32[1,32,3,128]{3,1,2,0:T(8,128)}, u32[]{:S(2)}) copy-start(f32[1,32,3,128]{3,1,2,0:T(8,128)} %param.10) | copy-start | bytes 147460
  81.0 19.9 %all-to-all-start = ((f32[32,4,385]{2,1,0:T(4,128)}), f32[32,4,385]{2,1,0:T(4,128)S(1)}, u32[]{:S(2)}, u32[]{:S(2)}) async-start(f32[32,4,385]{2,1,0:T(4,128)} %all_to_all.16), calls=%async_computation | async-start | bytes 524288 | tf_op jit(solution)/shard_map/all_to_all | solution.py:136
  123.0 2.0 %copy-start.3 = (f32[3,32,16,128]{1,2,3,0:T(8,128)}, f32[3,32,16,128]{1,2,3,0:T(8,128)S(1)}, u32[]{:S(2)}) copy-start(f32[3,32,16,128]{1,2,3,0:T(8,128)S(1)} %add.219) | copy-start | bytes 2359300
  124.9 3.1 %copy-start.9 = (f32[32,16,128]{0,1,2:T(8,128)}, f32[32,16,128]{0,1,2:T(8,128)S(1)}, u32[]{:S(2)}) copy-start(f32[32,16,128]{0,1,2:T(8,128)S(1)} %get-tuple-element.21) | copy-start | bytes 786436
  128.2 10.7 %collective-permute-start.6 = (f32[32,1,128]{0,1,2:T(1,128)S(1)}, f32[32,1,128]{0,1,2:T(1,128)S(1)}, u32[]{:S(2)}, u32[]{:S(2)}) collective-permute-start(f32[32,1,128]{0,1,2:T(1,128)S(1)} %get-tuple-element.55), channel_id=1, source_target_pairs={{1,0},{2,1},{3,2},{4,3},{5,4},{6,5},{7,6},{8,7},{9,8},{10,9},{11,1... | collective-permute-start | bytes 49160 | tf_op jit(solution)/shard_map/ppermute | solution.py:23
  130.6 5.4 %collective-permute-start.4 = (f32[1,16,128]{2,1,0:T(8,128)S(1)}, f32[1,16,128]{2,1,0:T(8,128)S(1)}, u32[]{:S(2)}, u32[]{:S(2)}) collective-permute-start(f32[1,16,128]{2,1,0:T(8,128)S(1)} %bitcast.105), channel_id=1, source_target_pairs={{32,0},{64,32},{96,64},{128,96},{160,128},{192,160},{224,192},{0,2... | collective-permute-start | bytes 24584 | tf_op jit(solution)/shard_map/ppermute | solution.py:23
  133.8 3.6 %collective-permute-start.5 = (f32[1,16,128]{2,1,0:T(8,128)S(1)}, f32[1,16,128]{2,1,0:T(8,128)S(1)}, u32[]{:S(2)}, u32[]{:S(2)}) collective-permute-start(f32[1,16,128]{2,1,0:T(8,128)S(1)} %bitcast.106), channel_id=1, source_target_pairs={{0,32},{32,64},{64,96},{96,128},{128,160},{160,192},{192,224},{224... | collective-permute-start | bytes 24584 | tf_op jit(solution)/shard_map/ppermute | solution.py:20
  135.2 6.8 %collective-permute-start.7 = (f32[32,1,128]{0,1,2:T(1,128)S(1)}, f32[32,1,128]{0,1,2:T(1,128)S(1)}, u32[]{:S(2)}, u32[]{:S(2)}) collective-permute-start(f32[32,1,128]{0,1,2:T(1,128)S(1)} %get-tuple-element.56), channel_id=1, source_target_pairs={{0,1},{1,2},{2,3},{3,4},{4,5},{5,6},{6,7},{7,8},{8,9},{9,10},{10,1... | collective-permute-start | bytes 49160 | tf_op jit(solution)/shard_map/ppermute | solution.py:20
  149.2 9.1 %copy-start.6 = (f32[32,16,128]{0,1,2:T(8,128)}, f32[32,16,128]{0,1,2:T(8,128)S(1)}, u32[]{:S(2)}) copy-start(f32[32,16,128]{0,1,2:T(8,128)S(1)} %get-tuple-element.12) | copy-start | bytes 786436
  152.1 12.7 %copy-start.10 = (f32[32,16,128]{0,1,2:T(8,128)S(1)}, f32[32,16,128]{0,1,2:T(8,128)}, u32[]{:S(2)}) copy-start(f32[32,16,128]{0,1,2:T(8,128)} %get-tuple-element.13) | copy-start | bytes 786436
  153.9 4.9 %collective-permute-start.10 = (f32[1,16,128]{2,1,0:T(8,128)S(1)}, f32[1,16,128]{2,1,0:T(8,128)S(1)}, u32[]{:S(2)}, u32[]{:S(2)}) collective-permute-start(f32[1,16,128]{2,1,0:T(8,128)S(1)} %copy.282), channel_id=1, source_target_pairs={{32,0},{64,32},{96,64},{128,96},{160,128},{192,160},{224,192},{0,2... | collective-permute-start | bytes 24584 | tf_op jit(solution)/shard_map/ppermute | solution.py:23
  154.7 4.6 %collective-permute-start.11 = (f32[1,16,128]{2,1,0:T(8,128)S(1)}, f32[1,16,128]{2,1,0:T(8,128)S(1)}, u32[]{:S(2)}, u32[]{:S(2)}) collective-permute-start(f32[1,16,128]{2,1,0:T(8,128)S(1)} %copy.284), channel_id=1, source_target_pairs={{0,32},{32,64},{64,96},{96,128},{128,160},{160,192},{192,224},{224... | collective-permute-start | bytes 24584 | tf_op jit(solution)/shard_map/ppermute | solution.py:20
  157.3 3.4 %collective-permute-start.9 = (f32[32,1,128]{0,1,2:T(1,128)S(1)}, f32[32,1,128]{0,1,2:T(1,128)S(1)}, u32[]{:S(2)}, u32[]{:S(2)}) collective-permute-start(f32[32,1,128]{0,1,2:T(1,128)S(1)} %get-tuple-element.49), channel_id=1, source_target_pairs={{1,0},{2,1},{3,2},{4,3},{5,4},{6,5},{7,6},{8,7},{9,8},{10,9},{11,1... | collective-permute-start | bytes 49160 | tf_op jit(solution)/shard_map/ppermute | solution.py:23
  158.3 6.4 %collective-permute-start.8 = (f32[32,1,128]{0,1,2:T(1,128)S(1)}, f32[32,1,128]{0,1,2:T(1,128)S(1)}, u32[]{:S(2)}, u32[]{:S(2)}) collective-permute-start(f32[32,1,128]{0,1,2:T(1,128)S(1)} %get-tuple-element.50), channel_id=1, source_target_pairs={{0,1},{1,2},{2,3},{3,4},{4,5},{5,6},{6,7},{7,8},{8,9},{9,10},{10,1... | collective-permute-start | bytes 49160 | tf_op jit(solution)/shard_map/ppermute | solution.py:20
  172.0 8.0 %collective-permute-start.14 = (f32[1,16,128]{2,1,0:T(8,128)S(1)}, f32[1,16,128]{2,1,0:T(8,128)S(1)}, u32[]{:S(2)}, u32[]{:S(2)}) collective-permute-start(f32[1,16,128]{2,1,0:T(8,128)S(1)} %copy.286), channel_id=1, source_target_pairs={{32,0},{64,32},{96,64},{128,96},{160,128},{192,160},{224,192},{0,2... | collective-permute-start | bytes 24584 | tf_op jit(solution)/shard_map/ppermute | solution.py:23
  172.5 8.0 %collective-permute-start.15 = (f32[1,16,128]{2,1,0:T(8,128)S(1)}, f32[1,16,128]{2,1,0:T(8,128)S(1)}, u32[]{:S(2)}, u32[]{:S(2)}) collective-permute-start(f32[1,16,128]{2,1,0:T(8,128)S(1)} %copy.288), channel_id=1, source_target_pairs={{0,32},{32,64},{64,96},{96,128},{128,160},{160,192},{192,224},{224... | collective-permute-start | bytes 24584 | tf_op jit(solution)/shard_map/ppermute | solution.py:20
  175.4 6.5 %collective-permute-start.13 = (f32[32,1,128]{0,1,2:T(1,128)S(1)}, f32[32,1,128]{0,1,2:T(1,128)S(1)}, u32[]{:S(2)}, u32[]{:S(2)}) collective-permute-start(f32[32,1,128]{0,1,2:T(1,128)S(1)} %get-tuple-element.41), channel_id=1, source_target_pairs={{1,0},{2,1},{3,2},{4,3},{5,4},{6,5},{7,6},{8,7},{9,8},{10,9},{11,1... | collective-permute-start | bytes 49160 | tf_op jit(solution)/shard_map/ppermute | solution.py:23
  178.7 6.7 %collective-permute-start.12 = (f32[32,1,128]{0,1,2:T(1,128)S(1)}, f32[32,1,128]{0,1,2:T(1,128)S(1)}, u32[]{:S(2)}, u32[]{:S(2)}) collective-permute-start(f32[32,1,128]{0,1,2:T(1,128)S(1)} %get-tuple-element.42), channel_id=1, source_target_pairs={{0,1},{1,2},{2,3},{3,4},{4,5},{5,6},{6,7},{7,8},{8,9},{9,10},{10,1... | collective-permute-start | bytes 49160 | tf_op jit(solution)/shard_map/ppermute | solution.py:20
  181.9 6.2 %copy-start.4 = (f32[3,32,16,128]{1,2,3,0:T(8,128)S(1)}, f32[3,32,16,128]{1,2,3,0:T(8,128)}, u32[]{:S(2)}) copy-start(f32[3,32,16,128]{1,2,3,0:T(8,128)} %copy-done.3) | copy-start | bytes 2359300
  188.1 5.1 %copy-start.1 = (bf16[1,32,128,128]{3,2,1,0:T(8,128)(2,1)S(1)}, bf16[1,32,128,128]{3,2,1,0:T(8,128)(2,1)}, u32[]{:S(2)}) copy-start(bf16[1,32,128,128]{3,2,1,0:T(8,128)(2,1)} %param.9) | copy-start | bytes 3145732

commit v2 on v1

--- a/solution.py
+++ b/solution.py
@@ -101,21 +101,23 @@
         rows_of.reshape(-1)[:, None] == jnp.arange(row_total, dtype=jnp.int32)[None, :]
     )
     lanes = jnp.arange(ny, dtype=jnp.int32)
-    y_select = (
-        lanes[None, :, None] == anchors[:, 2, None, None] + jnp.arange(BY, dtype=jnp.int32)[None, None, :]
-    )
 
     predicted_rows = predicted.astype(jnp.bfloat16).reshape(fields, row_total, ny)
-    box_lines = jnp.einsum(
-        "qr,cry->qcy",
-        row_select.astype(jnp.bfloat16),
-        predicted_rows,
-        preferred_element_type=jnp.float32,
-    ).astype(jnp.bfloat16)
-    box_lines = box_lines.reshape(pair_total, box_rows, fields, ny)
-    kernel_box_values = jnp.einsum(
-        "pkcy,pyj->pckj", box_lines, y_select.astype(jnp.bfloat16), preferred_element_type=jnp.float32
-    ).astype(jnp.bfloat16).reshape(pair_total, fields, -1)
+    row_pick = row_select.astype(jnp.bfloat16)
+    box_lines = jnp.stack(
+        [
+            jnp.dot(row_pick, predicted_rows[c], preferred_element_type=jnp.float32)
+            for c in range(fields)
+        ]
+    )
+    line_offset = jnp.repeat(anchors[:, 2], box_rows)[:, None]
+    window = jnp.stack(
+        [jnp.sum(jnp.where(lanes[None, None, :] == line_offset + j, box_lines, 0.0), axis=-1) for j in range(BY)],
+        axis=-1,
+    )
+    kernel_box_values = (
+        window.reshape(fields, pair_total, box_rows * BY).transpose(1, 0, 2).astype(jnp.bfloat16)
+    )
     partial_force_value = jnp.einsum(
         "pmb,pcb->pcm", delta_weights, kernel_box_values, preferred_element_type=jnp.float32
     )
@@ -157,19 +159,24 @@
         marker_pair_force.reshape(pair_total, fields, -1),
         preferred_element_type=jnp.float32,
     )
-    spread_lines = jnp.einsum(
-        "pckj,pyj->pkcy",
-        spread_force.reshape(pair_total, fields, box_rows, BY),
-        y_select.astype(jnp.float32),
-        precision=lax.Precision.HIGHEST,
-        preferred_element_type=jnp.float32,
-    ).reshape(pair_total * box_rows, fields, ny)
-    added = jnp.einsum(
-        "qr,qcy->cry",
-        row_select.astype(jnp.float32),
-        spread_lines,
-        precision=lax.Precision.HIGHEST,
-        preferred_element_type=jnp.float32,
+    spread_window = spread_force.transpose(1, 0, 2).reshape(fields, pair_total * box_rows, BY)
+    spread_lines = sum(
+        jnp.where(lanes[None, None, :] == line_offset + j, spread_window[:, :, j, None], 0.0)
+        for j in range(BY)
+    )
+    row_place = (
+        jnp.arange(row_total, dtype=jnp.int32)[:, None] == rows_of.reshape(-1)[None, :]
+    ).astype(jnp.float32)
+    added = jnp.stack(
+        [
+            jnp.dot(
+                row_place,
+                spread_lines[c],
+                precision=lax.Precision.HIGHEST,
+                preferred_element_type=jnp.float32,
+            )
+            for c in range(fields)
+        ]
     )
     forced_velocity = predicted + added.reshape(fields, cx, cz, ny)
 

time: 197 us -> 113 us (0.57)
  the two profiles are of different devices: /device:TPU:7 before, /device:TPU:1 now
where the time goes in v2:
time: 113 us
  starting transfers between devices  42.8 us (38%)
  waiting for transfers between devices  25.9 us (23%)
  local copies, waits for them, and re-layouts  21.6 us (19%)
  other arithmetic  15.6 us (14%)
  matrix products  5.14 us (5%)
  between operations  1.4 us (1%)
    ppermute x8, starting transfers between devices, faces(): high = lax.ppermute(lax.slice_in_dim(block, 0, 1, axis=dim), axis, backward)  24.8 us
    all_to_all x1, waiting for transfers between devices, body(): received = lax.all_to_all(send, 'yz', 0, 0, tiled=True)  10.3 us
    all_to_all x1, waiting for transfers between devices, body(): back = lax.all_to_all(returned, 'yz', 0, 0, tiled=True)  8.3 us
    ppermute x8, starting transfers between devices, faces(): lax.ppermute(lax.slice_in_dim(block, block.shape[dim] - 1, None, axis=dim...  6.7 us
    all_to_all x1, starting transfers between devices, body(): received = lax.all_to_all(send, 'yz', 0, 0, tiled=True)  6.7 us
    unnamed x70, local copies, waits for them, and re-layouts  4.68 us
    all_to_all x1, starting transfers between devices, body(): back = lax.all_to_all(returned, 'yz', 0, 0, tiled=True)  4.61 us
    ppermute x8, waiting for transfers between devices, faces(): high = lax.ppermute(lax.slice_in_dim(block, 0, 1, axis=dim), axis, backward)  4.41 us
  transfers between devices with their start and end apart: 18, of which 8 were waited for; matrix products, arithmetic and copies ran while one was open for 12% of the time, Pallas kernels for 0%

profile of v2, /device:TPU:1, one launch (start us, length us, event | category | flops | bytes accessed | tf_op | source)
XLA Modules:
  0.0 112.5 jit_solution(4867151948815460042)
XLA Ops:
  0.7 0.9 pad_maximum_fusion.38
  1.6 3.2 %collective-permute-start.2 = (f32[4,1,16,128]{3,2,1,0:T(8,128)S(1)}, f32[4,1,16,128]{3,2,1,0:T(8,128)S(1)}, u32[]{:S(2)}, u32[]{:S(2)}) collective-permute-start(f32[4,1,16,128]{3,2,1,0:T(8,128)S(1)} %get-tuple-element.25), channel_id=1, source_target_pairs={{32,0},{64,32},{96,64},{128,96},{160,128},{192,160},{224,192},{0,2... | collective-permute-start | bytes 98312 | tf_op jit(solution)/shard_map/ppermute | solution.py:23
  4.9 7.5 %collective-permute-start.1 = (f32[4,32,1,128]{3,2,1,0:T(1,128)S(1)}, f32[4,32,1,128]{3,2,1,0:T(1,128)S(1)}, u32[]{:S(2)}, u32[]{:S(2)}) collective-permute-start(f32[4,32,1,128]{3,2,1,0:T(1,128)S(1)} %get-tuple-element.23), channel_id=1, source_target_pairs={{1,0},{2,1},{3,2},{4,3},{5,4},{6,5},{7,6},{8,7},{9,8},{10,9},{11,1... | collective-permute-start | bytes 196616 | tf_op jit(solution)/shard_map/ppermute | solution.py:23
  12.4 0.7 multiply_bitcast_fusion.2
  13.1 1.4 %fusion.89 = (f32[3,32,16,1]{3,2,1,0:T(8,128)}, f32[3,32,16,1]{3,2,1,0:T(8,128)}) fusion(f32[3,32,16,128]{3,2,1,0:T(8,128)S(1)} %copy-done.1), kind=kLoop, calls=%fused_computation.226 | loop fusion | bytes 24576 | tf_op jit(solution)/shard_map/jit(_roll_static)/slice | solution.py:65
  14.5 1.4 %fusion.90 = (f32[3,32,16,127]{3,2,1,0:T(8,128)}, f32[3,32,16,127]{3,2,1,0:T(8,128)}) fusion(f32[3,32,16,128]{3,2,1,0:T(8,128)S(1)} %copy-done.1), kind=kLoop, calls=%fused_computation.227 | loop fusion | bytes 3121152 | tf_op jit(solution)/shard_map/jit(_roll_static)/slice | solution.py:65
  15.9 0.7 copy-done.27
  16.8 0.7 iota_compare_fusion.10
  17.5 0.7 copy-done.28
  18.3 0.5 multiply_add_fusion.1
  18.9 0.7 iota_compare_fusion.4
  19.6 0.7 iota_compare_fusion.8
  20.3 0.7 iota_compare_fusion.6
  21.1 0.6 copy-done.29
  21.7 0.6 add.298
  22.3 0.7 copy.57
  23.2 0.4 copy-done.21
  23.7 1.0 fusion.91
  24.9 1.0 multiply_bitcast_fusion.1
  26.7 1.3 %fusion.63 = f32[1,32,16,128]{3,2,1,0:T(8,128)S(1)} fusion(f32[1,32,16,1]{3,2,1,0:T(8,128)S(1)} %copy.52, f32[1,32,16,127]{3,2,1,0:T(8,128)S(1)} %get-tuple-element.40, f32[1,32,16,127]{3,2,1,0:T(8,128)} %get-tuple-element.41, f32[1,32,16,1]{3,2,1,0:T(8,128)S(1)} %copy.54), kind=kLoop, calls=%fused_computation.137 | loop fusion | flops 262144 | bytes 786432 | tf_op jit(solution)/shard_map/mul | solution.py:58
  28.0 2.6 %fusion.87 = (bf16[3,32,16,128]{3,2,1,0:T(8,128)(2,1)S(1)}, f32[3,32,16,128]{3,2,1,0:T(8,128)S(1)}) fusion(f32[1,32,16,128]{3,2,1,0:T(8,128)} %get-tuple-element.44, f32[1,32,16,128]{3,2,1,0:T(8,128)S(1)} %fusion.63, f32[1,32,16,128]{3,2,1,0:T(8,128)S(1)} %copy-done.12, f32[3,32,16,128]{3,2,1,0:T(8,128)S(1)} %copy-done.1, f32[32,16,128]{2,1,0:T(8,128)S(1)} %copy-done.9, ...), kind=kLoop, calls=%fused_computation.225 | loop fusion | flops 6094848 | bytes 5054464 | tf_op jit(solution)/shard_map/convert_element_type | solution.py:105
  30.7 0.6 copy-done.26
  31.3 0.4 convolution_bitcast_fusion
  31.8 0.4 convolution_bitcast_fusion.1
  32.3 0.4 convolution_bitcast_fusion.2
  32.7 0.3 copy-done.13
  33.2 0.6 select_reduce_fusion
  34.2 0.4 convert_element_type.63
  34.6 0.6 fusion.17
  35.3 0.7 copy-done.22
  36.2 0.8 all_to_all.16
  37.0 6.7 %all-to-all-start = ((f32[32,4,385]{2,1,0:T(4,128)}), f32[32,4,385]{2,1,0:T(4,128)S(1)}, u32[]{:S(2)}, u32[]{:S(2)}) async-start(f32[32,4,385]{2,1,0:T(4,128)} %all_to_all.16), calls=%async_computation | async-start | bytes 524288 | tf_op jit(solution)/shard_map/all_to_all | solution.py:138
  43.8 10.3 %all-to-all-done = f32[32,4,385]{2,1,0:T(4,128)S(1)} async-done(((f32[32,4,385]{2,1,0:T(4,128)}), f32[32,4,385]{2,1,0:T(4,128)S(1)}, u32[]{:S(2)}, u32[]{:S(2)}) %all-to-all-start) | async-done | bytes 197152 | tf_op jit(solution)/shard_map/all_to_all | solution.py:138
  54.6 0.3 convolution_convert_fusion
  54.9 0.7 all_to_all.19
  55.5 4.6 %all-to-all-start.1 = ((bf16[32,4,384]{2,1,0:T(4,128)(2,1)}), bf16[32,4,384]{2,1,0:T(4,128)(2,1)S(1)}, u32[]{:S(2)}, u32[]{:S(2)}) async-start(bf16[32,4,384]{2,1,0:T(4,128)(2,1)} %all_to_all.19), calls=%async_computation.1 | async-start | bytes 196608 | tf_op jit(solution)/shard_map/all_to_all | solution.py:151
  60.2 0.6 multiply_add_fusion
  60.8 8.3 %all-to-all-done.1 = bf16[32,4,384]{2,1,0:T(4,128)(2,1)S(1)} async-done(((bf16[32,4,384]{2,1,0:T(4,128)(2,1)}), bf16[32,4,384]{2,1,0:T(4,128)(2,1)S(1)}, u32[]{:S(2)}, u32[]{:S(2)}) %all-to-all-start.1) | async-done | bytes 98336 | tf_op jit(solution)/shard_map/all_to_all | solution.py:151
  69.3 0.4 convolution_bitcast_fusion.3
  69.7 0.4 reshape.581
  70.1 3.2 %slice_reduce_fusion.7 = (f32[3,512]{1,0:T(4,128)S(1)}, f32[3,512]{1,0:T(4,128)S(1)}, f32[3,512]{1,0:T(4,128)S(1)}, f32[3,512]{1,0:T(4,128)S(1)}, f32[3,512]{1,0...) fusion(f32[3,512,8]{2,1,0:T(8,128)S(1)} %reshape.581), kind=kLoop, calls=%fused_computation.28 | loop fusion | bytes 98304 | tf_op jit(solution)/shard_map/slice | solution.py:164
  73.3 0.5 select_add_fusion
  74.1 0.6 fusion.12
  74.7 0.6 fusion.9
  75.3 0.6 fusion.6
  76.6 4.7 %collective-permute-start.6 = (f32[32,1,128]{2,1,0:T(1,128)S(1)}, f32[32,1,128]{2,1,0:T(1,128)S(1)}, u32[]{:S(2)}, u32[]{:S(2)}) collective-permute-start(f32[32,1,128]{2,1,0:T(1,128)S(1)} %get-tuple-element.72), channel_id=1, source_target_pairs={{1,0},{2,1},{3,2},{4,3},{5,4},{6,5},{7,6},{8,7},{9,8},{10,9},{11,1... | collective-permute-start | bytes 49160 | tf_op jit(solution)/shard_map/ppermute | solution.py:23
  81.3 5.8 %collective-permute-start.5 = (f32[1,16,128]{2,1,0:T(8,128)S(1)}, f32[1,16,128]{2,1,0:T(8,128)S(1)}, u32[]{:S(2)}, u32[]{:S(2)}) collective-permute-start(f32[1,16,128]{2,1,0:T(8,128)S(1)} %get-tuple-element.27), channel_id=1, source_target_pairs={{0,32},{32,64},{64,96},{96,128},{128,160},{160,192},{192,224},{224... | collective-permute-start | bytes 24584 | tf_op jit(solution)/shard_map/ppermute | solution.py:20
  87.2 0.7 collective-permute-done.5
  88.0 2.3 %collective-permute-done.4 = f32[1,16,128]{2,1,0:T(8,128)S(1)} collective-permute-done((f32[1,16,128]{2,1,0:T(8,128)S(1)}, f32[1,16,128]{2,1,0:T(8,128)S(1)}, u32[]{:S(2)}, u32[]{:S(2)}) %collective-permute-start.4) | collective-permute-done | bytes 8224 | tf_op jit(solution)/shard_map/ppermute | solution.py:23
  90.3 0.4 fusion.66
  91.1 4.8 %collective-permute-start.9 = (f32[32,1,128]{2,1,0:T(1,128)S(1)}, f32[32,1,128]{2,1,0:T(1,128)S(1)}, u32[]{:S(2)}, u32[]{:S(2)}) collective-permute-start(f32[32,1,128]{2,1,0:T(1,128)S(1)} %get-tuple-element.66), channel_id=1, source_target_pairs={{1,0},{2,1},{3,2},{4,3},{5,4},{6,5},{7,6},{8,7},{9,8},{10,9},{11,1... | collective-permute-start | bytes 49160 | tf_op jit(solution)/shard_map/ppermute | solution.py:23
  95.9 0.6 collective-permute-start.11
  96.5 0.3 collective-permute-start.10
  97.1 0.4 collective-permute-done.11
  97.5 2.1 %collective-permute-done.10 = f32[1,16,128]{2,1,0:T(8,128)S(1)} collective-permute-done((f32[1,16,128]{2,1,0:T(8,128)S(1)}, f32[1,16,128]{2,1,0:T(8,128)S(1)}, u32[]{:S(2)}, u32[]{:S(2)}) %collective-permute-start.10) | collective-permute-done | bytes 8224 | tf_op jit(solution)/shard_map/ppermute | solution.py:23
  99.9 0.8 fusion.95
  100.7 0.9 slice_bitcast_fusion
  101.7 3.7 %collective-permute-start.13 = (f32[32,1,128]{2,1,0:T(1,128)S(1)}, f32[32,1,128]{2,1,0:T(1,128)S(1)}, u32[]{:S(2)}, u32[]{:S(2)}) collective-permute-start(f32[32,1,128]{2,1,0:T(1,128)S(1)} %get-tuple-element.58), channel_id=1, source_target_pairs={{1,0},{2,1},{3,2},{4,3},{5,4},{6,5},{7,6},{8,7},{9,8},{10,9},{11,1... | collective-permute-start | bytes 49160 | tf_op jit(solution)/shard_map/ppermute | solution.py:23
  105.4 0.6 collective-permute-start.14
  106.3 1.1 %copy.66 = f32[32,16,1]{0,1,2:T(8,128)S(1)} copy(f32[32,16,1]{2,1,0:T(8,128)} %get-tuple-element.54) | data formatting | bytes 4096 | tf_op jit(solution)/shard_map/jit(_roll_static)/slice | solution.py:58
  107.5 0.9 copy.67
  108.4 1.3 %fusion.67 = f32[1,32,16,128]{3,2,1,0:T(8,128)S(1)} fusion(f32[1,32,16,1]{3,2,1,0:T(8,128)S(1)} %copy.65, f32[1,32,16,127]{3,2,1,0:T(8,128)} %get-tuple-element.57, f32[1,32,16,127]{3,2,1,0:T(8,128)} %get-tuple-element.56, f32[1,32,16,1]{3,2,1,0:T(8,128)} %copy.67), kind=kLoop, calls=%fused_computation.144 | loop fusion | flops 262144 | bytes 786432 | tf_op jit(solution)/shard_map/mul | solution.py:58
  109.7 1.5 %collective-permute-done.12 = f32[32,1,128]{2,1,0:T(1,128)S(1)} collective-permute-done((f32[32,1,128]{2,1,0:T(1,128)S(1)}, f32[32,1,128]{2,1,0:T(1,128)S(1)}, u32[]{:S(2)}, u32[]{:S(2)}) %collective-permute-start.12) | collective-permute-done | bytes 16416 | tf_op jit(solution)/shard_map/ppermute | solution.py:20
  111.4 1.1 maximum_subtract_fusion
  (135 shorter events, 5.6 us)
Async XLA Ops:
  0.6 34.0 %copy-start = (bf16[1,32,128,128]{3,2,1,0:T(8,128)(2,1)S(1)}, bf16[1,32,128,128]{3,2,1,0:T(8,128)(2,1)}, u32[]{:S(2)}) copy-start(bf16[1,32,128,128]{3,2,1,0:T(8,128)(2,1)} %param.9) | copy-start | bytes 3145732
  0.6 4.2 %copy-start.1 = (f32[3,32,16,128]{3,2,1,0:T(8,128)S(1)}, f32[3,32,16,128]{3,2,1,0:T(8,128)}, u32[]{:S(2)}) copy-start(f32[3,32,16,128]{3,2,1,0:T(8,128)} %param.7) | copy-start | bytes 2359300
  0.7 4.2 %copy-start.3 = (f32[32,16,128]{2,1,0:T(8,128)S(1)}, f32[32,16,128]{2,1,0:T(8,128)}, u32[]{:S(2)}) copy-start(f32[32,16,128]{2,1,0:T(8,128)} %param.8) | copy-start | bytes 786436
  1.6 21.4 %collective-permute-start.2 = (f32[4,1,16,128]{3,2,1,0:T(8,128)S(1)}, f32[4,1,16,128]{3,2,1,0:T(8,128)S(1)}, u32[]{:S(2)}, u32[]{:S(2)}) collective-permute-start(f32[4,1,16,128]{3,2,1,0:T(8,128)S(1)} %get-tuple-element.25), channel_id=1, source_target_pairs={{32,0},{64,32},{96,64},{128,96},{160,128},{192,160},{224,192},{0,2... | collective-permute-start | bytes 98312 | tf_op jit(solution)/shard_map/ppermute | solution.py:23
  4.8 18.2 %collective-permute-start.3 = (f32[4,1,16,128]{3,2,1,0:T(8,128)S(1)}, f32[4,1,16,128]{3,2,1,0:T(8,128)S(1)}, u32[]{:S(2)}, u32[]{:S(2)}) collective-permute-start(f32[4,1,16,128]{3,2,1,0:T(8,128)S(1)} %get-tuple-element.24), channel_id=1, source_target_pairs={{0,32},{32,64},{64,96},{96,128},{128,160},{160,192},{192,224},{224... | collective-permute-start | bytes 98312 | tf_op jit(solution)/shard_map/ppermute | solution.py:20
  4.9 18.2 %collective-permute-start.1 = (f32[4,32,1,128]{3,2,1,0:T(1,128)S(1)}, f32[4,32,1,128]{3,2,1,0:T(1,128)S(1)}, u32[]{:S(2)}, u32[]{:S(2)}) collective-permute-start(f32[4,32,1,128]{3,2,1,0:T(1,128)S(1)} %get-tuple-element.23), channel_id=1, source_target_pairs={{1,0},{2,1},{3,2},{4,3},{5,4},{6,5},{7,6},{8,7},{9,8},{10,9},{11,1... | collective-permute-start | bytes 196616 | tf_op jit(solution)/shard_map/ppermute | solution.py:23
  12.4 10.7 %collective-permute-start = (f32[4,32,1,128]{3,2,1,0:T(1,128)S(1)}, f32[4,32,1,128]{3,2,1,0:T(1,128)S(1)}, u32[]{:S(2)}, u32[]{:S(2)}) collective-permute-start(f32[4,32,1,128]{3,2,1,0:T(1,128)S(1)} %get-tuple-element.22), channel_id=1, source_target_pairs={{0,1},{1,2},{2,3},{3,4},{4,5},{5,6},{6,7},{7,8},{8,9},{9,10},{10,1... | collective-permute-start | bytes 196616 | tf_op jit(solution)/shard_map/ppermute | solution.py:20
  15.9 0.7 copy-start.27
  17.5 0.7 copy-start.28
  21.0 0.7 copy-start.29
  23.1 0.6 copy-start.21
  24.9 1.0 copy-start.7
  24.9 1.4 %copy-start.5 = (f32[32,16,1]{2,1,0:T(8,128)}, f32[32,16,1]{2,1,0:T(8,128)S(1)}, u32[]{:S(2)}) copy-start(f32[32,16,1]{2,1,0:T(8,128)S(1)} %get-tuple-element.45) | copy-start | bytes 6148
  26.7 1.3 %copy-start.4 = (f32[3,32,16,1]{3,2,1,0:T(8,128)S(1)}, f32[3,32,16,1]{3,2,1,0:T(8,128)}, u32[]{:S(2)}) copy-start(f32[3,32,16,1]{3,2,1,0:T(8,128)} %get-tuple-element.35) | copy-start | bytes 18436
  26.7 1.3 %copy-start.9 = (f32[32,16,128]{2,1,0:T(8,128)S(1)}, f32[32,16,128]{2,1,0:T(8,128)}, u32[]{:S(2)}) copy-start(f32[32,16,128]{2,1,0:T(8,128)} %multiply_bitcast_fusion.2) | copy-start | bytes 786436
  26.7 1.3 %copy-start.12 = (f32[1,32,16,128]{3,2,1,0:T(8,128)S(1)}, f32[1,32,16,128]{3,2,1,0:T(8,128)}, u32[]{:S(2)}) copy-start(f32[1,32,16,128]{3,2,1,0:T(8,128)} %get-tuple-element.43) | copy-start | bytes 786436
  30.7 0.7 copy-start.26
  32.2 0.8 copy-start.13
  32.2 0.9 copy-start.14
  32.2 0.9 copy-start.15
  32.2 0.9 copy-start.16
  32.2 0.9 copy-start.17
  32.2 1.0 copy-start.18
  32.3 1.0 copy-start.19
  35.2 0.7 copy-start.22
  35.2 0.7 copy-start.25
  37.0 6.7 %copy-start.23 = (f32[1,32,3,128]{3,1,2,0:T(8,128)S(1)}, f32[1,32,3,128]{3,1,2,0:T(8,128)}, u32[]{:S(2)}) copy-start(f32[1,32,3,128]{3,1,2,0:T(8,128)} %param.10) | copy-start | bytes 147460
  37.0 17.1 %all-to-all-start = ((f32[32,4,385]{2,1,0:T(4,128)}), f32[32,4,385]{2,1,0:T(4,128)S(1)}, u32[]{:S(2)}, u32[]{:S(2)}) async-start(f32[32,4,385]{2,1,0:T(4,128)} %all_to_all.16), calls=%async_computation | async-start | bytes 524288 | tf_op jit(solution)/shard_map/all_to_all | solution.py:138
  55.5 13.5 %all-to-all-start.1 = ((bf16[32,4,384]{2,1,0:T(4,128)(2,1)}), bf16[32,4,384]{2,1,0:T(4,128)(2,1)S(1)}, u32[]{:S(2)}, u32[]{:S(2)}) async-start(bf16[32,4,384]{2,1,0:T(4,128)(2,1)} %all_to_all.19), calls=%async_computation.1 | async-start | bytes 196608 | tf_op jit(solution)/shard_map/all_to_all | solution.py:151
  70.1 3.2 %copy-start.20 = (pred[512,128]{0,1:T(8,128)(4,1)S(1)}, pred[512,128]{0,1:T(8,128)(4,1)}, u32[]{:S(2)}) copy-start(pred[512,128]{0,1:T(8,128)(4,1)} %get-tuple-element.89) | copy-start | bytes 196612
  73.3 0.7 copy-start.24
  76.3 14.0 %copy-start.6 = (f32[32,16,1]{2,1,0:T(8,128)S(1)}, f32[32,16,1]{2,1,0:T(8,128)}, u32[]{:S(2)}) copy-start(f32[32,16,1]{2,1,0:T(8,128)} %copy-done.5) | copy-start | bytes 6148
  76.3 14.0 %copy-start.8 = (f32[32,16,1]{2,1,0:T(8,128)S(1)}, f32[32,16,1]{2,1,0:T(8,128)}, u32[]{:S(2)}) copy-start(f32[32,16,1]{2,1,0:T(8,128)} %copy-done.7) | copy-start | bytes 6148
  76.3 14.0 %copy-start.10 = (f32[32,16,127]{2,1,0:T(8,128)S(1)}, f32[32,16,127]{2,1,0:T(8,128)}, u32[]{:S(2)}) copy-start(f32[32,16,127]{2,1,0:T(8,128)} %get-tuple-element.39) | copy-start | bytes 780292
  76.3 14.0 %copy-start.11 = (f32[32,16,127]{2,1,0:T(8,128)S(1)}, f32[32,16,127]{2,1,0:T(8,128)}, u32[]{:S(2)}) copy-start(f32[32,16,127]{2,1,0:T(8,128)} %get-tuple-element.42) | copy-start | bytes 780292
  76.5 10.7 %collective-permute-start.7 = (f32[32,1,128]{2,1,0:T(1,128)S(1)}, f32[32,1,128]{2,1,0:T(1,128)S(1)}, u32[]{:S(2)}, u32[]{:S(2)}) collective-permute-start(f32[32,1,128]{2,1,0:T(1,128)S(1)} %get-tuple-element.73), channel_id=1, source_target_pairs={{0,1},{1,2},{2,3},{3,4},{4,5},{5,6},{6,7},{7,8},{8,9},{9,10},{10,1... | collective-permute-start | bytes 49160 | tf_op jit(solution)/shard_map/ppermute | solution.py:20
  76.6 10.6 %collective-permute-start.6 = (f32[32,1,128]{2,1,0:T(1,128)S(1)}, f32[32,1,128]{2,1,0:T(1,128)S(1)}, u32[]{:S(2)}, u32[]{:S(2)}) collective-permute-start(f32[32,1,128]{2,1,0:T(1,128)S(1)} %get-tuple-element.72), channel_id=1, source_target_pairs={{1,0},{2,1},{3,2},{4,3},{5,4},{6,5},{7,6},{8,7},{9,8},{10,9},{11,1... | collective-permute-start | bytes 49160 | tf_op jit(solution)/shard_map/ppermute | solution.py:23
  81.3 6.6 %collective-permute-start.5 = (f32[1,16,128]{2,1,0:T(8,128)S(1)}, f32[1,16,128]{2,1,0:T(8,128)S(1)}, u32[]{:S(2)}, u32[]{:S(2)}) collective-permute-start(f32[1,16,128]{2,1,0:T(8,128)S(1)} %get-tuple-element.27), channel_id=1, source_target_pairs={{0,32},{32,64},{64,96},{96,128},{128,160},{160,192},{192,224},{224... | collective-permute-start | bytes 24584 | tf_op jit(solution)/shard_map/ppermute | solution.py:20
  87.2 3.1 %collective-permute-start.4 = (f32[1,16,128]{2,1,0:T(8,128)S(1)}, f32[1,16,128]{2,1,0:T(8,128)S(1)}, u32[]{:S(2)}, u32[]{:S(2)}) collective-permute-start(f32[1,16,128]{2,1,0:T(8,128)S(1)} %get-tuple-element.26), channel_id=1, source_target_pairs={{32,0},{64,32},{96,64},{128,96},{160,128},{192,160},{224,192},{0,2... | collective-permute-start | bytes 24584 | tf_op jit(solution)/shard_map/ppermute | solution.py:23
  91.0 6.0 %collective-permute-start.8 = (f32[32,1,128]{2,1,0:T(1,128)S(1)}, f32[32,1,128]{2,1,0:T(1,128)S(1)}, u32[]{:S(2)}, u32[]{:S(2)}) collective-permute-start(f32[32,1,128]{2,1,0:T(1,128)S(1)} %get-tuple-element.67), channel_id=1, source_target_pairs={{0,1},{1,2},{2,3},{3,4},{4,5},{5,6},{6,7},{7,8},{8,9},{9,10},{10,1... | collective-permute-start | bytes 49160 | tf_op jit(solution)/shard_map/ppermute | solution.py:20
  91.1 5.9 %collective-permute-start.9 = (f32[32,1,128]{2,1,0:T(1,128)S(1)}, f32[32,1,128]{2,1,0:T(1,128)S(1)}, u32[]{:S(2)}, u32[]{:S(2)}) collective-permute-start(f32[32,1,128]{2,1,0:T(1,128)S(1)} %get-tuple-element.66), channel_id=1, source_target_pairs={{1,0},{2,1},{3,2},{4,3},{5,4},{6,5},{7,6},{8,7},{9,8},{10,9},{11,1... | collective-permute-start | bytes 49160 | tf_op jit(solution)/shard_map/ppermute | solution.py:23
  95.9 1.6 %collective-permute-start.11 = (f32[1,16,128]{2,1,0:T(8,128)S(1)}, f32[1,16,128]{2,1,0:T(8,128)S(1)}, u32[]{:S(2)}, u32[]{:S(2)}) collective-permute-start(f32[1,16,128]{2,1,0:T(8,128)S(1)} %get-tuple-element.65), channel_id=1, source_target_pairs={{0,32},{32,64},{64,96},{96,128},{128,160},{160,192},{192,224},{224... | collective-permute-start | bytes 24584 | tf_op jit(solution)/shard_map/ppermute | solution.py:20
  96.5 3.1 %collective-permute-start.10 = (f32[1,16,128]{2,1,0:T(8,128)S(1)}, f32[1,16,128]{2,1,0:T(8,128)S(1)}, u32[]{:S(2)}, u32[]{:S(2)}) collective-permute-start(f32[1,16,128]{2,1,0:T(8,128)S(1)} %get-tuple-element.64), channel_id=1, source_target_pairs={{32,0},{64,32},{96,64},{128,96},{160,128},{192,160},{224,192},{0,2... | collective-permute-start | bytes 24584 | tf_op jit(solution)/shard_map/ppermute | solution.py:23
  99.8 11.5 %copy-start.2 = (f32[32,16,128]{2,1,0:T(8,128)}, f32[32,16,128]{2,1,0:T(8,128)S(1)}, u32[]{:S(2)}) copy-start(f32[32,16,128]{2,1,0:T(8,128)S(1)} %fusion.51) | copy-start | bytes 786436
  101.6 9.7 %collective-permute-start.15 = (f32[1,16,128]{2,1,0:T(8,128)S(1)}, f32[1,16,128]{2,1,0:T(8,128)S(1)}, u32[]{:S(2)}, u32[]{:S(2)}) collective-permute-start(f32[1,16,128]{2,1,0:T(8,128)S(1)} %get-tuple-element.53), channel_id=1, source_target_pairs={{0,32},{32,64},{64,96},{96,128},{128,160},{160,192},{192,224},{224... | collective-permute-start | bytes 24584 | tf_op jit(solution)/shard_map/ppermute | solution.py:20
  101.7 8.1 %collective-permute-start.13 = (f32[32,1,128]{2,1,0:T(1,128)S(1)}, f32[32,1,128]{2,1,0:T(1,128)S(1)}, u32[]{:S(2)}, u32[]{:S(2)}) collective-permute-start(f32[32,1,128]{2,1,0:T(1,128)S(1)} %get-tuple-element.58), channel_id=1, source_target_pairs={{1,0},{2,1},{3,2},{4,3},{5,4},{6,5},{7,6},{8,7},{9,8},{10,9},{11,1... | collective-permute-start | bytes 49160 | tf_op jit(solution)/shard_map/ppermute | solution.py:23
  105.4 5.9 %collective-permute-start.12 = (f32[32,1,128]{2,1,0:T(1,128)S(1)}, f32[32,1,128]{2,1,0:T(1,128)S(1)}, u32[]{:S(2)}, u32[]{:S(2)}) collective-permute-start(f32[32,1,128]{2,1,0:T(1,128)S(1)} %get-tuple-element.59), channel_id=1, source_target_pairs={{0,1},{1,2},{2,3},{3,4},{4,5},{5,6},{6,7},{7,8},{8,9},{9,10},{10,1... | collective-permute-start | bytes 49160 | tf_op jit(solution)/shard_map/ppermute | solution.py:20
  105.4 5.9 %collective-permute-start.14 = (f32[1,16,128]{2,1,0:T(8,128)S(1)}, f32[1,16,128]{2,1,0:T(8,128)S(1)}, u32[]{:S(2)}, u32[]{:S(2)}) collective-permute-start(f32[1,16,128]{2,1,0:T(8,128)S(1)} %get-tuple-element.52), channel_id=1, source_target_pairs={{32,0},{64,32},{96,64},{128,96},{160,128},{192,160},{224,192},{0,2... | collective-permute-start | bytes 24584 | tf_op jit(solution)/shard_map/ppermute | solution.py:23

commit v3 on v2

--- a/solution.py
+++ b/solution.py
@@ -42,6 +42,62 @@
     return jnp.concatenate([low_x, middle, high_x], axis=x_dim)
 
 
+def halo(block, width):
+    x_count = lax.axis_size("gx")
+    z_count = lax.axis_size("yz")
+    x_total, z_total = block.shape[-3], block.shape[-2]
+
+    def sent(piece, dx, dz):
+        if dz == 0:
+            pairs = [(i, (i + dx) % x_count) for i in range(x_count)]
+            return lax.ppermute(piece, "gx", pairs)
+        if dx == 0:
+            pairs = [(t, (t + dz) % z_count) for t in range(z_count)]
+            return lax.ppermute(piece, "yz", pairs)
+        pairs = [
+            (i * z_count + t, ((i + dx) % x_count) * z_count + (t + dz) % z_count)
+            for i in range(x_count)
+            for t in range(z_count)
+        ]
+        return lax.ppermute(piece, ("gx", "yz"), pairs)
+
+    top_x = slice(x_total - width, None)
+    low_x = slice(0, width)
+    top_z = slice(z_total - width, None)
+    low_z = slice(0, width)
+    every = slice(None)
+    lead = (Ellipsis,)
+    below = jnp.concatenate(
+        [
+            sent(block[lead + (top_x, top_z, every)], 1, 1),
+            sent(block[lead + (top_x, every, every)], 1, 0),
+            sent(block[lead + (top_x, low_z, every)], 1, -1),
+        ],
+        axis=-2,
+    )
+    middle = jnp.concatenate(
+        [sent(block[lead + (every, top_z, every)], 0, 1), block, sent(block[lead + (every, low_z, every)], 0, -1)],
+        axis=-2,
+    )
+    above = jnp.concatenate(
+        [
+            sent(block[lead + (low_x, top_z, every)], -1, 1),
+            sent(block[lead + (low_x, every, every)], -1, 0),
+            sent(block[lead + (low_x, low_z, every)], -1, -1),
+        ],
+        axis=-2,
+    )
+    return inside(jnp.concatenate([below, middle, above], axis=-3), width, z_total)
+
+
+def inside(field, width, z_total):
+    tile_index = lax.axis_index("yz")
+    z_count = lax.axis_size("yz")
+    position = lax.broadcasted_iota(jnp.int32, field.shape, field.ndim - 2) + tile_index * z_total - width
+    valid = jnp.logical_and(position >= 0, position < z_count * z_total)
+    return jnp.where(valid, field, jnp.zeros((), field.dtype))
+
+
 def inner(padded):
     return padded[..., 1:-1, 1:-1, :]
 
@@ -82,8 +138,10 @@
 def body(velocity, old_pressure, delta_weight, marker_target, pair_owner, pair_grain, box_anchor):
     fields, cx, cz, ny = velocity.shape
     flow_fields = jnp.concatenate([velocity, old_pressure[None]], 0)
-    flow_padded = padded_of(flow_fields, 1, 2)
-    predicted = predict(flow_padded)
+    reach = 3
+    flow_wide = halo(flow_fields, reach + 1)
+    predicted_wide = predict(flow_wide)
+    predicted = predicted_wide[:, reach:-reach, reach:-reach, :]
 
     anchors = box_anchor[0]
     owners = pair_owner[0, :, 0]
@@ -178,14 +236,15 @@
             for c in range(fields)
         ]
     )
-    forced_velocity = predicted + added.reshape(fields, cx, cz, ny)
-
-    forced_x = padded_of(forced_velocity[0], 0, 1, z_faces=(jnp.zeros((cx, 1, ny), jnp.float32),) * 2)
-    forced_z = padded_of(forced_velocity[2], 0, 1, x_faces=(jnp.zeros((1, cz, ny), jnp.float32),) * 2)
-    divergence = along_x(forced_x) + along_y(forced_velocity[1]) + along_z(forced_z)
-    pressure = (neighbours(flow_padded[3]) - divergence) / 6.0
-    pressure = (neighbours(padded_of(pressure, 0, 1)) - divergence) / 6.0
-    new_velocity = forced_velocity - gradient_of(padded_of(pressure, 0, 1))
+    added = added.reshape(fields, cx, cz, ny)
+    forced_wide = inside(predicted_wide + halo(added, reach), reach, cz)
+    divergence = (
+        along_x(forced_wide[0]) + along_y(inner(forced_wide[1])) + along_z(forced_wide[2])
+    )
+    pressure = inside((neighbours(inner(flow_wide[3])) - divergence) / 6.0, reach - 1, cz)
+    pressure = inside((neighbours(pressure) - inner(divergence)) / 6.0, reach - 2, cz)
+    new_velocity = forced_wide[:, reach:-reach, reach:-reach, :] - gradient_of(pressure)
+    pressure = inner(pressure)
     return (new_velocity, pressure)
 
 

time: 113 us -> 131 us (1.16)
  starting transfers between devices: 42.8 us -> 51.7 us
  other arithmetic: 15.6 us -> 22.8 us
  local copies, waits for them, and re-layouts: 21.6 us -> 24.2 us
    ppermute x16, starting transfers between devices: 31.5 us -> 41.3 us  [the longest x8 27.8 us: sent(): return lax.ppermute(piece, ('gx', 'yz'), pairs)]
    another operation x0 -> x2, other arithmetic: none -> 4.32 us
    select_n x8 -> x4, other arithmetic: 0.22 us -> 3.2 us  [inside(): return jnp.where(valid, field, jnp.zeros((), field.dtype))]
    convert_element_type x1 -> x0, other arithmetic: 2.6 us -> none  [body(): predicted.astype(jnp.bfloat16).reshape(fields, row_total, ny)]
    slice x4 -> x6, local copies, waits for them, and re-layouts: 3.06 us -> 5.44 us  [neighbours(): return total + jnp.roll(middle, 1, -1) + jnp.roll(middle, -1, -1)]
    unnamed x70 -> x68, local copies, waits for them, and re-layouts: 4.68 us -> 2.43 us
    concatenate x5 -> x6, local copies, waits for them, and re-layouts: 2.37 us -> 4.57 us  [along_y(): return 0.5 * (jnp.roll(field, -1, -1) - jnp.roll(field, 1, -1))]
    slice x1 -> x5, other arithmetic: 0.09 us -> 2.05 us  [the longest x2 1.1 us: halo(): block[lead + (top_x, top_z, every)]]
  transfers between devices with their start and end apart: 18 -> 18, of which waited for: 8 -> 4; matrix products, arithmetic and copies ran while one was open for 12% -> 6% of each run, Pallas kernels for 0% -> 0%
where the time goes in v3:
time: 131 us; the launch traced here: 130 us
  starting transfers between devices  51.7 us (39%)
  waiting for transfers between devices  25 us (19%)
  local copies, waits for them, and re-layouts  24.2 us (18%)
  other arithmetic  22.8 us (17%)
  matrix products  5.15 us (4%)
  between operations  1.32 us (1%)
    ppermute x8, starting transfers between devices, sent(): return lax.ppermute(piece, ('gx', 'yz'), pairs)  27.8 us
    all_to_all x1, waiting for transfers between devices, body(): received = lax.all_to_all(send, 'yz', 0, 0, tiled=True)  10.3 us
    ppermute x4, starting transfers between devices, sent(): return lax.ppermute(piece, 'yz', pairs)  9.71 us
    all_to_all x1, waiting for transfers between devices, body(): back = lax.all_to_all(returned, 'yz', 0, 0, tiled=True)  7.94 us
    ppermute x8, waiting for transfers between devices, sent(): return lax.ppermute(piece, ('gx', 'yz'), pairs)  6.77 us
    all_to_all x1, starting transfers between devices, body(): received = lax.all_to_all(send, 'yz', 0, 0, tiled=True)  6.32 us
    slice x6, local copies, waits for them, and re-layouts, neighbours(): return total + jnp.roll(middle, 1, -1) + jnp.roll(middle, -1, -1)  5.44 us
    concatenate x6, local copies, waits for them, and re-layouts, along_y(): return 0.5 * (jnp.roll(field, -1, -1) - jnp.roll(field, 1, -1))  4.57 us
  transfers between devices with their start and end apart: 18, of which 4 were waited for; matrix products, arithmetic and copies ran while one was open for 6% of the time, Pallas kernels for 0%

profile of v3, /device:TPU:1, one launch (start us, length us, event | category | flops | bytes accessed | tf_op | source)
XLA Modules:
  0.0 130.1 jit_solution(16421690044587005064)
XLA Ops:
  0.7 1.1 pad_maximum_fusion.7
  1.8 3.7 %collective-permute-start = (f32[4,4,4,128]{3,2,1,0:T(4,128)S(1)}, f32[4,4,4,128]{3,2,1,0:T(4,128)S(1)}, u32[]{:S(2)}, u32[]{:S(2)}) collective-permute-start(f32[4,4,4,128]{3,2,1,0:T(4,128)S(1)} %get-tuple-element.29), channel_id=1, source_target_pairs={{0,33},{1,34},{2,35},{3,36},{4,37},{5,38},{6,39},{7,40},{8,41},{9,... | collective-permute-start | bytes 98312 | tf_op jit(solution)/shard_map/ppermute | solution.py:62
  5.5 6.8 %collective-permute-start.2 = (f32[4,4,4,128]{3,2,1,0:T(4,128)S(1)}, f32[4,4,4,128]{3,2,1,0:T(4,128)S(1)}, u32[]{:S(2)}, u32[]{:S(2)}) collective-permute-start(f32[4,4,4,128]{3,2,1,0:T(4,128)S(1)} %get-tuple-element.32), channel_id=1, source_target_pairs={{0,63},{1,32},{2,33},{3,34},{4,35},{5,36},{6,37},{7,38},{8,39},{9,... | collective-permute-start | bytes 98312 | tf_op jit(solution)/shard_map/ppermute | solution.py:62
  12.3 1.1 fusion.56
  13.4 4.8 %collective-permute-start.4 = (f32[4,32,4,128]{3,2,1,0:T(4,128)S(1)}, f32[4,32,4,128]{3,2,1,0:T(4,128)}, u32[]{:S(2)}, u32[]{:S(2)}) collective-permute-start(f32[4,32,4,128]{3,2,1,0:T(4,128)S(1)} %get-tuple-element.36), channel_id=1, source_target_pairs={{0,31},{1,0},{2,1},{3,2},{4,3},{5,4},{6,5},{7,6},{8,7},{9,8},{10,9... | collective-permute-start | bytes 786440 | tf_op jit(solution)/shard_map/ppermute | solution.py:56
  18.4 0.7 iota_compare_fusion.10
  19.3 0.6 multiply_add_fusion.1
  19.9 0.5 convert_bitcast_fusion
  20.4 0.7 iota_compare_fusion.4
  21.1 0.7 iota_compare_fusion.6
  21.9 0.7 iota_compare_fusion.8
  22.7 1.8 %collective-permute-start.1 = (f32[4,4,16,128]{3,2,1,0:T(8,128)S(1)}, f32[4,4,16,128]{3,2,1,0:T(8,128)S(1)}, u32[]{:S(2)}, u32[]{:S(2)}) collective-permute-start(f32[4,4,16,128]{3,2,1,0:T(8,128)S(1)} %get-tuple-element.33), channel_id=1, source_target_pairs={{0,32},{32,64},{64,96},{96,128},{128,160},{160,192},{192,224},{224... | collective-permute-start | bytes 393224 | tf_op jit(solution)/shard_map/ppermute | solution.py:53
  24.7 0.5 iota_add_fusion
  25.2 4.5 %collective-permute-start.7 = (f32[4,4,4,128]{3,2,1,0:T(4,128)S(1)}, f32[4,4,4,128]{3,2,1,0:T(4,128)S(1)}, u32[]{:S(2)}, u32[]{:S(2)}) collective-permute-start(f32[4,4,4,128]{3,2,1,0:T(4,128)S(1)} %get-tuple-element.31), channel_id=1, source_target_pairs={{0,255},{1,224},{2,225},{3,226},{4,227},{5,228},{6,229},{7,230},{8... | collective-permute-start | bytes 98312 | tf_op jit(solution)/shard_map/ppermute | solution.py:62
  29.7 0.7 add.324
  30.4 0.4 collective-permute-done.7
  30.9 0.6 copy-done.21
  31.5 0.7 copy-done.18
  32.2 1.7 %maximum_select_fusion = f32[4,40,24,128]{3,2,1,0:T(8,128)S(1)} fusion(f32[4,4,4,128]{3,2,1,0:T(4,128)} %copy-done.21, f32[4,4,16,128]{3,2,1,0:T(8,128)} %copy-done.19, f32[4,4,4,128]{3,2,1,0:T(4,128)S(1)} %collective-permute-done.5, f32[4,32,4,128]{3,2,1,0:T(4,128)} %collective-permute-done.4, f32[1,32,16,128]{3,2,1,0:T(8,128)S(1)} %bitcast.117, ...), kind=kLoop, calls=%fused_computation.4 | loop fusion | flops 4915200 | bytes 3932184 | tf_op jit(solution)/shard_map/jit(_where)/select_n | solution.py:98
  34.0 1.1 fusion.92
  35.1 1.1 slice_bitcast_fusion.4
  36.2 1.1 fusion.41
  37.3 2.0 %fusion.86 = (f32[3,38,22,1]{3,2,1,0:T(8,128)}, f32[3,38,22,1]{3,2,1,0:T(8,128)}) fusion(f32[4,40,24,128]{3,2,1,0:T(8,128)S(1)} %maximum_select_fusion), kind=kLoop, calls=%fused_computation.203 | loop fusion | bytes 40128 | tf_op jit(solution)/shard_map/jit(_roll_static)/slice | solution.py:121
  39.3 2.0 %fusion.87 = (f32[3,38,22,127]{3,2,1,0:T(8,128)}, f32[3,38,22,127]{3,2,1,0:T(8,128)}) fusion(f32[4,40,24,128]{3,2,1,0:T(8,128)S(1)} %maximum_select_fusion), kind=kLoop, calls=%fused_computation.204 | loop fusion | bytes 5096256 | tf_op jit(solution)/shard_map/jit(_roll_static)/slice | solution.py:121
  41.3 0.9 fusion.42
  42.2 1.3 copy.50
  43.5 1.1 copy.51
  44.6 1.3 copy.52
  45.8 1.1 copy.53
  46.9 1.9 %fusion.43 = f32[1,38,22,128]{3,2,1,0:T(8,128)S(1)} fusion(f32[1,38,22,1]{3,2,1,0:T(8,128)} %copy.51, f32[1,38,22,127]{3,2,1,0:T(8,128)} %get-tuple-element.61, f32[1,38,22,127]{3,2,1,0:T(8,128)} %get-tuple-element.60, f32[1,38,22,1]{3,2,1,0:T(8,128)} %copy.53), kind=kLoop, calls=%fused_computation.87 | loop fusion | flops 428032 | bytes 1284096 | tf_op jit(solution)/shard_map/mul | solution.py:114
  49.1 4.3 %fusion.84 = (bf16[3,38,22,128]{3,2,1,0:T(8,128)(2,1)S(1)}, f32[3,38,22,128]{3,2,1,0:T(8,128)}) fusion(f32[1,38,22,128]{3,2,1,0:T(8,128)} %get-tuple-element.57, f32[1,38,22,128]{3,2,1,0:T(8,128)S(1)} %fusion.43, f32[1,38,22,128]{3,2,1,0:T(8,128)S(1)} %copy-done.6, f32[38,22,128]{2,1,0:T(8,128)S(1)} %copy-done.5, f32[3,38,22,1]{3,2,1,0:T(8,128)} %get-tuple-element.23, ...), kind=kLoop, calls=%fused_computation.202 | loop fusion | flops 6099456 | bytes 12626944 | tf_op jit(solution)/shard_map/convert.16
  53.5 0.4 convolution_bitcast_fusion
  54.0 0.4 convolution_bitcast_fusion.1
  54.4 0.4 convolution_bitcast_fusion.2
  55.0 0.6 select_reduce_fusion
  56.0 0.4 convert_element_type.50
  56.4 0.6 fusion.27
  57.3 0.8 all_to_all.16
  58.1 6.3 %all-to-all-start = ((f32[32,4,385]{2,1,0:T(4,128)}), f32[32,4,385]{2,1,0:T(4,128)S(1)}, u32[]{:S(2)}, u32[]{:S(2)}) async-start(f32[32,4,385]{2,1,0:T(4,128)} %all_to_all.16), calls=%async_computation | async-start | bytes 524288 | tf_op jit(solution)/shard_map/all_to_all | solution.py:196
  64.5 10.3 %all-to-all-done = f32[32,4,385]{2,1,0:T(4,128)S(1)} async-done(((f32[32,4,385]{2,1,0:T(4,128)}), f32[32,4,385]{2,1,0:T(4,128)S(1)}, u32[]{:S(2)}, u32[]{:S(2)}) %all-to-all-start) | async-done | bytes 197152 | tf_op jit(solution)/shard_map/all_to_all | solution.py:196
  75.5 0.7 all_to_all.19
  76.2 4.1 %all-to-all-start.1 = ((bf16[32,4,384]{2,1,0:T(4,128)(2,1)}), bf16[32,4,384]{2,1,0:T(4,128)(2,1)S(1)}, u32[]{:S(2)}, u32[]{:S(2)}) async-start(bf16[32,4,384]{2,1,0:T(4,128)(2,1)} %all_to_all.19), calls=%async_computation.1 | async-start | bytes 196608 | tf_op jit(solution)/shard_map/all_to_all | solution.py:209
  80.3 0.9 fusion.90
  81.2 7.9 %all-to-all-done.1 = bf16[32,4,384]{2,1,0:T(4,128)(2,1)S(1)} async-done(((bf16[32,4,384]{2,1,0:T(4,128)(2,1)}), bf16[32,4,384]{2,1,0:T(4,128)(2,1)S(1)}, u32[]{:S(2)}, u32[]{:S(2)}) %all-to-all-start.1) | async-done | bytes 98336 | tf_op jit(solution)/shard_map/all_to_all | solution.py:209
  89.4 0.4 convolution_bitcast_fusion.3
  89.8 0.4 reshape.579
  90.2 3.2 %slice_reduce_fusion.7 = (f32[3,512]{1,0:T(4,128)S(1)}, f32[3,512]{1,0:T(4,128)S(1)}, f32[3,512]{1,0:T(4,128)S(1)}, f32[3,512]{1,0:T(4,128)S(1)}, f32[3,512]{1,0...) fusion(f32[3,512,8]{2,1,0:T(8,128)S(1)} %reshape.579), kind=kLoop, calls=%fused_computation.51 | loop fusion | bytes 98304 | tf_op jit(solution)/shard_map/slice | solution.py:222
  93.4 0.5 select_add_fusion
  93.9 0.6 fusion.16
  94.6 0.6 fusion.19
  95.2 0.6 fusion.22
  96.0 6.4 %collective-permute-start.10 = (f32[3,3,3,128]{3,2,1,0:T(4,128)S(1)}, f32[3,3,3,128]{3,2,1,0:T(4,128)S(1)}, u32[]{:S(2)}, u32[]{:S(2)}) collective-permute-start(f32[3,3,3,128]{3,2,1,0:T(4,128)S(1)} %get-tuple-element.40), channel_id=1, source_target_pairs={{0,63},{1,32},{2,33},{3,34},{4,35},{5,36},{6,37},{7,38},{8,39},{9,... | collective-permute-start | bytes 41480 | tf_op jit(solution)/shard_map/ppermute | solution.py:62
  102.4 6.5 %collective-permute-start.15 = (f32[3,3,3,128]{3,2,1,0:T(4,128)S(1)}, f32[3,3,3,128]{3,2,1,0:T(4,128)S(1)}, u32[]{:S(2)}, u32[]{:S(2)}) collective-permute-start(f32[3,3,3,128]{3,2,1,0:T(4,128)S(1)} %get-tuple-element.38), channel_id=1, source_target_pairs={{0,255},{1,224},{2,225},{3,226},{4,227},{5,228},{6,229},{7,230},{8... | collective-permute-start | bytes 41480 | tf_op jit(solution)/shard_map/ppermute | solution.py:62
  109.0 4.8 %collective-permute-start.12 = (f32[3,32,3,128]{3,2,1,0:T(4,128)S(1)}, f32[3,32,3,128]{3,2,1,0:T(4,128)S(1)}, u32[]{:S(2)}, u32[]{:S(2)}) collective-permute-start(f32[3,32,3,128]{3,2,1,0:T(4,128)S(1)} %get-tuple-element.44), channel_id=1, source_target_pairs={{0,31},{1,0},{2,1},{3,2},{4,3},{5,4},{6,5},{7,6},{8,7},{9,8},{10,9... | collective-permute-start | bytes 442376 | tf_op jit(solution)/shard_map/ppermute | solution.py:56
  114.0 1.5 %collective-permute-start.9 = (f32[3,3,16,128]{3,2,1,0:T(8,128)S(1)}, f32[3,3,16,128]{3,2,1,0:T(8,128)S(1)}, u32[]{:S(2)}, u32[]{:S(2)}) collective-permute-start(f32[3,3,16,128]{3,2,1,0:T(8,128)S(1)} %get-tuple-element.41), channel_id=1, source_target_pairs={{0,32},{32,64},{64,96},{96,128},{128,160},{160,192},{192,224},{224... | collective-permute-start | bytes 221192 | tf_op jit(solution)/shard_map/ppermute | solution.py:53
  115.7 6.3 %collective-permute-done.8 = f32[3,3,3,128]{3,2,1,0:T(4,128)S(1)} collective-permute-done((f32[3,3,3,128]{3,2,1,0:T(4,128)S(1)}, f32[3,3,3,128]{3,2,1,0:T(4,128)S(1)}, u32[]{:S(2)}, u32[]{:S(2)}) %collective-permute-start.8) | collective-permute-done | bytes 13856 | tf_op jit(solution)/shard_map/ppermute | solution.py:62
  122.0 0.4 fusion.15
  122.9 0.6 copy-done.7
  123.5 0.7 fusion.51
  124.6 0.4 fusion.53
  125.1 0.9 slice_bitcast_fusion.6
  126.0 0.9 fusion.97
  127.8 1.3 fusion.62
  129.1 1.0 slice_subtract_fusion
  (128 shorter events, 5.4 us)
Async XLA Ops:
  0.6 55.7 %copy-start = (bf16[1,32,128,128]{3,2,1,0:T(8,128)(2,1)S(1)}, bf16[1,32,128,128]{3,2,1,0:T(8,128)(2,1)}, u32[]{:S(2)}) copy-start(bf16[1,32,128,128]{3,2,1,0:T(8,128)(2,1)} %param.9) | copy-start | bytes 3145732
  0.6 11.6 %copy-start.1 = (f32[3,32,16,128]{3,2,1,0:T(8,128)S(1)}, f32[3,32,16,128]{3,2,1,0:T(8,128)}, u32[]{:S(2)}) copy-start(f32[3,32,16,128]{3,2,1,0:T(8,128)} %param.7) | copy-start | bytes 2359300
  0.7 17.6 %copy-start.25 = (s32[1,32,3]{1,0,2:T(1,128)S(1)}, s32[1,32,3]{1,0,2:T(1,128)}, u32[]{:S(2)}) copy-start(s32[1,32,3]{1,0,2:T(1,128)} %param.13) | copy-start | bytes 1156
  0.7 18.5 %copy-start.27 = (s32[1,32,1]{1,2,0:T(1,128)S(1)}, s32[1,32,1]{1,2,0:T(1,128)}, u32[]{:S(2)}) copy-start(s32[1,32,1]{1,2,0:T(1,128)} %param.11) | copy-start | bytes 388
  0.7 19.2 %copy-start.28 = (s32[1,32]{1,0:T(1,128)S(1)}, s32[1,32]{1,0:T(1,128)}, u32[]{:S(2)}) copy-start(s32[1,32]{1,0:T(1,128)} %param.12) | copy-start | bytes 388
  1.8 20.9 %copy-start.4 = (f32[32,16,128]{2,1,0:T(8,128)S(1)}, f32[32,16,128]{2,1,0:T(8,128)}, u32[]{:S(2)}) copy-start(f32[32,16,128]{2,1,0:T(8,128)} %param.8) | copy-start | bytes 786436
  1.8 20.9 %collective-permute-start = (f32[4,4,4,128]{3,2,1,0:T(4,128)S(1)}, f32[4,4,4,128]{3,2,1,0:T(4,128)S(1)}, u32[]{:S(2)}, u32[]{:S(2)}) collective-permute-start(f32[4,4,4,128]{3,2,1,0:T(4,128)S(1)} %get-tuple-element.29), channel_id=1, source_target_pairs={{0,33},{1,34},{2,35},{3,36},{4,37},{5,38},{6,39},{7,40},{8,41},{9,... | collective-permute-start | bytes 98312 | tf_op jit(solution)/shard_map/ppermute | solution.py:62
  5.5 19.1 %collective-permute-start.2 = (f32[4,4,4,128]{3,2,1,0:T(4,128)S(1)}, f32[4,4,4,128]{3,2,1,0:T(4,128)S(1)}, u32[]{:S(2)}, u32[]{:S(2)}) collective-permute-start(f32[4,4,4,128]{3,2,1,0:T(4,128)S(1)} %get-tuple-element.32), channel_id=1, source_target_pairs={{0,63},{1,32},{2,33},{3,34},{4,35},{5,36},{6,37},{7,38},{8,39},{9,... | collective-permute-start | bytes 98312 | tf_op jit(solution)/shard_map/ppermute | solution.py:62
  12.3 12.9 %collective-permute-start.5 = (f32[4,4,4,128]{3,2,1,0:T(4,128)S(1)}, f32[4,4,4,128]{3,2,1,0:T(4,128)S(1)}, u32[]{:S(2)}, u32[]{:S(2)}) collective-permute-start(f32[4,4,4,128]{3,2,1,0:T(4,128)S(1)} %get-tuple-element.30), channel_id=1, source_target_pairs={{0,225},{1,226},{2,227},{3,228},{4,229},{5,230},{6,231},{7,232},{8... | collective-permute-start | bytes 98312 | tf_op jit(solution)/shard_map/ppermute | solution.py:62
  13.4 17.5 %collective-permute-start.3 = (f32[4,32,4,128]{3,2,1,0:T(4,128)S(1)}, f32[4,32,4,128]{3,2,1,0:T(4,128)S(1)}, u32[]{:S(2)}, u32[]{:S(2)}) collective-permute-start(f32[4,32,4,128]{3,2,1,0:T(4,128)S(1)} %get-tuple-element.35), channel_id=1, source_target_pairs={{0,1},{1,2},{2,3},{3,4},{4,5},{5,6},{6,7},{7,8},{8,9},{9,10},{10,1... | collective-permute-start | bytes 786440 | tf_op jit(solution)/shard_map/ppermute | solution.py:56
  13.4 18.8 %collective-permute-start.4 = (f32[4,32,4,128]{3,2,1,0:T(4,128)S(1)}, f32[4,32,4,128]{3,2,1,0:T(4,128)}, u32[]{:S(2)}, u32[]{:S(2)}) collective-permute-start(f32[4,32,4,128]{3,2,1,0:T(4,128)S(1)} %get-tuple-element.36), channel_id=1, source_target_pairs={{0,31},{1,0},{2,1},{3,2},{4,3},{5,4},{6,5},{7,6},{8,7},{9,8},{10,9... | collective-permute-start | bytes 786440 | tf_op jit(solution)/shard_map/ppermute | solution.py:56
  21.9 8.5 %copy-start.26 = (f32[32,1]{0,1:T(1,128)S(1)}, f32[32,1]{0,1:T(1,128)}, u32[]{:S(2)}) copy-start(f32[32,1]{0,1:T(1,128)} %convert_bitcast_fusion) | copy-start | bytes 388
  22.7 8.2 %collective-permute-start.1 = (f32[4,4,16,128]{3,2,1,0:T(8,128)S(1)}, f32[4,4,16,128]{3,2,1,0:T(8,128)S(1)}, u32[]{:S(2)}, u32[]{:S(2)}) collective-permute-start(f32[4,4,16,128]{3,2,1,0:T(8,128)S(1)} %get-tuple-element.33), channel_id=1, source_target_pairs={{0,32},{32,64},{64,96},{96,128},{128,160},{160,192},{192,224},{224... | collective-permute-start | bytes 393224 | tf_op jit(solution)/shard_map/ppermute | solution.py:53
  24.5 6.3 %collective-permute-start.6 = (f32[4,4,16,128]{3,2,1,0:T(8,128)S(1)}, f32[4,4,16,128]{3,2,1,0:T(8,128)S(1)}, u32[]{:S(2)}, u32[]{:S(2)}) collective-permute-start(f32[4,4,16,128]{3,2,1,0:T(8,128)S(1)} %get-tuple-element.34), channel_id=1, source_target_pairs={{0,224},{32,0},{64,32},{96,64},{128,96},{160,128},{192,160},{224,1... | collective-permute-start | bytes 393224 | tf_op jit(solution)/shard_map/ppermute | solution.py:53
  25.2 5.7 %collective-permute-start.7 = (f32[4,4,4,128]{3,2,1,0:T(4,128)S(1)}, f32[4,4,4,128]{3,2,1,0:T(4,128)S(1)}, u32[]{:S(2)}, u32[]{:S(2)}) collective-permute-start(f32[4,4,4,128]{3,2,1,0:T(4,128)S(1)} %get-tuple-element.31), channel_id=1, source_target_pairs={{0,255},{1,224},{2,225},{3,226},{4,227},{5,228},{6,229},{7,230},{8... | collective-permute-start | bytes 98312 | tf_op jit(solution)/shard_map/ppermute | solution.py:62
  30.9 0.6 copy-start.21
  30.9 0.7 copy-start.19
  31.5 0.7 copy-start.18
  46.9 1.9 %copy-start.2 = (f32[3,38,22,1]{3,2,1,0:T(8,128)S(1)}, f32[3,38,22,1]{3,2,1,0:T(8,128)}, u32[]{:S(2)}) copy-start(f32[3,38,22,1]{3,2,1,0:T(8,128)} %get-tuple-element.22) | copy-start | bytes 30100
  46.9 2.0 %copy-start.5 = (f32[38,22,128]{2,1,0:T(8,128)S(1)}, f32[38,22,128]{2,1,0:T(8,128)}, u32[]{:S(2)}) copy-start(f32[38,22,128]{2,1,0:T(8,128)} %fusion.42) | copy-start | bytes 1284100
  46.9 2.1 %copy-start.6 = (f32[1,38,22,128]{3,2,1,0:T(8,128)S(1)}, f32[1,38,22,128]{3,2,1,0:T(8,128)}, u32[]{:S(2)}) copy-start(f32[1,38,22,128]{3,2,1,0:T(8,128)} %get-tuple-element.56) | copy-start | bytes 1284100
  49.0 4.5 %copy-start.24 = (s32[512]{0:T(512)S(1)}, s32[512]{0:T(512)}, u32[]{:S(2)}) copy-start(s32[512]{0:T(512)} %add.324) | copy-start | bytes 6148
  53.3 1.6 %copy-start.10 = (pred[512,128]{0,1:T(8,128)(4,1)S(1)}, pred[512,128]{0,1:T(8,128)(4,1)}, u32[]{:S(2)}) copy-start(pred[512,128]{0,1:T(8,128)(4,1)} %get-tuple-element.95) | copy-start | bytes 196612
  53.3 1.6 %copy-start.11 = (pred[512,128]{0,1:T(8,128)(4,1)S(1)}, pred[512,128]{0,1:T(8,128)(4,1)}, u32[]{:S(2)}) copy-start(pred[512,128]{0,1:T(8,128)(4,1)} %get-tuple-element.96) | copy-start | bytes 196612
  53.3 1.6 %copy-start.12 = (pred[512,128]{0,1:T(8,128)(4,1)S(1)}, pred[512,128]{0,1:T(8,128)(4,1)}, u32[]{:S(2)}) copy-start(pred[512,128]{0,1:T(8,128)(4,1)} %get-tuple-element.89) | copy-start | bytes 196612
  53.3 1.6 %copy-start.13 = (pred[512,128]{0,1:T(8,128)(4,1)S(1)}, pred[512,128]{0,1:T(8,128)(4,1)}, u32[]{:S(2)}) copy-start(pred[512,128]{0,1:T(8,128)(4,1)} %get-tuple-element.90) | copy-start | bytes 196612
  53.3 1.6 %copy-start.14 = (pred[512,128]{0,1:T(8,128)(4,1)S(1)}, pred[512,128]{0,1:T(8,128)(4,1)}, u32[]{:S(2)}) copy-start(pred[512,128]{0,1:T(8,128)(4,1)} %get-tuple-element.91) | copy-start | bytes 196612
  53.4 1.6 %copy-start.15 = (pred[512,128]{0,1:T(8,128)(4,1)S(1)}, pred[512,128]{0,1:T(8,128)(4,1)}, u32[]{:S(2)}) copy-start(pred[512,128]{0,1:T(8,128)(4,1)} %get-tuple-element.92) | copy-start | bytes 196612
  53.4 1.6 %copy-start.16 = (pred[512,128]{0,1:T(8,128)(4,1)S(1)}, pred[512,128]{0,1:T(8,128)(4,1)}, u32[]{:S(2)}) copy-start(pred[512,128]{0,1:T(8,128)(4,1)} %get-tuple-element.93) | copy-start | bytes 196612
  53.4 1.6 %copy-start.17 = (pred[512,128]{0,1:T(8,128)(4,1)S(1)}, pred[512,128]{0,1:T(8,128)(4,1)}, u32[]{:S(2)}) copy-start(pred[512,128]{0,1:T(8,128)(4,1)} %get-tuple-element.94) | copy-start | bytes 196612
  55.6 1.4 %copy-start.22 = (s32[32]{0:T(128)S(1)}, s32[32]{0:T(128)}, u32[]{:S(2)}) copy-start(s32[32]{0:T(128)} %multiply_add_fusion.1) | copy-start | bytes 388
  56.3 8.1 %copy-start.20 = (f32[1,32,3,128]{3,1,2,0:T(8,128)S(1)}, f32[1,32,3,128]{3,1,2,0:T(8,128)}, u32[]{:S(2)}) copy-start(f32[1,32,3,128]{3,1,2,0:T(8,128)} %param.10) | copy-start | bytes 147460
  56.4 18.7 %copy-start.23 = (f32[32]{0:T(128)S(1)}, f32[32]{0:T(128)}, u32[]{:S(2)}) copy-start(f32[32]{0:T(128)} %iota_add_fusion) | copy-start | bytes 388
  58.1 16.7 %all-to-all-start = ((f32[32,4,385]{2,1,0:T(4,128)}), f32[32,4,385]{2,1,0:T(4,128)S(1)}, u32[]{:S(2)}, u32[]{:S(2)}) async-start(f32[32,4,385]{2,1,0:T(4,128)} %all_to_all.16), calls=%async_computation | async-start | bytes 524288 | tf_op jit(solution)/shard_map/all_to_all | solution.py:196
  76.2 12.9 %all-to-all-start.1 = ((bf16[32,4,384]{2,1,0:T(4,128)(2,1)}), bf16[32,4,384]{2,1,0:T(4,128)(2,1)S(1)}, u32[]{:S(2)}, u32[]{:S(2)}) async-start(bf16[32,4,384]{2,1,0:T(4,128)(2,1)} %all_to_all.19), calls=%async_computation.1 | async-start | bytes 196608 | tf_op jit(solution)/shard_map/all_to_all | solution.py:209
  96.0 26.0 %copy-start.3 = (f32[3,38,22,128]{3,2,1,0:T(8,128)S(1)}, f32[3,38,22,128]{3,2,1,0:T(8,128)}, u32[]{:S(2)}) copy-start(f32[3,38,22,128]{3,2,1,0:T(8,128)} %get-tuple-element.21) | copy-start | bytes 3852292
  96.0 17.7 %collective-permute-start.10 = (f32[3,3,3,128]{3,2,1,0:T(4,128)S(1)}, f32[3,3,3,128]{3,2,1,0:T(4,128)S(1)}, u32[]{:S(2)}, u32[]{:S(2)}) collective-permute-start(f32[3,3,3,128]{3,2,1,0:T(4,128)S(1)} %get-tuple-element.40), channel_id=1, source_target_pairs={{0,63},{1,32},{2,33},{3,34},{4,35},{5,36},{6,37},{7,38},{8,39},{9,... | collective-permute-start | bytes 41480 | tf_op jit(solution)/shard_map/ppermute | solution.py:62
  102.4 11.7 %collective-permute-start.13 = (f32[3,3,3,128]{3,2,1,0:T(4,128)S(1)}, f32[3,3,3,128]{3,2,1,0:T(4,128)S(1)}, u32[]{:S(2)}, u32[]{:S(2)}) collective-permute-start(f32[3,3,3,128]{3,2,1,0:T(4,128)S(1)} %get-tuple-element.39), channel_id=1, source_target_pairs={{0,225},{1,226},{2,227},{3,228},{4,229},{5,230},{6,231},{7,232},{8... | collective-permute-start | bytes 41480 | tf_op jit(solution)/shard_map/ppermute | solution.py:62
  102.4 13.1 %collective-permute-start.15 = (f32[3,3,3,128]{3,2,1,0:T(4,128)S(1)}, f32[3,3,3,128]{3,2,1,0:T(4,128)S(1)}, u32[]{:S(2)}, u32[]{:S(2)}) collective-permute-start(f32[3,3,3,128]{3,2,1,0:T(4,128)S(1)} %get-tuple-element.38), channel_id=1, source_target_pairs={{0,255},{1,224},{2,225},{3,226},{4,227},{5,228},{6,229},{7,230},{8... | collective-permute-start | bytes 41480 | tf_op jit(solution)/shard_map/ppermute | solution.py:62
  108.9 13.1 %collective-permute-start.11 = (f32[3,32,3,128]{3,2,1,0:T(4,128)S(1)}, f32[3,32,3,128]{3,2,1,0:T(4,128)S(1)}, u32[]{:S(2)}, u32[]{:S(2)}) collective-permute-start(f32[3,32,3,128]{3,2,1,0:T(4,128)S(1)} %get-tuple-element.43), channel_id=1, source_target_pairs={{0,1},{1,2},{2,3},{3,4},{4,5},{5,6},{6,7},{7,8},{8,9},{9,10},{10,1... | collective-permute-start | bytes 442376 | tf_op jit(solution)/shard_map/ppermute | solution.py:56
  109.0 13.1 %collective-permute-start.12 = (f32[3,32,3,128]{3,2,1,0:T(4,128)S(1)}, f32[3,32,3,128]{3,2,1,0:T(4,128)S(1)}, u32[]{:S(2)}, u32[]{:S(2)}) collective-permute-start(f32[3,32,3,128]{3,2,1,0:T(4,128)S(1)} %get-tuple-element.44), channel_id=1, source_target_pairs={{0,31},{1,0},{2,1},{3,2},{4,3},{5,4},{6,5},{7,6},{8,7},{9,8},{10,9... | collective-permute-start | bytes 442376 | tf_op jit(solution)/shard_map/ppermute | solution.py:56
  113.7 8.3 %collective-permute-start.14 = (f32[3,3,16,128]{3,2,1,0:T(8,128)S(1)}, f32[3,3,16,128]{3,2,1,0:T(8,128)S(1)}, u32[]{:S(2)}, u32[]{:S(2)}) collective-permute-start(f32[3,3,16,128]{3,2,1,0:T(8,128)S(1)} %get-tuple-element.42), channel_id=1, source_target_pairs={{0,224},{32,0},{64,32},{96,64},{128,96},{160,128},{192,160},{224,1... | collective-permute-start | bytes 221192 | tf_op jit(solution)/shard_map/ppermute | solution.py:53
  114.0 8.0 %collective-permute-start.9 = (f32[3,3,16,128]{3,2,1,0:T(8,128)S(1)}, f32[3,3,16,128]{3,2,1,0:T(8,128)S(1)}, u32[]{:S(2)}, u32[]{:S(2)}) collective-permute-start(f32[3,3,16,128]{3,2,1,0:T(8,128)S(1)} %get-tuple-element.41), channel_id=1, source_target_pairs={{0,32},{32,64},{64,96},{96,128},{128,160},{160,192},{192,224},{224... | collective-permute-start | bytes 221192 | tf_op jit(solution)/shard_map/ppermute | solution.py:53
  115.5 6.5 %collective-permute-start.8 = (f32[3,3,3,128]{3,2,1,0:T(4,128)S(1)}, f32[3,3,3,128]{3,2,1,0:T(4,128)S(1)}, u32[]{:S(2)}, u32[]{:S(2)}) collective-permute-start(f32[3,3,3,128]{3,2,1,0:T(4,128)S(1)} %get-tuple-element.37), channel_id=1, source_target_pairs={{0,33},{1,34},{2,35},{3,36},{4,37},{5,38},{6,39},{7,40},{8,41},{9,... | collective-permute-start | bytes 41480 | tf_op jit(solution)/shard_map/ppermute | solution.py:62
  122.5 1.0 copy-start.7
  127.7 1.3 %copy-start.8 = (f32[1,32,16,128]{3,2,1,0:T(8,128)S(1)}, f32[1,32,16,128]{3,2,1,0:T(8,128)}, u32[]{:S(2)}) copy-start(f32[1,32,16,128]{3,2,1,0:T(8,128)} %get-tuple-element.71) | copy-start | bytes 786436
  127.7 1.3 %copy-start.9 = (f32[1,32,16,128]{3,2,1,0:T(8,128)S(1)}, f32[1,32,16,128]{3,2,1,0:T(8,128)}, u32[]{:S(2)}) copy-start(f32[1,32,16,128]{3,2,1,0:T(8,128)} %get-tuple-element.72) | copy-start | bytes 786436

commit v4 on v2

--- a/solution.py
+++ b/solution.py
@@ -129,16 +129,15 @@
     slots = jnp.sum(jnp.logical_and(same_owner, earlier), axis=1).astype(jnp.int32)
     places = owners * S + slots
     dispatch = (jnp.arange(tiles * S, dtype=jnp.int32)[:, None] == places[None, :]).astype(jnp.float32)
-    packed = jnp.concatenate(
-        [flat_partial, (grains + 1).astype(jnp.float32)[:, None]], axis=1
-    )
     send = jnp.dot(
-        dispatch, packed, precision=lax.Precision.HIGHEST, preferred_element_type=jnp.float32
-    )
-    received = lax.all_to_all(send, "yz", 0, 0, tiled=True)
-    received_grain = received[:, row_width]
-    received_values = received[:, :row_width]
-    slot_numbers = jnp.arange(grain_slots, dtype=jnp.float32) + 1.0
+        dispatch, flat_partial, precision=lax.Precision.HIGHEST, preferred_element_type=jnp.float32
+    )
+    send_grain = jnp.sum(
+        jnp.where(dispatch > 0, (grains + 1)[None, :], 0), axis=1
+    ).astype(jnp.int32)
+    received_grain = lax.all_to_all(send_grain, "yz", 0, 0, tiled=True)
+    received_values = lax.all_to_all(send, "yz", 0, 0, tiled=True)
+    slot_numbers = jnp.arange(grain_slots, dtype=jnp.int32) + 1
     select = (slot_numbers[:, None] == received_grain[None, :]).astype(jnp.float32)
     summed = jnp.dot(
         select, received_values, precision=lax.Precision.HIGHEST, preferred_element_type=jnp.float32

time: 113 us -> 122 us (1.080)
  starting transfers between devices: 42.8 us -> 51.9 us
  waiting for transfers between devices: 25.9 us -> 21.9 us
  other arithmetic: 15.6 us -> 17.2 us
    all_to_all x1 -> x2, starting transfers between devices: 6.7 us -> 15.3 us  [the longest x1 9.28 us: body(): received_values = lax.all_to_all(send, 'yz', 0, 0, tiled=True)]
    all_to_all x1 -> x2, waiting for transfers between devices: 10.3 us -> 7.7 us  [the longest x1 7.7 us: body(): received_values = lax.all_to_all(send, 'yz', 0, 0, tiled=True)]
    ppermute x8, starting transfers between devices: 24.8 us -> 26.6 us  [faces(): high = lax.ppermute(lax.slice_in_dim(block, 0, 1, axis=dim), axis, backward)]
    all_to_all x0 -> x1, other arithmetic: none -> 1.43 us  [body(): received_grain = lax.all_to_all(send_grain, 'yz', 0, 0, tiled=True)]
    unnamed x70 -> x71, local copies, waits for them, and re-layouts: 4.68 us -> 5.23 us
  transfers between devices with their start and end apart: 18 -> 19, of which waited for: 8 -> 7; matrix products, arithmetic and copies ran while one was open for 12% -> 22% of each run, Pallas kernels for 0% -> 0%
where the time goes in v4:
time: 122 us; the launch traced here: 120 us
  starting transfers between devices  51.9 us (43%)
  local copies, waits for them, and re-layouts  22.8 us (19%)
  waiting for transfers between devices  21.9 us (18%)
  other arithmetic  17.2 us (14%)
  matrix products  5.16 us (4%)
  between operations  1.44 us (1%)
    ppermute x8, starting transfers between devices, faces(): high = lax.ppermute(lax.slice_in_dim(block, 0, 1, axis=dim), axis, backward)  26.6 us
    all_to_all x1, starting transfers between devices, body(): received_values = lax.all_to_all(send, 'yz', 0, 0, tiled=True)  9.28 us
    all_to_all x1, waiting for transfers between devices, body(): back = lax.all_to_all(returned, 'yz', 0, 0, tiled=True)  8.34 us
    all_to_all x1, waiting for transfers between devices, body(): received_values = lax.all_to_all(send, 'yz', 0, 0, tiled=True)  7.7 us
    all_to_all x1, starting transfers between devices, body(): received_grain = lax.all_to_all(send_grain, 'yz', 0, 0, tiled=True)  6.05 us
    ppermute x8, starting transfers between devices, faces(): lax.ppermute(lax.slice_in_dim(block, block.shape[dim] - 1, None, axis=dim...  5.98 us
    unnamed x71, local copies, waits for them, and re-layouts  5.23 us
    all_to_all x1, starting transfers between devices, body(): back = lax.all_to_all(returned, 'yz', 0, 0, tiled=True)  4.04 us
  transfers between devices with their start and end apart: 19, of which 7 were waited for; matrix products, arithmetic and copies ran while one was open for 22% of the time, Pallas kernels for 0%

profile of v4, /device:TPU:1, one launch (start us, length us, event | category | flops | bytes accessed | tf_op | source)
XLA Modules:
  0.0 120.4 jit_solution(11029747472557391842)
XLA Ops:
  0.7 0.9 pad_maximum_fusion.38
  1.6 3.2 %collective-permute-start.2 = (f32[4,1,16,128]{3,2,1,0:T(8,128)S(1)}, f32[4,1,16,128]{3,2,1,0:T(8,128)S(1)}, u32[]{:S(2)}, u32[]{:S(2)}) collective-permute-start(f32[4,1,16,128]{3,2,1,0:T(8,128)S(1)} %get-tuple-element.25), channel_id=1, source_target_pairs={{32,0},{64,32},{96,64},{128,96},{160,128},{192,160},{224,192},{0,2... | collective-permute-start | bytes 98312 | tf_op jit(solution)/shard_map/ppermute | solution.py:23
  4.9 7.5 %collective-permute-start.1 = (f32[4,32,1,128]{3,2,1,0:T(1,128)S(1)}, f32[4,32,1,128]{3,2,1,0:T(1,128)S(1)}, u32[]{:S(2)}, u32[]{:S(2)}) collective-permute-start(f32[4,32,1,128]{3,2,1,0:T(1,128)S(1)} %get-tuple-element.23), channel_id=1, source_target_pairs={{1,0},{2,1},{3,2},{4,3},{5,4},{6,5},{7,6},{8,7},{9,8},{10,9},{11,1... | collective-permute-start | bytes 196616 | tf_op jit(solution)/shard_map/ppermute | solution.py:23
  12.4 0.7 copy-done.29
  13.3 0.6 copy-done.30
  13.9 0.6 copy-done.27
  14.6 0.7 all_to_all.20
  15.3 6.1 %all-to-all-start = ((s32[32,4,1]{1,2,0:T(1,128)}), s32[32,4,1]{1,2,0:T(1,128)}, u32[]{:S(2)}, u32[]{:S(2)}) async-start(s32[32,4,1]{1,2,0:T(1,128)} %bitcast.14), calls=%async_computation | async-start | bytes 32768 | tf_op jit(solution)/shard_map/all_to_all | solution.py:138
  21.3 0.7 multiply_bitcast_fusion.2
  22.1 1.4 %fusion.86 = (f32[3,32,16,1]{3,2,1,0:T(8,128)}, f32[3,32,16,1]{3,2,1,0:T(8,128)}) fusion(f32[3,32,16,128]{3,2,1,0:T(8,128)S(1)} %copy-done.1), kind=kLoop, calls=%fused_computation.224 | loop fusion | bytes 24576 | tf_op jit(solution)/shard_map/jit(_roll_static)/slice | solution.py:65
  23.5 1.4 %fusion.87 = (f32[3,32,16,127]{3,2,1,0:T(8,128)}, f32[3,32,16,127]{3,2,1,0:T(8,128)}) fusion(f32[3,32,16,128]{3,2,1,0:T(8,128)S(1)} %copy-done.1), kind=kLoop, calls=%fused_computation.225 | loop fusion | bytes 3121152 | tf_op jit(solution)/shard_map/jit(_roll_static)/slice | solution.py:65
  24.9 0.7 copy-done.26
  25.7 0.7 iota_compare_fusion.10
  26.4 0.7 iota_compare_fusion.4
  27.1 0.7 iota_compare_fusion.8
  27.9 0.7 iota_compare_fusion.6
  28.7 0.6 multiply_add_fusion.1
  29.2 0.7 add.289
  30.1 0.4 copy-done.21
  30.6 1.0 fusion.88
  31.8 1.0 multiply_bitcast_fusion.1
  33.6 1.3 %fusion.63 = f32[1,32,16,128]{3,2,1,0:T(8,128)S(1)} fusion(f32[1,32,16,1]{3,2,1,0:T(8,128)S(1)} %copy.66, f32[1,32,16,127]{3,2,1,0:T(8,128)S(1)} %get-tuple-element.40, f32[1,32,16,127]{3,2,1,0:T(8,128)} %get-tuple-element.41, f32[1,32,16,1]{3,2,1,0:T(8,128)S(1)} %copy.68), kind=kLoop, calls=%fused_computation.137 | loop fusion | flops 262144 | bytes 786432 | tf_op jit(solution)/shard_map/mul | solution.py:58
  34.9 2.6 %fusion.84 = (bf16[3,32,16,128]{3,2,1,0:T(8,128)(2,1)S(1)}, f32[3,32,16,128]{3,2,1,0:T(8,128)S(1)}) fusion(f32[1,32,16,128]{3,2,1,0:T(8,128)} %get-tuple-element.44, f32[1,32,16,128]{3,2,1,0:T(8,128)S(1)} %fusion.63, f32[1,32,16,128]{3,2,1,0:T(8,128)S(1)} %copy-done.12, f32[3,32,16,128]{3,2,1,0:T(8,128)S(1)} %copy-done.1, f32[32,16,128]{2,1,0:T(8,128)S(1)} %copy-done.9, ...), kind=kLoop, calls=%fused_computation.223 | loop fusion | flops 6094848 | bytes 5054464 | tf_op jit(solution)/shard_map/convert_element_type | solution.py:105
  37.5 0.7 copy-done.25
  38.2 0.4 convolution_bitcast_fusion
  38.6 0.4 convolution_bitcast_fusion.1
  39.2 0.4 convolution_bitcast_fusion.2
  40.1 0.6 select_reduce_fusion
  41.5 0.6 fusion.17
  42.2 0.6 copy-done.24
  43.1 0.8 copy.73
  43.9 9.3 %all-to-all-start.1 = ((f32[32,4,384]{2,1,0:T(4,128)}), f32[32,4,384]{2,1,0:T(4,128)S(1)}, u32[]{:S(2)}, u32[]{:S(2)}) async-start(f32[32,4,384]{2,1,0:T(4,128)} %copy.73), calls=%async_computation.1 | async-start | bytes 393216 | tf_op jit(solution)/shard_map/all_to_all | solution.py:139
  53.3 0.6 broadcast.465
  53.8 1.4 %reduce.19 = s32[32,4]{1,0:T(8,128)S(1)} reduce(s32[32,4,1]{1,2,0:T(1,128)} %all-to-all-done, s32[]{:T(128)} %broadcast.465), dimensions={2}, to_apply=%all_to_all.21.reduce_sub_computation.3 | reduce | bytes 1028 | tf_op jit(solution)/shard_map/all_to_all | solution.py:138
  55.4 7.7 %all-to-all-done.1 = f32[32,4,384]{2,1,0:T(4,128)S(1)} async-done(((f32[32,4,384]{2,1,0:T(4,128)}), f32[32,4,384]{2,1,0:T(4,128)S(1)}, u32[]{:S(2)}, u32[]{:S(2)}) %all-to-all-start.1) | async-done | bytes 196640 | tf_op jit(solution)/shard_map/all_to_all | solution.py:139
  63.7 0.7 all_to_all.24
  64.3 4.0 %all-to-all-start.2 = ((bf16[32,4,384]{2,1,0:T(4,128)(2,1)}), bf16[32,4,384]{2,1,0:T(4,128)(2,1)S(1)}, u32[]{:S(2)}, u32[]{:S(2)}) async-start(bf16[32,4,384]{2,1,0:T(4,128)(2,1)} %all_to_all.24), calls=%async_computation.2 | async-start | bytes 196608 | tf_op jit(solution)/shard_map/all_to_all | solution.py:150
  68.4 0.6 multiply_add_fusion
  69.0 8.3 %all-to-all-done.2 = bf16[32,4,384]{2,1,0:T(4,128)(2,1)S(1)} async-done(((bf16[32,4,384]{2,1,0:T(4,128)(2,1)}), bf16[32,4,384]{2,1,0:T(4,128)(2,1)S(1)}, u32[]{:S(2)}, u32[]{:S(2)}) %all-to-all-start.2) | async-done | bytes 98336 | tf_op jit(solution)/shard_map/all_to_all | solution.py:150
  77.6 0.4 convolution_bitcast_fusion.3
  78.0 0.4 reshape.586
  78.4 3.2 %slice_reduce_fusion.7 = (f32[3,512]{1,0:T(4,128)S(1)}, f32[3,512]{1,0:T(4,128)S(1)}, f32[3,512]{1,0:T(4,128)S(1)}, f32[3,512]{1,0:T(4,128)S(1)}, f32[3,512]{1,0...) fusion(f32[3,512,8]{2,1,0:T(8,128)S(1)} %reshape.586), kind=kLoop, calls=%fused_computation.28 | loop fusion | bytes 98304 | tf_op jit(solution)/shard_map/slice | solution.py:163
  81.6 0.5 select_add_fusion
  82.3 0.6 fusion.12
  83.0 0.6 fusion.9
  83.6 0.6 fusion.6
  84.8 4.8 %collective-permute-start.6 = (f32[32,1,128]{2,1,0:T(1,128)S(1)}, f32[32,1,128]{2,1,0:T(1,128)S(1)}, u32[]{:S(2)}, u32[]{:S(2)}) collective-permute-start(f32[32,1,128]{2,1,0:T(1,128)S(1)} %get-tuple-element.72), channel_id=1, source_target_pairs={{1,0},{2,1},{3,2},{4,3},{5,4},{6,5},{7,6},{8,7},{9,8},{10,9},{11,1... | collective-permute-start | bytes 49160 | tf_op jit(solution)/shard_map/ppermute | solution.py:23
  89.6 5.5 %collective-permute-start.5 = (f32[1,16,128]{2,1,0:T(8,128)S(1)}, f32[1,16,128]{2,1,0:T(8,128)S(1)}, u32[]{:S(2)}, u32[]{:S(2)}) collective-permute-start(f32[1,16,128]{2,1,0:T(8,128)S(1)} %get-tuple-element.27), channel_id=1, source_target_pairs={{0,32},{32,64},{64,96},{96,128},{128,160},{160,192},{192,224},{224... | collective-permute-start | bytes 24584 | tf_op jit(solution)/shard_map/ppermute | solution.py:20
  95.1 0.7 collective-permute-done.5
  95.9 2.6 %collective-permute-done.4 = f32[1,16,128]{2,1,0:T(8,128)S(1)} collective-permute-done((f32[1,16,128]{2,1,0:T(8,128)S(1)}, f32[1,16,128]{2,1,0:T(8,128)S(1)}, u32[]{:S(2)}, u32[]{:S(2)}) %collective-permute-start.4) | collective-permute-done | bytes 8224 | tf_op jit(solution)/shard_map/ppermute | solution.py:23
  98.5 0.4 fusion.66
  99.3 4.8 %collective-permute-start.9 = (f32[32,1,128]{2,1,0:T(1,128)S(1)}, f32[32,1,128]{2,1,0:T(1,128)S(1)}, u32[]{:S(2)}, u32[]{:S(2)}) collective-permute-start(f32[32,1,128]{2,1,0:T(1,128)S(1)} %get-tuple-element.66), channel_id=1, source_target_pairs={{1,0},{2,1},{3,2},{4,3},{5,4},{6,5},{7,6},{8,7},{9,8},{10,9},{11,1... | collective-permute-start | bytes 49160 | tf_op jit(solution)/shard_map/ppermute | solution.py:23
  104.4 1.2 collective-permute-start.10
  105.6 0.6 collective-permute-done.11
  106.2 1.2 %collective-permute-done.10 = f32[1,16,128]{2,1,0:T(8,128)S(1)} collective-permute-done((f32[1,16,128]{2,1,0:T(8,128)S(1)}, f32[1,16,128]{2,1,0:T(8,128)S(1)}, u32[]{:S(2)}, u32[]{:S(2)}) %collective-permute-start.10) | collective-permute-done | bytes 8224 | tf_op jit(solution)/shard_map/ppermute | solution.py:23
  107.8 0.8 fusion.92
  108.6 0.9 slice_bitcast_fusion
  109.6 3.7 %collective-permute-start.13 = (f32[32,1,128]{2,1,0:T(1,128)S(1)}, f32[32,1,128]{2,1,0:T(1,128)S(1)}, u32[]{:S(2)}, u32[]{:S(2)}) collective-permute-start(f32[32,1,128]{2,1,0:T(1,128)S(1)} %get-tuple-element.58), channel_id=1, source_target_pairs={{1,0},{2,1},{3,2},{4,3},{5,4},{6,5},{7,6},{8,7},{9,8},{10,9},{11,1... | collective-permute-start | bytes 49160 | tf_op jit(solution)/shard_map/ppermute | solution.py:23
  113.3 1.4 %collective-permute-start.14 = (f32[1,16,128]{2,1,0:T(8,128)S(1)}, f32[1,16,128]{2,1,0:T(8,128)S(1)}, u32[]{:S(2)}, u32[]{:S(2)}) collective-permute-start(f32[1,16,128]{2,1,0:T(8,128)S(1)} %get-tuple-element.52), channel_id=1, source_target_pairs={{32,0},{64,32},{96,64},{128,96},{160,128},{192,160},{224,192},{0,2... | collective-permute-start | bytes 24584 | tf_op jit(solution)/shard_map/ppermute | solution.py:23
  115.1 1.1 copy.80
  116.2 0.9 copy.81
  117.1 1.3 %fusion.67 = f32[1,32,16,128]{3,2,1,0:T(8,128)S(1)} fusion(f32[1,32,16,1]{3,2,1,0:T(8,128)S(1)} %copy.79, f32[1,32,16,127]{3,2,1,0:T(8,128)} %get-tuple-element.57, f32[1,32,16,127]{3,2,1,0:T(8,128)} %get-tuple-element.56, f32[1,32,16,1]{3,2,1,0:T(8,128)} %copy.81), kind=kLoop, calls=%fused_computation.144 | loop fusion | flops 262144 | bytes 786432 | tf_op jit(solution)/shard_map/mul | solution.py:58
  118.5 0.7 collective-permute-done.12
  119.3 1.1 maximum_subtract_fusion
  (143 shorter events, 6.7 us)
Async XLA Ops:
  0.6 40.9 %copy-start = (bf16[1,32,128,128]{3,2,1,0:T(8,128)(2,1)S(1)}, bf16[1,32,128,128]{3,2,1,0:T(8,128)(2,1)}, u32[]{:S(2)}) copy-start(bf16[1,32,128,128]{3,2,1,0:T(8,128)(2,1)} %param.9) | copy-start | bytes 3145732
  0.6 4.2 %copy-start.1 = (f32[3,32,16,128]{3,2,1,0:T(8,128)S(1)}, f32[3,32,16,128]{3,2,1,0:T(8,128)}, u32[]{:S(2)}) copy-start(f32[3,32,16,128]{3,2,1,0:T(8,128)} %param.7) | copy-start | bytes 2359300
  0.7 4.2 %copy-start.3 = (f32[32,16,128]{2,1,0:T(8,128)S(1)}, f32[32,16,128]{2,1,0:T(8,128)}, u32[]{:S(2)}) copy-start(f32[32,16,128]{2,1,0:T(8,128)} %param.8) | copy-start | bytes 786436
  1.6 28.3 %collective-permute-start.2 = (f32[4,1,16,128]{3,2,1,0:T(8,128)S(1)}, f32[4,1,16,128]{3,2,1,0:T(8,128)S(1)}, u32[]{:S(2)}, u32[]{:S(2)}) collective-permute-start(f32[4,1,16,128]{3,2,1,0:T(8,128)S(1)} %get-tuple-element.25), channel_id=1, source_target_pairs={{32,0},{64,32},{96,64},{128,96},{160,128},{192,160},{224,192},{0,2... | collective-permute-start | bytes 98312 | tf_op jit(solution)/shard_map/ppermute | solution.py:23
  4.8 25.1 %collective-permute-start.3 = (f32[4,1,16,128]{3,2,1,0:T(8,128)S(1)}, f32[4,1,16,128]{3,2,1,0:T(8,128)S(1)}, u32[]{:S(2)}, u32[]{:S(2)}) collective-permute-start(f32[4,1,16,128]{3,2,1,0:T(8,128)S(1)} %get-tuple-element.24), channel_id=1, source_target_pairs={{0,32},{32,64},{64,96},{96,128},{128,160},{160,192},{192,224},{224... | collective-permute-start | bytes 98312 | tf_op jit(solution)/shard_map/ppermute | solution.py:20
  4.9 25.0 %collective-permute-start.1 = (f32[4,32,1,128]{3,2,1,0:T(1,128)S(1)}, f32[4,32,1,128]{3,2,1,0:T(1,128)S(1)}, u32[]{:S(2)}, u32[]{:S(2)}) collective-permute-start(f32[4,32,1,128]{3,2,1,0:T(1,128)S(1)} %get-tuple-element.23), channel_id=1, source_target_pairs={{1,0},{2,1},{3,2},{4,3},{5,4},{6,5},{7,6},{8,7},{9,8},{10,9},{11,1... | collective-permute-start | bytes 196616 | tf_op jit(solution)/shard_map/ppermute | solution.py:23
  12.4 0.7 copy-start.29
  12.4 17.6 %collective-permute-start = (f32[4,32,1,128]{3,2,1,0:T(1,128)S(1)}, f32[4,32,1,128]{3,2,1,0:T(1,128)S(1)}, u32[]{:S(2)}, u32[]{:S(2)}) collective-permute-start(f32[4,32,1,128]{3,2,1,0:T(1,128)S(1)} %get-tuple-element.22), channel_id=1, source_target_pairs={{0,1},{1,2},{2,3},{3,4},{4,5},{5,6},{6,7},{7,8},{8,9},{9,10},{10,1... | collective-permute-start | bytes 196616 | tf_op jit(solution)/shard_map/ppermute | solution.py:20
  13.2 0.7 copy-start.30
  13.9 0.6 copy-start.27
  15.3 28.6 %all-to-all-start = ((s32[32,4,1]{1,2,0:T(1,128)}), s32[32,4,1]{1,2,0:T(1,128)}, u32[]{:S(2)}, u32[]{:S(2)}) async-start(s32[32,4,1]{1,2,0:T(1,128)} %bitcast.14), calls=%async_computation | async-start | bytes 32768 | tf_op jit(solution)/shard_map/all_to_all | solution.py:138
  24.9 0.7 copy-start.26
  29.9 0.6 copy-start.21
  31.7 1.0 copy-start.7
  31.7 1.4 %copy-start.5 = (f32[32,16,1]{2,1,0:T(8,128)}, f32[32,16,1]{2,1,0:T(8,128)S(1)}, u32[]{:S(2)}) copy-start(f32[32,16,1]{2,1,0:T(8,128)S(1)} %get-tuple-element.45) | copy-start | bytes 6148
  33.5 1.3 %copy-start.4 = (f32[3,32,16,1]{3,2,1,0:T(8,128)S(1)}, f32[3,32,16,1]{3,2,1,0:T(8,128)}, u32[]{:S(2)}) copy-start(f32[3,32,16,1]{3,2,1,0:T(8,128)} %get-tuple-element.35) | copy-start | bytes 18436
  33.6 1.3 %copy-start.9 = (f32[32,16,128]{2,1,0:T(8,128)S(1)}, f32[32,16,128]{2,1,0:T(8,128)}, u32[]{:S(2)}) copy-start(f32[32,16,128]{2,1,0:T(8,128)} %multiply_bitcast_fusion.2) | copy-start | bytes 786436
  33.6 1.3 %copy-start.12 = (f32[1,32,16,128]{3,2,1,0:T(8,128)S(1)}, f32[1,32,16,128]{3,2,1,0:T(8,128)}, u32[]{:S(2)}) copy-start(f32[1,32,16,128]{3,2,1,0:T(8,128)} %get-tuple-element.43) | copy-start | bytes 786436
  37.5 0.7 copy-start.25
  39.1 0.8 copy-start.13
  39.1 0.9 copy-start.14
  39.1 0.9 copy-start.15
  39.1 0.9 copy-start.16
  39.1 0.9 copy-start.17
  39.1 1.0 copy-start.18
  39.2 1.0 copy-start.19
  42.1 0.7 copy-start.24
  42.1 0.7 copy-start.28
  43.9 9.3 %copy-start.22 = (f32[1,32,3,128]{3,1,2,0:T(8,128)S(1)}, f32[1,32,3,128]{3,1,2,0:T(8,128)}, u32[]{:S(2)}) copy-start(f32[1,32,3,128]{3,1,2,0:T(8,128)} %param.10) | copy-start | bytes 147460
  43.9 19.2 %all-to-all-start.1 = ((f32[32,4,384]{2,1,0:T(4,128)}), f32[32,4,384]{2,1,0:T(4,128)S(1)}, u32[]{:S(2)}, u32[]{:S(2)}) async-start(f32[32,4,384]{2,1,0:T(4,128)} %copy.73), calls=%async_computation.1 | async-start | bytes 393216 | tf_op jit(solution)/shard_map/all_to_all | solution.py:139
  64.3 13.0 %all-to-all-start.2 = ((bf16[32,4,384]{2,1,0:T(4,128)(2,1)}), bf16[32,4,384]{2,1,0:T(4,128)(2,1)S(1)}, u32[]{:S(2)}, u32[]{:S(2)}) async-start(bf16[32,4,384]{2,1,0:T(4,128)(2,1)} %all_to_all.24), calls=%async_computation.2 | async-start | bytes 196608 | tf_op jit(solution)/shard_map/all_to_all | solution.py:150
  78.4 3.2 %copy-start.20 = (pred[512,128]{0,1:T(8,128)(4,1)S(1)}, pred[512,128]{0,1:T(8,128)(4,1)}, u32[]{:S(2)}) copy-start(pred[512,128]{0,1:T(8,128)(4,1)} %get-tuple-element.89) | copy-start | bytes 196612
  81.6 0.7 copy-start.23
  84.5 13.9 %copy-start.6 = (f32[32,16,1]{2,1,0:T(8,128)S(1)}, f32[32,16,1]{2,1,0:T(8,128)}, u32[]{:S(2)}) copy-start(f32[32,16,1]{2,1,0:T(8,128)} %copy-done.5) | copy-start | bytes 6148
  84.5 13.9 %copy-start.8 = (f32[32,16,1]{2,1,0:T(8,128)S(1)}, f32[32,16,1]{2,1,0:T(8,128)}, u32[]{:S(2)}) copy-start(f32[32,16,1]{2,1,0:T(8,128)} %copy-done.7) | copy-start | bytes 6148
  84.6 13.9 %copy-start.10 = (f32[32,16,127]{2,1,0:T(8,128)S(1)}, f32[32,16,127]{2,1,0:T(8,128)}, u32[]{:S(2)}) copy-start(f32[32,16,127]{2,1,0:T(8,128)} %get-tuple-element.39) | copy-start | bytes 780292
  84.6 13.9 %copy-start.11 = (f32[32,16,127]{2,1,0:T(8,128)S(1)}, f32[32,16,127]{2,1,0:T(8,128)}, u32[]{:S(2)}) copy-start(f32[32,16,127]{2,1,0:T(8,128)} %get-tuple-element.42) | copy-start | bytes 780292
  84.7 10.3 %collective-permute-start.7 = (f32[32,1,128]{2,1,0:T(1,128)S(1)}, f32[32,1,128]{2,1,0:T(1,128)S(1)}, u32[]{:S(2)}, u32[]{:S(2)}) collective-permute-start(f32[32,1,128]{2,1,0:T(1,128)S(1)} %get-tuple-element.73), channel_id=1, source_target_pairs={{0,1},{1,2},{2,3},{3,4},{4,5},{5,6},{6,7},{7,8},{8,9},{9,10},{10,1... | collective-permute-start | bytes 49160 | tf_op jit(solution)/shard_map/ppermute | solution.py:20
  84.8 10.3 %collective-permute-start.6 = (f32[32,1,128]{2,1,0:T(1,128)S(1)}, f32[32,1,128]{2,1,0:T(1,128)S(1)}, u32[]{:S(2)}, u32[]{:S(2)}) collective-permute-start(f32[32,1,128]{2,1,0:T(1,128)S(1)} %get-tuple-element.72), channel_id=1, source_target_pairs={{1,0},{2,1},{3,2},{4,3},{5,4},{6,5},{7,6},{8,7},{9,8},{10,9},{11,1... | collective-permute-start | bytes 49160 | tf_op jit(solution)/shard_map/ppermute | solution.py:23
  89.6 6.3 %collective-permute-start.5 = (f32[1,16,128]{2,1,0:T(8,128)S(1)}, f32[1,16,128]{2,1,0:T(8,128)S(1)}, u32[]{:S(2)}, u32[]{:S(2)}) collective-permute-start(f32[1,16,128]{2,1,0:T(8,128)S(1)} %get-tuple-element.27), channel_id=1, source_target_pairs={{0,32},{32,64},{64,96},{96,128},{128,160},{160,192},{192,224},{224... | collective-permute-start | bytes 24584 | tf_op jit(solution)/shard_map/ppermute | solution.py:20
  95.1 3.4 %collective-permute-start.4 = (f32[1,16,128]{2,1,0:T(8,128)S(1)}, f32[1,16,128]{2,1,0:T(8,128)S(1)}, u32[]{:S(2)}, u32[]{:S(2)}) collective-permute-start(f32[1,16,128]{2,1,0:T(8,128)S(1)} %get-tuple-element.26), channel_id=1, source_target_pairs={{32,0},{64,32},{96,64},{128,96},{160,128},{192,160},{224,192},{0,2... | collective-permute-start | bytes 24584 | tf_op jit(solution)/shard_map/ppermute | solution.py:23
  99.2 6.3 %collective-permute-start.8 = (f32[32,1,128]{2,1,0:T(1,128)S(1)}, f32[32,1,128]{2,1,0:T(1,128)S(1)}, u32[]{:S(2)}, u32[]{:S(2)}) collective-permute-start(f32[32,1,128]{2,1,0:T(1,128)S(1)} %get-tuple-element.67), channel_id=1, source_target_pairs={{0,1},{1,2},{2,3},{3,4},{4,5},{5,6},{6,7},{7,8},{8,9},{9,10},{10,1... | collective-permute-start | bytes 49160 | tf_op jit(solution)/shard_map/ppermute | solution.py:20
  99.3 6.3 %collective-permute-start.9 = (f32[32,1,128]{2,1,0:T(1,128)S(1)}, f32[32,1,128]{2,1,0:T(1,128)S(1)}, u32[]{:S(2)}, u32[]{:S(2)}) collective-permute-start(f32[32,1,128]{2,1,0:T(1,128)S(1)} %get-tuple-element.66), channel_id=1, source_target_pairs={{1,0},{2,1},{3,2},{4,3},{5,4},{6,5},{7,6},{8,7},{9,8},{10,9},{11,1... | collective-permute-start | bytes 49160 | tf_op jit(solution)/shard_map/ppermute | solution.py:23
  104.1 2.1 %collective-permute-start.11 = (f32[1,16,128]{2,1,0:T(8,128)S(1)}, f32[1,16,128]{2,1,0:T(8,128)S(1)}, u32[]{:S(2)}, u32[]{:S(2)}) collective-permute-start(f32[1,16,128]{2,1,0:T(8,128)S(1)} %get-tuple-element.65), channel_id=1, source_target_pairs={{0,32},{32,64},{64,96},{96,128},{128,160},{160,192},{192,224},{224... | collective-permute-start | bytes 24584 | tf_op jit(solution)/shard_map/ppermute | solution.py:20
  104.4 3.1 %collective-permute-start.10 = (f32[1,16,128]{2,1,0:T(8,128)S(1)}, f32[1,16,128]{2,1,0:T(8,128)S(1)}, u32[]{:S(2)}, u32[]{:S(2)}) collective-permute-start(f32[1,16,128]{2,1,0:T(8,128)S(1)} %get-tuple-element.64), channel_id=1, source_target_pairs={{32,0},{64,32},{96,64},{128,96},{160,128},{192,160},{224,192},{0,2... | collective-permute-start | bytes 24584 | tf_op jit(solution)/shard_map/ppermute | solution.py:23
  107.7 11.5 %copy-start.2 = (f32[32,16,128]{2,1,0:T(8,128)}, f32[32,16,128]{2,1,0:T(8,128)S(1)}, u32[]{:S(2)}) copy-start(f32[32,16,128]{2,1,0:T(8,128)S(1)} %fusion.51) | copy-start | bytes 786436
  109.5 9.7 %collective-permute-start.15 = (f32[1,16,128]{2,1,0:T(8,128)S(1)}, f32[1,16,128]{2,1,0:T(8,128)S(1)}, u32[]{:S(2)}, u32[]{:S(2)}) collective-permute-start(f32[1,16,128]{2,1,0:T(8,128)S(1)} %get-tuple-element.53), channel_id=1, source_target_pairs={{0,32},{32,64},{64,96},{96,128},{128,160},{160,192},{192,224},{224... | collective-permute-start | bytes 24584 | tf_op jit(solution)/shard_map/ppermute | solution.py:20
  109.6 8.9 %collective-permute-start.13 = (f32[32,1,128]{2,1,0:T(1,128)S(1)}, f32[32,1,128]{2,1,0:T(1,128)S(1)}, u32[]{:S(2)}, u32[]{:S(2)}) collective-permute-start(f32[32,1,128]{2,1,0:T(1,128)S(1)} %get-tuple-element.58), channel_id=1, source_target_pairs={{1,0},{2,1},{3,2},{4,3},{5,4},{6,5},{7,6},{8,7},{9,8},{10,9},{11,1... | collective-permute-start | bytes 49160 | tf_op jit(solution)/shard_map/ppermute | solution.py:23
  113.3 5.9 %collective-permute-start.12 = (f32[32,1,128]{2,1,0:T(1,128)S(1)}, f32[32,1,128]{2,1,0:T(1,128)S(1)}, u32[]{:S(2)}, u32[]{:S(2)}) collective-permute-start(f32[32,1,128]{2,1,0:T(1,128)S(1)} %get-tuple-element.59), channel_id=1, source_target_pairs={{0,1},{1,2},{2,3},{3,4},{4,5},{5,6},{6,7},{7,8},{8,9},{9,10},{10,1... | collective-permute-start | bytes 49160 | tf_op jit(solution)/shard_map/ppermute | solution.py:20
  113.3 5.9 %collective-permute-start.14 = (f32[1,16,128]{2,1,0:T(8,128)S(1)}, f32[1,16,128]{2,1,0:T(8,128)S(1)}, u32[]{:S(2)}, u32[]{:S(2)}) collective-permute-start(f32[1,16,128]{2,1,0:T(8,128)S(1)} %get-tuple-element.52), channel_id=1, source_target_pairs={{32,0},{64,32},{96,64},{128,96},{160,128},{192,160},{224,192},{0,2... | collective-permute-start | bytes 24584 | tf_op jit(solution)/shard_map/ppermute | solution.py:23

commit v5 on v2

--- a/solution.py
+++ b/solution.py
@@ -13,14 +13,14 @@
 viscosity = 1.5
 
 
-def faces(block, axis, dim):
+def faces(block, axis, dim, width=1):
     count = lax.axis_size(axis)
     forward = [(i, (i + 1) % count) for i in range(count)]
     backward = [(target, source) for source, target in forward]
     low = lax.ppermute(
-        lax.slice_in_dim(block, block.shape[dim] - 1, None, axis=dim), axis, forward
-    )
-    high = lax.ppermute(lax.slice_in_dim(block, 0, 1, axis=dim), axis, backward)
+        lax.slice_in_dim(block, block.shape[dim] - width, None, axis=dim), axis, forward
+    )
+    high = lax.ppermute(lax.slice_in_dim(block, 0, width, axis=dim), axis, backward)
     return low, high
 
 
@@ -42,6 +42,22 @@
     return jnp.concatenate([low_x, middle, high_x], axis=x_dim)
 
 
+def halo(block, width):
+    x_total, z_total = block.shape[-3], block.shape[-2]
+    low, high = faces(block, "gx", block.ndim - 3, width)
+    grown = jnp.concatenate([low, block, high], axis=-3)
+    low, high = faces(grown, "yz", block.ndim - 2, width)
+    return inside(jnp.concatenate([low, grown, high], axis=-2), width, z_total)
+
+
+def inside(field, width, z_total):
+    tile_index = lax.axis_index("yz")
+    z_count = lax.axis_size("yz")
+    position = lax.broadcasted_iota(jnp.int32, field.shape, field.ndim - 2) + tile_index * z_total - width
+    valid = jnp.logical_and(position >= 0, position < z_count * z_total)
+    return jnp.where(valid, field, jnp.zeros((), field.dtype))
+
+
 def inner(padded):
     return padded[..., 1:-1, 1:-1, :]
 
@@ -84,6 +100,8 @@
     flow_fields = jnp.concatenate([velocity, old_pressure[None]], 0)
     flow_padded = padded_of(flow_fields, 1, 2)
     predicted = predict(flow_padded)
+    reach = 3
+    pressure_wide = halo(old_pressure, reach)
 
     anchors = box_anchor[0]
     owners = pair_owner[0, :, 0]
@@ -180,12 +198,14 @@
     )
     forced_velocity = predicted + added.reshape(fields, cx, cz, ny)
 
-    forced_x = padded_of(forced_velocity[0], 0, 1, z_faces=(jnp.zeros((cx, 1, ny), jnp.float32),) * 2)
-    forced_z = padded_of(forced_velocity[2], 0, 1, x_faces=(jnp.zeros((1, cz, ny), jnp.float32),) * 2)
-    divergence = along_x(forced_x) + along_y(forced_velocity[1]) + along_z(forced_z)
-    pressure = (neighbours(flow_padded[3]) - divergence) / 6.0
-    pressure = (neighbours(padded_of(pressure, 0, 1)) - divergence) / 6.0
-    new_velocity = forced_velocity - gradient_of(padded_of(pressure, 0, 1))
+    forced_wide = halo(forced_velocity, reach)
+    divergence = (
+        along_x(forced_wide[0]) + along_y(inner(forced_wide[1])) + along_z(forced_wide[2])
+    )
+    pressure = inside((neighbours(pressure_wide) - divergence) / 6.0, reach - 1, cz)
+    pressure = inside((neighbours(pressure) - inner(divergence)) / 6.0, reach - 2, cz)
+    new_velocity = forced_velocity - gradient_of(pressure)
+    pressure = inner(pressure)
     return (new_velocity, pressure)
 
 

time: 113 us -> 107 us (0.947)
  starting transfers between devices: 42.8 us -> 38.6 us
  other arithmetic: 15.6 us -> 18.9 us
  waiting for transfers between devices: 25.9 us -> 22.6 us
  local copies, waits for them, and re-layouts: 21.6 us -> 19.5 us
    all_to_all x1, waiting for transfers between devices: 10.3 us -> 4.78 us  [body(): received = lax.all_to_all(send, 'yz', 0, 0, tiled=True)]
    ppermute x16 -> x12, starting transfers between devices: 31.5 us -> 28 us  [the longest x6 18.5 us: faces(): lax.ppermute(lax.slice_in_dim(block, 0, width, axis=dim), axis, backward)]
    slice x9 -> x8, local copies, waits for them, and re-layouts: 3.91 us -> 1.39 us  [along_y(): return 0.5 * (jnp.roll(field, -1, -1) - jnp.roll(field, 1, -1))]
    slice x1 -> x3, other arithmetic: 0.09 us -> 2.47 us  [the longest x2 1.56 us: faces(): lax.slice_in_dim(block, block.shape[dim] - width, None, axis=dim)]
    unnamed x70 -> x90, local copies, waits for them, and re-layouts: 4.68 us -> 2.47 us
    ppermute x16 -> x12, waiting for transfers between devices: 7.3 us -> 9.03 us  [the longest x6 6.42 us: faces(): lax.ppermute(lax.slice_in_dim(block, block.shape[dim] - width, None, axis...]
    select_n x0 -> x4, other arithmetic: none -> 1.47 us  [inside(): return jnp.where(valid, field, jnp.zeros((), field.dtype))]
    concatenate x5 -> x6, local copies, waits for them, and re-layouts: 2.37 us -> 3.21 us  [along_y(): return 0.5 * (jnp.roll(field, -1, -1) - jnp.roll(field, 1, -1))]
  transfers between devices with their start and end apart: 18 -> 14, of which waited for: 8 -> 5; matrix products, arithmetic and copies ran while one was open for 12% -> 23% of each run, Pallas kernels for 0% -> 0%
where the time goes in v5:
time: 107 us; the launch traced here: 106 us
  starting transfers between devices  38.6 us (36%)
  waiting for transfers between devices  22.6 us (21%)
  local copies, waits for them, and re-layouts  19.5 us (18%)
  other arithmetic  18.9 us (18%)
  matrix products  5.14 us (5%)
  between operations  1.52 us (1%)
    ppermute x6, starting transfers between devices, faces(): lax.ppermute(lax.slice_in_dim(block, 0, width, axis=dim), axis, backward)  18.5 us
    ppermute x6, starting transfers between devices, faces(): lax.ppermute(lax.slice_in_dim(block, block.shape[dim] - width, None, axis...  9.48 us
    all_to_all x1, waiting for transfers between devices, body(): back = lax.all_to_all(returned, 'yz', 0, 0, tiled=True)  8.81 us
    all_to_all x1, starting transfers between devices, body(): received = lax.all_to_all(send, 'yz', 0, 0, tiled=True)  6.57 us
    ppermute x6, waiting for transfers between devices, faces(): lax.ppermute(lax.slice_in_dim(block, block.shape[dim] - width, None, axis...  6.42 us
    all_to_all x1, waiting for transfers between devices, body(): received = lax.all_to_all(send, 'yz', 0, 0, tiled=True)  4.78 us
    all_to_all x1, starting transfers between devices, body(): back = lax.all_to_all(returned, 'yz', 0, 0, tiled=True)  4.04 us
    slice x6, local copies, waits for them, and re-layouts, neighbours(): return total + jnp.roll(middle, 1, -1) + jnp.roll(middle, -1, -1)  3.5 us
  transfers between devices with their start and end apart: 14, of which 5 were waited for; matrix products, arithmetic and copies ran while one was open for 23% of the time, Pallas kernels for 0%

profile of v5, /device:TPU:1, one launch (start us, length us, event | category | flops | bytes accessed | tf_op | source)
XLA Modules:
  0.0 106.2 jit_solution(2335986787001605214)
XLA Ops:
  0.7 1.5 %pad_maximum_fusion.22 = (f32[4,32,1,128]{3,2,1,0:T(1,128)S(1)}, f32[4,32,1,128]{3,2,1,0:T(1,128)S(1)}) fusion(f32[1,32,16,128]{3,2,1,0:T(8,128)} %bitcast.114, f32[3,32,16,128]{3,2,1,0:T(8,128)} %param.7), kind=kLoop, calls=%fused_computation.145 | loop fusion | flops 32768 | bytes 1179648 | tf_op jit(solution)/shard_map/slice | solution.py:21
  2.1 8.9 %collective-permute-start.1 = (f32[4,32,1,128]{3,2,1,0:T(1,128)S(1)}, f32[4,32,1,128]{3,2,1,0:T(1,128)S(1)}, u32[]{:S(2)}, u32[]{:S(2)}) collective-permute-start(f32[4,32,1,128]{3,2,1,0:T(1,128)S(1)} %get-tuple-element.26), channel_id=1, source_target_pairs={{1,0},{2,1},{3,2},{4,3},{5,4},{6,5},{7,6},{8,7},{9,8},{10,9},{11,1... | collective-permute-start | bytes 196616 | tf_op jit(solution)/shard_map/ppermute | solution.py:23
  11.1 0.7 pad_maximum_fusion.23
  11.8 1.0 collective-permute-start.2
  12.8 1.1 %collective-permute-start.3 = (f32[4,1,16,128]{3,2,1,0:T(8,128)S(1)}, f32[4,1,16,128]{3,2,1,0:T(8,128)S(1)}, u32[]{:S(2)}, u32[]{:S(2)}) collective-permute-start(f32[4,1,16,128]{3,2,1,0:T(8,128)S(1)} %get-tuple-element.27), channel_id=1, source_target_pairs={{0,32},{32,64},{64,96},{96,128},{128,160},{160,192},{192,224},{224... | collective-permute-start | bytes 98312 | tf_op jit(solution)/shard_map/ppermute | solution.py:20
  13.9 0.6 fusion.96
  14.5 0.5 collective-permute-start.4
  15.0 1.4 %fusion.83 = (f32[3,32,16,1]{3,2,1,0:T(8,128)}, f32[3,32,16,1]{3,2,1,0:T(8,128)}) fusion(f32[3,32,16,128]{3,2,1,0:T(8,128)S(1)} %copy-done.1), kind=kLoop, calls=%fused_computation.207 | loop fusion | bytes 24576 | tf_op jit(solution)/shard_map/jit(_roll_static)/slice | solution.py:81
  16.4 1.4 %fusion.84 = (f32[3,32,16,127]{3,2,1,0:T(8,128)}, f32[3,32,16,127]{3,2,1,0:T(8,128)}) fusion(f32[3,32,16,128]{3,2,1,0:T(8,128)S(1)} %copy-done.1), kind=kLoop, calls=%fused_computation.208 | loop fusion | bytes 3121152 | tf_op jit(solution)/shard_map/jit(_roll_static)/slice | solution.py:81
  17.8 0.6 multiply_add_fusion
  18.4 0.5 compare_and_fusion.1
  19.1 0.7 iota_compare_fusion.10
  20.0 0.6 multiply_add_fusion.1
  20.6 0.7 iota_compare_fusion.4
  21.3 0.7 iota_compare_fusion.6
  22.1 0.7 iota_compare_fusion.8
  22.9 0.5 compare_and_fusion.2
  23.4 0.7 add.318
  24.1 0.7 copy.56
  24.7 0.7 copy.58
  25.4 0.3 collective-permute-start.5
  25.7 0.6 constant_dynamic-update-slice_fusion.10
  26.6 0.4 copy-done.25
  27.2 0.8 slice_bitcast_fusion.11
  28.0 0.9 fusion.58
  29.7 1.2 %fusion.59 = f32[1,32,16,128]{3,2,1,0:T(8,128)S(1)} fusion(f32[1,32,16,1]{3,2,1,0:T(8,128)S(1)} %copy.51, f32[1,32,16,127]{3,2,1,0:T(8,128)} %get-tuple-element.65, f32[1,32,16,127]{3,2,1,0:T(8,128)S(1)} %get-tuple-element.64, f32[1,32,16,1]{3,2,1,0:T(8,128)S(1)} %copy.53), kind=kLoop, calls=%fused_computation.125 | loop fusion | flops 262144 | bytes 786432 | tf_op jit(solution)/shard_map/mul | solution.py:74
  31.0 2.8 %fusion.80 = (bf16[3,32,16,128]{3,2,1,0:T(8,128)(2,1)S(1)}, f32[3,32,16,128]{3,2,1,0:T(8,128)S(1)}) fusion(f32[1,32,16,128]{3,2,1,0:T(8,128)S(1)} %copy-done.8, f32[1,32,16,128]{3,2,1,0:T(8,128)S(1)} %fusion.59, f32[1,32,16,128]{3,2,1,0:T(8,128)S(1)} %copy-done.7, f32[3,32,16,128]{3,2,1,0:T(8,128)S(1)} %copy-done.1, ...), kind=kLoop, calls=%fused_computation.205 | loop fusion | flops 6094848 | bytes 5054464 | tf_op jit(solution)/shard_map/convert_element_type | solution.py:123
  33.8 0.4 convolution_bitcast_fusion
  34.3 0.4 convolution_bitcast_fusion.1
  34.7 0.4 convolution_bitcast_fusion.2
  35.2 0.6 select_reduce_fusion
  36.3 0.4 convert_element_type.56
  36.6 0.6 fusion.17
  37.6 0.8 all_to_all.16
  38.4 6.6 %all-to-all-start = ((f32[32,4,385]{2,1,0:T(4,128)}), f32[32,4,385]{2,1,0:T(4,128)S(1)}, u32[]{:S(2)}, u32[]{:S(2)}) async-start(f32[32,4,385]{2,1,0:T(4,128)} %all_to_all.16), calls=%async_computation | async-start | bytes 524288 | tf_op jit(solution)/shard_map/all_to_all | solution.py:156
  45.0 0.7 constant_dynamic-update-slice_fusion.8
  45.8 1.3 %collective-permute-start.6 = (f32[38,3,128]{2,1,0:T(4,128)S(1)}, f32[38,3,128]{2,1,0:T(4,128)S(1)}, u32[]{:S(2)}, u32[]{:S(2)}) collective-permute-start(f32[38,3,128]{2,1,0:T(4,128)S(1)} %get-tuple-element.69), channel_id=1, source_target_pairs={{0,1},{1,2},{2,3},{3,4},{4,5},{5,6},{6,7},{7,8},{8,9},{9,10},{10,1... | collective-permute-start | bytes 175112 | tf_op jit(solution)/shard_map/ppermute | solution.py:20
  47.1 3.6 %collective-permute-start.7 = (f32[38,3,128]{2,1,0:T(4,128)S(1)}, f32[38,3,128]{2,1,0:T(4,128)S(1)}, u32[]{:S(2)}, u32[]{:S(2)}) collective-permute-start(f32[38,3,128]{2,1,0:T(4,128)S(1)} %get-tuple-element.70), channel_id=1, source_target_pairs={{1,0},{2,1},{3,2},{4,3},{5,4},{6,5},{7,6},{8,7},{9,8},{10,9},{11,1... | collective-permute-start | bytes 175112 | tf_op jit(solution)/shard_map/ppermute | solution.py:23
  50.6 4.8 %all-to-all-done = f32[32,4,385]{2,1,0:T(4,128)S(1)} async-done(((f32[32,4,385]{2,1,0:T(4,128)}), f32[32,4,385]{2,1,0:T(4,128)S(1)}, u32[]{:S(2)}, u32[]{:S(2)}) %all-to-all-start) | async-done | bytes 197152 | tf_op jit(solution)/shard_map/all_to_all | solution.py:156
  55.9 0.3 convolution_convert_fusion
  56.1 0.7 all_to_all.19
  56.8 4.0 %all-to-all-start.1 = ((bf16[32,4,384]{2,1,0:T(4,128)(2,1)}), bf16[32,4,384]{2,1,0:T(4,128)(2,1)S(1)}, u32[]{:S(2)}, u32[]{:S(2)}) async-start(bf16[32,4,384]{2,1,0:T(4,128)(2,1)} %all_to_all.19), calls=%async_computation.1 | async-start | bytes 196608 | tf_op jit(solution)/shard_map/all_to_all | solution.py:169
  61.0 8.8 %all-to-all-done.1 = bf16[32,4,384]{2,1,0:T(4,128)(2,1)S(1)} async-done(((bf16[32,4,384]{2,1,0:T(4,128)(2,1)}), bf16[32,4,384]{2,1,0:T(4,128)(2,1)S(1)}, u32[]{:S(2)}, u32[]{:S(2)}) %all-to-all-start.1) | async-done | bytes 98336 | tf_op jit(solution)/shard_map/all_to_all | solution.py:169
  70.0 0.4 convolution_bitcast_fusion.3
  70.4 0.4 reshape.579
  71.0 3.2 %slice_reduce_fusion.7 = (f32[3,512]{1,0:T(4,128)S(1)}, f32[3,512]{1,0:T(4,128)S(1)}, f32[3,512]{1,0:T(4,128)S(1)}, f32[3,512]{1,0:T(4,128)S(1)}, f32[3,512]{1,0...) fusion(f32[3,512,8]{2,1,0:T(8,128)S(1)} %reshape.579), kind=kLoop, calls=%fused_computation.29 | loop fusion | bytes 98304 | tf_op jit(solution)/shard_map/slice | solution.py:182
  74.2 0.5 select_add_fusion
  74.8 0.6 fusion.6
  75.4 0.6 fusion.9
  76.0 0.6 fusion.12
  76.8 6.4 %collective-permute-start.8 = (f32[3,3,16,128]{3,2,1,0:T(8,128)S(1)}, f32[3,3,16,128]{3,2,1,0:T(8,128)S(1)}, u32[]{:S(2)}, u32[]{:S(2)}) collective-permute-start(f32[3,3,16,128]{3,2,1,0:T(8,128)S(1)} %get-tuple-element.31), channel_id=1, source_target_pairs={{0,32},{32,64},{64,96},{96,128},{128,160},{160,192},{192,224},{224... | collective-permute-start | bytes 221192 | tf_op jit(solution)/shard_map/ppermute | solution.py:20
  83.4 1.2 %collective-permute-done.8 = f32[3,3,16,128]{3,2,1,0:T(8,128)S(1)} collective-permute-done((f32[3,3,16,128]{3,2,1,0:T(8,128)S(1)}, f32[3,3,16,128]{3,2,1,0:T(8,128)S(1)}, u32[]{:S(2)}, u32[]{:S(2)}) %collective-permute-start.8) | collective-permute-done | bytes 73760 | tf_op jit(solution)/shard_map/ppermute | solution.py:20
  84.7 2.6 %collective-permute-done.9 = f32[3,3,16,128]{3,2,1,0:T(8,128)S(1)} collective-permute-done((f32[3,3,16,128]{3,2,1,0:T(8,128)S(1)}, f32[3,3,16,128]{3,2,1,0:T(8,128)S(1)}, u32[]{:S(2)}, u32[]{:S(2)}) %collective-permute-start.9) | collective-permute-done | bytes 73760 | tf_op jit(solution)/shard_map/ppermute | solution.py:23
  87.5 4.7 %collective-permute-start.11 = (f32[3,38,3,128]{3,2,1,0:T(4,128)S(1)}, f32[3,38,3,128]{3,2,1,0:T(4,128)S(1)}, u32[]{:S(2)}, u32[]{:S(2)}) collective-permute-start(f32[3,38,3,128]{3,2,1,0:T(4,128)S(1)} %get-tuple-element.30), channel_id=1, source_target_pairs={{1,0},{2,1},{3,2},{4,3},{5,4},{6,5},{7,6},{8,7},{9,8},{10,9},{11,1... | collective-permute-start | bytes 525320 | tf_op jit(solution)/shard_map/ppermute | solution.py:23
  92.4 5.2 %collective-permute-done.10 = f32[3,38,3,128]{3,2,1,0:T(4,128)S(1)} collective-permute-done((f32[3,38,3,128]{3,2,1,0:T(4,128)S(1)}, f32[3,38,3,128]{3,2,1,0:T(4,128)S(1)}, u32[]{:S(2)}, u32[]{:S(2)}) %collective-permute-start.10) | collective-permute-done | bytes 175136 | tf_op jit(solution)/shard_map/ppermute | solution.py:20
  97.6 0.3 maximum_select_fusion
  98.6 0.7 fusion.45
  99.6 0.3 copy-done.36
  99.9 0.4 fusion.47
  100.5 0.9 slice_bitcast_fusion.3
  101.3 0.9 fusion.91
  102.8 0.9 copy.66
  103.7 1.4 %fusion.60 = f32[1,32,16,128]{3,2,1,0:T(8,128)S(1)} fusion(f32[1,32,16,1]{3,2,1,0:T(8,128)S(1)} %copy.64, f32[1,32,16,127]{3,2,1,0:T(8,128)} %get-tuple-element.59, f32[1,32,16,127]{3,2,1,0:T(8,128)} %get-tuple-element.58, f32[1,32,16,1]{3,2,1,0:T(8,128)} %copy.66), kind=kLoop, calls=%fused_computation.127 | loop fusion | flops 262144 | bytes 786432 | tf_op jit(solution)/shard_map/mul | solution.py:74
  105.1 1.1 %maximum_subtract_fusion = f32[3,32,16,128]{3,2,1,0:T(8,128)} fusion(f32[1,32,16,128]{3,2,1,0:T(8,128)S(1)} %copy-done.10, f32[1,32,16,128]{3,2,1,0:T(8,128)S(1)} %fusion.60, f32[1,32,16,128]{3,2,1,0:T(8,128)S(1)} %copy-done.9, f32[3,32,16,128]{3,2,1,0:T(8,128)S(1)} %get-tuple-element.21, f32[1,32,16,128]{3,2,1,0:T(8,128)S(1)} %copy-done.6, ...), kind=kLoop, calls=%fused_computation.54 | loop fusion | flops 1179648 | bytes 3145728 | tf_op jit(solution)/shard_map/sub | solution.py:207
  (146 shorter events, 5.7 us)
Async XLA Ops:
  0.6 36.0 %copy-start = (bf16[1,32,128,128]{3,2,1,0:T(8,128)(2,1)S(1)}, bf16[1,32,128,128]{3,2,1,0:T(8,128)(2,1)}, u32[]{:S(2)}) copy-start(bf16[1,32,128,128]{3,2,1,0:T(8,128)(2,1)} %param.9) | copy-start | bytes 3145732
  0.6 13.2 %copy-start.2 = (f32[32,16,128]{2,1,0:T(8,128)S(1)}, f32[32,16,128]{2,1,0:T(8,128)}, u32[]{:S(2)}) copy-start(f32[32,16,128]{2,1,0:T(8,128)} %param.8) | copy-start | bytes 786436
  0.7 10.4 %copy-start.1 = (f32[3,32,16,128]{3,2,1,0:T(8,128)S(1)}, f32[3,32,16,128]{3,2,1,0:T(8,128)}, u32[]{:S(2)}) copy-start(f32[3,32,16,128]{3,2,1,0:T(8,128)} %param.7) | copy-start | bytes 2359300
  2.1 24.3 %collective-permute-start.1 = (f32[4,32,1,128]{3,2,1,0:T(1,128)S(1)}, f32[4,32,1,128]{3,2,1,0:T(1,128)S(1)}, u32[]{:S(2)}, u32[]{:S(2)}) collective-permute-start(f32[4,32,1,128]{3,2,1,0:T(1,128)S(1)} %get-tuple-element.26), channel_id=1, source_target_pairs={{1,0},{2,1},{3,2},{4,3},{5,4},{6,5},{7,6},{8,7},{9,8},{10,9},{11,1... | collective-permute-start | bytes 196616 | tf_op jit(solution)/shard_map/ppermute | solution.py:23
  11.1 15.4 %collective-permute-start = (f32[4,32,1,128]{3,2,1,0:T(1,128)S(1)}, f32[4,32,1,128]{3,2,1,0:T(1,128)S(1)}, u32[]{:S(2)}, u32[]{:S(2)}) collective-permute-start(f32[4,32,1,128]{3,2,1,0:T(1,128)S(1)} %get-tuple-element.25), channel_id=1, source_target_pairs={{0,1},{1,2},{2,3},{3,4},{4,5},{5,6},{6,7},{7,8},{8,9},{9,10},{10,1... | collective-permute-start | bytes 196616 | tf_op jit(solution)/shard_map/ppermute | solution.py:20
  11.8 14.6 %collective-permute-start.2 = (f32[4,1,16,128]{3,2,1,0:T(8,128)S(1)}, f32[4,1,16,128]{3,2,1,0:T(8,128)S(1)}, u32[]{:S(2)}, u32[]{:S(2)}) collective-permute-start(f32[4,1,16,128]{3,2,1,0:T(8,128)S(1)} %get-tuple-element.28), channel_id=1, source_target_pairs={{32,0},{64,32},{96,64},{128,96},{160,128},{192,160},{224,192},{0,2... | collective-permute-start | bytes 98312 | tf_op jit(solution)/shard_map/ppermute | solution.py:23
  12.8 13.6 %collective-permute-start.3 = (f32[4,1,16,128]{3,2,1,0:T(8,128)S(1)}, f32[4,1,16,128]{3,2,1,0:T(8,128)S(1)}, u32[]{:S(2)}, u32[]{:S(2)}) collective-permute-start(f32[4,1,16,128]{3,2,1,0:T(8,128)S(1)} %get-tuple-element.27), channel_id=1, source_target_pairs={{0,32},{32,64},{64,96},{96,128},{128,160},{160,192},{192,224},{224... | collective-permute-start | bytes 98312 | tf_op jit(solution)/shard_map/ppermute | solution.py:20
  14.5 11.0 %collective-permute-start.4 = (f32[3,16,128]{2,1,0:T(8,128)S(1)}, f32[3,16,128]{2,1,0:T(8,128)S(1)}, u32[]{:S(2)}, u32[]{:S(2)}) collective-permute-start(f32[3,16,128]{2,1,0:T(8,128)S(1)} %get-tuple-element.72), channel_id=1, source_target_pairs={{0,32},{32,64},{64,96},{96,128},{128,160},{160,192},{192,224},{224... | collective-permute-start | bytes 73736 | tf_op jit(solution)/shard_map/ppermute | solution.py:20
  16.3 2.6 %copy-start.34 = (s32[1,32,3]{1,0,2:T(1,128)S(1)}, s32[1,32,3]{1,0,2:T(1,128)}, u32[]{:S(2)}) copy-start(s32[1,32,3]{1,0,2:T(1,128)} %param.13) | copy-start | bytes 1156
  16.4 3.5 %copy-start.37 = (s32[1,32,1]{1,2,0:T(1,128)S(1)}, s32[1,32,1]{1,2,0:T(1,128)}, u32[]{:S(2)}) copy-start(s32[1,32,1]{1,2,0:T(1,128)} %param.11) | copy-start | bytes 388
  16.4 4.3 %copy-start.38 = (s32[1,32]{1,0:T(1,128)S(1)}, s32[1,32]{1,0:T(1,128)}, u32[]{:S(2)}) copy-start(s32[1,32]{1,0:T(1,128)} %param.12) | copy-start | bytes 388
  16.4 8.4 %copy-start.29 = (f32[1,32,3,128]{3,1,2,0:T(8,128)S(1)}, f32[1,32,3,128]{3,1,2,0:T(8,128)}, u32[]{:S(2)}) copy-start(f32[1,32,3,128]{3,1,2,0:T(8,128)} %param.10) | copy-start | bytes 147460
  25.4 19.6 %collective-permute-start.5 = (f32[3,16,128]{2,1,0:T(8,128)}, f32[3,16,128]{2,1,0:T(8,128)}, u32[]{:S(2)}, u32[]{:S(2)}) collective-permute-start(f32[3,16,128]{2,1,0:T(8,128)} %get-tuple-element.71), channel_id=1, source_target_pairs={{32,0},{64,32},{96,64},{128,96},{160,128},{192,160},{224,192},{0,2... | collective-permute-start | bytes 73736 | tf_op jit(solution)/shard_map/ppermute | solution.py:23
  26.4 0.6 copy-start.25
  26.4 0.6 copy-start.26
  29.7 1.2 %copy-start.7 = (f32[1,32,16,128]{3,2,1,0:T(8,128)S(1)}, f32[1,32,16,128]{3,2,1,0:T(8,128)}, u32[]{:S(2)}) copy-start(f32[1,32,16,128]{3,2,1,0:T(8,128)} %get-tuple-element.60) | copy-start | bytes 786436
  29.7 1.2 %copy-start.8 = (f32[1,32,16,128]{3,2,1,0:T(8,128)S(1)}, f32[1,32,16,128]{3,2,1,0:T(8,128)}, u32[]{:S(2)}) copy-start(f32[1,32,16,128]{3,2,1,0:T(8,128)} %get-tuple-element.61) | copy-start | bytes 786436
  30.9 2.9 %copy-start.32 = (s32[512]{0:T(512)S(1)}, s32[512]{0:T(512)}, u32[]{:S(2)}) copy-start(s32[512]{0:T(512)} %add.318) | copy-start | bytes 6148
  33.7 1.5 %copy-start.12 = (pred[512,128]{0,1:T(8,128)(4,1)S(1)}, pred[512,128]{0,1:T(8,128)(4,1)}, u32[]{:S(2)}) copy-start(pred[512,128]{0,1:T(8,128)(4,1)} %get-tuple-element.92) | copy-start | bytes 196612
  33.7 1.5 %copy-start.13 = (pred[512,128]{0,1:T(8,128)(4,1)S(1)}, pred[512,128]{0,1:T(8,128)(4,1)}, u32[]{:S(2)}) copy-start(pred[512,128]{0,1:T(8,128)(4,1)} %get-tuple-element.85) | copy-start | bytes 196612
  33.7 1.5 %copy-start.15 = (pred[512,128]{0,1:T(8,128)(4,1)S(1)}, pred[512,128]{0,1:T(8,128)(4,1)}, u32[]{:S(2)}) copy-start(pred[512,128]{0,1:T(8,128)(4,1)} %get-tuple-element.86) | copy-start | bytes 196612
  33.7 1.5 %copy-start.17 = (pred[512,128]{0,1:T(8,128)(4,1)S(1)}, pred[512,128]{0,1:T(8,128)(4,1)}, u32[]{:S(2)}) copy-start(pred[512,128]{0,1:T(8,128)(4,1)} %get-tuple-element.87) | copy-start | bytes 196612
  33.8 1.5 %copy-start.19 = (pred[512,128]{0,1:T(8,128)(4,1)S(1)}, pred[512,128]{0,1:T(8,128)(4,1)}, u32[]{:S(2)}) copy-start(pred[512,128]{0,1:T(8,128)(4,1)} %get-tuple-element.88) | copy-start | bytes 196612
  33.8 1.5 %copy-start.21 = (pred[512,128]{0,1:T(8,128)(4,1)S(1)}, pred[512,128]{0,1:T(8,128)(4,1)}, u32[]{:S(2)}) copy-start(pred[512,128]{0,1:T(8,128)(4,1)} %get-tuple-element.89) | copy-start | bytes 196612
  33.8 1.5 %copy-start.23 = (pred[512,128]{0,1:T(8,128)(4,1)S(1)}, pred[512,128]{0,1:T(8,128)(4,1)}, u32[]{:S(2)}) copy-start(pred[512,128]{0,1:T(8,128)(4,1)} %get-tuple-element.90) | copy-start | bytes 196612
  35.9 1.4 %copy-start.28 = (f32[32,1]{1,0:T(8,128)S(1)}, f32[32,1]{1,0:T(8,128)}, u32[]{:S(2)}) copy-start(f32[32,1]{1,0:T(8,128)} %copy.56) | copy-start | bytes 388
  35.9 1.4 %copy-start.31 = (s32[32]{0:T(128)S(1)}, s32[32]{0:T(128)}, u32[]{:S(2)}) copy-start(s32[32]{0:T(128)} %multiply_add_fusion.1) | copy-start | bytes 388
  36.6 8.3 %copy-start.11 = (f32[38,16,128]{2,1,0:T(8,128)S(1)}, f32[38,16,128]{2,1,0:T(8,128)}, u32[]{:S(2)}) copy-start(f32[38,16,128]{2,1,0:T(8,128)} %constant_dynamic-update-slice_fusion.10) | copy-start | bytes 933892
  37.3 18.3 %copy-start.27 = (f32[1,32,3,128]{3,2,1,0:T(4,128)S(1)}, f32[1,32,3,128]{3,2,1,0:T(4,128)}, u32[]{:S(2)}) copy-start(f32[1,32,3,128]{3,2,1,0:T(4,128)} %copy.58) | copy-start | bytes 147460
  38.4 17.0 %all-to-all-start = ((f32[32,4,385]{2,1,0:T(4,128)}), f32[32,4,385]{2,1,0:T(4,128)S(1)}, u32[]{:S(2)}, u32[]{:S(2)}) async-start(f32[32,4,385]{2,1,0:T(4,128)} %all_to_all.16), calls=%async_computation | async-start | bytes 524288 | tf_op jit(solution)/shard_map/all_to_all | solution.py:156
  45.8 15.1 %collective-permute-start.6 = (f32[38,3,128]{2,1,0:T(4,128)S(1)}, f32[38,3,128]{2,1,0:T(4,128)S(1)}, u32[]{:S(2)}, u32[]{:S(2)}) collective-permute-start(f32[38,3,128]{2,1,0:T(4,128)S(1)} %get-tuple-element.69), channel_id=1, source_target_pairs={{0,1},{1,2},{2,3},{3,4},{4,5},{5,6},{6,7},{7,8},{8,9},{9,10},{10,1... | collective-permute-start | bytes 175112 | tf_op jit(solution)/shard_map/ppermute | solution.py:20
  47.1 13.8 %collective-permute-start.7 = (f32[38,3,128]{2,1,0:T(4,128)S(1)}, f32[38,3,128]{2,1,0:T(4,128)S(1)}, u32[]{:S(2)}, u32[]{:S(2)}) collective-permute-start(f32[38,3,128]{2,1,0:T(4,128)S(1)} %get-tuple-element.70), channel_id=1, source_target_pairs={{1,0},{2,1},{3,2},{4,3},{5,4},{6,5},{7,6},{8,7},{9,8},{10,9},{11,1... | collective-permute-start | bytes 175112 | tf_op jit(solution)/shard_map/ppermute | solution.py:23
  56.8 13.0 %all-to-all-start.1 = ((bf16[32,4,384]{2,1,0:T(4,128)(2,1)}), bf16[32,4,384]{2,1,0:T(4,128)(2,1)S(1)}, u32[]{:S(2)}, u32[]{:S(2)}) async-start(bf16[32,4,384]{2,1,0:T(4,128)(2,1)} %all_to_all.19), calls=%async_computation.1 | async-start | bytes 196608 | tf_op jit(solution)/shard_map/all_to_all | solution.py:169
  70.9 3.3 %copy-start.14 = (pred[512,128]{0,1:T(8,128)(4,1)S(1)}, pred[512,128]{0,1:T(8,128)(4,1)}, u32[]{:S(2)}) copy-start(pred[512,128]{0,1:T(8,128)(4,1)} %get-tuple-element.85) | copy-start | bytes 196612
  70.9 3.3 %copy-start.16 = (pred[512,128]{0,1:T(8,128)(4,1)S(1)}, pred[512,128]{0,1:T(8,128)(4,1)}, u32[]{:S(2)}) copy-start(pred[512,128]{0,1:T(8,128)(4,1)} %get-tuple-element.86) | copy-start | bytes 196612
  70.9 3.3 %copy-start.18 = (pred[512,128]{0,1:T(8,128)(4,1)S(1)}, pred[512,128]{0,1:T(8,128)(4,1)}, u32[]{:S(2)}) copy-start(pred[512,128]{0,1:T(8,128)(4,1)} %get-tuple-element.87) | copy-start | bytes 196612
  70.9 3.3 %copy-start.20 = (pred[512,128]{0,1:T(8,128)(4,1)S(1)}, pred[512,128]{0,1:T(8,128)(4,1)}, u32[]{:S(2)}) copy-start(pred[512,128]{0,1:T(8,128)(4,1)} %get-tuple-element.88) | copy-start | bytes 196612
  70.9 3.3 %copy-start.22 = (pred[512,128]{0,1:T(8,128)(4,1)S(1)}, pred[512,128]{0,1:T(8,128)(4,1)}, u32[]{:S(2)}) copy-start(pred[512,128]{0,1:T(8,128)(4,1)} %get-tuple-element.89) | copy-start | bytes 196612
  70.9 3.3 %copy-start.24 = (pred[512,128]{0,1:T(8,128)(4,1)S(1)}, pred[512,128]{0,1:T(8,128)(4,1)}, u32[]{:S(2)}) copy-start(pred[512,128]{0,1:T(8,128)(4,1)} %get-tuple-element.90) | copy-start | bytes 196612
  70.9 3.8 %copy-start.30 = (s32[32,16]{1,0:T(8,128)S(1)}, s32[32,16]{1,0:T(8,128)}, u32[]{:S(2)}) copy-start(s32[32,16]{1,0:T(8,128)} %multiply_add_fusion) | copy-start | bytes 6148
  70.9 3.8 %copy-start.33 = (s32[512]{0:T(512)S(1)}, s32[512]{0:T(512)}, u32[]{:S(2)}) copy-start(s32[512]{0:T(512)} %add.318) | copy-start | bytes 6148
  76.0 0.8 copy-start.3
  76.7 6.8 %copy-start.5 = (f32[1,32,16,128]{3,2,1,0:T(8,128)}, f32[1,32,16,128]{3,2,1,0:T(8,128)S(1)}, u32[]{:S(2)}) copy-start(f32[1,32,16,128]{3,2,1,0:T(8,128)S(1)} %fusion.12) | copy-start | bytes 786436
  76.8 7.8 %collective-permute-start.8 = (f32[3,3,16,128]{3,2,1,0:T(8,128)S(1)}, f32[3,3,16,128]{3,2,1,0:T(8,128)S(1)}, u32[]{:S(2)}, u32[]{:S(2)}) collective-permute-start(f32[3,3,16,128]{3,2,1,0:T(8,128)S(1)} %get-tuple-element.31), channel_id=1, source_target_pairs={{0,32},{32,64},{64,96},{96,128},{128,160},{160,192},{192,224},{224... | collective-permute-start | bytes 221192 | tf_op jit(solution)/shard_map/ppermute | solution.py:20
  83.3 4.0 %collective-permute-start.9 = (f32[3,3,16,128]{3,2,1,0:T(8,128)S(1)}, f32[3,3,16,128]{3,2,1,0:T(8,128)S(1)}, u32[]{:S(2)}, u32[]{:S(2)}) collective-permute-start(f32[3,3,16,128]{3,2,1,0:T(8,128)S(1)} %get-tuple-element.32), channel_id=1, source_target_pairs={{32,0},{64,32},{96,64},{128,96},{160,128},{192,160},{224,192},{0,2... | collective-permute-start | bytes 221192 | tf_op jit(solution)/shard_map/ppermute | solution.py:23
  87.3 10.2 %collective-permute-start.10 = (f32[3,38,3,128]{3,2,1,0:T(4,128)S(1)}, f32[3,38,3,128]{3,2,1,0:T(4,128)S(1)}, u32[]{:S(2)}, u32[]{:S(2)}) collective-permute-start(f32[3,38,3,128]{3,2,1,0:T(4,128)S(1)} %get-tuple-element.29), channel_id=1, source_target_pairs={{0,1},{1,2},{2,3},{3,4},{4,5},{5,6},{6,7},{7,8},{8,9},{9,10},{10,1... | collective-permute-start | bytes 525320 | tf_op jit(solution)/shard_map/ppermute | solution.py:20
  87.5 10.1 %collective-permute-start.11 = (f32[3,38,3,128]{3,2,1,0:T(4,128)S(1)}, f32[3,38,3,128]{3,2,1,0:T(4,128)S(1)}, u32[]{:S(2)}, u32[]{:S(2)}) collective-permute-start(f32[3,38,3,128]{3,2,1,0:T(4,128)S(1)} %get-tuple-element.30), channel_id=1, source_target_pairs={{1,0},{2,1},{3,2},{4,3},{5,4},{6,5},{7,6},{8,7},{9,8},{10,9},{11,1... | collective-permute-start | bytes 525320 | tf_op jit(solution)/shard_map/ppermute | solution.py:23
  98.0 0.6 copy-start.35
  99.3 0.6 copy-start.36
  102.3 2.8 %copy-start.4 = (f32[1,32,16,128]{3,2,1,0:T(8,128)S(1)}, f32[1,32,16,128]{3,2,1,0:T(8,128)}, u32[]{:S(2)}) copy-start(f32[1,32,16,128]{3,2,1,0:T(8,128)} %copy-done.3) | copy-start | bytes 786436
  102.3 2.9 %copy-start.6 = (f32[1,32,16,128]{3,2,1,0:T(8,128)S(1)}, f32[1,32,16,128]{3,2,1,0:T(8,128)}, u32[]{:S(2)}) copy-start(f32[1,32,16,128]{3,2,1,0:T(8,128)} %copy-done.5) | copy-start | bytes 786436
  103.7 1.4 %copy-start.9 = (f32[1,32,16,128]{3,2,1,0:T(8,128)S(1)}, f32[1,32,16,128]{3,2,1,0:T(8,128)}, u32[]{:S(2)}) copy-start(f32[1,32,16,128]{3,2,1,0:T(8,128)} %get-tuple-element.54) | copy-start | bytes 786436
  103.7 1.4 %copy-start.10 = (f32[1,32,16,128]{3,2,1,0:T(8,128)S(1)}, f32[1,32,16,128]{3,2,1,0:T(8,128)}, u32[]{:S(2)}) copy-start(f32[1,32,16,128]{3,2,1,0:T(8,128)} %get-tuple-element.55) | copy-start | bytes 786436

commit v6 on v5

--- a/solution.py
+++ b/solution.py
@@ -42,9 +42,9 @@
     return jnp.concatenate([low_x, middle, high_x], axis=x_dim)
 
 
-def halo(block, width):
+def halo(block, width, x_faces=None):
     x_total, z_total = block.shape[-3], block.shape[-2]
-    low, high = faces(block, "gx", block.ndim - 3, width)
+    low, high = x_faces if x_faces is not None else faces(block, "gx", block.ndim - 3, width)
     grown = jnp.concatenate([low, block, high], axis=-3)
     low, high = faces(grown, "yz", block.ndim - 2, width)
     return inside(jnp.concatenate([low, grown, high], axis=-2), width, z_total)
@@ -98,10 +98,11 @@
 def body(velocity, old_pressure, delta_weight, marker_target, pair_owner, pair_grain, box_anchor):
     fields, cx, cz, ny = velocity.shape
     flow_fields = jnp.concatenate([velocity, old_pressure[None]], 0)
-    flow_padded = padded_of(flow_fields, 1, 2)
+    reach = 3
+    low_x, high_x = faces(flow_fields, "gx", 1, reach)
+    flow_padded = padded_of(flow_fields, 1, 2, x_faces=(low_x[:, reach - 1 :], high_x[:, :1]))
     predicted = predict(flow_padded)
-    reach = 3
-    pressure_wide = halo(old_pressure, reach)
+    pressure_wide = halo(old_pressure, reach, x_faces=(low_x[fields], high_x[fields]))
 
     anchors = box_anchor[0]
     owners = pair_owner[0, :, 0]

time: 107 us -> 105 us (0.981)
  starting transfers between devices: 38.6 us -> 36.3 us
    ppermute x6 -> x5, starting transfers between devices: 9.48 us -> 6.52 us  [faces(): lax.ppermute(lax.slice_in_dim(block, block.shape[dim] - width, None, axis...]
    squeeze x0 -> x2, local copies, waits for them, and re-layouts: none -> 1.48 us  [the longest x1 0.74 us: body(): high_x[fields]]
    ppermute x6 -> x5, starting transfers between devices: 18.5 us -> 18.2 us  [faces(): lax.ppermute(lax.slice_in_dim(block, 0, width, axis=dim), axis, backward)]
    ppermute x6 -> x5, waiting for transfers between devices: 2.61 us -> 2.67 us  [faces(): lax.ppermute(lax.slice_in_dim(block, 0, width, axis=dim), axis, backward)]
    unnamed x90 -> x80, local copies, waits for them, and re-layouts: 2.47 us -> 2.48 us
    ppermute x6 -> x5, waiting for transfers between devices: 6.42 us -> 6.42 us  [faces(): lax.ppermute(lax.slice_in_dim(block, block.shape[dim] - width, None, axis...]
  transfers between devices with their start and end apart: 14 -> 12, of which waited for: 5 -> 5; matrix products, arithmetic and copies ran while one was open for 23% -> 13% of each run, Pallas kernels for 0% -> 0%
where the time goes in v6:
time: 105 us; the launch traced here: 104 us
  starting transfers between devices  36.3 us (35%)
  waiting for transfers between devices  23 us (22%)
  local copies, waits for them, and re-layouts  19.7 us (19%)
  other arithmetic  18.8 us (18%)
  matrix products  5.14 us (5%)
  between operations  1.44 us (1%)
    ppermute x5, starting transfers between devices, faces(): lax.ppermute(lax.slice_in_dim(block, 0, width, axis=dim), axis, backward)  18.2 us
    all_to_all x1, waiting for transfers between devices, body(): back = lax.all_to_all(returned, 'yz', 0, 0, tiled=True)  8.77 us
    all_to_all x1, starting transfers between devices, body(): received = lax.all_to_all(send, 'yz', 0, 0, tiled=True)  6.85 us
    ppermute x5, starting transfers between devices, faces(): lax.ppermute(lax.slice_in_dim(block, block.shape[dim] - width, None, axis...  6.52 us
    ppermute x5, waiting for transfers between devices, faces(): lax.ppermute(lax.slice_in_dim(block, block.shape[dim] - width, None, axis...  6.42 us
    all_to_all x1, waiting for transfers between devices, body(): received = lax.all_to_all(send, 'yz', 0, 0, tiled=True)  5.18 us
    all_to_all x1, starting transfers between devices, body(): back = lax.all_to_all(returned, 'yz', 0, 0, tiled=True)  4.68 us
    slice x6, local copies, waits for them, and re-layouts, neighbours(): return total + jnp.roll(middle, 1, -1) + jnp.roll(middle, -1, -1)  3.51 us
  transfers between devices with their start and end apart: 12, of which 5 were waited for; matrix products, arithmetic and copies ran while one was open for 13% of the time, Pallas kernels for 0%

profile of v6, /device:TPU:1, one launch (start us, length us, event | category | flops | bytes accessed | tf_op | source)
XLA Modules:
  0.0 104.4 jit_solution(17517627863910923214)
XLA Ops:
  0.7 1.5 %pad_maximum_fusion.27 = (f32[4,32,1,128]{3,2,1,0:T(1,128)S(1)}, f32[4,32,1,128]{3,2,1,0:T(1,128)S(1)}) fusion(f32[1,32,16,128]{3,2,1,0:T(8,128)} %bitcast.118, f32[3,32,16,128]{3,2,1,0:T(8,128)} %param.7), kind=kLoop, calls=%fused_computation.150 | loop fusion | flops 32768 | bytes 1179648 | tf_op jit(solution)/shard_map/slice | solution.py:21
  2.1 8.9 %collective-permute-start.1 = (f32[4,32,1,128]{3,2,1,0:T(1,128)S(1)}, f32[4,32,1,128]{3,2,1,0:T(1,128)S(1)}, u32[]{:S(2)}, u32[]{:S(2)}) collective-permute-start(f32[4,32,1,128]{3,2,1,0:T(1,128)S(1)} %get-tuple-element.26), channel_id=1, source_target_pairs={{1,0},{2,1},{3,2},{4,3},{5,4},{6,5},{7,6},{8,7},{9,8},{10,9},{11,1... | collective-permute-start | bytes 196616 | tf_op jit(solution)/shard_map/ppermute | solution.py:23
  11.1 0.8 pad_maximum_fusion.21
  11.8 1.0 collective-permute-start.2
  12.8 1.1 %collective-permute-start.3 = (f32[4,3,16,128]{3,2,1,0:T(8,128)S(1)}, f32[4,3,16,128]{3,2,1,0:T(8,128)S(1)}, u32[]{:S(2)}, u32[]{:S(2)}) collective-permute-start(f32[4,3,16,128]{3,2,1,0:T(8,128)S(1)} %get-tuple-element.27), channel_id=1, source_target_pairs={{0,32},{32,64},{64,96},{96,128},{128,160},{160,192},{192,224},{224... | collective-permute-start | bytes 294920 | tf_op jit(solution)/shard_map/ppermute | solution.py:20
  13.9 1.4 %fusion.83 = (f32[3,32,16,1]{3,2,1,0:T(8,128)}, f32[3,32,16,1]{3,2,1,0:T(8,128)}) fusion(f32[3,32,16,128]{3,2,1,0:T(8,128)S(1)} %copy-done.1), kind=kLoop, calls=%fused_computation.209 | loop fusion | bytes 24576 | tf_op jit(solution)/shard_map/jit(_roll_static)/slice | solution.py:81
  15.3 1.4 %fusion.84 = (f32[3,32,16,127]{3,2,1,0:T(8,128)}, f32[3,32,16,127]{3,2,1,0:T(8,128)}) fusion(f32[3,32,16,128]{3,2,1,0:T(8,128)S(1)} %copy-done.1), kind=kLoop, calls=%fused_computation.210 | loop fusion | bytes 3121152 | tf_op jit(solution)/shard_map/jit(_roll_static)/slice | solution.py:81
  16.8 0.6 multiply_add_fusion
  17.4 0.6 compare_and_fusion.1
  18.1 0.7 add.318
  18.9 0.7 iota_compare_fusion.10
  19.8 0.6 multiply_add_fusion.1
  20.4 0.7 copy.56
  21.1 0.7 copy.58
  21.7 0.7 iota_compare_fusion.4
  22.4 0.7 iota_compare_fusion.6
  23.2 0.7 iota_compare_fusion.8
  23.9 0.6 compare_and_fusion.2
  24.7 0.5 copy-done.24
  25.6 0.4 copy-done.20
  26.0 0.8 slice_bitcast_fusion.11
  26.8 0.8 fusion.58
  28.4 1.2 %fusion.59 = f32[1,32,16,128]{3,2,1,0:T(8,128)S(1)} fusion(f32[1,32,16,1]{3,2,1,0:T(8,128)S(1)} %copy.51, f32[1,32,16,127]{3,2,1,0:T(8,128)} %get-tuple-element.65, f32[1,32,16,127]{3,2,1,0:T(8,128)S(1)} %get-tuple-element.64, f32[1,32,16,1]{3,2,1,0:T(8,128)S(1)} %copy.53), kind=kLoop, calls=%fused_computation.125 | loop fusion | flops 262144 | bytes 786432 | tf_op jit(solution)/shard_map/mul | solution.py:74
  29.6 2.7 %fusion.80 = (bf16[3,32,16,128]{3,2,1,0:T(8,128)(2,1)S(1)}, f32[3,32,16,128]{3,2,1,0:T(8,128)S(1)}) fusion(f32[1,32,16,128]{3,2,1,0:T(8,128)S(1)} %copy-done.3, f32[1,32,16,128]{3,2,1,0:T(8,128)S(1)} %fusion.59, f32[1,32,16,128]{3,2,1,0:T(8,128)S(1)} %get-tuple-element.60, f32[3,32,16,128]{3,2,1,0:T(8,128)S(1)} %copy-done.1, ...), kind=kLoop, calls=%fused_computation.207 | loop fusion | flops 6094848 | bytes 5054464 | tf_op jit(solution)/shard_map/convert_element_type | solution.py:124
  32.5 0.4 convolution_bitcast_fusion
  32.9 0.4 convolution_bitcast_fusion.1
  33.4 0.4 convolution_bitcast_fusion.2
  33.9 0.6 select_reduce_fusion
  34.9 0.4 convert_element_type.56
  35.3 0.6 fusion.17
  36.0 0.3 fusion.62
  36.2 0.8 all_to_all.16
  37.0 6.8 %all-to-all-start = ((f32[32,4,385]{2,1,0:T(4,128)}), f32[32,4,385]{2,1,0:T(4,128)S(1)}, u32[]{:S(2)}, u32[]{:S(2)}) async-start(f32[32,4,385]{2,1,0:T(4,128)} %all_to_all.16), calls=%async_computation | async-start | bytes 524288 | tf_op jit(solution)/shard_map/all_to_all | solution.py:157
  43.9 0.7 slice_bitcast_fusion.13
  44.6 0.7 slice_bitcast_fusion.14
  45.4 1.3 %collective-permute-start.4 = (f32[38,3,128]{2,1,0:T(4,128)S(1)}, f32[38,3,128]{2,1,0:T(4,128)S(1)}, u32[]{:S(2)}, u32[]{:S(2)}) collective-permute-start(f32[38,3,128]{2,1,0:T(4,128)S(1)} %get-tuple-element.69), channel_id=1, source_target_pairs={{0,1},{1,2},{2,3},{3,4},{4,5},{5,6},{6,7},{7,8},{8,9},{9,10},{10,1... | collective-permute-start | bytes 175112 | tf_op jit(solution)/shard_map/ppermute | solution.py:20
  46.7 3.6 %collective-permute-start.5 = (f32[38,3,128]{2,1,0:T(4,128)S(1)}, f32[38,3,128]{2,1,0:T(4,128)S(1)}, u32[]{:S(2)}, u32[]{:S(2)}) collective-permute-start(f32[38,3,128]{2,1,0:T(4,128)S(1)} %get-tuple-element.70), channel_id=1, source_target_pairs={{1,0},{2,1},{3,2},{4,3},{5,4},{6,5},{7,6},{8,7},{9,8},{10,9},{11,1... | collective-permute-start | bytes 175112 | tf_op jit(solution)/shard_map/ppermute | solution.py:23
  50.2 5.2 %all-to-all-done = f32[32,4,385]{2,1,0:T(4,128)S(1)} async-done(((f32[32,4,385]{2,1,0:T(4,128)}), f32[32,4,385]{2,1,0:T(4,128)S(1)}, u32[]{:S(2)}, u32[]{:S(2)}) %all-to-all-start) | async-done | bytes 197152 | tf_op jit(solution)/shard_map/all_to_all | solution.py:157
  55.9 0.3 convolution_convert_fusion
  56.2 0.7 all_to_all.19
  56.8 4.7 %all-to-all-start.1 = ((bf16[32,4,384]{2,1,0:T(4,128)(2,1)}), bf16[32,4,384]{2,1,0:T(4,128)(2,1)S(1)}, u32[]{:S(2)}, u32[]{:S(2)}) async-start(bf16[32,4,384]{2,1,0:T(4,128)(2,1)} %all_to_all.19), calls=%async_computation.1 | async-start | bytes 196608 | tf_op jit(solution)/shard_map/all_to_all | solution.py:170
  61.6 8.8 %all-to-all-done.1 = bf16[32,4,384]{2,1,0:T(4,128)(2,1)S(1)} async-done(((bf16[32,4,384]{2,1,0:T(4,128)(2,1)}), bf16[32,4,384]{2,1,0:T(4,128)(2,1)S(1)}, u32[]{:S(2)}, u32[]{:S(2)}) %all-to-all-start.1) | async-done | bytes 98336 | tf_op jit(solution)/shard_map/all_to_all | solution.py:170
  70.6 0.4 convolution_bitcast_fusion.3
  71.0 0.4 reshape.579
  71.5 3.2 %slice_reduce_fusion.7 = (f32[3,512]{1,0:T(4,128)S(1)}, f32[3,512]{1,0:T(4,128)S(1)}, f32[3,512]{1,0:T(4,128)S(1)}, f32[3,512]{1,0:T(4,128)S(1)}, f32[3,512]{1,0...) fusion(f32[3,512,8]{2,1,0:T(8,128)S(1)} %reshape.579), kind=kLoop, calls=%fused_computation.29 | loop fusion | bytes 98304 | tf_op jit(solution)/shard_map/slice | solution.py:183
  74.8 0.5 select_add_fusion
  75.3 0.6 fusion.6
  76.0 0.6 fusion.9
  76.6 0.6 fusion.12
  77.4 4.0 %collective-permute-start.6 = (f32[3,3,16,128]{3,2,1,0:T(8,128)S(1)}, f32[3,3,16,128]{3,2,1,0:T(8,128)S(1)}, u32[]{:S(2)}, u32[]{:S(2)}) collective-permute-start(f32[3,3,16,128]{3,2,1,0:T(8,128)S(1)} %get-tuple-element.31), channel_id=1, source_target_pairs={{0,32},{32,64},{64,96},{96,128},{128,160},{160,192},{192,224},{224... | collective-permute-start | bytes 221192 | tf_op jit(solution)/shard_map/ppermute | solution.py:20
  81.5 1.2 %collective-permute-done.6 = f32[3,3,16,128]{3,2,1,0:T(8,128)S(1)} collective-permute-done((f32[3,3,16,128]{3,2,1,0:T(8,128)S(1)}, f32[3,3,16,128]{3,2,1,0:T(8,128)S(1)}, u32[]{:S(2)}, u32[]{:S(2)}) %collective-permute-start.6) | collective-permute-done | bytes 73760 | tf_op jit(solution)/shard_map/ppermute | solution.py:20
  82.8 2.7 %collective-permute-done.7 = f32[3,3,16,128]{3,2,1,0:T(8,128)S(1)} collective-permute-done((f32[3,3,16,128]{3,2,1,0:T(8,128)S(1)}, f32[3,3,16,128]{3,2,1,0:T(8,128)S(1)}, u32[]{:S(2)}, u32[]{:S(2)}) %collective-permute-start.7) | collective-permute-done | bytes 73760 | tf_op jit(solution)/shard_map/ppermute | solution.py:23
  85.6 4.8 %collective-permute-start.9 = (f32[3,38,3,128]{3,2,1,0:T(4,128)S(1)}, f32[3,38,3,128]{3,2,1,0:T(4,128)S(1)}, u32[]{:S(2)}, u32[]{:S(2)}) collective-permute-start(f32[3,38,3,128]{3,2,1,0:T(4,128)S(1)} %get-tuple-element.30), channel_id=1, source_target_pairs={{1,0},{2,1},{3,2},{4,3},{5,4},{6,5},{7,6},{8,7},{9,8},{10,9},{11,1... | collective-permute-start | bytes 525320 | tf_op jit(solution)/shard_map/ppermute | solution.py:23
  90.6 5.2 %collective-permute-done.8 = f32[3,38,3,128]{3,2,1,0:T(4,128)S(1)} collective-permute-done((f32[3,38,3,128]{3,2,1,0:T(4,128)S(1)}, f32[3,38,3,128]{3,2,1,0:T(4,128)S(1)}, u32[]{:S(2)}, u32[]{:S(2)}) %collective-permute-start.8) | collective-permute-done | bytes 175136 | tf_op jit(solution)/shard_map/ppermute | solution.py:20
  95.8 0.3 maximum_select_fusion
  96.5 0.3 copy-done.31
  96.8 0.7 fusion.45
  97.9 0.3 copy-done.32
  98.2 0.4 fusion.47
  98.7 0.9 slice_bitcast_fusion.3
  99.5 0.9 fusion.91
  101.0 0.9 copy.66
  101.9 1.4 %fusion.60 = f32[1,32,16,128]{3,2,1,0:T(8,128)S(1)} fusion(f32[1,32,16,1]{3,2,1,0:T(8,128)S(1)} %copy.64, f32[1,32,16,127]{3,2,1,0:T(8,128)} %get-tuple-element.59, f32[1,32,16,127]{3,2,1,0:T(8,128)} %get-tuple-element.58, f32[1,32,16,1]{3,2,1,0:T(8,128)} %copy.66), kind=kLoop, calls=%fused_computation.127 | loop fusion | flops 262144 | bytes 786432 | tf_op jit(solution)/shard_map/mul | solution.py:74
  103.3 1.1 %maximum_subtract_fusion = f32[3,32,16,128]{3,2,1,0:T(8,128)} fusion(f32[1,32,16,128]{3,2,1,0:T(8,128)S(1)} %copy-done.5, f32[1,32,16,128]{3,2,1,0:T(8,128)S(1)} %fusion.60, f32[1,32,16,128]{3,2,1,0:T(8,128)S(1)} %copy-done.4, f32[3,32,16,128]{3,2,1,0:T(8,128)S(1)} %get-tuple-element.21, f32[1,32,16,128]{3,2,1,0:T(8,128)S(1)} %fusion.12, ...), kind=kLoop, calls=%fused_computation.54 | loop fusion | flops 1179648 | bytes 3145728 | tf_op jit(solution)/shard_map/sub | solution.py:208
  (134 shorter events, 5.1 us)
Async XLA Ops:
  0.6 34.6 %copy-start = (bf16[1,32,128,128]{3,2,1,0:T(8,128)(2,1)S(1)}, bf16[1,32,128,128]{3,2,1,0:T(8,128)(2,1)}, u32[]{:S(2)}) copy-start(bf16[1,32,128,128]{3,2,1,0:T(8,128)(2,1)} %param.9) | copy-start | bytes 3145732
  0.6 10.4 %copy-start.1 = (f32[3,32,16,128]{3,2,1,0:T(8,128)S(1)}, f32[3,32,16,128]{3,2,1,0:T(8,128)}, u32[]{:S(2)}) copy-start(f32[3,32,16,128]{3,2,1,0:T(8,128)} %param.7) | copy-start | bytes 2359300
  2.1 22.3 %collective-permute-start.1 = (f32[4,32,1,128]{3,2,1,0:T(1,128)S(1)}, f32[4,32,1,128]{3,2,1,0:T(1,128)S(1)}, u32[]{:S(2)}, u32[]{:S(2)}) collective-permute-start(f32[4,32,1,128]{3,2,1,0:T(1,128)S(1)} %get-tuple-element.26), channel_id=1, source_target_pairs={{1,0},{2,1},{3,2},{4,3},{5,4},{6,5},{7,6},{8,7},{9,8},{10,9},{11,1... | collective-permute-start | bytes 196616 | tf_op jit(solution)/shard_map/ppermute | solution.py:23
  11.0 13.5 %collective-permute-start = (f32[4,32,1,128]{3,2,1,0:T(1,128)S(1)}, f32[4,32,1,128]{3,2,1,0:T(1,128)S(1)}, u32[]{:S(2)}, u32[]{:S(2)}) collective-permute-start(f32[4,32,1,128]{3,2,1,0:T(1,128)S(1)} %get-tuple-element.25), channel_id=1, source_target_pairs={{0,1},{1,2},{2,3},{3,4},{4,5},{5,6},{6,7},{7,8},{8,9},{9,10},{10,1... | collective-permute-start | bytes 196616 | tf_op jit(solution)/shard_map/ppermute | solution.py:20
  11.8 12.8 %collective-permute-start.2 = (f32[4,3,16,128]{3,2,1,0:T(8,128)S(1)}, f32[4,3,16,128]{3,2,1,0:T(8,128)S(1)}, u32[]{:S(2)}, u32[]{:S(2)}) collective-permute-start(f32[4,3,16,128]{3,2,1,0:T(8,128)S(1)} %get-tuple-element.28), channel_id=1, source_target_pairs={{32,0},{64,32},{96,64},{128,96},{160,128},{192,160},{224,192},{0,2... | collective-permute-start | bytes 294920 | tf_op jit(solution)/shard_map/ppermute | solution.py:23
  12.8 11.9 %collective-permute-start.3 = (f32[4,3,16,128]{3,2,1,0:T(8,128)S(1)}, f32[4,3,16,128]{3,2,1,0:T(8,128)S(1)}, u32[]{:S(2)}, u32[]{:S(2)}) collective-permute-start(f32[4,3,16,128]{3,2,1,0:T(8,128)S(1)} %get-tuple-element.27), channel_id=1, source_target_pairs={{0,32},{32,64},{64,96},{96,128},{128,160},{160,192},{192,224},{224... | collective-permute-start | bytes 294920 | tf_op jit(solution)/shard_map/ppermute | solution.py:20
  15.3 2.7 %copy-start.30 = (s32[1,32,3]{1,0,2:T(1,128)S(1)}, s32[1,32,3]{1,0,2:T(1,128)}, u32[]{:S(2)}) copy-start(s32[1,32,3]{1,0,2:T(1,128)} %param.13) | copy-start | bytes 1156
  15.3 4.3 %copy-start.33 = (s32[1,32,1]{1,2,0:T(1,128)S(1)}, s32[1,32,1]{1,2,0:T(1,128)}, u32[]{:S(2)}) copy-start(s32[1,32,1]{1,2,0:T(1,128)} %param.11) | copy-start | bytes 388
  15.3 5.1 %copy-start.34 = (s32[1,32]{1,0:T(1,128)S(1)}, s32[1,32]{1,0:T(1,128)}, u32[]{:S(2)}) copy-start(s32[1,32]{1,0:T(1,128)} %param.12) | copy-start | bytes 388
  15.3 5.8 %copy-start.23 = (f32[1,32,3,128]{3,1,2,0:T(8,128)S(1)}, f32[1,32,3,128]{3,1,2,0:T(8,128)}, u32[]{:S(2)}) copy-start(f32[1,32,3,128]{3,1,2,0:T(8,128)} %param.10) | copy-start | bytes 147460
  16.7 8.6 %copy-start.2 = (f32[32,16,128]{2,1,0:T(8,128)S(1)}, f32[32,16,128]{2,1,0:T(8,128)}, u32[]{:S(2)}) copy-start(f32[32,16,128]{2,1,0:T(8,128)} %param.8) | copy-start | bytes 786436
  24.6 0.6 copy-start.24
  24.7 0.9 copy-start.19
  24.7 0.6 copy-start.25
  25.3 0.6 copy-start.20
  28.4 1.2 %copy-start.3 = (f32[1,32,16,128]{3,2,1,0:T(8,128)S(1)}, f32[1,32,16,128]{3,2,1,0:T(8,128)}, u32[]{:S(2)}) copy-start(f32[1,32,16,128]{3,2,1,0:T(8,128)} %get-tuple-element.61) | copy-start | bytes 786436
  29.6 2.9 %copy-start.28 = (s32[512]{0:T(512)S(1)}, s32[512]{0:T(512)}, u32[]{:S(2)}) copy-start(s32[512]{0:T(512)} %add.318) | copy-start | bytes 6148
  32.3 1.5 %copy-start.6 = (pred[512,128]{0,1:T(8,128)(4,1)S(1)}, pred[512,128]{0,1:T(8,128)(4,1)}, u32[]{:S(2)}) copy-start(pred[512,128]{0,1:T(8,128)(4,1)} %get-tuple-element.89) | copy-start | bytes 196612
  32.4 1.5 %copy-start.7 = (pred[512,128]{0,1:T(8,128)(4,1)S(1)}, pred[512,128]{0,1:T(8,128)(4,1)}, u32[]{:S(2)}) copy-start(pred[512,128]{0,1:T(8,128)(4,1)} %get-tuple-element.90) | copy-start | bytes 196612
  32.4 1.5 %copy-start.8 = (pred[512,128]{0,1:T(8,128)(4,1)S(1)}, pred[512,128]{0,1:T(8,128)(4,1)}, u32[]{:S(2)}) copy-start(pred[512,128]{0,1:T(8,128)(4,1)} %get-tuple-element.83) | copy-start | bytes 196612
  32.4 1.5 %copy-start.9 = (pred[512,128]{0,1:T(8,128)(4,1)S(1)}, pred[512,128]{0,1:T(8,128)(4,1)}, u32[]{:S(2)}) copy-start(pred[512,128]{0,1:T(8,128)(4,1)} %get-tuple-element.84) | copy-start | bytes 196612
  32.4 1.5 %copy-start.11 = (pred[512,128]{0,1:T(8,128)(4,1)S(1)}, pred[512,128]{0,1:T(8,128)(4,1)}, u32[]{:S(2)}) copy-start(pred[512,128]{0,1:T(8,128)(4,1)} %get-tuple-element.85) | copy-start | bytes 196612
  32.4 1.5 %copy-start.13 = (pred[512,128]{0,1:T(8,128)(4,1)S(1)}, pred[512,128]{0,1:T(8,128)(4,1)}, u32[]{:S(2)}) copy-start(pred[512,128]{0,1:T(8,128)(4,1)} %get-tuple-element.86) | copy-start | bytes 196612
  32.4 1.5 %copy-start.15 = (pred[512,128]{0,1:T(8,128)(4,1)S(1)}, pred[512,128]{0,1:T(8,128)(4,1)}, u32[]{:S(2)}) copy-start(pred[512,128]{0,1:T(8,128)(4,1)} %get-tuple-element.87) | copy-start | bytes 196612
  32.4 1.5 %copy-start.17 = (pred[512,128]{0,1:T(8,128)(4,1)S(1)}, pred[512,128]{0,1:T(8,128)(4,1)}, u32[]{:S(2)}) copy-start(pred[512,128]{0,1:T(8,128)(4,1)} %get-tuple-element.88) | copy-start | bytes 196612
  34.5 1.4 %copy-start.22 = (f32[32,1]{1,0:T(8,128)S(1)}, f32[32,1]{1,0:T(8,128)}, u32[]{:S(2)}) copy-start(f32[32,1]{1,0:T(8,128)} %copy.56) | copy-start | bytes 388
  34.5 1.4 %copy-start.27 = (s32[32]{0:T(128)S(1)}, s32[32]{0:T(128)}, u32[]{:S(2)}) copy-start(s32[32]{0:T(128)} %multiply_add_fusion.1) | copy-start | bytes 388
  35.9 19.7 %copy-start.21 = (f32[1,32,3,128]{3,2,1,0:T(4,128)S(1)}, f32[1,32,3,128]{3,2,1,0:T(4,128)}, u32[]{:S(2)}) copy-start(f32[1,32,3,128]{3,2,1,0:T(4,128)} %copy.58) | copy-start | bytes 147460
  37.0 18.4 %all-to-all-start = ((f32[32,4,385]{2,1,0:T(4,128)}), f32[32,4,385]{2,1,0:T(4,128)S(1)}, u32[]{:S(2)}, u32[]{:S(2)}) async-start(f32[32,4,385]{2,1,0:T(4,128)} %all_to_all.16), calls=%async_computation | async-start | bytes 524288 | tf_op jit(solution)/shard_map/all_to_all | solution.py:157
  45.4 16.1 %collective-permute-start.4 = (f32[38,3,128]{2,1,0:T(4,128)S(1)}, f32[38,3,128]{2,1,0:T(4,128)S(1)}, u32[]{:S(2)}, u32[]{:S(2)}) collective-permute-start(f32[38,3,128]{2,1,0:T(4,128)S(1)} %get-tuple-element.69), channel_id=1, source_target_pairs={{0,1},{1,2},{2,3},{3,4},{4,5},{5,6},{6,7},{7,8},{8,9},{9,10},{10,1... | collective-permute-start | bytes 175112 | tf_op jit(solution)/shard_map/ppermute | solution.py:20
  46.7 14.8 %collective-permute-start.5 = (f32[38,3,128]{2,1,0:T(4,128)S(1)}, f32[38,3,128]{2,1,0:T(4,128)S(1)}, u32[]{:S(2)}, u32[]{:S(2)}) collective-permute-start(f32[38,3,128]{2,1,0:T(4,128)S(1)} %get-tuple-element.70), channel_id=1, source_target_pairs={{1,0},{2,1},{3,2},{4,3},{5,4},{6,5},{7,6},{8,7},{9,8},{10,9},{11,1... | collective-permute-start | bytes 175112 | tf_op jit(solution)/shard_map/ppermute | solution.py:23
  56.8 13.6 %all-to-all-start.1 = ((bf16[32,4,384]{2,1,0:T(4,128)(2,1)}), bf16[32,4,384]{2,1,0:T(4,128)(2,1)S(1)}, u32[]{:S(2)}, u32[]{:S(2)}) async-start(bf16[32,4,384]{2,1,0:T(4,128)(2,1)} %all_to_all.19), calls=%async_computation.1 | async-start | bytes 196608 | tf_op jit(solution)/shard_map/all_to_all | solution.py:170
  71.5 3.3 %copy-start.10 = (pred[512,128]{0,1:T(8,128)(4,1)S(1)}, pred[512,128]{0,1:T(8,128)(4,1)}, u32[]{:S(2)}) copy-start(pred[512,128]{0,1:T(8,128)(4,1)} %get-tuple-element.84) | copy-start | bytes 196612
  71.5 3.3 %copy-start.12 = (pred[512,128]{0,1:T(8,128)(4,1)S(1)}, pred[512,128]{0,1:T(8,128)(4,1)}, u32[]{:S(2)}) copy-start(pred[512,128]{0,1:T(8,128)(4,1)} %get-tuple-element.85) | copy-start | bytes 196612
  71.5 3.3 %copy-start.14 = (pred[512,128]{0,1:T(8,128)(4,1)S(1)}, pred[512,128]{0,1:T(8,128)(4,1)}, u32[]{:S(2)}) copy-start(pred[512,128]{0,1:T(8,128)(4,1)} %get-tuple-element.86) | copy-start | bytes 196612
  71.5 3.3 %copy-start.16 = (pred[512,128]{0,1:T(8,128)(4,1)S(1)}, pred[512,128]{0,1:T(8,128)(4,1)}, u32[]{:S(2)}) copy-start(pred[512,128]{0,1:T(8,128)(4,1)} %get-tuple-element.87) | copy-start | bytes 196612
  71.5 3.3 %copy-start.18 = (pred[512,128]{0,1:T(8,128)(4,1)S(1)}, pred[512,128]{0,1:T(8,128)(4,1)}, u32[]{:S(2)}) copy-start(pred[512,128]{0,1:T(8,128)(4,1)} %get-tuple-element.88) | copy-start | bytes 196612
  71.5 3.8 %copy-start.26 = (s32[32,16]{1,0:T(8,128)S(1)}, s32[32,16]{1,0:T(8,128)}, u32[]{:S(2)}) copy-start(s32[32,16]{1,0:T(8,128)} %multiply_add_fusion) | copy-start | bytes 6148
  71.5 3.8 %copy-start.29 = (s32[512]{0:T(512)S(1)}, s32[512]{0:T(512)}, u32[]{:S(2)}) copy-start(s32[512]{0:T(512)} %add.318) | copy-start | bytes 6148
  77.4 5.4 %collective-permute-start.6 = (f32[3,3,16,128]{3,2,1,0:T(8,128)S(1)}, f32[3,3,16,128]{3,2,1,0:T(8,128)S(1)}, u32[]{:S(2)}, u32[]{:S(2)}) collective-permute-start(f32[3,3,16,128]{3,2,1,0:T(8,128)S(1)} %get-tuple-element.31), channel_id=1, source_target_pairs={{0,32},{32,64},{64,96},{96,128},{128,160},{160,192},{192,224},{224... | collective-permute-start | bytes 221192 | tf_op jit(solution)/shard_map/ppermute | solution.py:20
  81.4 4.1 %collective-permute-start.7 = (f32[3,3,16,128]{3,2,1,0:T(8,128)S(1)}, f32[3,3,16,128]{3,2,1,0:T(8,128)S(1)}, u32[]{:S(2)}, u32[]{:S(2)}) collective-permute-start(f32[3,3,16,128]{3,2,1,0:T(8,128)S(1)} %get-tuple-element.32), channel_id=1, source_target_pairs={{32,0},{64,32},{96,64},{128,96},{160,128},{192,160},{224,192},{0,2... | collective-permute-start | bytes 221192 | tf_op jit(solution)/shard_map/ppermute | solution.py:23
  85.5 10.2 %collective-permute-start.8 = (f32[3,38,3,128]{3,2,1,0:T(4,128)S(1)}, f32[3,38,3,128]{3,2,1,0:T(4,128)S(1)}, u32[]{:S(2)}, u32[]{:S(2)}) collective-permute-start(f32[3,38,3,128]{3,2,1,0:T(4,128)S(1)} %get-tuple-element.29), channel_id=1, source_target_pairs={{0,1},{1,2},{2,3},{3,4},{4,5},{5,6},{6,7},{7,8},{8,9},{9,10},{10,1... | collective-permute-start | bytes 525320 | tf_op jit(solution)/shard_map/ppermute | solution.py:20
  85.6 10.1 %collective-permute-start.9 = (f32[3,38,3,128]{3,2,1,0:T(4,128)S(1)}, f32[3,38,3,128]{3,2,1,0:T(4,128)S(1)}, u32[]{:S(2)}, u32[]{:S(2)}) collective-permute-start(f32[3,38,3,128]{3,2,1,0:T(4,128)S(1)} %get-tuple-element.30), channel_id=1, source_target_pairs={{1,0},{2,1},{3,2},{4,3},{5,4},{6,5},{7,6},{8,7},{9,8},{10,9},{11,1... | collective-permute-start | bytes 525320 | tf_op jit(solution)/shard_map/ppermute | solution.py:23
  96.1 0.7 copy-start.31
  97.5 0.7 copy-start.32
  101.9 1.4 %copy-start.4 = (f32[1,32,16,128]{3,2,1,0:T(8,128)S(1)}, f32[1,32,16,128]{3,2,1,0:T(8,128)}, u32[]{:S(2)}) copy-start(f32[1,32,16,128]{3,2,1,0:T(8,128)} %get-tuple-element.54) | copy-start | bytes 786436
  101.9 1.4 %copy-start.5 = (f32[1,32,16,128]{3,2,1,0:T(8,128)S(1)}, f32[1,32,16,128]{3,2,1,0:T(8,128)}, u32[]{:S(2)}) copy-start(f32[1,32,16,128]{3,2,1,0:T(8,128)} %get-tuple-element.55) | copy-start | bytes 786436

commit v7 on v6

--- a/solution.py
+++ b/solution.py
@@ -13,15 +13,16 @@
 viscosity = 1.5
 
 
-def faces(block, axis, dim, width=1):
+def faces(block, axis, dim, width=1, carried=None):
     count = lax.axis_size(axis)
     forward = [(i, (i + 1) % count) for i in range(count)]
     backward = [(target, source) for source, target in forward]
+    kind = carried or block.dtype
     low = lax.ppermute(
-        lax.slice_in_dim(block, block.shape[dim] - width, None, axis=dim), axis, forward
-    )
-    high = lax.ppermute(lax.slice_in_dim(block, 0, width, axis=dim), axis, backward)
-    return low, high
+        lax.slice_in_dim(block, block.shape[dim] - width, None, axis=dim).astype(kind), axis, forward
+    )
+    high = lax.ppermute(lax.slice_in_dim(block, 0, width, axis=dim).astype(kind), axis, backward)
+    return low.astype(block.dtype), high.astype(block.dtype)
 
 
 def padded_of(block, x_dim, z_dim, x_faces=None, z_faces=None):
@@ -42,11 +43,11 @@
     return jnp.concatenate([low_x, middle, high_x], axis=x_dim)
 
 
-def halo(block, width, x_faces=None):
+def halo(block, width, x_faces=None, carried=None):
     x_total, z_total = block.shape[-3], block.shape[-2]
-    low, high = x_faces if x_faces is not None else faces(block, "gx", block.ndim - 3, width)
+    low, high = x_faces if x_faces is not None else faces(block, "gx", block.ndim - 3, width, carried)
     grown = jnp.concatenate([low, block, high], axis=-3)
-    low, high = faces(grown, "yz", block.ndim - 2, width)
+    low, high = faces(grown, "yz", block.ndim - 2, width, carried)
     return inside(jnp.concatenate([low, grown, high], axis=-2), width, z_total)
 
 
@@ -199,7 +200,7 @@
     )
     forced_velocity = predicted + added.reshape(fields, cx, cz, ny)
 
-    forced_wide = halo(forced_velocity, reach)
+    forced_wide = halo(forced_velocity, reach, carried=jnp.bfloat16)
     divergence = (
         along_x(forced_wide[0]) + along_y(inner(forced_wide[1])) + along_z(forced_wide[2])
     )

time: 105 us -> 108 us (1.029)
  local copies, waits for them, and re-layouts: 19.7 us -> 23.4 us
  waiting for transfers between devices: 23 us -> 20 us
  other arithmetic: 18.8 us -> 19.9 us
    ppermute x5, waiting for transfers between devices: 6.42 us -> 3.52 us  [faces(): lax.ppermute(lax.slice_in_dim(block, block.shape[dim] - width, None, axis...]
    slice x8, local copies, waits for them, and re-layouts: 1.39 us -> 4.2 us  [along_y(): return 0.5 * (jnp.roll(field, -1, -1) - jnp.roll(field, 1, -1))]
    unnamed x80 -> x68, local copies, waits for them, and re-layouts: 2.48 us -> 2.02 us
  transfers between devices with their start and end apart: 12 -> 12, of which waited for: 5 -> 5; matrix products, arithmetic and copies ran while one was open for 13% -> 15% of each run, Pallas kernels for 0% -> 0%
where the time goes in v7:
time: 108 us; the launch traced here: 107 us
  starting transfers between devices  37.2 us (34%)
  local copies, waits for them, and re-layouts  23.4 us (22%)
  waiting for transfers between devices  20 us (19%)
  other arithmetic  19.9 us (18%)
  matrix products  5.14 us (5%)
  between operations  1.3 us (1%)
    ppermute x5, starting transfers between devices, faces(): lax.ppermute(lax.slice_in_dim(block, 0, width, axis=dim).astype(kind), ax...  18.2 us
    all_to_all x1, waiting for transfers between devices, body(): back = lax.all_to_all(returned, 'yz', 0, 0, tiled=True)  8.79 us
    all_to_all x1, starting transfers between devices, body(): received = lax.all_to_all(send, 'yz', 0, 0, tiled=True)  7.68 us
    ppermute x5, starting transfers between devices, faces(): lax.ppermute(lax.slice_in_dim(block, block.shape[dim] - width, None, axis...  6.54 us
    all_to_all x1, waiting for transfers between devices, body(): received = lax.all_to_all(send, 'yz', 0, 0, tiled=True)  5.07 us
    all_to_all x1, starting transfers between devices, body(): back = lax.all_to_all(returned, 'yz', 0, 0, tiled=True)  4.76 us
    slice x8, local copies, waits for them, and re-layouts, along_y(): return 0.5 * (jnp.roll(field, -1, -1) - jnp.roll(field, 1, -1))  4.2 us
    concatenate x6, local copies, waits for them, and re-layouts, along_y(): return 0.5 * (jnp.roll(field, -1, -1) - jnp.roll(field, 1, -1))  3.88 us
  transfers between devices with their start and end apart: 12, of which 5 were waited for; matrix products, arithmetic and copies ran while one was open for 15% of the time, Pallas kernels for 0%

profile of v7, /device:TPU:1, one launch (start us, length us, event | category | flops | bytes accessed | tf_op | source)
XLA Modules:
  0.0 106.9 jit_solution(17422991149205515807)
XLA Ops:
  0.7 1.5 %pad_maximum_fusion.26 = (f32[4,32,1,128]{3,2,1,0:T(1,128)S(1)}, f32[4,32,1,128]{3,2,1,0:T(1,128)S(1)}) fusion(f32[1,32,16,128]{3,2,1,0:T(8,128)} %bitcast.118, f32[3,32,16,128]{3,2,1,0:T(8,128)} %param.7), kind=kLoop, calls=%fused_computation.151 | loop fusion | flops 32768 | bytes 1179648 | tf_op jit(solution)/shard_map/slice | solution.py:22
  2.1 8.9 %collective-permute-start.1 = (f32[4,32,1,128]{3,2,1,0:T(1,128)S(1)}, f32[4,32,1,128]{3,2,1,0:T(1,128)S(1)}, u32[]{:S(2)}, u32[]{:S(2)}) collective-permute-start(f32[4,32,1,128]{3,2,1,0:T(1,128)S(1)} %get-tuple-element.28), channel_id=1, source_target_pairs={{1,0},{2,1},{3,2},{4,3},{5,4},{6,5},{7,6},{8,7},{9,8},{10,9},{11,1... | collective-permute-start | bytes 196616 | tf_op jit(solution)/shard_map/ppermute | solution.py:24
  11.1 1.4 %pad_maximum_fusion.20 = (f32[4,3,16,128]{3,2,1,0:T(8,128)S(1)}, f32[4,3,16,128]{3,2,1,0:T(8,128)}) fusion(f32[1,32,16,128]{3,2,1,0:T(8,128)} %bitcast.119, f32[3,32,16,128]{3,2,1,0:T(8,128)S(1)} %copy-done.1), kind=kLoop, calls=%fused_computation.144 | loop fusion | flops 49152 | bytes 1245184 | tf_op jit(solution)/shard_map/concatenate | solution.py:101
  12.5 1.0 collective-permute-start.2
  13.4 1.1 %collective-permute-start.3 = (f32[4,3,16,128]{3,2,1,0:T(8,128)S(1)}, f32[4,3,16,128]{3,2,1,0:T(8,128)}, u32[]{:S(2)}, u32[]{:S(2)}) collective-permute-start(f32[4,3,16,128]{3,2,1,0:T(8,128)S(1)} %get-tuple-element.29), channel_id=1, source_target_pairs={{0,32},{32,64},{64,96},{96,128},{128,160},{160,192},{192,224},{224... | collective-permute-start | bytes 294920 | tf_op jit(solution)/shard_map/ppermute | solution.py:21
  14.5 1.1 %fusion.84 = (f32[3,32,16,1]{3,2,1,0:T(8,128)S(1)}, f32[3,32,16,1]{3,2,1,0:T(8,128)}) fusion(f32[3,32,16,128]{3,2,1,0:T(8,128)S(1)} %copy-done.1), kind=kLoop, calls=%fused_computation.210 | loop fusion | bytes 24576 | tf_op jit(solution)/shard_map/jit(_roll_static)/slice | solution.py:82
  15.7 1.4 %fusion.85 = (f32[3,32,16,127]{3,2,1,0:T(8,128)}, f32[3,32,16,127]{3,2,1,0:T(8,128)}) fusion(f32[3,32,16,128]{3,2,1,0:T(8,128)S(1)} %copy-done.1), kind=kLoop, calls=%fused_computation.211 | loop fusion | bytes 3121152 | tf_op jit(solution)/shard_map/jit(_roll_static)/slice | solution.py:82
  17.1 0.5 iota_add_fusion
  17.6 0.6 multiply_add_fusion
  18.2 0.5 compare_and_fusion
  18.8 0.6 compare_and_fusion.1
  19.4 0.7 add.318
  20.3 0.7 iota_compare_fusion.10
  21.2 0.6 multiply_add_fusion.1
  21.8 0.7 copy.58
  22.5 0.7 iota_compare_fusion.4
  23.2 0.7 iota_compare_fusion.6
  23.9 0.7 iota_compare_fusion.8
  24.7 0.5 compare_and_fusion.2
  25.3 0.8 slice.423
  26.1 0.8 slice.424
  26.9 0.6 copy-done.16
  27.6 0.8 fusion.94
  28.5 0.9 slice_bitcast_fusion.11
  29.3 0.9 fusion.58
  30.2 0.8 copy.50
  31.0 0.9 copy.51
  31.9 1.7 %copy.52 = f32[32,16,1]{0,1,2:T(8,128)} copy(f32[32,16,1]{2,1,0:T(8,128)} %get-tuple-element.62) | data formatting | bytes 4096 | tf_op jit(solution)/shard_map/jit(_roll_static)/slice | solution.py:75
  33.6 1.6 %copy.53 = f32[1,32,16,1]{3,2,1,0:T(8,128)} copy(f32[1,32,16,1]{1,2,3,0:T(8,128)} %bitcast.129) | data formatting | bytes 4096 | tf_op jit(solution)/shard_map/jit(_roll_static)/concatenate | solution.py:75
  35.2 1.4 %fusion.59 = f32[1,32,16,128]{3,2,1,0:T(8,128)S(1)} fusion(f32[1,32,16,1]{3,2,1,0:T(8,128)S(1)} %copy.51, f32[1,32,16,127]{3,2,1,0:T(8,128)} %get-tuple-element.65, f32[1,32,16,127]{3,2,1,0:T(8,128)} %get-tuple-element.64, f32[1,32,16,1]{3,2,1,0:T(8,128)} %copy.53), kind=kLoop, calls=%fused_computation.125 | loop fusion | flops 262144 | bytes 786432 | tf_op jit(solution)/shard_map/mul | solution.py:75
  36.6 3.2 %fusion.82 = (bf16[3,32,16,128]{3,2,1,0:T(8,128)(2,1)S(1)}, f32[3,32,16,128]{3,2,1,0:T(8,128)}) fusion(f32[1,32,16,128]{3,2,1,0:T(8,128)S(1)} %copy-done.6, f32[1,32,16,128]{3,2,1,0:T(8,128)S(1)} %fusion.59, f32[1,32,16,128]{3,2,1,0:T(8,128)S(1)} %copy-done.5, f32[3,32,16,128]{3,2,1,0:T(8,128)S(1)} %copy-done.1, ...), kind=kLoop, calls=%fused_computation.209 | loop fusion | flops 6094848 | bytes 5054464 | tf_op jit(solution)/shard_map/convert_element_type | solution.py:125
  39.9 0.4 convolution_bitcast_fusion
  40.4 0.4 convolution_bitcast_fusion.1
  40.8 0.4 convolution_bitcast_fusion.2
  41.3 0.6 select_reduce_fusion
  42.3 0.4 convert_element_type.72
  42.7 0.6 fusion.17
  43.7 0.8 all_to_all.16
  44.5 7.7 %all-to-all-start = ((f32[32,4,385]{2,1,0:T(4,128)}), f32[32,4,385]{2,1,0:T(4,128)S(1)}, u32[]{:S(2)}, u32[]{:S(2)}) async-start(f32[32,4,385]{2,1,0:T(4,128)} %all_to_all.16), calls=%async_computation | async-start | bytes 524288 | tf_op jit(solution)/shard_map/all_to_all | solution.py:158
  52.1 0.7 slice_bitcast_fusion.13
  52.9 0.7 slice_bitcast_fusion.14
  53.7 1.3 %collective-permute-start.4 = (f32[38,3,128]{2,1,0:T(4,128)S(1)}, f32[38,3,128]{2,1,0:T(4,128)S(1)}, u32[]{:S(2)}, u32[]{:S(2)}) collective-permute-start(f32[38,3,128]{2,1,0:T(4,128)S(1)} %get-tuple-element.71), channel_id=1, source_target_pairs={{0,1},{1,2},{2,3},{3,4},{4,5},{5,6},{6,7},{7,8},{8,9},{9,10},{10,1... | collective-permute-start | bytes 175112 | tf_op jit(solution)/shard_map/ppermute | solution.py:21
  55.0 3.6 %collective-permute-start.5 = (f32[38,3,128]{2,1,0:T(4,128)S(1)}, f32[38,3,128]{2,1,0:T(4,128)S(1)}, u32[]{:S(2)}, u32[]{:S(2)}) collective-permute-start(f32[38,3,128]{2,1,0:T(4,128)S(1)} %get-tuple-element.72), channel_id=1, source_target_pairs={{1,0},{2,1},{3,2},{4,3},{5,4},{6,5},{7,6},{8,7},{9,8},{10,9},{11,1... | collective-permute-start | bytes 175112 | tf_op jit(solution)/shard_map/ppermute | solution.py:24
  58.5 5.1 %all-to-all-done = f32[32,4,385]{2,1,0:T(4,128)S(1)} async-done(((f32[32,4,385]{2,1,0:T(4,128)}), f32[32,4,385]{2,1,0:T(4,128)S(1)}, u32[]{:S(2)}, u32[]{:S(2)}) %all-to-all-start) | async-done | bytes 197152 | tf_op jit(solution)/shard_map/all_to_all | solution.py:158
  64.1 0.3 convolution_convert_fusion
  64.3 0.7 all_to_all.19
  65.0 4.8 %all-to-all-start.1 = ((bf16[32,4,384]{2,1,0:T(4,128)(2,1)}), bf16[32,4,384]{2,1,0:T(4,128)(2,1)S(1)}, u32[]{:S(2)}, u32[]{:S(2)}) async-start(bf16[32,4,384]{2,1,0:T(4,128)(2,1)} %all_to_all.19), calls=%async_computation.1 | async-start | bytes 196608 | tf_op jit(solution)/shard_map/all_to_all | solution.py:171
  69.9 8.8 %all-to-all-done.1 = bf16[32,4,384]{2,1,0:T(4,128)(2,1)S(1)} async-done(((bf16[32,4,384]{2,1,0:T(4,128)(2,1)}), bf16[32,4,384]{2,1,0:T(4,128)(2,1)S(1)}, u32[]{:S(2)}, u32[]{:S(2)}) %all-to-all-start.1) | async-done | bytes 98336 | tf_op jit(solution)/shard_map/all_to_all | solution.py:171
  78.9 0.4 convolution_bitcast_fusion.3
  79.3 0.4 reshape.579
  79.8 3.2 %slice_reduce_fusion.7 = (f32[3,512]{1,0:T(4,128)S(1)}, f32[3,512]{1,0:T(4,128)S(1)}, f32[3,512]{1,0:T(4,128)S(1)}, f32[3,512]{1,0:T(4,128)S(1)}, f32[3,512]{1,0...) fusion(f32[3,512,8]{2,1,0:T(8,128)S(1)} %reshape.579), kind=kLoop, calls=%fused_computation.29 | loop fusion | bytes 98304 | tf_op jit(solution)/shard_map/slice | solution.py:184
  83.0 0.5 select_add_fusion
  83.5 0.6 fusion.6
  84.2 0.6 fusion.9
  84.8 0.6 fusion.12
  85.6 4.0 %collective-permute-start.6 = (bf16[3,3,16,128]{3,2,1,0:T(8,128)(2,1)S(1)}, bf16[3,3,16,128]{3,2,1,0:T(8,128)(2,1)S(1)}, u32[]{:S(2)}, u32[]{:S(2)}) collective-permute-start(bf16[3,3,16,128]{3,2,1,0:T(8,128)(2,1)S(1)} %get-tuple-element.66), channel_id=1, source_target_pairs={{0,32},{32,64},{64,96},{96,128},{128,160},{160,192},{192,224},{224... | collective-permute-start | bytes 110600 | tf_op jit(solution)/shard_map/ppermute | solution.py:21
  89.8 0.9 collective-permute-done.6
  90.7 2.6 %collective-permute-done.7 = bf16[3,3,16,128]{3,2,1,0:T(8,128)(2,1)S(1)} collective-permute-done((bf16[3,3,16,128]{3,2,1,0:T(8,128)(2,1)S(1)}, bf16[3,3,16,128]{3,2,1,0:T(8,128)(2,1)S(1)}, u32[]{:S(2)}, u32[]{:S(2)}) %collective-permute-start.7) | collective-permute-done | bytes 36896 | tf_op jit(solution)/shard_map/ppermute | solution.py:24
  93.5 4.8 %collective-permute-start.9 = (bf16[3,38,3,128]{3,2,1,0:T(4,128)(2,1)S(1)}, bf16[3,38,3,128]{3,2,1,0:T(4,128)(2,1)S(1)}, u32[]{:S(2)}, u32[]{:S(2)}) collective-permute-start(bf16[3,38,3,128]{3,2,1,0:T(4,128)(2,1)S(1)} %get-tuple-element.32), channel_id=1, source_target_pairs={{1,0},{2,1},{3,2},{4,3},{5,4},{6,5},{7,6},{8,7},{9,8},{10,9},{11,1... | collective-permute-start | bytes 262664 | tf_op jit(solution)/shard_map/ppermute | solution.py:24
  98.4 2.6 %collective-permute-done.8 = bf16[3,38,3,128]{3,2,1,0:T(4,128)(2,1)S(1)} collective-permute-done((bf16[3,38,3,128]{3,2,1,0:T(4,128)(2,1)S(1)}, bf16[3,38,3,128]{3,2,1,0:T(4,128)(2,1)S(1)}, u32[]{:S(2)}, u32[]{:S(2)}) %collective-permute-start.8) | collective-permute-done | bytes 87584 | tf_op jit(solution)/shard_map/ppermute | solution.py:21
  102.1 0.7 fusion.45
  103.4 0.4 fusion.47
  104.1 0.8 fusion.92
  105.9 1.0 maximum_subtract_fusion
  (126 shorter events, 5.9 us)
Async XLA Ops:
  0.6 42.1 %copy-start = (bf16[1,32,128,128]{3,2,1,0:T(8,128)(2,1)S(1)}, bf16[1,32,128,128]{3,2,1,0:T(8,128)(2,1)}, u32[]{:S(2)}) copy-start(bf16[1,32,128,128]{3,2,1,0:T(8,128)(2,1)} %param.9) | copy-start | bytes 3145732
  0.6 10.4 %copy-start.1 = (f32[3,32,16,128]{3,2,1,0:T(8,128)S(1)}, f32[3,32,16,128]{3,2,1,0:T(8,128)}, u32[]{:S(2)}) copy-start(f32[3,32,16,128]{3,2,1,0:T(8,128)} %param.7) | copy-start | bytes 2359300
  2.1 23.1 %collective-permute-start.1 = (f32[4,32,1,128]{3,2,1,0:T(1,128)S(1)}, f32[4,32,1,128]{3,2,1,0:T(1,128)S(1)}, u32[]{:S(2)}, u32[]{:S(2)}) collective-permute-start(f32[4,32,1,128]{3,2,1,0:T(1,128)S(1)} %get-tuple-element.28), channel_id=1, source_target_pairs={{1,0},{2,1},{3,2},{4,3},{5,4},{6,5},{7,6},{8,7},{9,8},{10,9},{11,1... | collective-permute-start | bytes 196616 | tf_op jit(solution)/shard_map/ppermute | solution.py:24
  11.0 14.2 %collective-permute-start = (f32[4,32,1,128]{3,2,1,0:T(1,128)S(1)}, f32[4,32,1,128]{3,2,1,0:T(1,128)}, u32[]{:S(2)}, u32[]{:S(2)}) collective-permute-start(f32[4,32,1,128]{3,2,1,0:T(1,128)S(1)} %get-tuple-element.27), channel_id=1, source_target_pairs={{0,1},{1,2},{2,3},{3,4},{4,5},{5,6},{6,7},{7,8},{8,9},{9,10},{10,1... | collective-permute-start | bytes 196616 | tf_op jit(solution)/shard_map/ppermute | solution.py:21
  12.5 12.9 %collective-permute-start.2 = (f32[4,3,16,128]{3,2,1,0:T(8,128)}, f32[4,3,16,128]{3,2,1,0:T(8,128)}, u32[]{:S(2)}, u32[]{:S(2)}) collective-permute-start(f32[4,3,16,128]{3,2,1,0:T(8,128)} %get-tuple-element.30), channel_id=1, source_target_pairs={{32,0},{64,32},{96,64},{128,96},{160,128},{192,160},{224,192},{0,2... | collective-permute-start | bytes 294920 | tf_op jit(solution)/shard_map/ppermute | solution.py:24
  13.4 12.7 %collective-permute-start.3 = (f32[4,3,16,128]{3,2,1,0:T(8,128)S(1)}, f32[4,3,16,128]{3,2,1,0:T(8,128)}, u32[]{:S(2)}, u32[]{:S(2)}) collective-permute-start(f32[4,3,16,128]{3,2,1,0:T(8,128)S(1)} %get-tuple-element.29), channel_id=1, source_target_pairs={{0,32},{32,64},{64,96},{96,128},{128,160},{160,192},{192,224},{224... | collective-permute-start | bytes 294920 | tf_op jit(solution)/shard_map/ppermute | solution.py:21
  15.6 3.7 %copy-start.24 = (s32[1,32,3]{1,0,2:T(1,128)S(1)}, s32[1,32,3]{1,0,2:T(1,128)}, u32[]{:S(2)}) copy-start(s32[1,32,3]{1,0,2:T(1,128)} %param.13) | copy-start | bytes 1156
  15.6 5.3 %copy-start.27 = (s32[1,32,1]{1,2,0:T(1,128)S(1)}, s32[1,32,1]{1,2,0:T(1,128)}, u32[]{:S(2)}) copy-start(s32[1,32,1]{1,2,0:T(1,128)} %param.11) | copy-start | bytes 388
  15.6 6.1 %copy-start.28 = (s32[1,32]{1,0:T(1,128)S(1)}, s32[1,32]{1,0:T(1,128)}, u32[]{:S(2)}) copy-start(s32[1,32]{1,0:T(1,128)} %param.12) | copy-start | bytes 388
  15.6 6.2 %copy-start.18 = (f32[1,32,3,128]{3,1,2,0:T(8,128)S(1)}, f32[1,32,3,128]{3,1,2,0:T(8,128)}, u32[]{:S(2)}) copy-start(f32[1,32,3,128]{3,1,2,0:T(8,128)} %param.10) | copy-start | bytes 147460
  17.1 10.5 %copy-start.2 = (f32[32,16,128]{2,1,0:T(8,128)S(1)}, f32[32,16,128]{2,1,0:T(8,128)}, u32[]{:S(2)}) copy-start(f32[32,16,128]{2,1,0:T(8,128)} %param.8) | copy-start | bytes 786436
  26.1 0.8 copy-start.15
  26.9 0.6 copy-start.16
  35.1 1.4 %copy-start.4 = (f32[3,32,16,1]{3,2,1,0:T(8,128)S(1)}, f32[3,32,16,1]{3,2,1,0:T(8,128)}, u32[]{:S(2)}) copy-start(f32[3,32,16,1]{3,2,1,0:T(8,128)} %get-tuple-element.38) | copy-start | bytes 18436
  35.1 1.4 %copy-start.5 = (f32[1,32,16,128]{3,2,1,0:T(8,128)S(1)}, f32[1,32,16,128]{3,2,1,0:T(8,128)}, u32[]{:S(2)}) copy-start(f32[1,32,16,128]{3,2,1,0:T(8,128)} %get-tuple-element.60) | copy-start | bytes 786436
  35.1 1.5 %copy-start.6 = (f32[1,32,16,128]{3,2,1,0:T(8,128)S(1)}, f32[1,32,16,128]{3,2,1,0:T(8,128)}, u32[]{:S(2)}) copy-start(f32[1,32,16,128]{3,2,1,0:T(8,128)} %get-tuple-element.61) | copy-start | bytes 786436
  36.6 3.3 %copy-start.23 = (s32[512]{0:T(512)S(1)}, s32[512]{0:T(512)}, u32[]{:S(2)}) copy-start(s32[512]{0:T(512)} %add.318) | copy-start | bytes 6148
  39.8 1.4 %copy-start.7 = (pred[512,128]{0,1:T(8,128)(4,1)S(1)}, pred[512,128]{0,1:T(8,128)(4,1)}, u32[]{:S(2)}) copy-start(pred[512,128]{0,1:T(8,128)(4,1)} %get-tuple-element.91) | copy-start | bytes 196612
  39.8 1.4 %copy-start.8 = (pred[512,128]{0,1:T(8,128)(4,1)S(1)}, pred[512,128]{0,1:T(8,128)(4,1)}, u32[]{:S(2)}) copy-start(pred[512,128]{0,1:T(8,128)(4,1)} %get-tuple-element.92) | copy-start | bytes 196612
  39.8 1.5 %copy-start.9 = (pred[512,128]{0,1:T(8,128)(4,1)S(1)}, pred[512,128]{0,1:T(8,128)(4,1)}, u32[]{:S(2)}) copy-start(pred[512,128]{0,1:T(8,128)(4,1)} %get-tuple-element.85) | copy-start | bytes 196612
  39.8 1.5 %copy-start.10 = (pred[512,128]{0,1:T(8,128)(4,1)S(1)}, pred[512,128]{0,1:T(8,128)(4,1)}, u32[]{:S(2)}) copy-start(pred[512,128]{0,1:T(8,128)(4,1)} %get-tuple-element.86) | copy-start | bytes 196612
  39.8 1.5 %copy-start.11 = (pred[512,128]{0,1:T(8,128)(4,1)S(1)}, pred[512,128]{0,1:T(8,128)(4,1)}, u32[]{:S(2)}) copy-start(pred[512,128]{0,1:T(8,128)(4,1)} %get-tuple-element.87) | copy-start | bytes 196612
  39.8 1.5 %copy-start.12 = (pred[512,128]{0,1:T(8,128)(4,1)S(1)}, pred[512,128]{0,1:T(8,128)(4,1)}, u32[]{:S(2)}) copy-start(pred[512,128]{0,1:T(8,128)(4,1)} %get-tuple-element.88) | copy-start | bytes 196612
  39.8 1.5 %copy-start.13 = (pred[512,128]{0,1:T(8,128)(4,1)S(1)}, pred[512,128]{0,1:T(8,128)(4,1)}, u32[]{:S(2)}) copy-start(pred[512,128]{0,1:T(8,128)(4,1)} %get-tuple-element.89) | copy-start | bytes 196612
  39.9 1.5 %copy-start.14 = (pred[512,128]{0,1:T(8,128)(4,1)S(1)}, pred[512,128]{0,1:T(8,128)(4,1)}, u32[]{:S(2)}) copy-start(pred[512,128]{0,1:T(8,128)(4,1)} %get-tuple-element.90) | copy-start | bytes 196612
  42.0 1.4 %copy-start.22 = (s32[32]{0:T(128)S(1)}, s32[32]{0:T(128)}, u32[]{:S(2)}) copy-start(s32[32]{0:T(128)} %multiply_add_fusion.1) | copy-start | bytes 388
  43.4 20.5 %copy-start.17 = (f32[1,32,3,128]{3,2,1,0:T(4,128)S(1)}, f32[1,32,3,128]{3,2,1,0:T(4,128)}, u32[]{:S(2)}) copy-start(f32[1,32,3,128]{3,2,1,0:T(4,128)} %copy.58) | copy-start | bytes 147460
  43.4 20.5 %copy-start.21 = (f32[32]{0:T(128)S(1)}, f32[32]{0:T(128)}, u32[]{:S(2)}) copy-start(f32[32]{0:T(128)} %iota_add_fusion) | copy-start | bytes 388
  43.7 26.1 %copy-start.20 = (pred[22]{0:T(512)(128)(4,1)S(1)}, pred[22]{0:T(512)(128)(4,1)}, u32[]{:S(2)}) copy-start(pred[22]{0:T(512)(128)(4,1)} %compare_and_fusion) | copy-start | bytes 70
  44.5 19.1 %all-to-all-start = ((f32[32,4,385]{2,1,0:T(4,128)}), f32[32,4,385]{2,1,0:T(4,128)S(1)}, u32[]{:S(2)}, u32[]{:S(2)}) async-start(f32[32,4,385]{2,1,0:T(4,128)} %all_to_all.16), calls=%async_computation | async-start | bytes 524288 | tf_op jit(solution)/shard_map/all_to_all | solution.py:158
  53.7 16.1 %collective-permute-start.4 = (f32[38,3,128]{2,1,0:T(4,128)S(1)}, f32[38,3,128]{2,1,0:T(4,128)S(1)}, u32[]{:S(2)}, u32[]{:S(2)}) collective-permute-start(f32[38,3,128]{2,1,0:T(4,128)S(1)} %get-tuple-element.71), channel_id=1, source_target_pairs={{0,1},{1,2},{2,3},{3,4},{4,5},{5,6},{6,7},{7,8},{8,9},{9,10},{10,1... | collective-permute-start | bytes 175112 | tf_op jit(solution)/shard_map/ppermute | solution.py:21
  55.0 14.8 %collective-permute-start.5 = (f32[38,3,128]{2,1,0:T(4,128)S(1)}, f32[38,3,128]{2,1,0:T(4,128)S(1)}, u32[]{:S(2)}, u32[]{:S(2)}) collective-permute-start(f32[38,3,128]{2,1,0:T(4,128)S(1)} %get-tuple-element.72), channel_id=1, source_target_pairs={{1,0},{2,1},{3,2},{4,3},{5,4},{6,5},{7,6},{8,7},{9,8},{10,9},{11,1... | collective-permute-start | bytes 175112 | tf_op jit(solution)/shard_map/ppermute | solution.py:24
  65.0 13.7 %all-to-all-start.1 = ((bf16[32,4,384]{2,1,0:T(4,128)(2,1)}), bf16[32,4,384]{2,1,0:T(4,128)(2,1)S(1)}, u32[]{:S(2)}, u32[]{:S(2)}) async-start(bf16[32,4,384]{2,1,0:T(4,128)(2,1)} %all_to_all.19), calls=%async_computation.1 | async-start | bytes 196608 | tf_op jit(solution)/shard_map/all_to_all | solution.py:171
  79.8 3.7 %copy-start.19 = (s32[32,16]{1,0:T(8,128)S(1)}, s32[32,16]{1,0:T(8,128)}, u32[]{:S(2)}) copy-start(s32[32,16]{1,0:T(8,128)} %multiply_add_fusion) | copy-start | bytes 6148
  83.0 2.4 %copy-start.3 = (f32[3,32,16,128]{3,2,1,0:T(8,128)S(1)}, f32[3,32,16,128]{3,2,1,0:T(8,128)}, u32[]{:S(2)}) copy-start(f32[3,32,16,128]{3,2,1,0:T(8,128)} %get-tuple-element.23) | copy-start | bytes 2359300
  85.6 5.1 %collective-permute-start.6 = (bf16[3,3,16,128]{3,2,1,0:T(8,128)(2,1)S(1)}, bf16[3,3,16,128]{3,2,1,0:T(8,128)(2,1)S(1)}, u32[]{:S(2)}, u32[]{:S(2)}) collective-permute-start(bf16[3,3,16,128]{3,2,1,0:T(8,128)(2,1)S(1)} %get-tuple-element.66), channel_id=1, source_target_pairs={{0,32},{32,64},{64,96},{96,128},{128,160},{160,192},{192,224},{224... | collective-permute-start | bytes 110600 | tf_op jit(solution)/shard_map/ppermute | solution.py:21
  89.6 3.7 %collective-permute-start.7 = (bf16[3,3,16,128]{3,2,1,0:T(8,128)(2,1)S(1)}, bf16[3,3,16,128]{3,2,1,0:T(8,128)(2,1)S(1)}, u32[]{:S(2)}, u32[]{:S(2)}) collective-permute-start(bf16[3,3,16,128]{3,2,1,0:T(8,128)(2,1)S(1)} %get-tuple-element.67), channel_id=1, source_target_pairs={{32,0},{64,32},{96,64},{128,96},{160,128},{192,160},{224,192},{0,2... | collective-permute-start | bytes 110600 | tf_op jit(solution)/shard_map/ppermute | solution.py:24
  93.4 7.7 %collective-permute-start.8 = (bf16[3,38,3,128]{3,2,1,0:T(4,128)(2,1)S(1)}, bf16[3,38,3,128]{3,2,1,0:T(4,128)(2,1)S(1)}, u32[]{:S(2)}, u32[]{:S(2)}) collective-permute-start(bf16[3,38,3,128]{3,2,1,0:T(4,128)(2,1)S(1)} %get-tuple-element.31), channel_id=1, source_target_pairs={{0,1},{1,2},{2,3},{3,4},{4,5},{5,6},{6,7},{7,8},{8,9},{9,10},{10,1... | collective-permute-start | bytes 262664 | tf_op jit(solution)/shard_map/ppermute | solution.py:21
  93.5 7.6 %collective-permute-start.9 = (bf16[3,38,3,128]{3,2,1,0:T(4,128)(2,1)S(1)}, bf16[3,38,3,128]{3,2,1,0:T(4,128)(2,1)S(1)}, u32[]{:S(2)}, u32[]{:S(2)}) collective-permute-start(bf16[3,38,3,128]{3,2,1,0:T(4,128)(2,1)S(1)} %get-tuple-element.32), channel_id=1, source_target_pairs={{1,0},{2,1},{3,2},{4,3},{5,4},{6,5},{7,6},{8,7},{9,8},{10,9},{11,1... | collective-permute-start | bytes 262664 | tf_op jit(solution)/shard_map/ppermute | solution.py:24
  101.5 0.6 copy-start.25
  102.8 0.6 copy-start.26

commit v8 on v7

--- a/solution.py
+++ b/solution.py
@@ -71,15 +71,27 @@
     return 0.5 * (padded[..., 1:-1, 2:, :] - padded[..., 1:-1, :-2, :])
 
 
+def across_y(field, weights):
+    size = field.shape[-1]
+    source = lax.broadcasted_iota(jnp.int32, (size, size), 0)
+    target = lax.broadcasted_iota(jnp.int32, (size, size), 1)
+    above = (source == (target + 1) % size).astype(jnp.float32)
+    below = (source == (target + size - 1) % size).astype(jnp.float32)
+    matrix = weights[0] * above + weights[1] * below
+    return jnp.einsum(
+        "...i,ij->...j", field, matrix, precision=lax.Precision.HIGHEST, preferred_element_type=jnp.float32
+    )
+
+
 def along_y(field):
-    return 0.5 * (jnp.roll(field, -1, -1) - jnp.roll(field, 1, -1))
+    return across_y(field, (0.5, -0.5))
 
 
 def neighbours(padded):
     middle = inner(padded)
     total = padded[..., 2:, 1:-1, :] + padded[..., :-2, 1:-1, :]
     total = total + padded[..., 1:-1, 2:, :] + padded[..., 1:-1, :-2, :]
-    return total + jnp.roll(middle, 1, -1) + jnp.roll(middle, -1, -1)
+    return total + across_y(middle, (1.0, 1.0))
 
 
 def gradient_of(padded):

time: 108 us -> 89.9 us (0.83)
  other arithmetic: 19.9 us -> 5.33 us
  local copies, waits for them, and re-layouts: 23.4 us -> 16.7 us
  matrix products: 5.14 us -> 8.85 us
    slice x14 -> x0, local copies, waits for them, and re-layouts: 7.44 us -> none  [the longest x8 4.2 us: along_y(): return 0.5 * (jnp.roll(field, -1, -1) - jnp.roll(field, 1, -1))]
    all_to_all x1, waiting for transfers between devices: 5.07 us -> 9 us  [body(): received = lax.all_to_all(send, 'yz', 0, 0, tiled=True)]
    concatenate x6 -> x0, local copies, waits for them, and re-layouts: 3.88 us -> none  [along_y(): return 0.5 * (jnp.roll(field, -1, -1) - jnp.roll(field, 1, -1))]
    unnamed x68 -> x30, local copies, waits for them, and re-layouts: 2.02 us -> 5.89 us
    dot_general x0 -> x6, matrix products: none -> 3.5 us  [across_y(): jnp.einsum('...i,ij->...j', field, matrix, precision=lax.Precision.HIGHES...]
    convert_element_type x1 -> x0, other arithmetic: 3.17 us -> none  [body(): predicted.astype(jnp.bfloat16).reshape(fields, row_total, ny)]
    ppermute x5, waiting for transfers between devices: 2.62 us -> 0.01 us  [faces(): lax.ppermute(lax.slice_in_dim(block, 0, width, axis=dim).astype(kind), ax...]
    eq x4, other arithmetic: 2.9 us -> 0.3 us  [body(): lanes[None, None, :] == line_offset + j]
  transfers between devices with their start and end apart: 12 -> 12, of which waited for: 5 -> 4; matrix products, arithmetic and copies ran while one was open for 15% -> 8% of each run, Pallas kernels for 0% -> 0%
where the time goes in v8:
time: 89.9 us; the launch traced here: 88.5 us
  starting transfers between devices  36.8 us (41%)
  waiting for transfers between devices  19.5 us (22%)
  local copies, waits for them, and re-layouts  16.7 us (19%)
  matrix products  8.85 us (10%)
  other arithmetic  5.33 us (6%)
  between operations  1.24 us (1%)
    ppermute x5, starting transfers between devices, faces(): lax.ppermute(lax.slice_in_dim(block, 0, width, axis=dim).astype(kind), ax...  19.4 us
    all_to_all x1, waiting for transfers between devices, body(): received = lax.all_to_all(send, 'yz', 0, 0, tiled=True)  9 us
    all_to_all x1, waiting for transfers between devices, body(): back = lax.all_to_all(returned, 'yz', 0, 0, tiled=True)  8.14 us
    all_to_all x1, starting transfers between devices, body(): received = lax.all_to_all(send, 'yz', 0, 0, tiled=True)  6.33 us
    ppermute x5, starting transfers between devices, faces(): lax.ppermute(lax.slice_in_dim(block, block.shape[dim] - width, None, axis...  6.02 us
    unnamed x30, local copies, waits for them, and re-layouts  5.89 us
    all_to_all x1, starting transfers between devices, body(): back = lax.all_to_all(returned, 'yz', 0, 0, tiled=True)  5.08 us
    dot_general x6, matrix products, across_y(): jnp.einsum('...i,ij->...j', field, matrix, precision=lax.Precision.HIGHES...  3.5 us
  transfers between devices with their start and end apart: 12, of which 4 were waited for; matrix products, arithmetic and copies ran while one was open for 8% of the time, Pallas kernels for 0%

profile of v8, /device:TPU:1, one launch (start us, length us, event | category | flops | bytes accessed | tf_op | source)
XLA Modules:
  0.0 88.5 jit_solution(2951864531120279622)
XLA Ops:
  0.6 1.1 %copy.148 = f32[32,16,128]{2,0,1:T(8,128)S(1)} copy(f32[32,16,128]{2,1,0:T(8,128)} %param.8) | data formatting | bytes 524288 | tf_op args[1]
  1.8 1.4 %copy.89 = f32[3,32,16,128]{3,1,2,0:T(8,128)S(1)} copy(f32[3,32,16,128]{3,2,1,0:T(8,128)} %param.7) | data formatting | bytes 1572864 | tf_op args[0]
  3.2 8.9 %collective-permute-start.1 = (f32[4,32,1,128]{3,1,2,0:T(8,128)S(1)}, f32[4,32,1,128]{3,1,2,0:T(8,128)S(1)}, u32[]{:S(2)}, u32[]{:S(2)}) collective-permute-start(f32[4,32,1,128]{3,1,2,0:T(8,128)S(1)} %get-tuple-element.33), channel_id=1, source_target_pairs={{1,0},{2,1},{3,2},{4,3},{5,4},{6,5},{7,6},{8,7},{9,8},{10,9},{11,1... | collective-permute-start | bytes 196616 | tf_op jit(solution)/shard_map/ppermute | solution.py:24
  12.2 1.0 %collective-permute-start.2 = (f32[4,3,16,128]{3,1,2,0:T(4,128)S(1)}, f32[4,3,16,128]{3,1,2,0:T(4,128)}, u32[]{:S(2)}, u32[]{:S(2)}) collective-permute-start(f32[4,3,16,128]{3,1,2,0:T(4,128)S(1)} %get-tuple-element.32), channel_id=1, source_target_pairs={{32,0},{64,32},{96,64},{128,96},{160,128},{192,160},{224,192},{0,2... | collective-permute-start | bytes 294920 | tf_op jit(solution)/shard_map/ppermute | solution.py:24
  13.2 1.1 %collective-permute-start.3 = (f32[4,3,16,128]{3,1,2,0:T(4,128)S(1)}, f32[4,3,16,128]{3,1,2,0:T(4,128)}, u32[]{:S(2)}, u32[]{:S(2)}) collective-permute-start(f32[4,3,16,128]{3,1,2,0:T(4,128)S(1)} %get-tuple-element.31), channel_id=1, source_target_pairs={{0,32},{32,64},{64,96},{96,128},{128,160},{160,192},{192,224},{224... | collective-permute-start | bytes 294920 | tf_op jit(solution)/shard_map/ppermute | solution.py:21
  14.3 1.0 %multiply_bitcast_fusion = f32[32,16,128]{2,1,0:T(8,128)S(1)} fusion(f32[3,32,16,128]{3,2,1,0:T(8,128)} %param.7), kind=kLoop, calls=%fused_computation.125 | loop fusion | flops 65536 | bytes 524288 | tf_op jit(solution)/shard_map/mul | solution.py:107
  15.3 0.8 copy.88
  16.5 0.2 convert_reduce_fusion
  16.8 0.1 copy.97
  17.1 0.9 %broadcast_compare_fusion = pred[32,16,512]{2,1,0:T(8,128)(4,1)} fusion(s32[512]{0:T(512)S(1)} %add.411, s32[32,16]{1,0:T(8,128)S(1)} %multiply_add_fusion), kind=kLoop, calls=%fused_computation.72 | loop fusion | flops 262144 | bytes 266240 | tf_op jit(solution)/shard_map/eq | solution.py:200
  18.0 0.5 collective-permute-done
  18.6 0.9 %slice.298 = f32[4,1,16,128]{3,1,2,0:T(1,128)S(1)} slice(f32[4,3,16,128]{3,1,2,0:T(4,128)} %collective-permute-done.2), slice={[0:4], [0:1], [0:16], [0:128]} | slice | bytes 65536 | tf_op jit(solution)/shard_map/slice | solution.py:116
  19.6 0.9 %slice.299 = f32[4,1,16,128]{3,1,2,0:T(1,128)S(1)} slice(f32[4,3,16,128]{3,1,2,0:T(4,128)} %collective-permute-done.3), slice={[0:4], [2:3], [0:16], [0:128]} | slice | bytes 65536 | tf_op jit(solution)/shard_map/slice | solution.py:116
  20.7 0.4 convolution_bitcast_fusion.8
  21.1 0.5 copy-done.2
  21.6 1.2 %fusion.136 = (bf16[3,32,16,128]{3,1,2,0:T(8,128)(2,1)S(1)}, f32[3,32,16,128]{3,1,2,0:T(8,128)S(1)}) fusion(f32[1,32,16,128]{3,1,2,0:T(8,128)S(1)} %get-tuple-element.50, f32[1,32,16,128]{3,1,2,0:T(8,128)S(1)} %convolution_bitcast_fusion.8, f32[1,32,16,128]{3,1,2,0:T(8,128)S(1)} %get-tuple-element.49, f32[3,32,16,128]{3,1,2,0:T(8,128)S(1)} %copy.89, ...), kind=kOutput, calls=%fused_computation.280 | convolution fusion | flops 307609600 | bytes 3483904 | tf_op jit(solution)/shard_map/...i,ij->...j/dot_general | solution.py:81
  22.9 0.4 convolution_bitcast_fusion.4
  23.4 0.4 convolution_bitcast_fusion.5
  23.9 0.4 convolution_bitcast_fusion.6
  24.3 0.6 select_reduce_fusion
  25.1 0.2 copy.95
  25.3 0.4 convert_element_type.98
  25.7 0.6 fusion.6
  26.3 0.3 fusion.45
  26.6 0.8 all_to_all.16
  27.4 6.3 %all-to-all-start = ((f32[32,4,385]{2,1,0:T(4,128)}), f32[32,4,385]{2,1,0:T(4,128)S(1)}, u32[]{:S(2)}, u32[]{:S(2)}) async-start(f32[32,4,385]{2,1,0:T(4,128)} %all_to_all.16), calls=%async_computation | async-start | bytes 524288 | tf_op jit(solution)/shard_map/all_to_all | solution.py:170
  33.7 0.6 compare_and_fusion.1
  34.4 0.8 slice_bitcast_fusion.10
  35.1 9.0 %all-to-all-done = f32[32,4,385]{2,1,0:T(4,128)S(1)} async-done(((f32[32,4,385]{2,1,0:T(4,128)}), f32[32,4,385]{2,1,0:T(4,128)S(1)}, u32[]{:S(2)}, u32[]{:S(2)}) %all-to-all-start) | async-done | bytes 197152 | tf_op jit(solution)/shard_map/all_to_all | solution.py:170
  44.1 0.1 all_to_all.18
  44.2 0.1 slice_reduce_fusion.8
  44.3 0.2 fusion.4
  44.6 0.3 convolution_convert_fusion
  44.9 0.7 all_to_all.19
  45.5 5.1 %all-to-all-start.1 = ((bf16[32,4,384]{2,1,0:T(4,128)(2,1)}), bf16[32,4,384]{2,1,0:T(4,128)(2,1)S(1)}, u32[]{:S(2)}, u32[]{:S(2)}) async-start(bf16[32,4,384]{2,1,0:T(4,128)(2,1)} %all_to_all.19), calls=%async_computation.1 | async-start | bytes 196608 | tf_op jit(solution)/shard_map/all_to_all | solution.py:183
  50.6 0.8 slice_bitcast_fusion.9
  51.4 8.1 %all-to-all-done.1 = bf16[32,4,384]{2,1,0:T(4,128)(2,1)S(1)} async-done(((bf16[32,4,384]{2,1,0:T(4,128)(2,1)}), bf16[32,4,384]{2,1,0:T(4,128)(2,1)S(1)}, u32[]{:S(2)}, u32[]{:S(2)}) %all-to-all-start.1) | async-done | bytes 98336 | tf_op jit(solution)/shard_map/all_to_all | solution.py:183
  59.6 0.2 convolution_convert_fusion.1
  59.8 0.4 convolution_bitcast_fusion.9
  60.2 0.4 reshape.463
  60.6 3.2 %slice_reduce_fusion.7 = (f32[3,512]{1,0:T(4,128)S(1)}, f32[3,512]{1,0:T(4,128)S(1)}, f32[3,512]{1,0:T(4,128)S(1)}, f32[3,512]{1,0:T(4,128)S(1)}, f32[3,512]{1,0...) fusion(f32[3,512,8]{2,1,0:T(8,128)S(1)} %reshape.463), kind=kLoop, calls=%fused_computation.32 | loop fusion | bytes 98304 | tf_op jit(solution)/shard_map/slice | solution.py:196
  63.8 0.5 select_add_fusion
  64.3 0.4 copy-done.1
  64.7 0.7 convolution_bitcast_fusion.3
  65.4 0.7 convolution_bitcast_fusion.2
  66.1 0.7 convolution_bitcast_fusion.1
  66.8 0.2 fusion.131
  67.0 4.7 %collective-permute-start.6 = (bf16[3,3,16,128]{3,1,2,0:T(4,128)(2,1)S(1)}, bf16[3,3,16,128]{3,1,2,0:T(4,128)(2,1)S(1)}, u32[]{:S(2)}, u32[]{:S(2)}) collective-permute-start(bf16[3,3,16,128]{3,1,2,0:T(4,128)(2,1)S(1)} %get-tuple-element.41), channel_id=1, source_target_pairs={{0,32},{32,64},{64,96},{96,128},{128,160},{160,192},{192,224},{224... | collective-permute-start | bytes 110600 | tf_op jit(solution)/shard_map/ppermute | solution.py:21
  71.8 0.1 collective-permute-start.4
  71.9 4.7 %collective-permute-start.5 = (f32[38,3,128]{2,0,1:T(8,128)S(1)}, f32[38,3,128]{2,0,1:T(8,128)S(1)}, u32[]{:S(2)}, u32[]{:S(2)}) collective-permute-start(f32[38,3,128]{2,0,1:T(8,128)S(1)} %get-tuple-element.52), channel_id=1, source_target_pairs={{1,0},{2,1},{3,2},{4,3},{5,4},{6,5},{7,6},{8,7},{9,8},{10,9},{11,1... | collective-permute-start | bytes 175112 | tf_op jit(solution)/shard_map/ppermute | solution.py:24
  76.8 4.8 %collective-permute-start.9 = (bf16[3,38,3,128]{3,1,2,0:T(8,128)(2,1)S(1)}, bf16[3,38,3,128]{3,1,2,0:T(8,128)(2,1)S(1)}, u32[]{:S(2)}, u32[]{:S(2)}) collective-permute-start(bf16[3,38,3,128]{3,1,2,0:T(8,128)(2,1)S(1)} %get-tuple-element.36), channel_id=1, source_target_pairs={{1,0},{2,1},{3,2},{4,3},{5,4},{6,5},{7,6},{8,7},{9,8},{10,9},{11,1... | collective-permute-start | bytes 262664 | tf_op jit(solution)/shard_map/ppermute | solution.py:24
  81.6 0.1 maximum_select_fusion.1
  81.7 1.8 %collective-permute-done.8 = bf16[3,38,3,128]{3,1,2,0:T(8,128)(2,1)S(1)} collective-permute-done((bf16[3,38,3,128]{3,1,2,0:T(8,128)(2,1)S(1)}, bf16[3,38,3,128]{3,1,2,0:T(8,128)(2,1)S(1)}, u32[]{:S(2)}, u32[]{:S(2)}) %collective-permute-start.8) | collective-permute-done | bytes 87584 | tf_op jit(solution)/shard_map/ppermute | solution.py:21
  83.6 0.2 maximum_select_fusion
  83.8 0.1 slice_bitcast_fusion.2
  83.9 0.5 fusion
  84.4 0.1 copy-done.7
  84.5 0.5 fusion.31
  85.1 0.5 fusion.3
  85.6 0.1 fusion.134
  85.7 0.4 convolution_bitcast_fusion.7
  86.1 0.2 maximum_subtract_fusion
  86.3 1.3 %copy.110 = f32[3,32,16,128]{3,2,1,0:T(8,128)} copy(f32[3,32,16,128]{3,1,2,0:T(8,128)S(1)} %maximum_subtract_fusion) | data formatting | bytes 1572864
  87.6 0.9 copy.111
  (78 shorter events, 1.6 us)
Async XLA Ops:
  0.6 25.0 %copy-start = (bf16[1,32,128,128]{3,2,1,0:T(8,128)(2,1)S(1)}, bf16[1,32,128,128]{3,2,1,0:T(8,128)(2,1)}, u32[]{:S(2)}) copy-start(bf16[1,32,128,128]{3,2,1,0:T(8,128)(2,1)} %param.9) | copy-start | bytes 3145732
  3.2 12.9 %copy-start.4 = (s32[1,32,3]{1,0,2:T(1,128)S(1)}, s32[1,32,3]{1,0,2:T(1,128)}, u32[]{:S(2)}) copy-start(s32[1,32,3]{1,0,2:T(1,128)} %param.13) | copy-start | bytes 1156
  3.2 13.3 %copy-start.5 = (s32[1,32,1]{1,2,0:T(1,128)S(1)}, s32[1,32,1]{1,2,0:T(1,128)}, u32[]{:S(2)}) copy-start(s32[1,32,1]{1,2,0:T(1,128)} %param.11) | copy-start | bytes 388
  3.2 13.5 %copy-start.6 = (s32[1,32]{1,0:T(1,128)S(1)}, s32[1,32]{1,0:T(1,128)}, u32[]{:S(2)}) copy-start(s32[1,32]{1,0:T(1,128)} %param.12) | copy-start | bytes 388
  3.2 14.8 %collective-permute-start.1 = (f32[4,32,1,128]{3,1,2,0:T(8,128)S(1)}, f32[4,32,1,128]{3,1,2,0:T(8,128)S(1)}, u32[]{:S(2)}, u32[]{:S(2)}) collective-permute-start(f32[4,32,1,128]{3,1,2,0:T(8,128)S(1)} %get-tuple-element.33), channel_id=1, source_target_pairs={{1,0},{2,1},{3,2},{4,3},{5,4},{6,5},{7,6},{8,7},{9,8},{10,9},{11,1... | collective-permute-start | bytes 196616 | tf_op jit(solution)/shard_map/ppermute | solution.py:24
  12.1 6.4 %collective-permute-start = (f32[4,32,1,128]{3,1,2,0:T(8,128)S(1)}, f32[4,32,1,128]{3,1,2,0:T(8,128)S(1)}, u32[]{:S(2)}, u32[]{:S(2)}) collective-permute-start(f32[4,32,1,128]{3,1,2,0:T(8,128)S(1)} %get-tuple-element.34), channel_id=1, source_target_pairs={{0,1},{1,2},{2,3},{3,4},{4,5},{5,6},{6,7},{7,8},{8,9},{9,10},{10,1... | collective-permute-start | bytes 196616 | tf_op jit(solution)/shard_map/ppermute | solution.py:21
  12.2 6.4 %collective-permute-start.2 = (f32[4,3,16,128]{3,1,2,0:T(4,128)S(1)}, f32[4,3,16,128]{3,1,2,0:T(4,128)}, u32[]{:S(2)}, u32[]{:S(2)}) collective-permute-start(f32[4,3,16,128]{3,1,2,0:T(4,128)S(1)} %get-tuple-element.32), channel_id=1, source_target_pairs={{32,0},{64,32},{96,64},{128,96},{160,128},{192,160},{224,192},{0,2... | collective-permute-start | bytes 294920 | tf_op jit(solution)/shard_map/ppermute | solution.py:24
  13.2 6.4 %collective-permute-start.3 = (f32[4,3,16,128]{3,1,2,0:T(4,128)S(1)}, f32[4,3,16,128]{3,1,2,0:T(4,128)}, u32[]{:S(2)}, u32[]{:S(2)}) collective-permute-start(f32[4,3,16,128]{3,1,2,0:T(4,128)S(1)} %get-tuple-element.31), channel_id=1, source_target_pairs={{0,32},{32,64},{64,96},{96,128},{128,160},{160,192},{192,224},{224... | collective-permute-start | bytes 294920 | tf_op jit(solution)/shard_map/ppermute | solution.py:21
  20.6 1.0 %copy-start.2 = (f32[32,16,128]{2,0,1:T(8,128)S(1)}, f32[32,16,128]{2,0,1:T(8,128)}, u32[]{:S(2)}) copy-start(f32[32,16,128]{2,0,1:T(8,128)} %copy.88) | copy-start | bytes 786436
  25.7 8.6 %copy-start.3 = (f32[1,32,3,128]{3,1,2,0:T(8,128)S(1)}, f32[1,32,3,128]{3,1,2,0:T(8,128)}, u32[]{:S(2)}) copy-start(f32[1,32,3,128]{3,1,2,0:T(8,128)} %param.10) | copy-start | bytes 147460
  27.4 16.7 %all-to-all-start = ((f32[32,4,385]{2,1,0:T(4,128)}), f32[32,4,385]{2,1,0:T(4,128)S(1)}, u32[]{:S(2)}, u32[]{:S(2)}) async-start(f32[32,4,385]{2,1,0:T(4,128)} %all_to_all.16), calls=%async_computation | async-start | bytes 524288 | tf_op jit(solution)/shard_map/all_to_all | solution.py:170
  45.5 14.0 %all-to-all-start.1 = ((bf16[32,4,384]{2,1,0:T(4,128)(2,1)}), bf16[32,4,384]{2,1,0:T(4,128)(2,1)S(1)}, u32[]{:S(2)}, u32[]{:S(2)}) async-start(bf16[32,4,384]{2,1,0:T(4,128)(2,1)} %all_to_all.19), calls=%async_computation.1 | async-start | bytes 196608 | tf_op jit(solution)/shard_map/all_to_all | solution.py:183
  63.8 1.0 %copy-start.1 = (pred[32,16,512]{2,1,0:T(8,128)(4,1)S(1)}, pred[32,16,512]{2,1,0:T(8,128)(4,1)}, u32[]{:S(2)}) copy-start(pred[32,16,512]{2,1,0:T(8,128)(4,1)} %broadcast_compare_fusion) | copy-start | bytes 786436
  67.0 9.6 %collective-permute-start.6 = (bf16[3,3,16,128]{3,1,2,0:T(4,128)(2,1)S(1)}, bf16[3,3,16,128]{3,1,2,0:T(4,128)(2,1)S(1)}, u32[]{:S(2)}, u32[]{:S(2)}) collective-permute-start(bf16[3,3,16,128]{3,1,2,0:T(4,128)(2,1)S(1)} %get-tuple-element.41), channel_id=1, source_target_pairs={{0,32},{32,64},{64,96},{96,128},{128,160},{160,192},{192,224},{224... | collective-permute-start | bytes 110600 | tf_op jit(solution)/shard_map/ppermute | solution.py:21
  71.7 4.9 %collective-permute-start.7 = (bf16[3,3,16,128]{3,1,2,0:T(4,128)(2,1)S(1)}, bf16[3,3,16,128]{3,1,2,0:T(4,128)(2,1)S(1)}, u32[]{:S(2)}, u32[]{:S(2)}) collective-permute-start(bf16[3,3,16,128]{3,1,2,0:T(4,128)(2,1)S(1)} %get-tuple-element.42), channel_id=1, source_target_pairs={{32,0},{64,32},{96,64},{128,96},{160,128},{192,160},{224,192},{0,2... | collective-permute-start | bytes 110600 | tf_op jit(solution)/shard_map/ppermute | solution.py:24
  71.8 9.8 %collective-permute-start.4 = (f32[38,3,128]{2,0,1:T(8,128)S(1)}, f32[38,3,128]{2,0,1:T(8,128)S(1)}, u32[]{:S(2)}, u32[]{:S(2)}) collective-permute-start(f32[38,3,128]{2,0,1:T(8,128)S(1)} %get-tuple-element.51), channel_id=1, source_target_pairs={{0,1},{1,2},{2,3},{3,4},{4,5},{5,6},{6,7},{7,8},{8,9},{9,10},{10,1... | collective-permute-start | bytes 175112 | tf_op jit(solution)/shard_map/ppermute | solution.py:21
  71.9 9.7 %collective-permute-start.5 = (f32[38,3,128]{2,0,1:T(8,128)S(1)}, f32[38,3,128]{2,0,1:T(8,128)S(1)}, u32[]{:S(2)}, u32[]{:S(2)}) collective-permute-start(f32[38,3,128]{2,0,1:T(8,128)S(1)} %get-tuple-element.52), channel_id=1, source_target_pairs={{1,0},{2,1},{3,2},{4,3},{5,4},{6,5},{7,6},{8,7},{9,8},{10,9},{11,1... | collective-permute-start | bytes 175112 | tf_op jit(solution)/shard_map/ppermute | solution.py:24
  76.7 6.8 %collective-permute-start.8 = (bf16[3,38,3,128]{3,1,2,0:T(8,128)(2,1)S(1)}, bf16[3,38,3,128]{3,1,2,0:T(8,128)(2,1)S(1)}, u32[]{:S(2)}, u32[]{:S(2)}) collective-permute-start(bf16[3,38,3,128]{3,1,2,0:T(8,128)(2,1)S(1)} %get-tuple-element.35), channel_id=1, source_target_pairs={{0,1},{1,2},{2,3},{3,4},{4,5},{5,6},{6,7},{7,8},{8,9},{9,10},{10,1... | collective-permute-start | bytes 262664 | tf_op jit(solution)/shard_map/ppermute | solution.py:21
  76.8 6.7 %collective-permute-start.9 = (bf16[3,38,3,128]{3,1,2,0:T(8,128)(2,1)S(1)}, bf16[3,38,3,128]{3,1,2,0:T(8,128)(2,1)S(1)}, u32[]{:S(2)}, u32[]{:S(2)}) collective-permute-start(bf16[3,38,3,128]{3,1,2,0:T(8,128)(2,1)S(1)} %get-tuple-element.36), channel_id=1, source_target_pairs={{1,0},{2,1},{3,2},{4,3},{5,4},{6,5},{7,6},{8,7},{9,8},{10,9},{11,1... | collective-permute-start | bytes 262664 | tf_op jit(solution)/shard_map/ppermute | solution.py:24
  83.9 0.7 copy-start.7

commit v9 on v8

--- a/solution.py
+++ b/solution.py
@@ -180,6 +180,7 @@
     returned = jnp.einsum(
         "gq,gw->qw", select.astype(jnp.bfloat16), grain_force, preferred_element_type=jnp.float32
     ).astype(jnp.bfloat16)
+    pressure_wide, returned = lax.optimization_barrier((pressure_wide, returned))
     back = lax.all_to_all(returned, "yz", 0, 0, tiled=True)
     marker_pair_force = jnp.einsum(
         "qr,qw->rw", dispatch.astype(jnp.bfloat16), back, preferred_element_type=jnp.float32

time: 89.9 us -> 91 us (1.012)
  the two profiles are of different devices: /device:TPU:1 before, /device:TPU:7 now
where the time goes in v9:
time: 91 us; the launch traced here: 90.5 us
  starting transfers between devices  37.4 us (41%)
  waiting for transfers between devices  21.5 us (24%)
  local copies, waits for them, and re-layouts  16.6 us (18%)
  matrix products  8.85 us (10%)
  other arithmetic  4.81 us (5%)
  between operations  1.22 us (1%)
    ppermute x5, starting transfers between devices, faces(): lax.ppermute(lax.slice_in_dim(block, 0, width, axis=dim).astype(kind), ax...  17.4 us
    ppermute x5, waiting for transfers between devices, faces(): lax.ppermute(lax.slice_in_dim(block, block.shape[dim] - width, None, axis...  9.26 us
    all_to_all x1, waiting for transfers between devices, body(): back = lax.all_to_all(returned, 'yz', 0, 0, tiled=True)  8.69 us
    ppermute x5, starting transfers between devices, faces(): lax.ppermute(lax.slice_in_dim(block, block.shape[dim] - width, None, axis...  8.58 us
    all_to_all x1, starting transfers between devices, body(): received = lax.all_to_all(send, 'yz', 0, 0, tiled=True)  6.04 us
    unnamed x28, local copies, waits for them, and re-layouts  5.82 us
    all_to_all x1, starting transfers between devices, body(): back = lax.all_to_all(returned, 'yz', 0, 0, tiled=True)  5.46 us
    ppermute x5, waiting for transfers between devices, faces(): lax.ppermute(lax.slice_in_dim(block, 0, width, axis=dim).astype(kind), ax...  3.55 us
  transfers between devices with their start and end apart: 12, of which 6 were waited for; matrix products, arithmetic and copies ran while one was open for 7% of the time, Pallas kernels for 0%

profile of v9, /device:TPU:7, one launch (start us, length us, event | category | flops | bytes accessed | tf_op | source)
XLA Modules:
  0.0 90.5 jit_solution(14977525437043600893)
XLA Ops:
  0.6 1.1 %copy.148 = f32[32,16,128]{2,0,1:T(8,128)S(1)} copy(f32[32,16,128]{2,1,0:T(8,128)} %param.8) | data formatting | bytes 524288 | tf_op args[1]
  1.8 1.4 %copy.89 = f32[3,32,16,128]{3,1,2,0:T(8,128)S(1)} copy(f32[3,32,16,128]{3,2,1,0:T(8,128)} %param.7) | data formatting | bytes 1572864 | tf_op args[0]
  3.2 8.1 %collective-permute-start.1 = (f32[4,32,1,128]{3,1,2,0:T(8,128)S(1)}, f32[4,32,1,128]{3,1,2,0:T(8,128)S(1)}, u32[]{:S(2)}, u32[]{:S(2)}) collective-permute-start(f32[4,32,1,128]{3,1,2,0:T(8,128)S(1)} %get-tuple-element.37), channel_id=1, source_target_pairs={{1,0},{2,1},{3,2},{4,3},{5,4},{6,5},{7,6},{8,7},{9,8},{10,9},{11,1... | collective-permute-start | bytes 196616 | tf_op jit(solution)/shard_map/ppermute | solution.py:24
  11.4 1.0 %collective-permute-start.2 = (f32[4,3,16,128]{3,1,2,0:T(4,128)S(1)}, f32[4,3,16,128]{3,1,2,0:T(4,128)}, u32[]{:S(2)}, u32[]{:S(2)}) collective-permute-start(f32[4,3,16,128]{3,1,2,0:T(4,128)S(1)} %get-tuple-element.36), channel_id=1, source_target_pairs={{32,0},{64,32},{96,64},{128,96},{160,128},{192,160},{224,192},{0,2... | collective-permute-start | bytes 294920 | tf_op jit(solution)/shard_map/ppermute | solution.py:24
  12.4 2.0 %collective-permute-start.3 = (f32[4,3,16,128]{3,1,2,0:T(4,128)S(1)}, f32[4,3,16,128]{3,1,2,0:T(4,128)}, u32[]{:S(2)}, u32[]{:S(2)}) collective-permute-start(f32[4,3,16,128]{3,1,2,0:T(4,128)S(1)} %get-tuple-element.35), channel_id=1, source_target_pairs={{0,32},{32,64},{64,96},{96,128},{128,160},{160,192},{192,224},{224... | collective-permute-start | bytes 294920 | tf_op jit(solution)/shard_map/ppermute | solution.py:21
  14.4 1.0 %multiply_bitcast_fusion = f32[32,16,128]{2,1,0:T(8,128)S(1)} fusion(f32[3,32,16,128]{3,2,1,0:T(8,128)} %param.7), kind=kLoop, calls=%fused_computation.121 | loop fusion | flops 65536 | bytes 524288 | tf_op jit(solution)/shard_map/mul | solution.py:107
  15.4 0.8 copy.88
  16.6 0.2 convert_reduce_fusion
  17.2 0.5 collective-permute-done
  17.8 0.9 %slice.298 = f32[4,1,16,128]{3,1,2,0:T(1,128)S(1)} slice(f32[4,3,16,128]{3,1,2,0:T(4,128)} %collective-permute-done.2), slice={[0:4], [0:1], [0:16], [0:128]} | slice | bytes 65536 | tf_op jit(solution)/shard_map/slice | solution.py:116
  18.8 0.9 %slice.299 = f32[4,1,16,128]{3,1,2,0:T(1,128)S(1)} slice(f32[4,3,16,128]{3,1,2,0:T(4,128)} %collective-permute-done.3), slice={[0:4], [2:3], [0:16], [0:128]} | slice | bytes 65536 | tf_op jit(solution)/shard_map/slice | solution.py:116
  19.9 0.4 convolution_bitcast_fusion.8
  20.3 0.5 copy-done.2
  20.8 1.2 %fusion.130 = (bf16[3,32,16,128]{3,1,2,0:T(8,128)(2,1)S(1)}, f32[3,32,16,128]{3,1,2,0:T(8,128)S(1)}) fusion(f32[1,32,16,128]{3,1,2,0:T(8,128)S(1)} %get-tuple-element.54, f32[1,32,16,128]{3,1,2,0:T(8,128)S(1)} %convolution_bitcast_fusion.8, f32[1,32,16,128]{3,1,2,0:T(8,128)S(1)} %get-tuple-element.53, f32[3,32,16,128]{3,1,2,0:T(8,128)S(1)} %copy.89, ...), kind=kOutput, calls=%fused_computation.276 | convolution fusion | flops 307609600 | bytes 3483904 | tf_op jit(solution)/shard_map/...i,ij->...j/dot_general | solution.py:81
  22.1 0.4 convolution_bitcast_fusion.4
  22.6 0.4 convolution_bitcast_fusion.5
  23.1 0.4 convolution_bitcast_fusion.6
  23.5 0.6 select_reduce_fusion
  24.3 0.2 copy.96
  24.5 0.4 convert_element_type.98
  24.9 0.6 fusion.9
  25.5 0.3 fusion.43
  25.8 0.8 all_to_all.16
  26.6 6.0 %all-to-all-start = ((f32[32,4,385]{2,1,0:T(4,128)}), f32[32,4,385]{2,1,0:T(4,128)S(1)}, u32[]{:S(2)}, u32[]{:S(2)}) async-start(f32[32,4,385]{2,1,0:T(4,128)} %all_to_all.16), calls=%async_computation | async-start | bytes 524288 | tf_op jit(solution)/shard_map/all_to_all | solution.py:170
  32.6 0.8 slice_bitcast_fusion.10
  33.4 0.8 slice_bitcast_fusion.9
  34.2 1.3 %collective-permute-start.4 = (f32[38,3,128]{2,0,1:T(8,128)S(1)}, f32[38,3,128]{2,0,1:T(8,128)S(1)}, u32[]{:S(2)}, u32[]{:S(2)}) collective-permute-start(f32[38,3,128]{2,0,1:T(8,128)S(1)} %get-tuple-element.55), channel_id=1, source_target_pairs={{0,1},{1,2},{2,3},{3,4},{4,5},{5,6},{6,7},{7,8},{8,9},{9,10},{10,1... | collective-permute-start | bytes 175112 | tf_op jit(solution)/shard_map/ppermute | solution.py:21
  35.5 3.6 %collective-permute-start.5 = (f32[38,3,128]{2,0,1:T(8,128)S(1)}, f32[38,3,128]{2,0,1:T(8,128)S(1)}, u32[]{:S(2)}, u32[]{:S(2)}) collective-permute-start(f32[38,3,128]{2,0,1:T(8,128)S(1)} %get-tuple-element.56), channel_id=1, source_target_pairs={{1,0},{2,1},{3,2},{4,3},{5,4},{6,5},{7,6},{8,7},{9,8},{10,9},{11,1... | collective-permute-start | bytes 175112 | tf_op jit(solution)/shard_map/ppermute | solution.py:24
  39.1 5.6 %collective-permute-done.4 = f32[38,3,128]{2,0,1:T(8,128)S(1)} collective-permute-done((f32[38,3,128]{2,0,1:T(8,128)S(1)}, f32[38,3,128]{2,0,1:T(8,128)S(1)}, u32[]{:S(2)}, u32[]{:S(2)}) %collective-permute-start.4) | collective-permute-done | bytes 58400 | tf_op jit(solution)/shard_map/ppermute | solution.py:21
  44.7 0.9 maximum_select_fusion.1
  45.5 0.1 all_to_all.18
  45.6 0.1 slice_reduce_fusion.8
  45.8 0.2 fusion.7
  46.0 0.3 convolution_convert_fusion
  46.3 0.7 all_to_all.19
  47.0 5.5 %all-to-all-start.1 = ((bf16[32,4,384]{2,1,0:T(4,128)(2,1)}), bf16[32,4,384]{2,1,0:T(4,128)(2,1)S(1)}, u32[]{:S(2)}, u32[]{:S(2)}) async-start(bf16[32,4,384]{2,1,0:T(4,128)(2,1)} %all_to_all.19), calls=%async_computation.1 | async-start | bytes 196608 | tf_op jit(solution)/shard_map/all_to_all | solution.py:184
  52.4 0.2 broadcast_compare_fusion
  52.6 8.7 %all-to-all-done.1 = bf16[32,4,384]{2,1,0:T(4,128)(2,1)S(1)} async-done(((bf16[32,4,384]{2,1,0:T(4,128)(2,1)}), bf16[32,4,384]{2,1,0:T(4,128)(2,1)S(1)}, u32[]{:S(2)}, u32[]{:S(2)}) %all-to-all-start.1) | async-done | bytes 98336 | tf_op jit(solution)/shard_map/all_to_all | solution.py:184
  61.4 0.2 convolution_convert_fusion.1
  61.6 0.4 convolution_bitcast_fusion.9
  61.9 0.4 reshape.463
  62.4 3.2 %slice_reduce_fusion.7 = (f32[3,512]{1,0:T(4,128)S(1)}, f32[3,512]{1,0:T(4,128)S(1)}, f32[3,512]{1,0:T(4,128)S(1)}, f32[3,512]{1,0:T(4,128)S(1)}, f32[3,512]{1,0...) fusion(f32[3,512,8]{2,1,0:T(8,128)S(1)} %reshape.463), kind=kLoop, calls=%fused_computation.36 | loop fusion | bytes 98304 | tf_op jit(solution)/shard_map/slice | solution.py:197
  65.6 0.5 select_add_fusion
  66.1 0.7 convolution_bitcast_fusion.3
  66.8 0.7 convolution_bitcast_fusion.2
  67.5 0.7 convolution_bitcast_fusion.1
  68.2 0.2 fusion.125
  68.4 5.1 %collective-permute-start.6 = (bf16[3,3,16,128]{3,1,2,0:T(4,128)(2,1)S(1)}, bf16[3,3,16,128]{3,1,2,0:T(4,128)(2,1)S(1)}, u32[]{:S(2)}, u32[]{:S(2)}) collective-permute-start(bf16[3,3,16,128]{3,1,2,0:T(4,128)(2,1)S(1)} %get-tuple-element.45), channel_id=1, source_target_pairs={{0,32},{32,64},{64,96},{96,128},{128,160},{160,192},{192,224},{224... | collective-permute-start | bytes 110600 | tf_op jit(solution)/shard_map/ppermute | solution.py:21
  73.6 1.2 %collective-permute-done.6 = bf16[3,3,16,128]{3,1,2,0:T(4,128)(2,1)S(1)} collective-permute-done((bf16[3,3,16,128]{3,1,2,0:T(4,128)(2,1)S(1)}, bf16[3,3,16,128]{3,1,2,0:T(4,128)(2,1)S(1)}, u32[]{:S(2)}, u32[]{:S(2)}) %collective-permute-start.6) | collective-permute-done | bytes 36896 | tf_op jit(solution)/shard_map/ppermute | solution.py:21
  74.7 3.5 %collective-permute-done.7 = bf16[3,3,16,128]{3,1,2,0:T(4,128)(2,1)S(1)} collective-permute-done((bf16[3,3,16,128]{3,1,2,0:T(4,128)(2,1)S(1)}, bf16[3,3,16,128]{3,1,2,0:T(4,128)(2,1)S(1)}, u32[]{:S(2)}, u32[]{:S(2)}) %collective-permute-start.7) | collective-permute-done | bytes 36896 | tf_op jit(solution)/shard_map/ppermute | solution.py:24
  78.4 0.1 collective-permute-start.8
  78.5 4.7 %collective-permute-start.9 = (bf16[3,38,3,128]{3,1,2,0:T(8,128)(2,1)S(1)}, bf16[3,38,3,128]{3,1,2,0:T(8,128)(2,1)S(1)}, u32[]{:S(2)}, u32[]{:S(2)}) collective-permute-start(bf16[3,38,3,128]{3,1,2,0:T(8,128)(2,1)S(1)} %get-tuple-element.40), channel_id=1, source_target_pairs={{1,0},{2,1},{3,2},{4,3},{5,4},{6,5},{7,6},{8,7},{9,8},{10,9},{11,1... | collective-permute-start | bytes 262664 | tf_op jit(solution)/shard_map/ppermute | solution.py:24
  83.2 1.9 %collective-permute-done.8 = bf16[3,38,3,128]{3,1,2,0:T(8,128)(2,1)S(1)} collective-permute-done((bf16[3,38,3,128]{3,1,2,0:T(8,128)(2,1)S(1)}, bf16[3,38,3,128]{3,1,2,0:T(8,128)(2,1)S(1)}, u32[]{:S(2)}, u32[]{:S(2)}) %collective-permute-start.8) | collective-permute-done | bytes 87584 | tf_op jit(solution)/shard_map/ppermute | solution.py:21
  85.2 0.2 maximum_select_fusion
  85.4 0.1 slice_bitcast_fusion.2
  85.5 0.5 fusion.3
  86.1 0.5 copy-done.1
  86.5 0.5 fusion.2
  87.1 0.5 fusion.6
  87.6 0.1 fusion.128
  87.7 0.4 convolution_bitcast_fusion.7
  88.1 0.2 maximum_subtract_fusion
  88.3 1.3 %copy.110 = f32[3,32,16,128]{3,2,1,0:T(8,128)} copy(f32[3,32,16,128]{3,1,2,0:T(8,128)S(1)} %maximum_subtract_fusion) | data formatting | bytes 1572864
  89.6 0.9 copy.111
  (75 shorter events, 1.6 us)
Async XLA Ops:
  0.6 24.2 %copy-start = (bf16[1,32,128,128]{3,2,1,0:T(8,128)(2,1)S(1)}, bf16[1,32,128,128]{3,2,1,0:T(8,128)(2,1)}, u32[]{:S(2)}) copy-start(bf16[1,32,128,128]{3,2,1,0:T(8,128)(2,1)} %param.9) | copy-start | bytes 3145732
  3.2 13.0 %copy-start.4 = (s32[1,32,3]{1,0,2:T(1,128)S(1)}, s32[1,32,3]{1,0,2:T(1,128)}, u32[]{:S(2)}) copy-start(s32[1,32,3]{1,0,2:T(1,128)} %param.13) | copy-start | bytes 1156
  3.2 13.4 %copy-start.5 = (s32[1,32,1]{1,2,0:T(1,128)S(1)}, s32[1,32,1]{1,2,0:T(1,128)}, u32[]{:S(2)}) copy-start(s32[1,32,1]{1,2,0:T(1,128)} %param.11) | copy-start | bytes 388
  3.2 13.6 %copy-start.6 = (s32[1,32]{1,0:T(1,128)S(1)}, s32[1,32]{1,0:T(1,128)}, u32[]{:S(2)}) copy-start(s32[1,32]{1,0:T(1,128)} %param.12) | copy-start | bytes 388
  3.2 13.7 %copy-start.3 = (f32[1,32,3,128]{3,1,2,0:T(8,128)S(1)}, f32[1,32,3,128]{3,1,2,0:T(8,128)}, u32[]{:S(2)}) copy-start(f32[1,32,3,128]{3,1,2,0:T(8,128)} %param.10) | copy-start | bytes 147460
  3.2 14.0 %collective-permute-start.1 = (f32[4,32,1,128]{3,1,2,0:T(8,128)S(1)}, f32[4,32,1,128]{3,1,2,0:T(8,128)S(1)}, u32[]{:S(2)}, u32[]{:S(2)}) collective-permute-start(f32[4,32,1,128]{3,1,2,0:T(8,128)S(1)} %get-tuple-element.37), channel_id=1, source_target_pairs={{1,0},{2,1},{3,2},{4,3},{5,4},{6,5},{7,6},{8,7},{9,8},{10,9},{11,1... | collective-permute-start | bytes 196616 | tf_op jit(solution)/shard_map/ppermute | solution.py:24
  11.3 6.4 %collective-permute-start = (f32[4,32,1,128]{3,1,2,0:T(8,128)S(1)}, f32[4,32,1,128]{3,1,2,0:T(8,128)S(1)}, u32[]{:S(2)}, u32[]{:S(2)}) collective-permute-start(f32[4,32,1,128]{3,1,2,0:T(8,128)S(1)} %get-tuple-element.38), channel_id=1, source_target_pairs={{0,1},{1,2},{2,3},{3,4},{4,5},{5,6},{6,7},{7,8},{8,9},{9,10},{10,1... | collective-permute-start | bytes 196616 | tf_op jit(solution)/shard_map/ppermute | solution.py:21
  11.4 6.4 %collective-permute-start.2 = (f32[4,3,16,128]{3,1,2,0:T(4,128)S(1)}, f32[4,3,16,128]{3,1,2,0:T(4,128)}, u32[]{:S(2)}, u32[]{:S(2)}) collective-permute-start(f32[4,3,16,128]{3,1,2,0:T(4,128)S(1)} %get-tuple-element.36), channel_id=1, source_target_pairs={{32,0},{64,32},{96,64},{128,96},{160,128},{192,160},{224,192},{0,2... | collective-permute-start | bytes 294920 | tf_op jit(solution)/shard_map/ppermute | solution.py:24
  12.4 6.4 %collective-permute-start.3 = (f32[4,3,16,128]{3,1,2,0:T(4,128)S(1)}, f32[4,3,16,128]{3,1,2,0:T(4,128)}, u32[]{:S(2)}, u32[]{:S(2)}) collective-permute-start(f32[4,3,16,128]{3,1,2,0:T(4,128)S(1)} %get-tuple-element.35), channel_id=1, source_target_pairs={{0,32},{32,64},{64,96},{96,128},{128,160},{160,192},{192,224},{224... | collective-permute-start | bytes 294920 | tf_op jit(solution)/shard_map/ppermute | solution.py:21
  19.8 1.0 %copy-start.2 = (f32[32,16,128]{2,0,1:T(8,128)S(1)}, f32[32,16,128]{2,0,1:T(8,128)}, u32[]{:S(2)}) copy-start(f32[32,16,128]{2,0,1:T(8,128)} %copy.88) | copy-start | bytes 786436
  26.6 19.0 %all-to-all-start = ((f32[32,4,385]{2,1,0:T(4,128)}), f32[32,4,385]{2,1,0:T(4,128)S(1)}, u32[]{:S(2)}, u32[]{:S(2)}) async-start(f32[32,4,385]{2,1,0:T(4,128)} %all_to_all.16), calls=%async_computation | async-start | bytes 524288 | tf_op jit(solution)/shard_map/all_to_all | solution.py:170
  34.2 10.5 %collective-permute-start.4 = (f32[38,3,128]{2,0,1:T(8,128)S(1)}, f32[38,3,128]{2,0,1:T(8,128)S(1)}, u32[]{:S(2)}, u32[]{:S(2)}) collective-permute-start(f32[38,3,128]{2,0,1:T(8,128)S(1)} %get-tuple-element.55), channel_id=1, source_target_pairs={{0,1},{1,2},{2,3},{3,4},{4,5},{5,6},{6,7},{7,8},{8,9},{9,10},{10,1... | collective-permute-start | bytes 175112 | tf_op jit(solution)/shard_map/ppermute | solution.py:21
  35.5 9.2 %collective-permute-start.5 = (f32[38,3,128]{2,0,1:T(8,128)S(1)}, f32[38,3,128]{2,0,1:T(8,128)S(1)}, u32[]{:S(2)}, u32[]{:S(2)}) collective-permute-start(f32[38,3,128]{2,0,1:T(8,128)S(1)} %get-tuple-element.56), channel_id=1, source_target_pairs={{1,0},{2,1},{3,2},{4,3},{5,4},{6,5},{7,6},{8,7},{9,8},{10,9},{11,1... | collective-permute-start | bytes 175112 | tf_op jit(solution)/shard_map/ppermute | solution.py:24
  47.0 14.4 %all-to-all-start.1 = ((bf16[32,4,384]{2,1,0:T(4,128)(2,1)}), bf16[32,4,384]{2,1,0:T(4,128)(2,1)S(1)}, u32[]{:S(2)}, u32[]{:S(2)}) async-start(bf16[32,4,384]{2,1,0:T(4,128)(2,1)} %all_to_all.19), calls=%async_computation.1 | async-start | bytes 196608 | tf_op jit(solution)/shard_map/all_to_all | solution.py:184
  68.4 6.3 %collective-permute-start.6 = (bf16[3,3,16,128]{3,1,2,0:T(4,128)(2,1)S(1)}, bf16[3,3,16,128]{3,1,2,0:T(4,128)(2,1)S(1)}, u32[]{:S(2)}, u32[]{:S(2)}) collective-permute-start(bf16[3,3,16,128]{3,1,2,0:T(4,128)(2,1)S(1)} %get-tuple-element.45), channel_id=1, source_target_pairs={{0,32},{32,64},{64,96},{96,128},{128,160},{160,192},{192,224},{224... | collective-permute-start | bytes 110600 | tf_op jit(solution)/shard_map/ppermute | solution.py:21
  73.6 4.7 %collective-permute-start.7 = (bf16[3,3,16,128]{3,1,2,0:T(4,128)(2,1)S(1)}, bf16[3,3,16,128]{3,1,2,0:T(4,128)(2,1)S(1)}, u32[]{:S(2)}, u32[]{:S(2)}) collective-permute-start(bf16[3,3,16,128]{3,1,2,0:T(4,128)(2,1)S(1)} %get-tuple-element.46), channel_id=1, source_target_pairs={{32,0},{64,32},{96,64},{128,96},{160,128},{192,160},{224,192},{0,2... | collective-permute-start | bytes 110600 | tf_op jit(solution)/shard_map/ppermute | solution.py:24
  78.4 6.8 %collective-permute-start.8 = (bf16[3,38,3,128]{3,1,2,0:T(8,128)(2,1)S(1)}, bf16[3,38,3,128]{3,1,2,0:T(8,128)(2,1)S(1)}, u32[]{:S(2)}, u32[]{:S(2)}) collective-permute-start(bf16[3,38,3,128]{3,1,2,0:T(8,128)(2,1)S(1)} %get-tuple-element.39), channel_id=1, source_target_pairs={{0,1},{1,2},{2,3},{3,4},{4,5},{5,6},{6,7},{7,8},{8,9},{9,10},{10,1... | collective-permute-start | bytes 262664 | tf_op jit(solution)/shard_map/ppermute | solution.py:21
  78.5 6.7 %collective-permute-start.9 = (bf16[3,38,3,128]{3,1,2,0:T(8,128)(2,1)S(1)}, bf16[3,38,3,128]{3,1,2,0:T(8,128)(2,1)S(1)}, u32[]{:S(2)}, u32[]{:S(2)}) collective-permute-start(bf16[3,38,3,128]{3,1,2,0:T(8,128)(2,1)S(1)} %get-tuple-element.40), channel_id=1, source_target_pairs={{1,0},{2,1},{3,2},{4,3},{5,4},{6,5},{7,6},{8,7},{9,8},{10,9},{11,1... | collective-permute-start | bytes 262664 | tf_op jit(solution)/shard_map/ppermute | solution.py:24
  85.5 1.0 %copy-start.1 = (f32[38,22,128]{2,0,1:T(8,128)S(1)}, f32[38,22,128]{2,0,1:T(8,128)}, u32[]{:S(2)}) copy-start(f32[38,22,128]{2,0,1:T(8,128)} %maximum_select_fusion.1) | copy-start | bytes 1284100

commit v10 on v8

--- a/solution.py
+++ b/solution.py
@@ -167,6 +167,7 @@
     send = jnp.dot(
         dispatch, packed, precision=lax.Precision.HIGHEST, preferred_element_type=jnp.float32
     )
+    pressure_wide, send = lax.optimization_barrier((pressure_wide, send))
     received = lax.all_to_all(send, "yz", 0, 0, tiled=True)
     received_grain = received[:, row_width]
     received_values = received[:, :row_width]

time: 89.9 us -> 98 us (1.090); the launches traced: 88.5 us -> 97.6 us
  waiting for transfers between devices: 19.5 us -> 26.2 us
  other arithmetic: 5.33 us -> 7.52 us
    ppermute x5, waiting for transfers between devices: 2.37 us -> 4.87 us  [faces(): lax.ppermute(lax.slice_in_dim(block, block.shape[dim] - width, None, axis...]
    ppermute x5, waiting for transfers between devices: 0.01 us -> 2.34 us  [faces(): lax.ppermute(lax.slice_in_dim(block, 0, width, axis=dim).astype(kind), ax...]
    all_to_all x1, waiting for transfers between devices: 9 us -> 10.3 us  [body(): received = lax.all_to_all(send, 'yz', 0, 0, tiled=True)]
    ppermute x5, starting transfers between devices: 6.02 us -> 7.09 us  [faces(): lax.ppermute(lax.slice_in_dim(block, block.shape[dim] - width, None, axis...]
    unnamed x30 -> x62, local copies, waits for them, and re-layouts: 5.89 us -> 5.99 us
  transfers between devices with their start and end apart: 12 -> 12, of which waited for: 4 -> 6; matrix products, arithmetic and copies ran while one was open for 8% -> 7% of each run, Pallas kernels for 0% -> 0%
where the time goes in v10:
time: 98 us; the launch traced here: 97.6 us
  starting transfers between devices  37.6 us (38%)
  waiting for transfers between devices  26.2 us (27%)
  local copies, waits for them, and re-layouts  15.9 us (16%)
  matrix products  8.93 us (9%)
  other arithmetic  7.52 us (8%)
  between operations  1.41 us (1%)
    ppermute x5, starting transfers between devices, faces(): lax.ppermute(lax.slice_in_dim(block, 0, width, axis=dim).astype(kind), ax...  19.8 us
    all_to_all x1, waiting for transfers between devices, body(): received = lax.all_to_all(send, 'yz', 0, 0, tiled=True)  10.3 us
    all_to_all x1, waiting for transfers between devices, body(): back = lax.all_to_all(returned, 'yz', 0, 0, tiled=True)  8.69 us
    ppermute x5, starting transfers between devices, faces(): lax.ppermute(lax.slice_in_dim(block, block.shape[dim] - width, None, axis...  7.09 us
    all_to_all x1, starting transfers between devices, body(): received = lax.all_to_all(send, 'yz', 0, 0, tiled=True)  6.53 us
    unnamed x62, local copies, waits for them, and re-layouts  5.99 us
    ppermute x5, waiting for transfers between devices, faces(): lax.ppermute(lax.slice_in_dim(block, block.shape[dim] - width, None, axis...  4.87 us
    all_to_all x1, starting transfers between devices, body(): back = lax.all_to_all(returned, 'yz', 0, 0, tiled=True)  4.22 us
  transfers between devices with their start and end apart: 12, of which 6 were waited for; matrix products, arithmetic and copies ran while one was open for 7% of the time, Pallas kernels for 0%

profile of v10, /device:TPU:1, one launch (start us, length us, event | category | flops | bytes accessed | tf_op | source)
XLA Modules:
  0.0 97.6 jit_solution(18218426880227861454)
XLA Ops:
  0.6 1.1 %copy.147 = f32[32,16,128]{2,0,1:T(8,128)S(1)} copy(f32[32,16,128]{2,1,0:T(8,128)} %param.8) | data formatting | bytes 524288 | tf_op args[1]
  1.8 1.4 %copy.89 = f32[3,32,16,128]{3,1,2,0:T(8,128)S(1)} copy(f32[3,32,16,128]{3,2,1,0:T(8,128)} %param.7) | data formatting | bytes 1572864 | tf_op args[0]
  3.2 8.9 %collective-permute-start.1 = (f32[4,32,1,128]{3,1,2,0:T(8,128)S(1)}, f32[4,32,1,128]{3,1,2,0:T(8,128)S(1)}, u32[]{:S(2)}, u32[]{:S(2)}) collective-permute-start(f32[4,32,1,128]{3,1,2,0:T(8,128)S(1)} %get-tuple-element.37), channel_id=1, source_target_pairs={{1,0},{2,1},{3,2},{4,3},{5,4},{6,5},{7,6},{8,7},{9,8},{10,9},{11,1... | collective-permute-start | bytes 196616 | tf_op jit(solution)/shard_map/ppermute | solution.py:24
  12.2 1.0 collective-permute-start.2
  13.2 1.1 %collective-permute-start.3 = (f32[4,3,16,128]{3,1,2,0:T(4,128)S(1)}, f32[4,3,16,128]{3,1,2,0:T(4,128)}, u32[]{:S(2)}, u32[]{:S(2)}) collective-permute-start(f32[4,3,16,128]{3,1,2,0:T(4,128)S(1)} %get-tuple-element.35), channel_id=1, source_target_pairs={{0,32},{32,64},{64,96},{96,128},{128,160},{160,192},{192,224},{224... | collective-permute-start | bytes 294920 | tf_op jit(solution)/shard_map/ppermute | solution.py:21
  14.3 0.5 compare_select_fusion
  14.8 0.5 compare_and_fusion.3
  15.3 0.6 broadcast_add_fusion.7
  15.9 1.0 multiply_bitcast_fusion
  16.9 0.8 copy.88
  17.8 0.7 add.411
  18.7 0.2 convert_reduce_fusion
  18.9 0.5 multiply_add_fusion.1
  19.8 0.6 compare_and_fusion.2
  20.5 0.9 slice.299
  21.6 0.4 copy-done.9
  22.2 0.4 convolution_bitcast_fusion.8
  22.5 1.2 %fusion.130 = (bf16[3,32,16,128]{3,1,2,0:T(8,128)(2,1)S(1)}, f32[3,32,16,128]{3,1,2,0:T(8,128)S(1)}) fusion(f32[1,32,16,128]{3,1,2,0:T(8,128)S(1)} %get-tuple-element.54, f32[1,32,16,128]{3,1,2,0:T(8,128)S(1)} %convolution_bitcast_fusion.8, f32[1,32,16,128]{3,1,2,0:T(8,128)S(1)} %get-tuple-element.53, f32[3,32,16,128]{3,1,2,0:T(8,128)S(1)} %copy.89, ...), kind=kOutput, calls=%fused_computation.276 | convolution fusion | flops 307609600 | bytes 3483904 | tf_op jit(solution)/shard_map/...i,ij->...j/dot_general | solution.py:81
  23.9 0.4 convolution_bitcast_fusion.4
  24.4 0.4 convolution_bitcast_fusion.5
  24.9 0.4 convolution_bitcast_fusion.6
  25.3 0.6 select_reduce_fusion
  26.1 0.2 copy.96
  26.3 0.4 convert_element_type.98
  26.7 0.6 fusion.9
  27.3 0.8 slice_bitcast_fusion.10
  28.3 5.1 %collective-permute-start.5 = (f32[38,3,128]{2,0,1:T(8,128)S(1)}, f32[38,3,128]{2,0,1:T(8,128)S(1)}, u32[]{:S(2)}, u32[]{:S(2)}) collective-permute-start(f32[38,3,128]{2,0,1:T(8,128)S(1)} %get-tuple-element.56), channel_id=1, source_target_pairs={{1,0},{2,1},{3,2},{4,3},{5,4},{6,5},{7,6},{8,7},{9,8},{10,9},{11,1... | collective-permute-start | bytes 175112 | tf_op jit(solution)/shard_map/ppermute | solution.py:24
  33.4 0.4 fusion.43
  33.8 1.1 %collective-permute-done.4 = f32[38,3,128]{2,0,1:T(8,128)S(1)} collective-permute-done((f32[38,3,128]{2,0,1:T(8,128)S(1)}, f32[38,3,128]{2,0,1:T(8,128)S(1)}, u32[]{:S(2)}, u32[]{:S(2)}) %collective-permute-start.4) | collective-permute-done | bytes 58400 | tf_op jit(solution)/shard_map/ppermute | solution.py:21
  34.9 0.9 maximum_select_fusion.1
  35.8 0.1 copy.99
  35.9 0.8 all_to_all.16
  36.7 6.5 %all-to-all-start = ((f32[32,4,385]{2,1,0:T(4,128)}), f32[32,4,385]{2,1,0:T(4,128)S(1)}, u32[]{:S(2)}, u32[]{:S(2)}) async-start(f32[32,4,385]{2,1,0:T(4,128)} %all_to_all.16), calls=%async_computation | async-start | bytes 524288 | tf_op jit(solution)/shard_map/all_to_all | solution.py:171
  43.3 10.3 %all-to-all-done = f32[32,4,385]{2,1,0:T(4,128)S(1)} async-done(((f32[32,4,385]{2,1,0:T(4,128)}), f32[32,4,385]{2,1,0:T(4,128)S(1)}, u32[]{:S(2)}, u32[]{:S(2)}) %all-to-all-start) | async-done | bytes 197152 | tf_op jit(solution)/shard_map/all_to_all | solution.py:171
  53.8 0.1 slice_reduce_fusion.8
  53.9 0.2 fusion.7
  54.1 0.3 convolution_convert_fusion
  54.4 0.7 all_to_all.19
  55.1 4.2 %all-to-all-start.1 = ((bf16[32,4,384]{2,1,0:T(4,128)(2,1)}), bf16[32,4,384]{2,1,0:T(4,128)(2,1)S(1)}, u32[]{:S(2)}, u32[]{:S(2)}) async-start(bf16[32,4,384]{2,1,0:T(4,128)(2,1)} %all_to_all.19), calls=%async_computation.1 | async-start | bytes 196608 | tf_op jit(solution)/shard_map/all_to_all | solution.py:184
  59.3 0.2 broadcast_compare_fusion
  59.5 8.7 %all-to-all-done.1 = bf16[32,4,384]{2,1,0:T(4,128)(2,1)S(1)} async-done(((bf16[32,4,384]{2,1,0:T(4,128)(2,1)}), bf16[32,4,384]{2,1,0:T(4,128)(2,1)S(1)}, u32[]{:S(2)}, u32[]{:S(2)}) %all-to-all-start.1) | async-done | bytes 98336 | tf_op jit(solution)/shard_map/all_to_all | solution.py:184
  68.3 0.2 convolution_convert_fusion.1
  68.5 0.4 convolution_bitcast_fusion.9
  68.8 0.4 reshape.463
  69.3 3.2 %slice_reduce_fusion.7 = (f32[3,512]{1,0:T(4,128)S(1)}, f32[3,512]{1,0:T(4,128)S(1)}, f32[3,512]{1,0:T(4,128)S(1)}, f32[3,512]{1,0:T(4,128)S(1)}, f32[3,512]{1,0...) fusion(f32[3,512,8]{2,1,0:T(8,128)S(1)} %reshape.463), kind=kLoop, calls=%fused_computation.36 | loop fusion | bytes 98304 | tf_op jit(solution)/shard_map/slice | solution.py:197
  72.5 0.5 select_add_fusion
  73.0 0.7 convolution_bitcast_fusion.3
  73.7 0.7 convolution_bitcast_fusion.2
  74.4 0.7 convolution_bitcast_fusion.1
  75.1 0.2 fusion.125
  75.3 5.8 %collective-permute-start.6 = (bf16[3,3,16,128]{3,1,2,0:T(4,128)(2,1)S(1)}, bf16[3,3,16,128]{3,1,2,0:T(4,128)(2,1)S(1)}, u32[]{:S(2)}, u32[]{:S(2)}) collective-permute-start(bf16[3,3,16,128]{3,1,2,0:T(4,128)(2,1)S(1)} %get-tuple-element.45), channel_id=1, source_target_pairs={{0,32},{32,64},{64,96},{96,128},{128,160},{160,192},{192,224},{224... | collective-permute-start | bytes 110600 | tf_op jit(solution)/shard_map/ppermute | solution.py:21
  81.1 1.2 %collective-permute-done.6 = bf16[3,3,16,128]{3,1,2,0:T(4,128)(2,1)S(1)} collective-permute-done((bf16[3,3,16,128]{3,1,2,0:T(4,128)(2,1)S(1)}, bf16[3,3,16,128]{3,1,2,0:T(4,128)(2,1)S(1)}, u32[]{:S(2)}, u32[]{:S(2)}) %collective-permute-start.6) | collective-permute-done | bytes 36896 | tf_op jit(solution)/shard_map/ppermute | solution.py:21
  82.3 2.3 %collective-permute-done.7 = bf16[3,3,16,128]{3,1,2,0:T(4,128)(2,1)S(1)} collective-permute-done((bf16[3,3,16,128]{3,1,2,0:T(4,128)(2,1)S(1)}, bf16[3,3,16,128]{3,1,2,0:T(4,128)(2,1)S(1)}, u32[]{:S(2)}, u32[]{:S(2)}) %collective-permute-start.7) | collective-permute-done | bytes 36896 | tf_op jit(solution)/shard_map/ppermute | solution.py:24
  84.8 4.8 %collective-permute-start.9 = (bf16[3,38,3,128]{3,1,2,0:T(8,128)(2,1)S(1)}, bf16[3,38,3,128]{3,1,2,0:T(8,128)(2,1)S(1)}, u32[]{:S(2)}, u32[]{:S(2)}) collective-permute-start(bf16[3,38,3,128]{3,1,2,0:T(8,128)(2,1)S(1)} %get-tuple-element.40), channel_id=1, source_target_pairs={{1,0},{2,1},{3,2},{4,3},{5,4},{6,5},{7,6},{8,7},{9,8},{10,9},{11,1... | collective-permute-start | bytes 262664 | tf_op jit(solution)/shard_map/ppermute | solution.py:24
  89.6 2.5 %collective-permute-done.8 = bf16[3,38,3,128]{3,1,2,0:T(8,128)(2,1)S(1)} collective-permute-done((bf16[3,38,3,128]{3,1,2,0:T(8,128)(2,1)S(1)}, bf16[3,38,3,128]{3,1,2,0:T(8,128)(2,1)S(1)}, u32[]{:S(2)}, u32[]{:S(2)}) %collective-permute-start.8) | collective-permute-done | bytes 87584 | tf_op jit(solution)/shard_map/ppermute | solution.py:21
  92.2 0.2 maximum_select_fusion
  92.6 0.5 copy-done.10
  93.1 0.5 fusion.3
  93.7 0.5 fusion.2
  94.2 0.5 fusion.6
  94.9 0.4 convolution_bitcast_fusion.7
  95.2 0.2 maximum_subtract_fusion
  95.4 1.3 %copy.110 = f32[3,32,16,128]{3,2,1,0:T(8,128)} copy(f32[3,32,16,128]{3,1,2,0:T(8,128)S(1)} %maximum_subtract_fusion) | data formatting | bytes 1572864
  96.7 0.9 copy.111
  (110 shorter events, 2.3 us)
Async XLA Ops:
  0.6 26.1 %copy-start = (bf16[1,32,128,128]{3,2,1,0:T(8,128)(2,1)S(1)}, bf16[1,32,128,128]{3,2,1,0:T(8,128)(2,1)}, u32[]{:S(2)}) copy-start(bf16[1,32,128,128]{3,2,1,0:T(8,128)(2,1)} %param.9) | copy-start | bytes 3145732
  3.2 14.5 %copy-start.21 = (s32[1,32,3]{1,0,2:T(1,128)S(1)}, s32[1,32,3]{1,0,2:T(1,128)}, u32[]{:S(2)}) copy-start(s32[1,32,3]{1,0,2:T(1,128)} %param.13) | copy-start | bytes 1156
  3.2 15.5 %copy-start.22 = (s32[1,32,1]{1,2,0:T(1,128)S(1)}, s32[1,32,1]{1,2,0:T(1,128)}, u32[]{:S(2)}) copy-start(s32[1,32,1]{1,2,0:T(1,128)} %param.11) | copy-start | bytes 388
  3.2 16.2 %copy-start.23 = (s32[1,32]{1,0:T(1,128)S(1)}, s32[1,32]{1,0:T(1,128)}, u32[]{:S(2)}) copy-start(s32[1,32]{1,0:T(1,128)} %param.12) | copy-start | bytes 388
  3.2 17.1 %collective-permute-start.1 = (f32[4,32,1,128]{3,1,2,0:T(8,128)S(1)}, f32[4,32,1,128]{3,1,2,0:T(8,128)S(1)}, u32[]{:S(2)}, u32[]{:S(2)}) collective-permute-start(f32[4,32,1,128]{3,1,2,0:T(8,128)S(1)} %get-tuple-element.37), channel_id=1, source_target_pairs={{1,0},{2,1},{3,2},{4,3},{5,4},{6,5},{7,6},{8,7},{9,8},{10,9},{11,1... | collective-permute-start | bytes 196616 | tf_op jit(solution)/shard_map/ppermute | solution.py:24
  12.1 8.2 %collective-permute-start = (f32[4,32,1,128]{3,1,2,0:T(8,128)S(1)}, f32[4,32,1,128]{3,1,2,0:T(8,128)S(1)}, u32[]{:S(2)}, u32[]{:S(2)}) collective-permute-start(f32[4,32,1,128]{3,1,2,0:T(8,128)S(1)} %get-tuple-element.38), channel_id=1, source_target_pairs={{0,1},{1,2},{2,3},{3,4},{4,5},{5,6},{6,7},{7,8},{8,9},{9,10},{10,1... | collective-permute-start | bytes 196616 | tf_op jit(solution)/shard_map/ppermute | solution.py:21
  12.2 8.2 %collective-permute-start.2 = (f32[4,3,16,128]{3,1,2,0:T(4,128)S(1)}, f32[4,3,16,128]{3,1,2,0:T(4,128)S(1)}, u32[]{:S(2)}, u32[]{:S(2)}) collective-permute-start(f32[4,3,16,128]{3,1,2,0:T(4,128)S(1)} %get-tuple-element.36), channel_id=1, source_target_pairs={{32,0},{64,32},{96,64},{128,96},{160,128},{192,160},{224,192},{0,2... | collective-permute-start | bytes 294920 | tf_op jit(solution)/shard_map/ppermute | solution.py:24
  13.2 7.3 %collective-permute-start.3 = (f32[4,3,16,128]{3,1,2,0:T(4,128)S(1)}, f32[4,3,16,128]{3,1,2,0:T(4,128)}, u32[]{:S(2)}, u32[]{:S(2)}) collective-permute-start(f32[4,3,16,128]{3,1,2,0:T(4,128)S(1)} %get-tuple-element.35), channel_id=1, source_target_pairs={{0,32},{32,64},{64,96},{96,128},{128,160},{160,192},{192,224},{224... | collective-permute-start | bytes 294920 | tf_op jit(solution)/shard_map/ppermute | solution.py:21
  21.4 0.6 copy-start.9
  21.4 0.6 copy-start.11
  21.5 0.6 copy-start.13
  21.5 0.6 copy-start.15
  21.5 0.7 copy-start.17
  21.5 0.7 copy-start.19
  21.5 1.0 %copy-start.2 = (f32[32,16,128]{2,0,1:T(8,128)S(1)}, f32[32,16,128]{2,0,1:T(8,128)}, u32[]{:S(2)}) copy-start(f32[32,16,128]{2,0,1:T(8,128)} %copy.88) | copy-start | bytes 786436
  22.5 1.4 %copy-start.4 = (s32[512]{0:T(512)S(1)}, s32[512]{0:T(512)}, u32[]{:S(2)}) copy-start(s32[512]{0:T(512)} %add.411) | copy-start | bytes 6148
  26.1 7.4 %copy-start.8 = (s32[32]{0:T(128)S(1)}, s32[32]{0:T(128)}, u32[]{:S(2)}) copy-start(s32[32]{0:T(128)} %multiply_add_fusion.1) | copy-start | bytes 388
  26.3 8.6 %copy-start.6 = (pred[22]{0:T(512)(128)(4,1)S(1)}, pred[22]{0:T(512)(128)(4,1)}, u32[]{:S(2)}) copy-start(pred[22]{0:T(512)(128)(4,1)} %compare_and_fusion.2) | copy-start | bytes 70
  28.2 15.1 %copy-start.3 = (f32[1,32,3,128]{3,1,2,0:T(8,128)S(1)}, f32[1,32,3,128]{3,1,2,0:T(8,128)}, u32[]{:S(2)}) copy-start(f32[1,32,3,128]{3,1,2,0:T(8,128)} %param.10) | copy-start | bytes 147460
  28.2 6.8 %collective-permute-start.4 = (f32[38,3,128]{2,0,1:T(8,128)S(1)}, f32[38,3,128]{2,0,1:T(8,128)S(1)}, u32[]{:S(2)}, u32[]{:S(2)}) collective-permute-start(f32[38,3,128]{2,0,1:T(8,128)S(1)} %get-tuple-element.55), channel_id=1, source_target_pairs={{0,1},{1,2},{2,3},{3,4},{4,5},{5,6},{6,7},{7,8},{8,9},{9,10},{10,1... | collective-permute-start | bytes 175112 | tf_op jit(solution)/shard_map/ppermute | solution.py:21
  28.3 6.7 %collective-permute-start.5 = (f32[38,3,128]{2,0,1:T(8,128)S(1)}, f32[38,3,128]{2,0,1:T(8,128)S(1)}, u32[]{:S(2)}, u32[]{:S(2)}) collective-permute-start(f32[38,3,128]{2,0,1:T(8,128)S(1)} %get-tuple-element.56), channel_id=1, source_target_pairs={{1,0},{2,1},{3,2},{4,3},{5,4},{6,5},{7,6},{8,7},{9,8},{10,9},{11,1... | collective-permute-start | bytes 175112 | tf_op jit(solution)/shard_map/ppermute | solution.py:24
  35.9 23.4 %copy-start.5 = (s32[512]{0:T(512)S(1)}, s32[512]{0:T(512)}, u32[]{:S(2)}) copy-start(s32[512]{0:T(512)} %add.411) | copy-start | bytes 6148
  36.7 16.9 %all-to-all-start = ((f32[32,4,385]{2,1,0:T(4,128)}), f32[32,4,385]{2,1,0:T(4,128)S(1)}, u32[]{:S(2)}, u32[]{:S(2)}) async-start(f32[32,4,385]{2,1,0:T(4,128)} %all_to_all.16), calls=%async_computation | async-start | bytes 524288 | tf_op jit(solution)/shard_map/all_to_all | solution.py:171
  55.1 13.2 %all-to-all-start.1 = ((bf16[32,4,384]{2,1,0:T(4,128)(2,1)}), bf16[32,4,384]{2,1,0:T(4,128)(2,1)S(1)}, u32[]{:S(2)}, u32[]{:S(2)}) async-start(bf16[32,4,384]{2,1,0:T(4,128)(2,1)} %all_to_all.19), calls=%async_computation.1 | async-start | bytes 196608 | tf_op jit(solution)/shard_map/all_to_all | solution.py:184
  75.3 16.9 %copy-start.7 = (pred[22]{0:T(512)(128)(4,1)S(1)}, pred[22]{0:T(512)(128)(4,1)}, u32[]{:S(2)}) copy-start(pred[22]{0:T(512)(128)(4,1)} %compare_and_fusion.2) | copy-start | bytes 70
  75.3 7.0 %collective-permute-start.6 = (bf16[3,3,16,128]{3,1,2,0:T(4,128)(2,1)S(1)}, bf16[3,3,16,128]{3,1,2,0:T(4,128)(2,1)S(1)}, u32[]{:S(2)}, u32[]{:S(2)}) collective-permute-start(bf16[3,3,16,128]{3,1,2,0:T(4,128)(2,1)S(1)} %get-tuple-element.45), channel_id=1, source_target_pairs={{0,32},{32,64},{64,96},{96,128},{128,160},{160,192},{192,224},{224... | collective-permute-start | bytes 110600 | tf_op jit(solution)/shard_map/ppermute | solution.py:21
  81.1 3.5 %collective-permute-start.7 = (bf16[3,3,16,128]{3,1,2,0:T(4,128)(2,1)S(1)}, bf16[3,3,16,128]{3,1,2,0:T(4,128)(2,1)S(1)}, u32[]{:S(2)}, u32[]{:S(2)}) collective-permute-start(bf16[3,3,16,128]{3,1,2,0:T(4,128)(2,1)S(1)} %get-tuple-element.46), channel_id=1, source_target_pairs={{32,0},{64,32},{96,64},{128,96},{160,128},{192,160},{224,192},{0,2... | collective-permute-start | bytes 110600 | tf_op jit(solution)/shard_map/ppermute | solution.py:24
  84.7 7.4 %collective-permute-start.8 = (bf16[3,38,3,128]{3,1,2,0:T(8,128)(2,1)S(1)}, bf16[3,38,3,128]{3,1,2,0:T(8,128)(2,1)S(1)}, u32[]{:S(2)}, u32[]{:S(2)}) collective-permute-start(bf16[3,38,3,128]{3,1,2,0:T(8,128)(2,1)S(1)} %get-tuple-element.39), channel_id=1, source_target_pairs={{0,1},{1,2},{2,3},{3,4},{4,5},{5,6},{6,7},{7,8},{8,9},{9,10},{10,1... | collective-permute-start | bytes 262664 | tf_op jit(solution)/shard_map/ppermute | solution.py:21
  84.8 7.4 %collective-permute-start.9 = (bf16[3,38,3,128]{3,1,2,0:T(8,128)(2,1)S(1)}, bf16[3,38,3,128]{3,1,2,0:T(8,128)(2,1)S(1)}, u32[]{:S(2)}, u32[]{:S(2)}) collective-permute-start(bf16[3,38,3,128]{3,1,2,0:T(8,128)(2,1)S(1)} %get-tuple-element.40), channel_id=1, source_target_pairs={{1,0},{2,1},{3,2},{4,3},{5,4},{6,5},{7,6},{8,7},{9,8},{10,9},{11,1... | collective-permute-start | bytes 262664 | tf_op jit(solution)/shard_map/ppermute | solution.py:24
  92.4 0.6 copy-start.10
  92.4 0.6 copy-start.12
  92.4 0.6 copy-start.14
  92.4 0.6 copy-start.16
  92.4 0.7 copy-start.18
  92.5 0.7 copy-start.20
  92.6 1.1 %copy-start.1 = (f32[38,22,128]{2,0,1:T(8,128)S(1)}, f32[38,22,128]{2,0,1:T(8,128)}, u32[]{:S(2)}) copy-start(f32[38,22,128]{2,0,1:T(8,128)} %maximum_select_fusion.1) | copy-start | bytes 1284100

commit v11 on v8

--- a/solution.py
+++ b/solution.py
@@ -167,7 +167,7 @@
     send = jnp.dot(
         dispatch, packed, precision=lax.Precision.HIGHEST, preferred_element_type=jnp.float32
     )
-    received = lax.all_to_all(send, "yz", 0, 0, tiled=True)
+    received = lax.all_to_all(send.reshape(tiles, -1), "yz", 0, 0, tiled=True).reshape(send.shape)
     received_grain = received[:, row_width]
     received_values = received[:, :row_width]
     slot_numbers = jnp.arange(grain_slots, dtype=jnp.float32) + 1.0

time: 89.9 us -> 89.9 us (level)
    all_to_all x1, starting transfers between devices: 5.08 us -> 4.04 us  [body(): back = lax.all_to_all(returned, 'yz', 0, 0, tiled=True)]
where the time goes in v11:
time: 89.9 us; the launch traced here: 88.2 us
  starting transfers between devices  36.1 us (40%)
  waiting for transfers between devices  19.2 us (21%)
  local copies, waits for them, and re-layouts  17 us (19%)
  matrix products  8.84 us (10%)
  other arithmetic  5.83 us (6%)
  between operations  1.24 us (1%)
    ppermute x5, starting transfers between devices, faces(): lax.ppermute(lax.slice_in_dim(block, 0, width, axis=dim).astype(kind), ax...  19.4 us
    all_to_all x1, waiting for transfers between devices, body(): lax.all_to_all(send.reshape(tiles, -1), 'yz', 0, 0, tiled=True)  8.6 us
    all_to_all x1, waiting for transfers between devices, body(): back = lax.all_to_all(returned, 'yz', 0, 0, tiled=True)  8.18 us
    ppermute x5, starting transfers between devices, faces(): lax.ppermute(lax.slice_in_dim(block, block.shape[dim] - width, None, axis...  6.36 us
    all_to_all x1, starting transfers between devices, body(): lax.all_to_all(send.reshape(tiles, -1), 'yz', 0, 0, tiled=True)  6.33 us
    unnamed x30, local copies, waits for them, and re-layouts  5.89 us
    all_to_all x1, starting transfers between devices, body(): back = lax.all_to_all(returned, 'yz', 0, 0, tiled=True)  4.04 us
    dot_general x6, matrix products, across_y(): jnp.einsum('...i,ij->...j', field, matrix, precision=lax.Precision.HIGHES...  3.5 us
  transfers between devices with their start and end apart: 12, of which 4 were waited for; matrix products, arithmetic and copies ran while one was open for 8% of the time, Pallas kernels for 0%

profile of v11, /device:TPU:1, one launch (start us, length us, event | category | flops | bytes accessed | tf_op | source)
XLA Modules:
  0.0 88.2 jit_solution(15338528392628579172)
XLA Ops:
  0.6 1.1 %copy.178 = f32[32,16,128]{2,0,1:T(8,128)S(1)} copy(f32[32,16,128]{2,1,0:T(8,128)} %param.8) | data formatting | bytes 524288 | tf_op args[1]
  1.8 1.4 %copy.118 = f32[3,32,16,128]{3,1,2,0:T(8,128)S(1)} copy(f32[3,32,16,128]{3,2,1,0:T(8,128)} %param.7) | data formatting | bytes 1572864 | tf_op args[0]
  3.2 8.9 %collective-permute-start.1 = (f32[4,32,1,128]{3,1,2,0:T(8,128)S(1)}, f32[4,32,1,128]{3,1,2,0:T(8,128)S(1)}, u32[]{:S(2)}, u32[]{:S(2)}) collective-permute-start(f32[4,32,1,128]{3,1,2,0:T(8,128)S(1)} %get-tuple-element.35), channel_id=1, source_target_pairs={{1,0},{2,1},{3,2},{4,3},{5,4},{6,5},{7,6},{8,7},{9,8},{10,9},{11,1... | collective-permute-start | bytes 196616 | tf_op jit(solution)/shard_map/ppermute | solution.py:24
  12.2 1.0 %collective-permute-start.2 = (f32[4,3,16,128]{3,1,2,0:T(4,128)S(1)}, f32[4,3,16,128]{3,1,2,0:T(4,128)}, u32[]{:S(2)}, u32[]{:S(2)}) collective-permute-start(f32[4,3,16,128]{3,1,2,0:T(4,128)S(1)} %get-tuple-element.34), channel_id=1, source_target_pairs={{32,0},{64,32},{96,64},{128,96},{160,128},{192,160},{224,192},{0,2... | collective-permute-start | bytes 294920 | tf_op jit(solution)/shard_map/ppermute | solution.py:24
  13.2 1.1 %collective-permute-start.3 = (f32[4,3,16,128]{3,1,2,0:T(4,128)S(1)}, f32[4,3,16,128]{3,1,2,0:T(4,128)}, u32[]{:S(2)}, u32[]{:S(2)}) collective-permute-start(f32[4,3,16,128]{3,1,2,0:T(4,128)S(1)} %get-tuple-element.33), channel_id=1, source_target_pairs={{0,32},{32,64},{64,96},{96,128},{128,160},{160,192},{192,224},{224... | collective-permute-start | bytes 294920 | tf_op jit(solution)/shard_map/ppermute | solution.py:21
  14.3 1.0 %multiply_bitcast_fusion = f32[32,16,128]{2,1,0:T(8,128)S(1)} fusion(f32[3,32,16,128]{3,2,1,0:T(8,128)} %param.7), kind=kLoop, calls=%fused_computation.125 | loop fusion | flops 65536 | bytes 524288 | tf_op jit(solution)/shard_map/mul | solution.py:107
  15.3 0.8 copy.117
  16.5 0.2 convert_reduce_fusion
  17.1 0.9 %broadcast_compare_fusion = pred[32,16,512]{2,1,0:T(8,128)(4,1)} fusion(s32[512]{0:T(512)S(1)} %add.411, s32[32,16]{1,0:T(8,128)S(1)} %multiply_add_fusion), kind=kLoop, calls=%fused_computation.72 | loop fusion | flops 262144 | bytes 266240 | tf_op jit(solution)/shard_map/eq | solution.py:200
  18.0 0.5 collective-permute-done
  18.6 0.9 %slice.298 = f32[4,1,16,128]{3,1,2,0:T(1,128)S(1)} slice(f32[4,3,16,128]{3,1,2,0:T(4,128)} %collective-permute-done.2), slice={[0:4], [0:1], [0:16], [0:128]} | slice | bytes 65536 | tf_op jit(solution)/shard_map/slice | solution.py:116
  19.6 0.9 %slice.299 = f32[4,1,16,128]{3,1,2,0:T(1,128)S(1)} slice(f32[4,3,16,128]{3,1,2,0:T(4,128)} %collective-permute-done.3), slice={[0:4], [2:3], [0:16], [0:128]} | slice | bytes 65536 | tf_op jit(solution)/shard_map/slice | solution.py:116
  20.7 0.4 convolution_bitcast_fusion.8
  21.1 0.5 copy-done.2
  21.6 1.2 %fusion.136 = (bf16[3,32,16,128]{3,1,2,0:T(8,128)(2,1)S(1)}, f32[3,32,16,128]{3,1,2,0:T(8,128)S(1)}) fusion(f32[1,32,16,128]{3,1,2,0:T(8,128)S(1)} %get-tuple-element.52, f32[1,32,16,128]{3,1,2,0:T(8,128)S(1)} %convolution_bitcast_fusion.8, f32[1,32,16,128]{3,1,2,0:T(8,128)S(1)} %get-tuple-element.51, f32[3,32,16,128]{3,1,2,0:T(8,128)S(1)} %copy.118, ...), kind=kOutput, calls=%fused_computation.280 | convolution fusion | flops 307609600 | bytes 3483904 | tf_op jit(solution)/shard_map/...i,ij->...j/dot_general | solution.py:81
  22.9 0.4 convolution_bitcast_fusion.4
  23.4 0.4 convolution_bitcast_fusion.5
  23.9 0.4 convolution_bitcast_fusion.6
  24.3 0.6 select_reduce_fusion
  25.1 0.2 copy.124
  25.3 0.4 convert_element_type.98
  25.7 0.6 fusion.6
  26.3 0.3 fusion.45
  26.6 1.0 %all_to_all.19 = f32[32,1,1540]{2,1,0:T(1,128)} reshape(f32[128,385]{1,0:T(8,128)S(1)} %fusion.45) | data formatting | bytes 394240 | tf_op jit(solution)/shard_map/all_to_all | solution.py:170
  27.7 6.3 %all-to-all-start = ((f32[32,1,1540]{2,1,0:T(1,128)}), f32[32,1,1540]{2,1,0:T(1,128)S(1)}, u32[]{:S(2)}, u32[]{:S(2)}) async-start(f32[32,1,1540]{2,1,0:T(1,128)} %all_to_all.19), calls=%async_computation | async-start | bytes 425984 | tf_op jit(solution)/shard_map/all_to_all | solution.py:170
  34.0 0.6 compare_and_fusion.1
  34.6 0.8 slice_bitcast_fusion.10
  35.4 8.6 %all-to-all-done = f32[32,1,1540]{2,1,0:T(1,128)S(1)} async-done(((f32[32,1,1540]{2,1,0:T(1,128)}), f32[32,1,1540]{2,1,0:T(1,128)S(1)}, u32[]{:S(2)}, u32[]{:S(2)}) %all-to-all-start) | async-done | bytes 197152 | tf_op jit(solution)/shard_map/all_to_all | solution.py:170
  44.0 0.5 reduce
  44.5 0.1 reshape.468
  44.7 0.1 slice_reduce_fusion.8
  44.8 0.2 fusion.4
  45.0 0.3 convolution_convert_fusion
  45.3 0.7 all_to_all.16
  46.0 4.0 %all-to-all-start.1 = ((bf16[32,4,384]{2,1,0:T(4,128)(2,1)}), bf16[32,4,384]{2,1,0:T(4,128)(2,1)S(1)}, u32[]{:S(2)}, u32[]{:S(2)}) async-start(bf16[32,4,384]{2,1,0:T(4,128)(2,1)} %all_to_all.16), calls=%async_computation.1 | async-start | bytes 196608 | tf_op jit(solution)/shard_map/all_to_all | solution.py:183
  50.0 0.8 slice_bitcast_fusion.9
  50.8 8.2 %all-to-all-done.1 = bf16[32,4,384]{2,1,0:T(4,128)(2,1)S(1)} async-done(((bf16[32,4,384]{2,1,0:T(4,128)(2,1)}), bf16[32,4,384]{2,1,0:T(4,128)(2,1)S(1)}, u32[]{:S(2)}, u32[]{:S(2)}) %all-to-all-start.1) | async-done | bytes 98336 | tf_op jit(solution)/shard_map/all_to_all | solution.py:183
  59.0 0.2 convolution_convert_fusion.1
  59.2 0.4 convolution_bitcast_fusion.9
  59.6 0.4 reshape.470
  60.0 3.2 %slice_reduce_fusion.7 = (f32[3,512]{1,0:T(4,128)S(1)}, f32[3,512]{1,0:T(4,128)S(1)}, f32[3,512]{1,0:T(4,128)S(1)}, f32[3,512]{1,0:T(4,128)S(1)}, f32[3,512]{1,0...) fusion(f32[3,512,8]{2,1,0:T(8,128)S(1)} %reshape.470), kind=kLoop, calls=%fused_computation.32 | loop fusion | bytes 98304 | tf_op jit(solution)/shard_map/slice | solution.py:196
  63.2 0.5 select_add_fusion
  63.8 0.4 copy-done.1
  64.2 0.7 convolution_bitcast_fusion.3
  64.9 0.7 convolution_bitcast_fusion.2
  65.5 0.7 convolution_bitcast_fusion.1
  66.2 0.2 fusion.131
  66.5 5.0 %collective-permute-start.6 = (bf16[3,3,16,128]{3,1,2,0:T(4,128)(2,1)S(1)}, bf16[3,3,16,128]{3,1,2,0:T(4,128)(2,1)S(1)}, u32[]{:S(2)}, u32[]{:S(2)}) collective-permute-start(bf16[3,3,16,128]{3,1,2,0:T(4,128)(2,1)S(1)} %get-tuple-element.43), channel_id=1, source_target_pairs={{0,32},{32,64},{64,96},{96,128},{128,160},{160,192},{192,224},{224... | collective-permute-start | bytes 110600 | tf_op jit(solution)/shard_map/ppermute | solution.py:21
  71.5 0.1 collective-permute-start.4
  71.6 4.7 %collective-permute-start.5 = (f32[38,3,128]{2,0,1:T(8,128)S(1)}, f32[38,3,128]{2,0,1:T(8,128)S(1)}, u32[]{:S(2)}, u32[]{:S(2)}) collective-permute-start(f32[38,3,128]{2,0,1:T(8,128)S(1)} %get-tuple-element.54), channel_id=1, source_target_pairs={{1,0},{2,1},{3,2},{4,3},{5,4},{6,5},{7,6},{8,7},{9,8},{10,9},{11,1... | collective-permute-start | bytes 175112 | tf_op jit(solution)/shard_map/ppermute | solution.py:24
  76.6 4.8 %collective-permute-start.9 = (bf16[3,38,3,128]{3,1,2,0:T(8,128)(2,1)S(1)}, bf16[3,38,3,128]{3,1,2,0:T(8,128)(2,1)S(1)}, u32[]{:S(2)}, u32[]{:S(2)}) collective-permute-start(bf16[3,38,3,128]{3,1,2,0:T(8,128)(2,1)S(1)} %get-tuple-element.38), channel_id=1, source_target_pairs={{1,0},{2,1},{3,2},{4,3},{5,4},{6,5},{7,6},{8,7},{9,8},{10,9},{11,1... | collective-permute-start | bytes 262664 | tf_op jit(solution)/shard_map/ppermute | solution.py:24
  81.4 0.1 maximum_select_fusion.1
  81.5 1.8 %collective-permute-done.8 = bf16[3,38,3,128]{3,1,2,0:T(8,128)(2,1)S(1)} collective-permute-done((bf16[3,38,3,128]{3,1,2,0:T(8,128)(2,1)S(1)}, bf16[3,38,3,128]{3,1,2,0:T(8,128)(2,1)S(1)}, u32[]{:S(2)}, u32[]{:S(2)}) %collective-permute-start.8) | collective-permute-done | bytes 87584 | tf_op jit(solution)/shard_map/ppermute | solution.py:21
  83.3 0.2 maximum_select_fusion
  83.5 0.1 slice_bitcast_fusion.2
  83.6 0.5 fusion
  84.2 0.1 copy-done.7
  84.3 0.5 fusion.31
  84.8 0.5 fusion.3
  85.4 0.1 fusion.134
  85.5 0.4 convolution_bitcast_fusion.7
  85.9 0.2 maximum_subtract_fusion
  86.0 1.3 %copy.140 = f32[3,32,16,128]{3,2,1,0:T(8,128)} copy(f32[3,32,16,128]{3,1,2,0:T(8,128)S(1)} %maximum_subtract_fusion) | data formatting | bytes 1572864
  87.4 0.9 copy.141
  (79 shorter events, 1.7 us)
Async XLA Ops:
  0.6 25.0 %copy-start = (bf16[1,32,128,128]{3,2,1,0:T(8,128)(2,1)S(1)}, bf16[1,32,128,128]{3,2,1,0:T(8,128)(2,1)}, u32[]{:S(2)}) copy-start(bf16[1,32,128,128]{3,2,1,0:T(8,128)(2,1)} %param.9) | copy-start | bytes 3145732
  3.2 12.9 %copy-start.4 = (s32[1,32,3]{1,0,2:T(1,128)S(1)}, s32[1,32,3]{1,0,2:T(1,128)}, u32[]{:S(2)}) copy-start(s32[1,32,3]{1,0,2:T(1,128)} %param.13) | copy-start | bytes 1156
  3.2 13.3 %copy-start.5 = (s32[1,32,1]{1,2,0:T(1,128)S(1)}, s32[1,32,1]{1,2,0:T(1,128)}, u32[]{:S(2)}) copy-start(s32[1,32,1]{1,2,0:T(1,128)} %param.11) | copy-start | bytes 388
  3.2 13.5 %copy-start.6 = (s32[1,32]{1,0:T(1,128)S(1)}, s32[1,32]{1,0:T(1,128)}, u32[]{:S(2)}) copy-start(s32[1,32]{1,0:T(1,128)} %param.12) | copy-start | bytes 388
  3.2 14.8 %collective-permute-start.1 = (f32[4,32,1,128]{3,1,2,0:T(8,128)S(1)}, f32[4,32,1,128]{3,1,2,0:T(8,128)S(1)}, u32[]{:S(2)}, u32[]{:S(2)}) collective-permute-start(f32[4,32,1,128]{3,1,2,0:T(8,128)S(1)} %get-tuple-element.35), channel_id=1, source_target_pairs={{1,0},{2,1},{3,2},{4,3},{5,4},{6,5},{7,6},{8,7},{9,8},{10,9},{11,1... | collective-permute-start | bytes 196616 | tf_op jit(solution)/shard_map/ppermute | solution.py:24
  12.1 6.4 %collective-permute-start = (f32[4,32,1,128]{3,1,2,0:T(8,128)S(1)}, f32[4,32,1,128]{3,1,2,0:T(8,128)S(1)}, u32[]{:S(2)}, u32[]{:S(2)}) collective-permute-start(f32[4,32,1,128]{3,1,2,0:T(8,128)S(1)} %get-tuple-element.36), channel_id=1, source_target_pairs={{0,1},{1,2},{2,3},{3,4},{4,5},{5,6},{6,7},{7,8},{8,9},{9,10},{10,1... | collective-permute-start | bytes 196616 | tf_op jit(solution)/shard_map/ppermute | solution.py:21
  12.2 6.4 %collective-permute-start.2 = (f32[4,3,16,128]{3,1,2,0:T(4,128)S(1)}, f32[4,3,16,128]{3,1,2,0:T(4,128)}, u32[]{:S(2)}, u32[]{:S(2)}) collective-permute-start(f32[4,3,16,128]{3,1,2,0:T(4,128)S(1)} %get-tuple-element.34), channel_id=1, source_target_pairs={{32,0},{64,32},{96,64},{128,96},{160,128},{192,160},{224,192},{0,2... | collective-permute-start | bytes 294920 | tf_op jit(solution)/shard_map/ppermute | solution.py:24
  13.2 6.4 %collective-permute-start.3 = (f32[4,3,16,128]{3,1,2,0:T(4,128)S(1)}, f32[4,3,16,128]{3,1,2,0:T(4,128)}, u32[]{:S(2)}, u32[]{:S(2)}) collective-permute-start(f32[4,3,16,128]{3,1,2,0:T(4,128)S(1)} %get-tuple-element.33), channel_id=1, source_target_pairs={{0,32},{32,64},{64,96},{96,128},{128,160},{160,192},{192,224},{224... | collective-permute-start | bytes 294920 | tf_op jit(solution)/shard_map/ppermute | solution.py:21
  20.6 1.0 %copy-start.2 = (f32[32,16,128]{2,0,1:T(8,128)S(1)}, f32[32,16,128]{2,0,1:T(8,128)}, u32[]{:S(2)}) copy-start(f32[32,16,128]{2,0,1:T(8,128)} %copy.117) | copy-start | bytes 786436
  25.7 8.9 %copy-start.3 = (f32[1,32,3,128]{3,1,2,0:T(8,128)S(1)}, f32[1,32,3,128]{3,1,2,0:T(8,128)}, u32[]{:S(2)}) copy-start(f32[1,32,3,128]{3,1,2,0:T(8,128)} %param.10) | copy-start | bytes 147460
  27.7 16.3 %all-to-all-start = ((f32[32,1,1540]{2,1,0:T(1,128)}), f32[32,1,1540]{2,1,0:T(1,128)S(1)}, u32[]{:S(2)}, u32[]{:S(2)}) async-start(f32[32,1,1540]{2,1,0:T(1,128)} %all_to_all.19), calls=%async_computation | async-start | bytes 425984 | tf_op jit(solution)/shard_map/all_to_all | solution.py:170
  46.0 13.0 %all-to-all-start.1 = ((bf16[32,4,384]{2,1,0:T(4,128)(2,1)}), bf16[32,4,384]{2,1,0:T(4,128)(2,1)S(1)}, u32[]{:S(2)}, u32[]{:S(2)}) async-start(bf16[32,4,384]{2,1,0:T(4,128)(2,1)} %all_to_all.16), calls=%async_computation.1 | async-start | bytes 196608 | tf_op jit(solution)/shard_map/all_to_all | solution.py:183
  63.2 1.0 %copy-start.1 = (pred[32,16,512]{2,1,0:T(8,128)(4,1)S(1)}, pred[32,16,512]{2,1,0:T(8,128)(4,1)}, u32[]{:S(2)}) copy-start(pred[32,16,512]{2,1,0:T(8,128)(4,1)} %broadcast_compare_fusion) | copy-start | bytes 786436
  66.5 9.9 %collective-permute-start.6 = (bf16[3,3,16,128]{3,1,2,0:T(4,128)(2,1)S(1)}, bf16[3,3,16,128]{3,1,2,0:T(4,128)(2,1)S(1)}, u32[]{:S(2)}, u32[]{:S(2)}) collective-permute-start(bf16[3,3,16,128]{3,1,2,0:T(4,128)(2,1)S(1)} %get-tuple-element.43), channel_id=1, source_target_pairs={{0,32},{32,64},{64,96},{96,128},{128,160},{160,192},{192,224},{224... | collective-permute-start | bytes 110600 | tf_op jit(solution)/shard_map/ppermute | solution.py:21
  71.5 4.9 %collective-permute-start.7 = (bf16[3,3,16,128]{3,1,2,0:T(4,128)(2,1)S(1)}, bf16[3,3,16,128]{3,1,2,0:T(4,128)(2,1)S(1)}, u32[]{:S(2)}, u32[]{:S(2)}) collective-permute-start(bf16[3,3,16,128]{3,1,2,0:T(4,128)(2,1)S(1)} %get-tuple-element.44), channel_id=1, source_target_pairs={{32,0},{64,32},{96,64},{128,96},{160,128},{192,160},{224,192},{0,2... | collective-permute-start | bytes 110600 | tf_op jit(solution)/shard_map/ppermute | solution.py:24
  71.5 9.8 %collective-permute-start.4 = (f32[38,3,128]{2,0,1:T(8,128)S(1)}, f32[38,3,128]{2,0,1:T(8,128)S(1)}, u32[]{:S(2)}, u32[]{:S(2)}) collective-permute-start(f32[38,3,128]{2,0,1:T(8,128)S(1)} %get-tuple-element.53), channel_id=1, source_target_pairs={{0,1},{1,2},{2,3},{3,4},{4,5},{5,6},{6,7},{7,8},{8,9},{9,10},{10,1... | collective-permute-start | bytes 175112 | tf_op jit(solution)/shard_map/ppermute | solution.py:21
  71.6 9.7 %collective-permute-start.5 = (f32[38,3,128]{2,0,1:T(8,128)S(1)}, f32[38,3,128]{2,0,1:T(8,128)S(1)}, u32[]{:S(2)}, u32[]{:S(2)}) collective-permute-start(f32[38,3,128]{2,0,1:T(8,128)S(1)} %get-tuple-element.54), channel_id=1, source_target_pairs={{1,0},{2,1},{3,2},{4,3},{5,4},{6,5},{7,6},{8,7},{9,8},{10,9},{11,1... | collective-permute-start | bytes 175112 | tf_op jit(solution)/shard_map/ppermute | solution.py:24
  76.5 6.8 %collective-permute-start.8 = (bf16[3,38,3,128]{3,1,2,0:T(8,128)(2,1)S(1)}, bf16[3,38,3,128]{3,1,2,0:T(8,128)(2,1)S(1)}, u32[]{:S(2)}, u32[]{:S(2)}) collective-permute-start(bf16[3,38,3,128]{3,1,2,0:T(8,128)(2,1)S(1)} %get-tuple-element.37), channel_id=1, source_target_pairs={{0,1},{1,2},{2,3},{3,4},{4,5},{5,6},{6,7},{7,8},{8,9},{9,10},{10,1... | collective-permute-start | bytes 262664 | tf_op jit(solution)/shard_map/ppermute | solution.py:21
  76.6 6.7 %collective-permute-start.9 = (bf16[3,38,3,128]{3,1,2,0:T(8,128)(2,1)S(1)}, bf16[3,38,3,128]{3,1,2,0:T(8,128)(2,1)S(1)}, u32[]{:S(2)}, u32[]{:S(2)}) collective-permute-start(bf16[3,38,3,128]{3,1,2,0:T(8,128)(2,1)S(1)} %get-tuple-element.38), channel_id=1, source_target_pairs={{1,0},{2,1},{3,2},{4,3},{5,4},{6,5},{7,6},{8,7},{9,8},{10,9},{11,1... | collective-permute-start | bytes 262664 | tf_op jit(solution)/shard_map/ppermute | solution.py:24
  83.6 0.7 copy-start.7

commit v12 on v11

--- a/solution.py
+++ b/solution.py
@@ -192,10 +192,8 @@
         preferred_element_type=jnp.float32,
     )
     spread_window = spread_force.transpose(1, 0, 2).reshape(fields, pair_total * box_rows, BY)
-    spread_lines = sum(
-        jnp.where(lanes[None, None, :] == line_offset + j, spread_window[:, :, j, None], 0.0)
-        for j in range(BY)
-    )
+    spread_mask = lanes[None, None, :] == line_offset[:, :, None] + jnp.arange(BY, dtype=jnp.int32)[None, :, None]
+    spread_lines = jnp.sum(jnp.where(spread_mask[None], spread_window[..., None], 0.0), axis=2)
     row_place = (
         jnp.arange(row_total, dtype=jnp.int32)[:, None] == rows_of.reshape(-1)[None, :]
     ).astype(jnp.float32)

time: 89.9 us -> 101 us (1.12)
  other arithmetic: 5.83 us -> 18.6 us
  local copies, waits for them, and re-layouts: 17 us -> 13.9 us
    reduce_sum x0 -> x1, other arithmetic: none -> 8.28 us  [body(): jnp.sum(jnp.where(spread_mask[None], spread_window[..., None], 0.0), axis=2)]
    slice x1 -> x0, local copies, waits for them, and re-layouts: 3.19 us -> none  [body(): spread_window[:, :, j, None]]
    eq x0 -> x1, other arithmetic: none -> 1.32 us  [body(): lanes[None, None, :]]
    all_to_all x1, waiting for transfers between devices: 8.6 us -> 9.88 us  [body(): lax.all_to_all(send.reshape(tiles, -1), 'yz', 0, 0, tiled=True)]
    ppermute x5, starting transfers between devices: 6.36 us -> 5.23 us  [faces(): lax.ppermute(lax.slice_in_dim(block, block.shape[dim] - width, None, axis...]
    unnamed x30 -> x62, local copies, waits for them, and re-layouts: 5.89 us -> 5.98 us
  transfers between devices with their start and end apart: 12 -> 12, of which waited for: 4 -> 3; matrix products, arithmetic and copies ran while one was open for 8% -> 12% of each run, Pallas kernels for 0% -> 0%
where the time goes in v12:
time: 101 us; the launch traced here: 99.2 us
  starting transfers between devices  36 us (36%)
  waiting for transfers between devices  19.9 us (20%)
  other arithmetic  18.6 us (18%)
  local copies, waits for them, and re-layouts  13.9 us (14%)
  matrix products  9.54 us (9%)
  between operations  1.4 us (1%)
    ppermute x5, starting transfers between devices, faces(): lax.ppermute(lax.slice_in_dim(block, 0, width, axis=dim).astype(kind), ax...  19.4 us
    all_to_all x1, waiting for transfers between devices, body(): lax.all_to_all(send.reshape(tiles, -1), 'yz', 0, 0, tiled=True)  9.88 us
    reduce_sum x1, other arithmetic, body(): jnp.sum(jnp.where(spread_mask[None], spread_window[..., None], 0.0), axis=2)  8.28 us
    all_to_all x1, waiting for transfers between devices, body(): back = lax.all_to_all(returned, 'yz', 0, 0, tiled=True)  8.14 us
    all_to_all x1, starting transfers between devices, body(): lax.all_to_all(send.reshape(tiles, -1), 'yz', 0, 0, tiled=True)  6.85 us
    unnamed x62, local copies, waits for them, and re-layouts  5.98 us
    ppermute x5, starting transfers between devices, faces(): lax.ppermute(lax.slice_in_dim(block, block.shape[dim] - width, None, axis...  5.23 us
    all_to_all x1, starting transfers between devices, body(): back = lax.all_to_all(returned, 'yz', 0, 0, tiled=True)  4.49 us
  transfers between devices with their start and end apart: 12, of which 3 were waited for; matrix products, arithmetic and copies ran while one was open for 12% of the time, Pallas kernels for 0%

profile of v12, /device:TPU:1, one launch (start us, length us, event | category | flops | bytes accessed | tf_op | source)
XLA Modules:
  0.0 99.2 jit_solution(18411400172115253038)
XLA Ops:
  0.6 1.1 %copy.157 = f32[32,16,128]{2,0,1:T(8,128)S(1)} copy(f32[32,16,128]{2,1,0:T(8,128)} %param.8) | data formatting | bytes 524288 | tf_op args[1]
  1.8 1.4 %copy.106 = f32[3,32,16,128]{3,1,2,0:T(8,128)S(1)} copy(f32[3,32,16,128]{3,2,1,0:T(8,128)} %param.7) | data formatting | bytes 1572864 | tf_op args[0]
  3.2 8.9 %collective-permute-start.1 = (f32[4,32,1,128]{3,1,2,0:T(8,128)S(1)}, f32[4,32,1,128]{3,1,2,0:T(8,128)}, u32[]{:S(2)}, u32[]{:S(2)}) collective-permute-start(f32[4,32,1,128]{3,1,2,0:T(8,128)S(1)} %get-tuple-element.27), channel_id=1, source_target_pairs={{1,0},{2,1},{3,2},{4,3},{5,4},{6,5},{7,6},{8,7},{9,8},{10,9},{11,1... | collective-permute-start | bytes 196616 | tf_op jit(solution)/shard_map/ppermute | solution.py:24
  12.2 1.0 collective-permute-start.2
  13.1 1.1 %collective-permute-start.3 = (f32[4,3,16,128]{3,1,2,0:T(4,128)S(1)}, f32[4,3,16,128]{3,1,2,0:T(4,128)}, u32[]{:S(2)}, u32[]{:S(2)}) collective-permute-start(f32[4,3,16,128]{3,1,2,0:T(4,128)S(1)} %get-tuple-element.25), channel_id=1, source_target_pairs={{0,32},{32,64},{64,96},{96,128},{128,160},{160,192},{192,224},{224... | collective-permute-start | bytes 294920 | tf_op jit(solution)/shard_map/ppermute | solution.py:21
  14.3 0.5 compare_and_fusion.3
  14.8 0.5 broadcast_add_fusion.8
  15.3 0.6 compare_select_fusion
  15.9 1.0 multiply_bitcast_fusion
  16.8 0.6 iota_add_fusion.3
  17.6 0.1 iota_add_fusion
  17.8 0.8 copy.105
  18.8 0.2 convert_reduce_fusion
  19.0 0.6 multiply_add_fusion.1
  19.7 1.3 %iota_compare_fusion = pred[512,8,128]{2,1,0:T(8,128)(4,1)S(1)} fusion(s32[512,8]{1,0:T(8,128)S(1)} %iota_add_fusion), kind=kLoop, calls=%fused_computation.1 | loop fusion | flops 524288 | bytes 540672 | tf_op jit(solution)/shard_map/eq | solution.py:195
  21.2 0.9 broadcast_compare_fusion
  22.2 0.5 compare_and_fusion
  22.7 0.8 broadcast_select_fusion
  23.6 0.9 slice.266
  24.5 0.9 slice.267
  25.7 0.4 copy-done.15
  26.2 0.4 convolution_bitcast_fusion.8
  26.6 1.9 %fusion.136 = (bf16[3,32,16,128]{3,1,2,0:T(8,128)(2,1)S(1)}, f32[3,32,16,128]{3,1,2,0:T(8,128)S(1)}) fusion(f32[1,32,16,128]{3,1,2,0:T(8,128)S(1)} %get-tuple-element.44, f32[1,32,16,128]{3,1,2,0:T(8,128)S(1)} %convolution_bitcast_fusion.8, f32[1,32,16,128]{3,1,2,0:T(8,128)S(1)} %get-tuple-element.43, f32[3,32,16,128]{3,1,2,0:T(8,128)S(1)} %copy.106, ...), kind=kOutput, calls=%fused_computation.274 | convolution fusion | flops 307609600 | bytes 3483904 | tf_op jit(solution)/shard_map/...i,ij->...j/dot_general | solution.py:81
  28.6 0.4 convolution_bitcast_fusion.4
  29.1 0.4 convolution_bitcast_fusion.5
  29.6 0.4 convolution_bitcast_fusion.6
  30.1 0.6 select_reduce_fusion.1
  30.9 0.2 copy.112
  31.1 0.4 convert_element_type.98
  31.5 0.6 fusion.6
  32.1 0.3 fusion.45
  32.4 1.0 %all_to_all.19 = f32[32,1,1540]{2,1,0:T(1,128)} reshape(f32[128,385]{1,0:T(8,128)S(1)} %fusion.45) | data formatting | bytes 394240 | tf_op jit(solution)/shard_map/all_to_all | solution.py:170
  33.5 6.8 %all-to-all-start = ((f32[32,1,1540]{2,1,0:T(1,128)}), f32[32,1,1540]{2,1,0:T(1,128)S(1)}, u32[]{:S(2)}, u32[]{:S(2)}) async-start(f32[32,1,1540]{2,1,0:T(1,128)} %all_to_all.19), calls=%async_computation | async-start | bytes 425984 | tf_op jit(solution)/shard_map/all_to_all | solution.py:170
  40.4 0.8 slice_bitcast_fusion.10
  41.2 9.9 %all-to-all-done = f32[32,1,1540]{2,1,0:T(1,128)S(1)} async-done(((f32[32,1,1540]{2,1,0:T(1,128)}), f32[32,1,1540]{2,1,0:T(1,128)S(1)}, u32[]{:S(2)}, u32[]{:S(2)}) %all-to-all-start) | async-done | bytes 197152 | tf_op jit(solution)/shard_map/all_to_all | solution.py:170
  51.0 0.5 reduce
  51.5 0.1 reshape.471
  51.8 0.2 fusion.4
  52.0 0.3 convolution_convert_fusion
  52.3 0.7 all_to_all.16
  53.0 4.5 %all-to-all-start.1 = ((bf16[32,4,384]{2,1,0:T(4,128)(2,1)}), bf16[32,4,384]{2,1,0:T(4,128)(2,1)S(1)}, u32[]{:S(2)}, u32[]{:S(2)}) async-start(bf16[32,4,384]{2,1,0:T(4,128)(2,1)} %all_to_all.16), calls=%async_computation.1 | async-start | bytes 196608 | tf_op jit(solution)/shard_map/all_to_all | solution.py:183
  57.5 0.8 slice_bitcast_fusion.9
  58.3 8.1 %all-to-all-done.1 = bf16[32,4,384]{2,1,0:T(4,128)(2,1)S(1)} async-done(((bf16[32,4,384]{2,1,0:T(4,128)(2,1)}), bf16[32,4,384]{2,1,0:T(4,128)(2,1)S(1)}, u32[]{:S(2)}, u32[]{:S(2)}) %all-to-all-start.1) | async-done | bytes 98336 | tf_op jit(solution)/shard_map/all_to_all | solution.py:183
  66.4 0.2 convolution_convert_fusion.1
  66.6 0.4 convolution_bitcast_fusion.9
  67.0 0.4 broadcast_in_dim.138
  67.5 8.3 %select_reduce_fusion = f32[3,512,128]{2,1,0:T(8,128)S(1)} fusion(f32[3,512,8]{2,1,0:T(8,128)S(1)} %broadcast_in_dim.138, pred[512,8,128]{2,1,0:T(8,128)(4,1)S(1)} %iota_compare_fusion), kind=kLoop, calls=%fused_computation | loop fusion | flops 2949120 | bytes 1359872 | tf_op jit(solution)/shard_map/reduce_sum | solution.py:196
  75.8 0.7 convolution_bitcast_fusion.3
  76.5 0.7 convolution_bitcast_fusion.2
  77.2 0.7 convolution_bitcast_fusion.1
  77.9 0.2 fusion.131
  78.1 3.9 %collective-permute-start.6 = (bf16[3,3,16,128]{3,1,2,0:T(4,128)(2,1)S(1)}, bf16[3,3,16,128]{3,1,2,0:T(4,128)(2,1)S(1)}, u32[]{:S(2)}, u32[]{:S(2)}) collective-permute-start(bf16[3,3,16,128]{3,1,2,0:T(4,128)(2,1)S(1)} %get-tuple-element.35), channel_id=1, source_target_pairs={{0,32},{32,64},{64,96},{96,128},{128,160},{160,192},{192,224},{224... | collective-permute-start | bytes 110600 | tf_op jit(solution)/shard_map/ppermute | solution.py:21
  82.2 4.7 %collective-permute-start.5 = (f32[38,3,128]{2,0,1:T(8,128)S(1)}, f32[38,3,128]{2,0,1:T(8,128)S(1)}, u32[]{:S(2)}, u32[]{:S(2)}) collective-permute-start(f32[38,3,128]{2,0,1:T(8,128)S(1)} %get-tuple-element.46), channel_id=1, source_target_pairs={{1,0},{2,1},{3,2},{4,3},{5,4},{6,5},{7,6},{8,7},{9,8},{10,9},{11,1... | collective-permute-start | bytes 175112 | tf_op jit(solution)/shard_map/ppermute | solution.py:24
  87.1 4.8 %collective-permute-start.9 = (bf16[3,38,3,128]{3,1,2,0:T(8,128)(2,1)S(1)}, bf16[3,38,3,128]{3,1,2,0:T(8,128)(2,1)S(1)}, u32[]{:S(2)}, u32[]{:S(2)}) collective-permute-start(bf16[3,38,3,128]{3,1,2,0:T(8,128)(2,1)S(1)} %get-tuple-element.30), channel_id=1, source_target_pairs={{1,0},{2,1},{3,2},{4,3},{5,4},{6,5},{7,6},{8,7},{9,8},{10,9},{11,1... | collective-permute-start | bytes 262664 | tf_op jit(solution)/shard_map/ppermute | solution.py:24
  92.0 1.8 %collective-permute-done.8 = bf16[3,38,3,128]{3,1,2,0:T(8,128)(2,1)S(1)} collective-permute-done((bf16[3,38,3,128]{3,1,2,0:T(8,128)(2,1)S(1)}, bf16[3,38,3,128]{3,1,2,0:T(8,128)(2,1)S(1)}, u32[]{:S(2)}, u32[]{:S(2)}) %collective-permute-start.8) | collective-permute-done | bytes 87584 | tf_op jit(solution)/shard_map/ppermute | solution.py:21
  93.9 0.2 maximum_select_fusion
  94.2 0.4 copy-done.10
  94.8 0.5 fusion
  95.3 0.5 fusion.31
  95.9 0.5 fusion.3
  96.5 0.4 convolution_bitcast_fusion.7
  96.9 0.2 maximum_subtract_fusion
  97.1 1.3 %copy.125 = f32[3,32,16,128]{3,2,1,0:T(8,128)} copy(f32[3,32,16,128]{3,1,2,0:T(8,128)S(1)} %maximum_subtract_fusion) | data formatting | bytes 1572864
  98.4 0.9 copy.126
  (112 shorter events, 2.5 us)
Async XLA Ops:
  0.6 30.8 %copy-start = (bf16[1,32,128,128]{3,2,1,0:T(8,128)(2,1)S(1)}, bf16[1,32,128,128]{3,2,1,0:T(8,128)(2,1)}, u32[]{:S(2)}) copy-start(bf16[1,32,128,128]{3,2,1,0:T(8,128)(2,1)} %param.9) | copy-start | bytes 3145732
  3.2 14.3 %copy-start.21 = (s32[1,32,3]{1,0,2:T(1,128)S(1)}, s32[1,32,3]{1,0,2:T(1,128)}, u32[]{:S(2)}) copy-start(s32[1,32,3]{1,0,2:T(1,128)} %param.13) | copy-start | bytes 1156
  3.2 19.5 %collective-permute-start.1 = (f32[4,32,1,128]{3,1,2,0:T(8,128)S(1)}, f32[4,32,1,128]{3,1,2,0:T(8,128)}, u32[]{:S(2)}, u32[]{:S(2)}) collective-permute-start(f32[4,32,1,128]{3,1,2,0:T(8,128)S(1)} %get-tuple-element.27), channel_id=1, source_target_pairs={{1,0},{2,1},{3,2},{4,3},{5,4},{6,5},{7,6},{8,7},{9,8},{10,9},{11,1... | collective-permute-start | bytes 196616 | tf_op jit(solution)/shard_map/ppermute | solution.py:24
  12.1 6.7 %copy-start.22 = (s32[1,32,1]{1,2,0:T(1,128)S(1)}, s32[1,32,1]{1,2,0:T(1,128)}, u32[]{:S(2)}) copy-start(s32[1,32,1]{1,2,0:T(1,128)} %param.11) | copy-start | bytes 388
  12.1 7.4 %copy-start.23 = (s32[1,32]{1,0:T(1,128)S(1)}, s32[1,32]{1,0:T(1,128)}, u32[]{:S(2)}) copy-start(s32[1,32]{1,0:T(1,128)} %param.12) | copy-start | bytes 388
  12.1 11.4 %collective-permute-start = (f32[4,32,1,128]{3,1,2,0:T(8,128)S(1)}, f32[4,32,1,128]{3,1,2,0:T(8,128)S(1)}, u32[]{:S(2)}, u32[]{:S(2)}) collective-permute-start(f32[4,32,1,128]{3,1,2,0:T(8,128)S(1)} %get-tuple-element.28), channel_id=1, source_target_pairs={{0,1},{1,2},{2,3},{3,4},{4,5},{5,6},{6,7},{7,8},{8,9},{9,10},{10,1... | collective-permute-start | bytes 196616 | tf_op jit(solution)/shard_map/ppermute | solution.py:21
  12.2 11.4 %collective-permute-start.2 = (f32[4,3,16,128]{3,1,2,0:T(4,128)S(1)}, f32[4,3,16,128]{3,1,2,0:T(4,128)}, u32[]{:S(2)}, u32[]{:S(2)}) collective-permute-start(f32[4,3,16,128]{3,1,2,0:T(4,128)S(1)} %get-tuple-element.26), channel_id=1, source_target_pairs={{32,0},{64,32},{96,64},{128,96},{160,128},{192,160},{224,192},{0,2... | collective-permute-start | bytes 294920 | tf_op jit(solution)/shard_map/ppermute | solution.py:24
  13.1 11.4 %collective-permute-start.3 = (f32[4,3,16,128]{3,1,2,0:T(4,128)S(1)}, f32[4,3,16,128]{3,1,2,0:T(4,128)}, u32[]{:S(2)}, u32[]{:S(2)}) collective-permute-start(f32[4,3,16,128]{3,1,2,0:T(4,128)S(1)} %get-tuple-element.25), channel_id=1, source_target_pairs={{0,32},{32,64},{64,96},{96,128},{128,160},{160,192},{192,224},{224... | collective-permute-start | bytes 294920 | tf_op jit(solution)/shard_map/ppermute | solution.py:21
  14.3 12.3 %copy-start.9 = (s32[128]{0:T(128)}, s32[128]{0:T(128)S(1)}, u32[]{:S(2)}) copy-start(s32[128]{0:T(128)S(1)} %get-tuple-element.61) | copy-start | bytes 1540
  14.3 12.3 %copy-start.11 = (s32[128]{0:T(128)}, s32[128]{0:T(128)S(1)}, u32[]{:S(2)}) copy-start(s32[128]{0:T(128)S(1)} %get-tuple-element.62) | copy-start | bytes 1540
  14.8 11.8 %copy-start.13 = (pred[128]{0:T(512)(128)(4,1)}, pred[128]{0:T(512)(128)(4,1)S(1)}, u32[]{:S(2)}) copy-start(pred[128]{0:T(512)(128)(4,1)S(1)} %get-tuple-element.63) | copy-start | bytes 388
  18.7 6.9 %copy-start.4 = (s32[512]{0:T(512)}, s32[512]{0:T(512)S(1)}, u32[]{:S(2)}) copy-start(s32[512]{0:T(512)S(1)} %add.424) | copy-start | bytes 6148
  25.5 0.6 copy-start.15
  25.5 0.6 copy-start.17
  25.5 0.7 copy-start.19
  25.6 1.0 copy-start.2
  26.6 2.0 %copy-start.5 = (s32[512]{0:T(512)S(1)}, s32[512]{0:T(512)}, u32[]{:S(2)}) copy-start(s32[512]{0:T(512)} %copy-done.4) | copy-start | bytes 6148
  30.7 1.4 %copy-start.8 = (s32[32]{0:T(128)S(1)}, s32[32]{0:T(128)}, u32[]{:S(2)}) copy-start(s32[32]{0:T(128)} %multiply_add_fusion.1) | copy-start | bytes 388
  31.5 8.9 %copy-start.3 = (f32[1,32,3,128]{3,1,2,0:T(8,128)S(1)}, f32[1,32,3,128]{3,1,2,0:T(8,128)}, u32[]{:S(2)}) copy-start(f32[1,32,3,128]{3,1,2,0:T(8,128)} %param.10) | copy-start | bytes 147460
  32.1 19.7 %copy-start.7 = (f32[32]{0:T(128)S(1)}, f32[32]{0:T(128)}, u32[]{:S(2)}) copy-start(f32[32]{0:T(128)} %iota_add_fusion.3) | copy-start | bytes 388
  33.5 17.6 %all-to-all-start = ((f32[32,1,1540]{2,1,0:T(1,128)}), f32[32,1,1540]{2,1,0:T(1,128)S(1)}, u32[]{:S(2)}, u32[]{:S(2)}) async-start(f32[32,1,1540]{2,1,0:T(1,128)} %all_to_all.19), calls=%async_computation | async-start | bytes 425984 | tf_op jit(solution)/shard_map/all_to_all | solution.py:170
  53.0 13.4 %all-to-all-start.1 = ((bf16[32,4,384]{2,1,0:T(4,128)(2,1)}), bf16[32,4,384]{2,1,0:T(4,128)(2,1)S(1)}, u32[]{:S(2)}, u32[]{:S(2)}) async-start(bf16[32,4,384]{2,1,0:T(4,128)(2,1)} %all_to_all.16), calls=%async_computation.1 | async-start | bytes 196608 | tf_op jit(solution)/shard_map/all_to_all | solution.py:183
  67.5 8.3 %copy-start.1 = (pred[32,16,512]{2,1,0:T(8,128)(4,1)S(1)}, pred[32,16,512]{2,1,0:T(8,128)(4,1)}, u32[]{:S(2)}) copy-start(pred[32,16,512]{2,1,0:T(8,128)(4,1)} %broadcast_compare_fusion) | copy-start | bytes 786436
  78.0 13.8 %copy-start.6 = (pred[22]{0:T(512)(128)(4,1)S(1)}, pred[22]{0:T(512)(128)(4,1)}, u32[]{:S(2)}) copy-start(pred[22]{0:T(512)(128)(4,1)} %compare_and_fusion) | copy-start | bytes 70
  78.1 8.8 %collective-permute-start.6 = (bf16[3,3,16,128]{3,1,2,0:T(4,128)(2,1)S(1)}, bf16[3,3,16,128]{3,1,2,0:T(4,128)(2,1)S(1)}, u32[]{:S(2)}, u32[]{:S(2)}) collective-permute-start(bf16[3,3,16,128]{3,1,2,0:T(4,128)(2,1)S(1)} %get-tuple-element.35), channel_id=1, source_target_pairs={{0,32},{32,64},{64,96},{96,128},{128,160},{160,192},{192,224},{224... | collective-permute-start | bytes 110600 | tf_op jit(solution)/shard_map/ppermute | solution.py:21
  82.0 4.9 %collective-permute-start.7 = (bf16[3,3,16,128]{3,1,2,0:T(4,128)(2,1)S(1)}, bf16[3,3,16,128]{3,1,2,0:T(4,128)(2,1)S(1)}, u32[]{:S(2)}, u32[]{:S(2)}) collective-permute-start(bf16[3,3,16,128]{3,1,2,0:T(4,128)(2,1)S(1)} %get-tuple-element.36), channel_id=1, source_target_pairs={{32,0},{64,32},{96,64},{128,96},{160,128},{192,160},{224,192},{0,2... | collective-permute-start | bytes 110600 | tf_op jit(solution)/shard_map/ppermute | solution.py:24
  82.0 9.8 %collective-permute-start.4 = (f32[38,3,128]{2,0,1:T(8,128)S(1)}, f32[38,3,128]{2,0,1:T(8,128)S(1)}, u32[]{:S(2)}, u32[]{:S(2)}) collective-permute-start(f32[38,3,128]{2,0,1:T(8,128)S(1)} %get-tuple-element.45), channel_id=1, source_target_pairs={{0,1},{1,2},{2,3},{3,4},{4,5},{5,6},{6,7},{7,8},{8,9},{9,10},{10,1... | collective-permute-start | bytes 175112 | tf_op jit(solution)/shard_map/ppermute | solution.py:21
  82.2 9.7 %collective-permute-start.5 = (f32[38,3,128]{2,0,1:T(8,128)S(1)}, f32[38,3,128]{2,0,1:T(8,128)S(1)}, u32[]{:S(2)}, u32[]{:S(2)}) collective-permute-start(f32[38,3,128]{2,0,1:T(8,128)S(1)} %get-tuple-element.46), channel_id=1, source_target_pairs={{1,0},{2,1},{3,2},{4,3},{5,4},{6,5},{7,6},{8,7},{9,8},{10,9},{11,1... | collective-permute-start | bytes 175112 | tf_op jit(solution)/shard_map/ppermute | solution.py:24
  87.0 6.8 %collective-permute-start.8 = (bf16[3,38,3,128]{3,1,2,0:T(8,128)(2,1)S(1)}, bf16[3,38,3,128]{3,1,2,0:T(8,128)(2,1)S(1)}, u32[]{:S(2)}, u32[]{:S(2)}) collective-permute-start(bf16[3,38,3,128]{3,1,2,0:T(8,128)(2,1)S(1)} %get-tuple-element.29), channel_id=1, source_target_pairs={{0,1},{1,2},{2,3},{3,4},{4,5},{5,6},{6,7},{7,8},{8,9},{9,10},{10,1... | collective-permute-start | bytes 262664 | tf_op jit(solution)/shard_map/ppermute | solution.py:21
  87.1 6.7 %collective-permute-start.9 = (bf16[3,38,3,128]{3,1,2,0:T(8,128)(2,1)S(1)}, bf16[3,38,3,128]{3,1,2,0:T(8,128)(2,1)S(1)}, u32[]{:S(2)}, u32[]{:S(2)}) collective-permute-start(bf16[3,38,3,128]{3,1,2,0:T(8,128)(2,1)S(1)} %get-tuple-element.30), channel_id=1, source_target_pairs={{1,0},{2,1},{3,2},{4,3},{5,4},{6,5},{7,6},{8,7},{9,8},{10,9},{11,1... | collective-permute-start | bytes 262664 | tf_op jit(solution)/shard_map/ppermute | solution.py:24
  94.1 0.6 copy-start.10
  94.1 0.7 copy-start.12
  94.1 0.7 copy-start.14
  94.1 0.7 copy-start.16
  94.1 0.6 copy-start.18
  94.1 0.7 copy-start.20

commit v13 on v11

--- a/solution.py
+++ b/solution.py
@@ -79,7 +79,7 @@
     below = (source == (target + size - 1) % size).astype(jnp.float32)
     matrix = weights[0] * above + weights[1] * below
     return jnp.einsum(
-        "...i,ij->...j", field, matrix, precision=lax.Precision.HIGHEST, preferred_element_type=jnp.float32
+        "...i,ij->...j", field, matrix, precision=lax.Precision.HIGH, preferred_element_type=jnp.float32
     )
 
 

time: 89.9 us -> 89.2 us (level)
  matrix products: 8.84 us -> 7.81 us
    dot_general x6, matrix products: 3.5 us -> 2.47 us  [across_y(): jnp.einsum('...i,ij->...j', field, matrix, precision=lax.Precision.HIGH,...]
where the time goes in v13:
time: 89.2 us; the launch traced here: 87.5 us
  starting transfers between devices  36.1 us (40%)
  waiting for transfers between devices  19.2 us (22%)
  local copies, waits for them, and re-layouts  17.3 us (19%)
  matrix products  7.81 us (9%)
  other arithmetic  5.83 us (7%)
  between operations  1.24 us (1%)
    ppermute x5, starting transfers between devices, faces(): lax.ppermute(lax.slice_in_dim(block, 0, width, axis=dim).astype(kind), ax...  19.4 us
    all_to_all x1, waiting for transfers between devices, body(): lax.all_to_all(send.reshape(tiles, -1), 'yz', 0, 0, tiled=True)  8.6 us
    all_to_all x1, waiting for transfers between devices, body(): back = lax.all_to_all(returned, 'yz', 0, 0, tiled=True)  8.18 us
    ppermute x5, starting transfers between devices, faces(): lax.ppermute(lax.slice_in_dim(block, block.shape[dim] - width, None, axis...  6.37 us
    all_to_all x1, starting transfers between devices, body(): lax.all_to_all(send.reshape(tiles, -1), 'yz', 0, 0, tiled=True)  6.32 us
    unnamed x30, local copies, waits for them, and re-layouts  6.17 us
    all_to_all x1, starting transfers between devices, body(): back = lax.all_to_all(returned, 'yz', 0, 0, tiled=True)  4.04 us
    slice x1, local copies, waits for them, and re-layouts, body(): spread_window[:, :, j, None]  3.19 us
  transfers between devices with their start and end apart: 12, of which 4 were waited for; matrix products, arithmetic and copies ran while one was open for 8% of the time, Pallas kernels for 0%

profile of v13, /device:TPU:1, one launch (start us, length us, event | category | flops | bytes accessed | tf_op | source)
XLA Modules:
  0.0 87.5 jit_solution(17611234817869564121)
XLA Ops:
  0.6 1.1 %copy.178 = f32[32,16,128]{2,0,1:T(8,128)S(1)} copy(f32[32,16,128]{2,1,0:T(8,128)} %param.8) | data formatting | bytes 524288 | tf_op args[1]
  1.8 1.4 %copy.118 = f32[3,32,16,128]{3,1,2,0:T(8,128)S(1)} copy(f32[3,32,16,128]{3,2,1,0:T(8,128)} %param.7) | data formatting | bytes 1572864 | tf_op args[0]
  3.2 8.9 %collective-permute-start.1 = (f32[4,32,1,128]{3,1,2,0:T(8,128)S(1)}, f32[4,32,1,128]{3,1,2,0:T(8,128)S(1)}, u32[]{:S(2)}, u32[]{:S(2)}) collective-permute-start(f32[4,32,1,128]{3,1,2,0:T(8,128)S(1)} %get-tuple-element.35), channel_id=1, source_target_pairs={{1,0},{2,1},{3,2},{4,3},{5,4},{6,5},{7,6},{8,7},{9,8},{10,9},{11,1... | collective-permute-start | bytes 196616 | tf_op jit(solution)/shard_map/ppermute | solution.py:24
  12.2 1.0 %collective-permute-start.2 = (f32[4,3,16,128]{3,1,2,0:T(4,128)S(1)}, f32[4,3,16,128]{3,1,2,0:T(4,128)}, u32[]{:S(2)}, u32[]{:S(2)}) collective-permute-start(f32[4,3,16,128]{3,1,2,0:T(4,128)S(1)} %get-tuple-element.34), channel_id=1, source_target_pairs={{32,0},{64,32},{96,64},{128,96},{160,128},{192,160},{224,192},{0,2... | collective-permute-start | bytes 294920 | tf_op jit(solution)/shard_map/ppermute | solution.py:24
  13.2 1.1 %collective-permute-start.3 = (f32[4,3,16,128]{3,1,2,0:T(4,128)S(1)}, f32[4,3,16,128]{3,1,2,0:T(4,128)}, u32[]{:S(2)}, u32[]{:S(2)}) collective-permute-start(f32[4,3,16,128]{3,1,2,0:T(4,128)S(1)} %get-tuple-element.33), channel_id=1, source_target_pairs={{0,32},{32,64},{64,96},{96,128},{128,160},{160,192},{192,224},{224... | collective-permute-start | bytes 294920 | tf_op jit(solution)/shard_map/ppermute | solution.py:21
  14.3 1.0 %multiply_bitcast_fusion = f32[32,16,128]{2,1,0:T(8,128)S(1)} fusion(f32[3,32,16,128]{3,2,1,0:T(8,128)} %param.7), kind=kLoop, calls=%fused_computation.125 | loop fusion | flops 65536 | bytes 524288 | tf_op jit(solution)/shard_map/mul | solution.py:107
  15.3 0.8 copy.117
  16.5 0.2 convert_reduce_fusion
  17.1 0.9 %broadcast_compare_fusion = pred[32,16,512]{2,1,0:T(8,128)(4,1)} fusion(s32[512]{0:T(512)S(1)} %add.411, s32[32,16]{1,0:T(8,128)S(1)} %multiply_add_fusion), kind=kLoop, calls=%fused_computation.72 | loop fusion | flops 262144 | bytes 266240 | tf_op jit(solution)/shard_map/eq | solution.py:200
  18.0 0.5 collective-permute-done
  18.6 0.9 %slice.298 = f32[4,1,16,128]{3,1,2,0:T(1,128)S(1)} slice(f32[4,3,16,128]{3,1,2,0:T(4,128)} %collective-permute-done.2), slice={[0:4], [0:1], [0:16], [0:128]} | slice | bytes 65536 | tf_op jit(solution)/shard_map/slice | solution.py:116
  19.6 0.9 %slice.299 = f32[4,1,16,128]{3,1,2,0:T(1,128)S(1)} slice(f32[4,3,16,128]{3,1,2,0:T(4,128)} %collective-permute-done.3), slice={[0:4], [2:3], [0:16], [0:128]} | slice | bytes 65536 | tf_op jit(solution)/shard_map/slice | solution.py:116
  20.7 0.3 convolution_bitcast_fusion.8
  21.0 0.6 copy-done.2
  21.6 0.9 fusion.136
  22.5 0.4 convolution_bitcast_fusion.4
  23.0 0.4 convolution_bitcast_fusion.5
  23.5 0.4 convolution_bitcast_fusion.6
  24.0 0.6 select_reduce_fusion
  24.7 0.2 copy.124
  25.0 0.4 convert_element_type.98
  25.4 0.6 fusion.6
  26.0 0.3 fusion.45
  26.3 1.0 %all_to_all.19 = f32[32,1,1540]{2,1,0:T(1,128)} reshape(f32[128,385]{1,0:T(8,128)S(1)} %fusion.45) | data formatting | bytes 394240 | tf_op jit(solution)/shard_map/all_to_all | solution.py:170
  27.3 6.3 %all-to-all-start = ((f32[32,1,1540]{2,1,0:T(1,128)}), f32[32,1,1540]{2,1,0:T(1,128)S(1)}, u32[]{:S(2)}, u32[]{:S(2)}) async-start(f32[32,1,1540]{2,1,0:T(1,128)} %all_to_all.19), calls=%async_computation | async-start | bytes 425984 | tf_op jit(solution)/shard_map/all_to_all | solution.py:170
  33.7 0.6 compare_and_fusion.1
  34.3 0.8 slice_bitcast_fusion.10
  35.1 8.6 %all-to-all-done = f32[32,1,1540]{2,1,0:T(1,128)S(1)} async-done(((f32[32,1,1540]{2,1,0:T(1,128)}), f32[32,1,1540]{2,1,0:T(1,128)S(1)}, u32[]{:S(2)}, u32[]{:S(2)}) %all-to-all-start) | async-done | bytes 197152 | tf_op jit(solution)/shard_map/all_to_all | solution.py:170
  43.7 0.5 reduce
  44.2 0.1 reshape.468
  44.3 0.1 slice_reduce_fusion.8
  44.4 0.2 fusion.4
  44.7 0.3 convolution_convert_fusion
  45.0 0.7 all_to_all.16
  45.6 4.0 %all-to-all-start.1 = ((bf16[32,4,384]{2,1,0:T(4,128)(2,1)}), bf16[32,4,384]{2,1,0:T(4,128)(2,1)S(1)}, u32[]{:S(2)}, u32[]{:S(2)}) async-start(bf16[32,4,384]{2,1,0:T(4,128)(2,1)} %all_to_all.16), calls=%async_computation.1 | async-start | bytes 196608 | tf_op jit(solution)/shard_map/all_to_all | solution.py:183
  49.7 0.8 slice_bitcast_fusion.9
  50.4 8.2 %all-to-all-done.1 = bf16[32,4,384]{2,1,0:T(4,128)(2,1)S(1)} async-done(((bf16[32,4,384]{2,1,0:T(4,128)(2,1)}), bf16[32,4,384]{2,1,0:T(4,128)(2,1)S(1)}, u32[]{:S(2)}, u32[]{:S(2)}) %all-to-all-start.1) | async-done | bytes 98336 | tf_op jit(solution)/shard_map/all_to_all | solution.py:183
  58.7 0.2 convolution_convert_fusion.1
  58.9 0.4 convolution_bitcast_fusion.9
  59.2 0.4 reshape.470
  59.7 3.2 %slice_reduce_fusion.7 = (f32[3,512]{1,0:T(4,128)S(1)}, f32[3,512]{1,0:T(4,128)S(1)}, f32[3,512]{1,0:T(4,128)S(1)}, f32[3,512]{1,0:T(4,128)S(1)}, f32[3,512]{1,0...) fusion(f32[3,512,8]{2,1,0:T(8,128)S(1)} %reshape.470), kind=kLoop, calls=%fused_computation.32 | loop fusion | bytes 98304 | tf_op jit(solution)/shard_map/slice | solution.py:196
  62.9 0.5 select_add_fusion
  63.4 0.4 copy-done.1
  63.8 0.7 convolution_bitcast_fusion.3
  64.5 0.7 convolution_bitcast_fusion.2
  65.2 0.7 convolution_bitcast_fusion.1
  65.9 0.2 fusion.131
  66.1 5.0 %collective-permute-start.6 = (bf16[3,3,16,128]{3,1,2,0:T(4,128)(2,1)S(1)}, bf16[3,3,16,128]{3,1,2,0:T(4,128)(2,1)S(1)}, u32[]{:S(2)}, u32[]{:S(2)}) collective-permute-start(bf16[3,3,16,128]{3,1,2,0:T(4,128)(2,1)S(1)} %get-tuple-element.43), channel_id=1, source_target_pairs={{0,32},{32,64},{64,96},{96,128},{128,160},{160,192},{192,224},{224... | collective-permute-start | bytes 110600 | tf_op jit(solution)/shard_map/ppermute | solution.py:21
  71.2 0.1 collective-permute-start.4
  71.3 4.7 %collective-permute-start.5 = (f32[38,3,128]{2,0,1:T(8,128)S(1)}, f32[38,3,128]{2,0,1:T(8,128)S(1)}, u32[]{:S(2)}, u32[]{:S(2)}) collective-permute-start(f32[38,3,128]{2,0,1:T(8,128)S(1)} %get-tuple-element.54), channel_id=1, source_target_pairs={{1,0},{2,1},{3,2},{4,3},{5,4},{6,5},{7,6},{8,7},{9,8},{10,9},{11,1... | collective-permute-start | bytes 175112 | tf_op jit(solution)/shard_map/ppermute | solution.py:24
  76.3 4.8 %collective-permute-start.9 = (bf16[3,38,3,128]{3,1,2,0:T(8,128)(2,1)S(1)}, bf16[3,38,3,128]{3,1,2,0:T(8,128)(2,1)S(1)}, u32[]{:S(2)}, u32[]{:S(2)}) collective-permute-start(bf16[3,38,3,128]{3,1,2,0:T(8,128)(2,1)S(1)} %get-tuple-element.38), channel_id=1, source_target_pairs={{1,0},{2,1},{3,2},{4,3},{5,4},{6,5},{7,6},{8,7},{9,8},{10,9},{11,1... | collective-permute-start | bytes 262664 | tf_op jit(solution)/shard_map/ppermute | solution.py:24
  81.0 0.1 maximum_select_fusion.1
  81.1 1.8 %collective-permute-done.8 = bf16[3,38,3,128]{3,1,2,0:T(8,128)(2,1)S(1)} collective-permute-done((bf16[3,38,3,128]{3,1,2,0:T(8,128)(2,1)S(1)}, bf16[3,38,3,128]{3,1,2,0:T(8,128)(2,1)S(1)}, u32[]{:S(2)}, u32[]{:S(2)}) %collective-permute-start.8) | collective-permute-done | bytes 87584 | tf_op jit(solution)/shard_map/ppermute | solution.py:21
  83.0 0.2 maximum_select_fusion
  83.2 0.1 slice_bitcast_fusion.2
  83.3 0.4 fusion
  83.7 0.3 copy-done.7
  84.0 0.4 fusion.31
  84.4 0.4 fusion.3
  84.7 0.1 fusion.134
  84.8 0.3 convolution_bitcast_fusion.7
  85.1 0.2 maximum_subtract_fusion
  85.3 1.3 %copy.140 = f32[3,32,16,128]{3,2,1,0:T(8,128)} copy(f32[3,32,16,128]{3,1,2,0:T(8,128)S(1)} %maximum_subtract_fusion) | data formatting | bytes 1572864
  86.6 0.9 copy.141
  (79 shorter events, 1.7 us)
Async XLA Ops:
  0.6 24.7 %copy-start = (bf16[1,32,128,128]{3,2,1,0:T(8,128)(2,1)S(1)}, bf16[1,32,128,128]{3,2,1,0:T(8,128)(2,1)}, u32[]{:S(2)}) copy-start(bf16[1,32,128,128]{3,2,1,0:T(8,128)(2,1)} %param.9) | copy-start | bytes 3145732
  3.2 12.9 %copy-start.4 = (s32[1,32,3]{1,0,2:T(1,128)S(1)}, s32[1,32,3]{1,0,2:T(1,128)}, u32[]{:S(2)}) copy-start(s32[1,32,3]{1,0,2:T(1,128)} %param.13) | copy-start | bytes 1156
  3.2 13.3 %copy-start.5 = (s32[1,32,1]{1,2,0:T(1,128)S(1)}, s32[1,32,1]{1,2,0:T(1,128)}, u32[]{:S(2)}) copy-start(s32[1,32,1]{1,2,0:T(1,128)} %param.11) | copy-start | bytes 388
  3.2 13.5 %copy-start.6 = (s32[1,32]{1,0:T(1,128)S(1)}, s32[1,32]{1,0:T(1,128)}, u32[]{:S(2)}) copy-start(s32[1,32]{1,0:T(1,128)} %param.12) | copy-start | bytes 388
  3.2 14.8 %collective-permute-start.1 = (f32[4,32,1,128]{3,1,2,0:T(8,128)S(1)}, f32[4,32,1,128]{3,1,2,0:T(8,128)S(1)}, u32[]{:S(2)}, u32[]{:S(2)}) collective-permute-start(f32[4,32,1,128]{3,1,2,0:T(8,128)S(1)} %get-tuple-element.35), channel_id=1, source_target_pairs={{1,0},{2,1},{3,2},{4,3},{5,4},{6,5},{7,6},{8,7},{9,8},{10,9},{11,1... | collective-permute-start | bytes 196616 | tf_op jit(solution)/shard_map/ppermute | solution.py:24
  12.1 6.4 %collective-permute-start = (f32[4,32,1,128]{3,1,2,0:T(8,128)S(1)}, f32[4,32,1,128]{3,1,2,0:T(8,128)S(1)}, u32[]{:S(2)}, u32[]{:S(2)}) collective-permute-start(f32[4,32,1,128]{3,1,2,0:T(8,128)S(1)} %get-tuple-element.36), channel_id=1, source_target_pairs={{0,1},{1,2},{2,3},{3,4},{4,5},{5,6},{6,7},{7,8},{8,9},{9,10},{10,1... | collective-permute-start | bytes 196616 | tf_op jit(solution)/shard_map/ppermute | solution.py:21
  12.2 6.4 %collective-permute-start.2 = (f32[4,3,16,128]{3,1,2,0:T(4,128)S(1)}, f32[4,3,16,128]{3,1,2,0:T(4,128)}, u32[]{:S(2)}, u32[]{:S(2)}) collective-permute-start(f32[4,3,16,128]{3,1,2,0:T(4,128)S(1)} %get-tuple-element.34), channel_id=1, source_target_pairs={{32,0},{64,32},{96,64},{128,96},{160,128},{192,160},{224,192},{0,2... | collective-permute-start | bytes 294920 | tf_op jit(solution)/shard_map/ppermute | solution.py:24
  13.2 6.4 %collective-permute-start.3 = (f32[4,3,16,128]{3,1,2,0:T(4,128)S(1)}, f32[4,3,16,128]{3,1,2,0:T(4,128)}, u32[]{:S(2)}, u32[]{:S(2)}) collective-permute-start(f32[4,3,16,128]{3,1,2,0:T(4,128)S(1)} %get-tuple-element.33), channel_id=1, source_target_pairs={{0,32},{32,64},{64,96},{96,128},{128,160},{160,192},{192,224},{224... | collective-permute-start | bytes 294920 | tf_op jit(solution)/shard_map/ppermute | solution.py:21
  20.6 1.0 %copy-start.2 = (f32[32,16,128]{2,0,1:T(8,128)S(1)}, f32[32,16,128]{2,0,1:T(8,128)}, u32[]{:S(2)}) copy-start(f32[32,16,128]{2,0,1:T(8,128)} %copy.117) | copy-start | bytes 786436
  25.4 8.9 %copy-start.3 = (f32[1,32,3,128]{3,1,2,0:T(8,128)S(1)}, f32[1,32,3,128]{3,1,2,0:T(8,128)}, u32[]{:S(2)}) copy-start(f32[1,32,3,128]{3,1,2,0:T(8,128)} %param.10) | copy-start | bytes 147460
  27.3 16.3 %all-to-all-start = ((f32[32,1,1540]{2,1,0:T(1,128)}), f32[32,1,1540]{2,1,0:T(1,128)S(1)}, u32[]{:S(2)}, u32[]{:S(2)}) async-start(f32[32,1,1540]{2,1,0:T(1,128)} %all_to_all.19), calls=%async_computation | async-start | bytes 425984 | tf_op jit(solution)/shard_map/all_to_all | solution.py:170
  45.6 13.0 %all-to-all-start.1 = ((bf16[32,4,384]{2,1,0:T(4,128)(2,1)}), bf16[32,4,384]{2,1,0:T(4,128)(2,1)S(1)}, u32[]{:S(2)}, u32[]{:S(2)}) async-start(bf16[32,4,384]{2,1,0:T(4,128)(2,1)} %all_to_all.16), calls=%async_computation.1 | async-start | bytes 196608 | tf_op jit(solution)/shard_map/all_to_all | solution.py:183
  62.9 1.0 %copy-start.1 = (pred[32,16,512]{2,1,0:T(8,128)(4,1)S(1)}, pred[32,16,512]{2,1,0:T(8,128)(4,1)}, u32[]{:S(2)}) copy-start(pred[32,16,512]{2,1,0:T(8,128)(4,1)} %broadcast_compare_fusion) | copy-start | bytes 786436
  66.1 9.9 %collective-permute-start.6 = (bf16[3,3,16,128]{3,1,2,0:T(4,128)(2,1)S(1)}, bf16[3,3,16,128]{3,1,2,0:T(4,128)(2,1)S(1)}, u32[]{:S(2)}, u32[]{:S(2)}) collective-permute-start(bf16[3,3,16,128]{3,1,2,0:T(4,128)(2,1)S(1)} %get-tuple-element.43), channel_id=1, source_target_pairs={{0,32},{32,64},{64,96},{96,128},{128,160},{160,192},{192,224},{224... | collective-permute-start | bytes 110600 | tf_op jit(solution)/shard_map/ppermute | solution.py:21
  71.2 4.9 %collective-permute-start.7 = (bf16[3,3,16,128]{3,1,2,0:T(4,128)(2,1)S(1)}, bf16[3,3,16,128]{3,1,2,0:T(4,128)(2,1)S(1)}, u32[]{:S(2)}, u32[]{:S(2)}) collective-permute-start(bf16[3,3,16,128]{3,1,2,0:T(4,128)(2,1)S(1)} %get-tuple-element.44), channel_id=1, source_target_pairs={{32,0},{64,32},{96,64},{128,96},{160,128},{192,160},{224,192},{0,2... | collective-permute-start | bytes 110600 | tf_op jit(solution)/shard_map/ppermute | solution.py:24
  71.2 9.8 %collective-permute-start.4 = (f32[38,3,128]{2,0,1:T(8,128)S(1)}, f32[38,3,128]{2,0,1:T(8,128)S(1)}, u32[]{:S(2)}, u32[]{:S(2)}) collective-permute-start(f32[38,3,128]{2,0,1:T(8,128)S(1)} %get-tuple-element.53), channel_id=1, source_target_pairs={{0,1},{1,2},{2,3},{3,4},{4,5},{5,6},{6,7},{7,8},{8,9},{9,10},{10,1... | collective-permute-start | bytes 175112 | tf_op jit(solution)/shard_map/ppermute | solution.py:21
  71.3 9.7 %collective-permute-start.5 = (f32[38,3,128]{2,0,1:T(8,128)S(1)}, f32[38,3,128]{2,0,1:T(8,128)S(1)}, u32[]{:S(2)}, u32[]{:S(2)}) collective-permute-start(f32[38,3,128]{2,0,1:T(8,128)S(1)} %get-tuple-element.54), channel_id=1, source_target_pairs={{1,0},{2,1},{3,2},{4,3},{5,4},{6,5},{7,6},{8,7},{9,8},{10,9},{11,1... | collective-permute-start | bytes 175112 | tf_op jit(solution)/shard_map/ppermute | solution.py:24
  76.2 6.8 %collective-permute-start.8 = (bf16[3,38,3,128]{3,1,2,0:T(8,128)(2,1)S(1)}, bf16[3,38,3,128]{3,1,2,0:T(8,128)(2,1)S(1)}, u32[]{:S(2)}, u32[]{:S(2)}) collective-permute-start(bf16[3,38,3,128]{3,1,2,0:T(8,128)(2,1)S(1)} %get-tuple-element.37), channel_id=1, source_target_pairs={{0,1},{1,2},{2,3},{3,4},{4,5},{5,6},{6,7},{7,8},{8,9},{9,10},{10,1... | collective-permute-start | bytes 262664 | tf_op jit(solution)/shard_map/ppermute | solution.py:21
  76.3 6.7 %collective-permute-start.9 = (bf16[3,38,3,128]{3,1,2,0:T(8,128)(2,1)S(1)}, bf16[3,38,3,128]{3,1,2,0:T(8,128)(2,1)S(1)}, u32[]{:S(2)}, u32[]{:S(2)}) collective-permute-start(bf16[3,38,3,128]{3,1,2,0:T(8,128)(2,1)S(1)} %get-tuple-element.38), channel_id=1, source_target_pairs={{1,0},{2,1},{3,2},{4,3},{5,4},{6,5},{7,6},{8,7},{9,8},{10,9},{11,1... | collective-permute-start | bytes 262664 | tf_op jit(solution)/shard_map/ppermute | solution.py:24
  83.3 0.7 copy-start.7
